TPU v7x, 32 devices: a whole 2x2x4 slice. The times are simulated.
32 devices in a mesh: dp: 2 (over x), seq: 16 (over z, y, core).
Axes of the slice: x: 2, y: 2, z: 4, core: 2. Of those that a mesh axis runs over, the one named last changes fastest.
Arguments:
- frames: bfloat16 [2, 16, 64, 48, 128], P('dp', None, 'seq'), may hold values from -6 to 6
- frame_counts: int32 [2, 4], P('dp'), may hold values from 1 to 12, 16 in all within a row
- clip_group: int32 [2, 4], P('dp'), may hold values 0 or 1
- timesteps: int32 [2, 4], P('dp'), may hold values from 0 to 999
- owner_map: int32 [2, 16, 192, 1], P('dp', 'seq'), may hold values from 0 to 15; in each aligned block of 192 rows (0 to 191, 192 to 383, ..., all dimensions but the last counted through in order) at most 18 rows name the same one
- conv_weight: bfloat16 [3, 3, 3, 128, 128], replicated, may hold values from -0.109375 to 0.109375
- w_latent: bfloat16 [2048, 64], replicated, may hold values from -0.125 to 0.125
- hidden: bfloat16 [2, 4608, 3072], P('dp', 'seq'), may hold values from -6 to 6
- noise: float32 [2, 4608, 64], P('dp', 'seq'), may hold values from -6 to 6
- teacher: float32 [2, 4608, 64], P('dp', 'seq'), may hold values from -6 to 6
- w_out: bfloat16 [3072, 64], replicated, may hold values from -0.109375 to 0.109375
Outputs:
- latent: bfloat16 [2, 16, 16, 768], P('dp', None, 'seq')
- clip_loss: float32 [2, 4], P('dp')
- grad_out: float32 [3072, 64], P('seq')
Inputs may be any that keep to these rules, and one draw needn't show every extreme that they name: `owner_map`: among the tokens of one device no owner is named more than 18 times, a bound that some block reaches. `frame_counts`: the counts of a group sum to 16; the largest is exactly 12.
All inputs are finite; a program needn't handle non-finite values. No bound on the sum of `clip_group` on one device may be relied on, other than what follows from the above.
Results may differ from a plain program's by a relative error of at most 0.0055.
Values may be sent and summed in bfloat16 or wider, within the bound.
No kernel may reach another device: no remote copies, remote signals or barrier semaphores. Data moves between devices by JAX's collectives and lax.ppermute only.
A program may use at most 64 MiB of HBM per device.

v0:
```python
import jax
import jax.numpy as jnp
from jax import lax
from jax.sharding import PartitionSpec as P

LAT = 64
CLIPS = 4


def with_halo(cells, sides, width):
    for axis, dim in sides:
        count = lax.axis_size(axis)
        ends = count - 1
        head = lax.slice_in_dim(cells, 0, width, axis=dim)
        tail = lax.slice_in_dim(cells, cells.shape[dim] - width, cells.shape[dim], axis=dim)
        cells = jnp.concatenate(
            [
                lax.ppermute(tail, axis, [(i, (i + 1) % count) for i in range(ends)]),
                cells,
                lax.ppermute(head, axis, [((i + 1) % count, i) for i in range(ends)]),
            ],
            axis=dim,
        )
    return cells


def conv_rows(padded, kernel, keep, first, count):
    nframes = keep.shape[1]
    width = padded.shape[2] - 2
    chans = padded.shape[3]
    total = jnp.zeros((nframes, count * width, chans), jnp.float32)
    for lag in range(3):
        pieces = [
            padded[2 - lag : 2 - lag + nframes, first + i : first + i + count, j : j + width, :]
            for i in range(3)
            for j in range(3)
        ]
        columns = jnp.concatenate(pieces, axis=-1).reshape(-1, 9 * chans)
        part = jnp.dot(
            columns, kernel[lag].reshape(9 * chans, chans), preferred_element_type=jnp.float32
        )
        total = total + part.reshape(nframes, count * width, chans) * keep[lag][:, None, None]
    return total.reshape(nframes, count, width, chans)


def per_device(
    frames,
    frame_counts,
    clip_group,
    timesteps,
    owner_map,
    conv_weight,
    w_latent,
    hidden,
    noise,
    teacher,
    w_out,
):
    nseq = lax.axis_size("seq")
    local = frames[0]
    nframes, nrows, width, chans = local.shape
    tok_rows = nrows // 4
    tok_cols = width // 4
    per_frame = nrows * nseq // 4 * tok_cols
    counts = frame_counts[0]
    ends = jnp.cumsum(counts)
    index = jnp.arange(nframes, dtype=jnp.int32)
    clip_of = jnp.sum((index[:, None] >= ends[None, :]).astype(jnp.int32), axis=1)
    clip_hot = (clip_of[:, None] == jnp.arange(CLIPS, dtype=jnp.int32)[None, :]).astype(jnp.int32)
    starts = jnp.sum(clip_hot * (ends - counts)[None, :], axis=1)
    keep = jnp.stack([(index - lag >= starts).astype(jnp.float32) for lag in range(3)])
    rimmed = with_halo(frames, (("seq", 2),), 1)[0]
    outer_pad = jnp.pad(rimmed, ((2, 0), (0, 0), (1, 1), (0, 0)))
    conv = conv_rows(outer_pad, conv_weight, keep, 0, nrows)
    cells = (local.astype(jnp.float32) + jax.nn.silu(conv)).astype(jnp.bfloat16)
    patches = (
        cells.reshape(nframes, tok_rows, 4, tok_cols, 4, chans)
        .transpose(0, 1, 3, 2, 4, 5)
        .reshape(-1, 16 * chans)
    )
    tokens = jnp.dot(patches, w_latent, preferred_element_type=jnp.float32).astype(jnp.bfloat16)
    latent_out = tokens.reshape(1, nframes, tok_rows, tok_cols * LAT)
    slots = hidden.shape[1]
    capacity = slots // nseq
    owners = owner_map.reshape(-1)
    owner_hot = (owners[:, None] == jnp.arange(nseq, dtype=jnp.int32)[None, :]).astype(jnp.int32)
    rank = jnp.sum(jnp.cumsum(owner_hot, axis=0) * owner_hot, axis=1) - 1
    dest = owners * capacity + rank
    select = (dest[None, :] == jnp.arange(slots, dtype=jnp.int32)[:, None]).astype(jnp.bfloat16)
    tok_clip = jnp.repeat(clip_of, tok_rows * tok_cols).astype(jnp.float32) + 1.0
    outgoing = (
        jnp.dot(select, tokens, preferred_element_type=jnp.float32)
        .astype(jnp.bfloat16)
        .reshape(nseq, capacity, LAT)
    )
    labels = (
        jnp.dot(select, tok_clip.astype(jnp.bfloat16)[:, None], preferred_element_type=jnp.float32)
        .astype(jnp.bfloat16)
        .reshape(nseq, capacity)
    )
    arrived, arrived_tags = (
        lax.all_to_all(outgoing, "seq", split_axis=0, concat_axis=0, tiled=True),
        lax.all_to_all(labels, "seq", split_axis=0, concat_axis=0, tiled=True),
    )
    x0 = arrived.reshape(slots, LAT).astype(jnp.float32)
    tag = arrived_tags.reshape(slots).astype(jnp.float32)
    kind = clip_group[0].astype(jnp.float32)
    coef = (
        (2.0 * kind - 1.0)
        * (0.1 + timesteps[0].astype(jnp.float32) / 1000.0)
        / (counts.astype(jnp.float32) * per_frame)
    )
    slot_hot = (tag[:, None] == (jnp.arange(CLIPS, dtype=jnp.float32) + 1.0)[None, :]).astype(
        jnp.float32
    )
    slot_coef = jnp.sum(slot_hot * coef[None, :], axis=1)
    slot_kind = jnp.sum(slot_hot * kind[None, :], axis=1)
    states = hidden[0].astype(jnp.float32)
    mean = jnp.mean(states, axis=1, keepdims=True)
    centred = states - mean
    var = jnp.mean(centred * centred, axis=1, keepdims=True)
    normed = (centred * lax.rsqrt(var + 1e-06)).astype(jnp.bfloat16)
    pred = jnp.dot(normed, w_out, preferred_element_type=jnp.float32)
    target = slot_kind[:, None] * teacher[0] + (1.0 - slot_kind[:, None]) * (noise[0] - x0)
    diff = pred - target
    err = jnp.sum(diff * diff, axis=1)
    partial_loss = coef * jnp.sum(slot_hot * err[:, None], axis=0)
    clip_loss = lax.psum(partial_loss, "seq").reshape(1, CLIPS)
    dpred = (2.0 * slot_coef[:, None] * diff).astype(jnp.bfloat16)
    share_rows = normed.shape[1] // nseq
    grad_part = lax.dot_general(
        normed, dpred, (((0,), (0,)), ((), ())), preferred_element_type=jnp.float32
    )
    summed = lax.psum(grad_part, ("dp", "seq"))
    grad_mine = lax.dynamic_slice_in_dim(summed, lax.axis_index("seq") * share_rows, share_rows, 0)
    return (latent_out, clip_loss, grad_mine)


def solution(mesh):
    return jax.shard_map(
        per_device,
        mesh=mesh,
        in_specs=(
            P("dp", None, "seq", None, None),
            P("dp", None),
            P("dp", None),
            P("dp", None),
            P("dp", "seq", None, None),
            P(),
            P(),
            P("dp", "seq", None),
            P("dp", "seq", None),
            P("dp", "seq", None),
            P(),
        ),
        out_specs=(P("dp", None, "seq", None), P("dp", None), P("seq", None)),
        check_vma=False,
    )
```

profile of v0, /device:TPU:0, one launch (start us, length us, event | category | flops | bytes accessed | tf_op | source)
XLA Modules:
  0.0 210.9 jit_solution(1002889426171956777)
XLA Ops:
  7.2 2.0 fusion.43
  9.1 3.1 %collective-permute-start = (bf16[1,16,1,48,128]{4,3,2,1,0:T(8,128)(2,1)}, bf16[1,16,1,48,128]{4,3,2,1,0:T(8,128)(2,1)}, u32[]{:S(2)}, u32[]{:S(2)}) collective-permute-start(bf16[1,16,1,48,128]{4,3,2,1,0:T(8,128)(2,1)} %get-tuple-element.17), channel_id=1, source_target_pairs={{0,1},{1,2},{2,3},{3,4},{4,5},{5,6},{6,7},{7,8},{8,9},{9,10},{10,1... | collective-permute-start | bytes 589832 | tf_op jit(solution)/shard_map/ppermute | solution.py:18
  12.2 1.3 collective-permute-start.1
  13.5 0.8 reduce-window.10
  14.4 0.7 iota_compare_fusion.3
  15.1 0.6 reduce-window.11
  16.0 0.7 fusion.36
  16.7 0.7 add_add_fusion
  17.6 0.2 convolution_reduce_fusion
  17.8 0.7 all_to_all.12
  18.5 8.6 %all-to-all-start = ((bf16[16,1,18]{2,1,0:T(2,128)(2,1)}), bf16[16,1,18]{2,1,0:T(2,128)(2,1)S(1)}, u32[]{:S(2)}, u32[]{:S(2)}) async-start(bf16[16,1,18]{2,1,0:T(2,128)(2,1)} %all_to_all.12), calls=%async_computation | async-start | bytes 16384 | tf_op jit(solution)/shard_map/all_to_all | solution.py:103
  27.1 0.8 fusion.40
  27.9 1.9 fusion.42
  29.9 0.6 compare_convert_fusion.2
  30.5 1.2 convert_bitcast_fusion.2
  31.8 0.3 convert_reduce_fusion
  32.1 0.6 fusion.3
  32.7 0.7 fusion.4
  33.5 0.5 fusion.41
  34.0 0.6 iota_add_fusion
  34.6 1.6 copy.40
  36.3 0.8 fusion.37
  37.1 1.2 maximum_bitcast_fusion
  38.3 0.2 fusion.20
  38.5 0.2 fusion.21
  38.7 0.3 fusion.22
  39.0 0.3 fusion.23
  39.4 0.2 fusion.24
  39.6 0.3 fusion.25
  39.9 0.5 fusion.26
  40.4 0.5 fusion.27
  40.9 1.0 fusion.28
  41.9 0.3 fusion.7
  42.3 0.2 slice_dynamic-update-slice_fusion.1
  42.5 0.4 fusion.8
  42.9 0.4 fusion.9
  43.3 0.2 slice_dynamic-update-slice_fusion
  43.5 0.6 fusion.10
  44.1 0.4 fusion.13
  44.4 0.3 fusion.14
  44.8 0.2 fusion.15
  45.0 0.4 fusion.16
  45.4 0.3 fusion.17
  45.7 0.2 fusion.18
  45.9 0.4 fusion.19
  46.3 2.2 %fusion.45 = f32[16,192,128]{2,1,0:T(8,128)S(1)} fusion(bf16[16,192,1152]{2,1,0:T(8,128)(2,1)S(1)} %bitcast.85, bf16[1152,128,1]{1,0,2:T(8,128)(2,1)S(1)} %bitcast.90), kind=kOutput, calls=%fused_computation.117 | convolution fusion | flops 905969664 | bytes 8945664 | tf_op jit(solution)/shard_map/dot_general | solution.py:39
  48.6 2.0 fusion.44
  50.6 2.1 %multiply_add_fusion = f32[16,192,128]{2,1,0:T(8,128)S(1)} fusion(f32[16,192,128]{2,1,0:T(8,128)S(1)} %fusion.45, f32[16,192,128]{2,1,0:T(8,128)S(1)} %fusion.44, bf16[16,192,1152]{2,1,0:T(8,128)(2,1)S(1)} %bitcast.84, bf16[1152,128,1]{1,0,2:T(8,128)(2,1)S(1)} %bitcast.91, f32[16]{0:T(128)S(1)} %copy-done.10, f32[16]{0:T(128)S(1)} %copy-done.11, ...), kind=kOutput, calls=%fused_computation.8 | convolution fusion | flops 907935744 | bytes 12091584 | tf_op jit(solution)/shard_map/dot_general | solution.py:39
  52.8 0.9 copy.41
  53.7 0.5 copy-done.3
  54.2 0.4 fusion.29
  54.6 0.4 copy.42
  55.0 1.5 reshape.209
  56.5 1.5 convolution_convert_fusion.1
  58.0 0.2 convolution_convert_fusion
  58.4 0.7 reshape.236
  59.1 6.0 %all-to-all-start.1 = ((bf16[16,2,576]{2,1,0:T(2,128)(2,1)}), bf16[16,2,576]{2,1,0:T(2,128)(2,1)S(1)}, u32[]{:S(2)}, u32[]{:S(2)}) async-start(bf16[16,2,576]{2,1,0:T(2,128)(2,1)} %reshape.236), calls=%async_computation.1 | async-start | bytes 81920 | tf_op jit(solution)/shard_map/all_to_all | solution.py:102
  65.2 6.6 %all-to-all-done.1 = bf16[16,2,576]{2,1,0:T(2,128)(2,1)S(1)} async-done(((bf16[16,2,576]{2,1,0:T(2,128)(2,1)}), bf16[16,2,576]{2,1,0:T(2,128)(2,1)S(1)}, u32[]{:S(2)}, u32[]{:S(2)}) %all-to-all-start.1) | async-done | bytes 36896 | tf_op jit(solution)/shard_map/all_to_all | solution.py:102
  72.1 0.7 multiply_reduce_fusion
  73.1 1.4 fusion.34
  74.7 0.7 reshape.210
  75.4 30.2 %psum.14 = f32[1,4]{1,0:T(1,128)} all-reduce(f32[1,4]{1,0:T(1,128)S(1)} %multiply_bitcast_fusion), channel_id=1, replica_groups=mesh['dp'=2,'seq'=16] {'seq'}, use_global_device_ids=true, to_apply=%region_11.12 | all-reduce | flops 4 | bytes 32 | tf_op jit(solution)/shard_map/psum | solution.py:128
  105.5 96.9 %all-reduce.4.cloned.1.call-done = f32[3072,64]{0,1:T(8,128)} async-done(((f32[3072,64]{0,1:T(8,128)}), f32[3072,64]{0,1:T(8,128)}) %all-reduce.4.cloned.1.call-update) | async-done | bytes 786448 | tf_op jit(solution)/shard_map/psum | solution.py:134
  202.4 1.6 constant_dynamic-slice_fusion
  (66 shorter events, 1.7 us)
Async XLA Ops:
  7.2 64.9 %copy-start = (bf16[3072,64]{0,1:T(8,128)(2,1)S(1)}, bf16[3072,64]{0,1:T(8,128)(2,1)}, u32[]{:S(2)}) copy-start(bf16[3072,64]{0,1:T(8,128)(2,1)} %param.21) | copy-start | bytes 1179652
  7.2 24.6 %copy-start.1 = (bf16[1,288,3072]{2,1,0:T(8,128)(2,1)S(1)}, bf16[1,288,3072]{2,1,0:T(8,128)(2,1)}, u32[]{:S(2)}) copy-start(bf16[1,288,3072]{2,1,0:T(8,128)(2,1)} %param.18) | copy-start | bytes 5308420
  9.1 27.9 %collective-permute-start = (bf16[1,16,1,48,128]{4,3,2,1,0:T(8,128)(2,1)}, bf16[1,16,1,48,128]{4,3,2,1,0:T(8,128)(2,1)}, u32[]{:S(2)}, u32[]{:S(2)}) collective-permute-start(bf16[1,16,1,48,128]{4,3,2,1,0:T(8,128)(2,1)} %get-tuple-element.17), channel_id=1, source_target_pairs={{0,1},{1,2},{2,3},{3,4},{4,5},{5,6},{6,7},{7,8},{8,9},{9,10},{10,1... | collective-permute-start | bytes 589832 | tf_op jit(solution)/shard_map/ppermute | solution.py:18
  12.2 24.9 %collective-permute-start.1 = (bf16[1,16,1,48,128]{4,3,2,1,0:T(8,128)(2,1)}, bf16[1,16,1,48,128]{4,3,2,1,0:T(8,128)(2,1)}, u32[]{:S(2)}, u32[]{:S(2)}) collective-permute-start(bf16[1,16,1,48,128]{4,3,2,1,0:T(8,128)(2,1)} %get-tuple-element.18), channel_id=1, source_target_pairs={{1,0},{2,1},{3,2},{4,3},{5,4},{6,5},{7,6},{8,7},{9,8},{10,9},{11,1... | collective-permute-start | bytes 589832 | tf_op jit(solution)/shard_map/ppermute | solution.py:20
  17.4 1.1 copy-start.14
  18.5 17.7 %all-to-all-start = ((bf16[16,1,18]{2,1,0:T(2,128)(2,1)}), bf16[16,1,18]{2,1,0:T(2,128)(2,1)S(1)}, u32[]{:S(2)}, u32[]{:S(2)}) async-start(bf16[16,1,18]{2,1,0:T(2,128)(2,1)} %all_to_all.12), calls=%async_computation | async-start | bytes 16384 | tf_op jit(solution)/shard_map/all_to_all | solution.py:103
  27.1 5.6 %copy-start.2 = (bf16[1,288,3072]{2,1,0:T(8,128)(2,1)S(1)}, bf16[1,288,3072]{2,1,0:T(8,128)(2,1)}, u32[]{:S(2)}) copy-start(bf16[1,288,3072]{2,1,0:T(8,128)(2,1)} %param.18) | copy-start | bytes 5308420
  31.8 1.7 copy-start.16
  31.8 1.7 copy-start.17
  31.8 1.7 copy-start.18
  31.8 2.8 %copy-start.4 = (bf16[1,16,4,48,128]{4,3,2,1,0:T(8,128)(2,1)S(1)}, bf16[1,16,4,48,128]{4,3,2,1,0:T(8,128)(2,1)}, u32[]{:S(2)}) copy-start(bf16[1,16,4,48,128]{4,3,2,1,0:T(8,128)(2,1)} %param.11) | copy-start | bytes 2359300
  48.5 2.1 copy-start.5
  48.5 2.1 copy-start.9
  48.5 2.1 copy-start.10
  48.6 2.1 copy-start.11
  52.8 1.4 copy-start.3
  54.2 2.3 %copy-start.6 = (bf16[2048,64]{0,1:T(8,128)(2,1)S(1)}, bf16[2048,64]{0,1:T(8,128)(2,1)}, u32[]{:S(2)}) copy-start(bf16[2048,64]{0,1:T(8,128)(2,1)} %param.17) | copy-start | bytes 786436
  54.2 3.8 %copy-start.15 = (s32[192]{0:T(256)S(1)}, s32[192]{0:T(256)}, u32[]{:S(2)}) copy-start(s32[192]{0:T(256)} %copy-done.14) | copy-start | bytes 2308
  54.6 17.5 %copy-start.7 = (f32[1,288,64]{1,2,0:T(8,128)S(1)}, f32[1,288,64]{1,2,0:T(8,128)}, u32[]{:S(2)}) copy-start(f32[1,288,64]{1,2,0:T(8,128)} %param.19) | copy-start | bytes 221188
  54.6 17.5 %copy-start.8 = (f32[1,288,64]{1,2,0:T(8,128)S(1)}, f32[1,288,64]{1,2,0:T(8,128)}, u32[]{:S(2)}) copy-start(f32[1,288,64]{1,2,0:T(8,128)} %param.20) | copy-start | bytes 221188
  56.5 16.4 %copy-start.12 = (f32[4]{0:T(128)S(1)}, f32[4]{0:T(128)}, u32[]{:S(2)}) copy-start(f32[4]{0:T(128)} %iota_add_fusion) | copy-start | bytes 52
  56.5 16.4 %copy-start.13 = (f32[4]{0:T(128)S(1)}, f32[4]{0:T(128)}, u32[]{:S(2)}) copy-start(f32[4]{0:T(128)} %fusion.41) | copy-start | bytes 52
  59.1 12.7 %all-to-all-start.1 = ((bf16[16,2,576]{2,1,0:T(2,128)(2,1)}), bf16[16,2,576]{2,1,0:T(2,128)(2,1)S(1)}, u32[]{:S(2)}, u32[]{:S(2)}) async-start(bf16[16,2,576]{2,1,0:T(2,128)(2,1)} %reshape.236), calls=%async_computation.1 | async-start | bytes 81920 | tf_op jit(solution)/shard_map/all_to_all | solution.py:102
  65.1 137.3 %all-reduce.4.cloned.1.call-start = ((), (), s32[]{:S(2)}) async-start(), calls=%async_computation.2 | async-start | bytes 1572864 | tf_op jit(solution)/shard_map/psum | solution.py:134
Sparse Core Ops, SparseCore 0:
  74.7 127.7 all-reduce.3
where the time goes:
time: 211 us
  waiting for transfers between devices  104 us (49%)
  blocking collectives  30.2 us (14%)
  local copies, waits for them, and re-layouts  21.4 us (10%)
  starting transfers between devices  19 us (9%)
  between operations  14.6 us (7%)
  other arithmetic  11.7 us (6%)
  matrix products  10.4 us (5%)
    psum x1, waiting for transfers between devices, per_device(): summed = lax.psum(grad_part, ('dp', 'seq'))  96.9 us
    psum x1, blocking collectives, per_device(): clip_loss = lax.psum(partial_loss, 'seq').reshape(1, CLIPS)  30.2 us
    all_to_all x1, starting transfers between devices, per_device(): lax.all_to_all(labels, 'seq', split_axis=0, concat_axis=0, tiled=True)  8.62 us
    unnamed x59, local copies, waits for them, and re-layouts  7.35 us
    all_to_all x1, waiting for transfers between devices, per_device(): lax.all_to_all(outgoing, 'seq', split_axis=0, concat_axis=0, tiled=True)  6.64 us
    dot_general x3, matrix products, conv_rows(): jnp.dot(columns, kernel[lag].reshape(9 * chans, chans), preferred_element...  6.37 us
    all_to_all x1, starting transfers between devices, per_device(): lax.all_to_all(outgoing, 'seq', split_axis=0, concat_axis=0, tiled=True)  6.01 us
  transfers between devices with their start and end apart: 5, of which 2 were waited for; matrix products, arithmetic and copies ran while one was open for 7% of the time, Pallas kernels for 0%

commit v1 on v0

--- a/solution.py
+++ b/solution.py
@@ -22,6 +22,28 @@
             axis=dim,
         )
     return cells
+
+
+def tree_reduce(grad_part, loss_row, nseq, ndp):
+    rows = grad_part.shape[0] // nseq
+    nbits = nseq.bit_length() - 1
+    assert 1 << nbits == nseq and ndp & (ndp - 1) == 0
+    blocks = grad_part.reshape(nseq, rows, LAT)
+    extra = jnp.broadcast_to(loss_row[None, None, :], (nseq, 1, LAT))
+    x = jnp.concatenate([blocks, extra], axis=1).reshape((2,) * nbits + (rows + 1, LAT))
+    me = lax.axis_index("seq")
+    left = list(range(nbits - 1, -1, -1))
+    for k in range(nbits):
+        axis = left.index(k)
+        bit = (me >> k) & 1
+        keep = lax.dynamic_index_in_dim(x, bit, axis, keepdims=False)
+        send = lax.dynamic_index_in_dim(x, 1 - bit, axis, keepdims=False)
+        x = keep + lax.ppermute(send, "seq", [(i, i ^ (1 << k)) for i in range(nseq)])
+        left.pop(axis)
+    x = x.reshape(rows + 1, LAT)
+    for k in range(ndp.bit_length() - 1):
+        x = x + lax.ppermute(x, "dp", [(i, i ^ (1 << k)) for i in range(ndp)])
+    return x
 
 
 def conv_rows(padded, kernel, keep, first, count):
@@ -125,14 +147,16 @@
     diff = pred - target
     err = jnp.sum(diff * diff, axis=1)
     partial_loss = coef * jnp.sum(slot_hot * err[:, None], axis=0)
-    clip_loss = lax.psum(partial_loss, "seq").reshape(1, CLIPS)
     dpred = (2.0 * slot_coef[:, None] * diff).astype(jnp.bfloat16)
-    share_rows = normed.shape[1] // nseq
     grad_part = lax.dot_general(
         normed, dpred, (((0,), (0,)), ((), ())), preferred_element_type=jnp.float32
     )
-    summed = lax.psum(grad_part, ("dp", "seq"))
-    grad_mine = lax.dynamic_slice_in_dim(summed, lax.axis_index("seq") * share_rows, share_rows, 0)
+    ndp = lax.axis_size("dp")
+    place = lax.axis_index("dp") * CLIPS
+    loss_row = lax.dynamic_update_slice(jnp.zeros((LAT,), jnp.float32), partial_loss, (place,))
+    summed = tree_reduce(grad_part, loss_row, nseq, ndp)
+    grad_mine = summed[:-1]
+    clip_loss = lax.dynamic_slice_in_dim(summed[-1], place, CLIPS).reshape(1, CLIPS)
     return (latent_out, clip_loss, grad_mine)
 
 

time: 211 us -> 97.8 us (0.46)
  waiting for transfers between devices: 104 us -> 19.5 us
  blocking collectives: 30.2 us -> 0 us
  between operations: 14.6 us -> 1.23 us
  starting transfers between devices: 19 us -> 25.1 us
  local copies, waits for them, and re-layouts: 21.4 us -> 26.6 us
  other arithmetic: 11.7 us -> 14.6 us
    psum x1 -> x0, waiting for transfers between devices: 96.9 us -> none  [per_device(): summed = lax.psum(grad_part, ('dp', 'seq'))]
    psum x1 -> x0, blocking collectives: 30.2 us -> none  [per_device(): clip_loss = lax.psum(partial_loss, 'seq').reshape(1, CLIPS)]
    ppermute x0 -> x5, waiting for transfers between devices: none -> 18.7 us  [the longest x4 16.8 us: tree_reduce(): x = keep + lax.ppermute(send, 'seq', [(i, i ^ 1 << k) for i in range(nseq)])]
    ppermute x0 -> x5, starting transfers between devices: none -> 6.13 us  [the longest x4 4.57 us: tree_reduce(): x = keep + lax.ppermute(send, 'seq', [(i, i ^ 1 << k) for i in range(nseq)])]
    all_to_all x1, waiting for transfers between devices: 6.64 us -> 0.79 us  [per_device(): lax.all_to_all(outgoing, 'seq', split_axis=0, concat_axis=0, tiled=True)]
    dot_general x0 -> x1, local copies, waits for them, and re-layouts: none -> 4.02 us  [per_device(): lax.dot_general(normed, dpred, (((0,), (0,)), ((), ())), preferred_elemen...]
    unnamed x59 -> x70, local copies, waits for them, and re-layouts: 7.35 us -> 8.58 us
  transfers between devices with their start and end apart: 5 -> 9, of which waited for: 2 -> 6; matrix products, arithmetic and copies ran while one was open for 7% -> 23% of each run, Pallas kernels for 0% -> 0%
where the time goes in v1:
time: 97.8 us; the launch traced here: 97.1 us
  local copies, waits for them, and re-layouts  26.6 us (27%)
  starting transfers between devices  25.1 us (26%)
  waiting for transfers between devices  19.5 us (20%)
  other arithmetic  14.6 us (15%)
  matrix products  10.1 us (10%)
  between operations  1.23 us (1%)
    ppermute x4, waiting for transfers between devices, tree_reduce(): x = keep + lax.ppermute(send, 'seq', [(i, i ^ 1 << k) for i in range(nseq)])  16.8 us
    all_to_all x1, starting transfers between devices, per_device(): lax.all_to_all(labels, 'seq', split_axis=0, concat_axis=0, tiled=True)  8.63 us
    unnamed x70, local copies, waits for them, and re-layouts  8.58 us
    dot_general x3, matrix products, conv_rows(): jnp.dot(columns, kernel[lag].reshape(9 * chans, chans), preferred_element...  6.3 us
    all_to_all x1, starting transfers between devices, per_device(): lax.all_to_all(outgoing, 'seq', split_axis=0, concat_axis=0, tiled=True)  6 us
    ppermute x4, starting transfers between devices, tree_reduce(): x = keep + lax.ppermute(send, 'seq', [(i, i ^ 1 << k) for i in range(nseq)])  4.57 us
    dot_general x1, local copies, waits for them, and re-layouts, per_device(): lax.dot_general(normed, dpred, (((0,), (0,)), ((), ())), preferred_elemen...  4.02 us
    ppermute x1, starting transfers between devices, with_halo(): lax.ppermute(tail, axis, [(i, (i + 1) % count) for i in range(ends)])  3.07 us
  transfers between devices with their start and end apart: 9, of which 6 were waited for; matrix products, arithmetic and copies ran while one was open for 23% of the time, Pallas kernels for 0%

profile of v1, /device:TPU:0, one launch (start us, length us, event | category | flops | bytes accessed | tf_op | source)
XLA Modules:
  0.0 97.1 jit_solution(6023270840954456060)
XLA Ops:
  0.7 2.0 %fusion.47 = (bf16[1,16,1,48,128]{4,3,2,1,0:T(8,128)(2,1)}, bf16[1,16,1,48,128]{4,3,2,1,0:T(8,128)(2,1)}) fusion(bf16[1,16,4,48,128]{4,3,2,1,0:T(8,128)(2,1)} %param.11), kind=kLoop, calls=%fused_computation.126 | loop fusion | bytes 786432 | tf_op jit(solution)/shard_map/slice | solution.py:15
  2.6 3.1 %collective-permute-start = (bf16[1,16,1,48,128]{4,3,2,1,0:T(8,128)(2,1)}, bf16[1,16,1,48,128]{4,3,2,1,0:T(8,128)(2,1)}, u32[]{:S(2)}, u32[]{:S(2)}) collective-permute-start(bf16[1,16,1,48,128]{4,3,2,1,0:T(8,128)(2,1)} %get-tuple-element.32), channel_id=1, source_target_pairs={{0,1},{1,2},{2,3},{3,4},{4,5},{5,6},{6,7},{7,8},{8,9},{9,10},{10,1... | collective-permute-start | bytes 589832 | tf_op jit(solution)/shard_map/ppermute | solution.py:18
  5.7 1.3 %collective-permute-start.1 = (bf16[1,16,1,48,128]{4,3,2,1,0:T(8,128)(2,1)}, bf16[1,16,1,48,128]{4,3,2,1,0:T(8,128)(2,1)}, u32[]{:S(2)}, u32[]{:S(2)}) collective-permute-start(bf16[1,16,1,48,128]{4,3,2,1,0:T(8,128)(2,1)} %get-tuple-element.33), channel_id=1, source_target_pairs={{1,0},{2,1},{3,2},{4,3},{5,4},{6,5},{7,6},{8,7},{9,8},{10,9},{11,1... | collective-permute-start | bytes 589832 | tf_op jit(solution)/shard_map/ppermute | solution.py:20
  7.0 0.8 reduce-window.10
  7.9 0.7 iota_compare_fusion.3
  8.6 0.6 reduce-window.11
  9.5 0.7 fusion.38
  10.2 0.7 add_add_fusion
  11.3 0.7 all_to_all.12
  12.0 8.6 %all-to-all-start = ((bf16[16,1,18]{2,1,0:T(2,128)(2,1)}), bf16[16,1,18]{2,1,0:T(2,128)(2,1)S(1)}, u32[]{:S(2)}, u32[]{:S(2)}) async-start(bf16[16,1,18]{2,1,0:T(2,128)(2,1)} %all_to_all.12), calls=%async_computation | async-start | bytes 16384 | tf_op jit(solution)/shard_map/all_to_all | solution.py:125
  20.6 0.7 fusion.42
  21.3 2.8 %copy.48 = f32[1,16,4,48,128]{4,1,3,2,0:T(8,128)} copy(bf16[1,16,4,48,128]{4,3,2,1,0:T(8,128)(2,1)} %param.11) | data formatting | bytes 2359296 | tf_op jit(solution)/shard_map/convert_element_type | solution.py:97
  24.1 0.6 iota_add_fusion
  24.7 1.9 %fusion.46 = (bf16[1,3,3,128,128]{4,3,2,1,0:T(8,128)(2,1)}, bf16[1,3,3,128,128]{4,3,2,1,0:T(8,128)(2,1)S(1)}, bf16[1,3,3,128,128]{4,3,2,1,0:T(8,128)(2,1)S(1)}) fusion(bf16[3,3,3,128,128]{4,3,2,1,0:T(8,128)(2,1)} %param.16), kind=kLoop, calls=%fused_computation.125 | loop fusion | bytes 1769472 | tf_op jit(solution)/shard_map/slice | solution.py:62
  26.6 0.7 select_reduce_fusion
  27.4 0.6 compare_convert_fusion.2
  28.0 0.6 convert_bitcast_fusion.2
  28.9 1.2 %fusion.3 = f32[288]{0:T(512)} fusion(bf16[1,288,3072]{2,1,0:T(8,128)(2,1)S(1)} %copy-done.1, f32[288]{0:T(512)S(1)} %broadcast_multiply_fusion.1), kind=kLoop, calls=%fused_computation.5 | loop fusion | flops 3538656 | bytes 1771776 | tf_op jit(solution)/shard_map/reduce_sum | solution.py:143
  30.1 0.5 fusion.43
  30.8 0.8 fusion.40
  31.6 0.7 add_rsqrt_fusion
  32.3 1.2 %maximum_bitcast_fusion = bf16[16,6,48,128]{3,2,1,0:T(8,128)(2,1)S(1)} fusion(bf16[1,16,1,48,128]{4,3,2,1,0:T(8,128)(2,1)} %collective-permute-done.1, bf16[1,16,4,48,128]{4,3,2,1,0:T(8,128)(2,1)S(1)} %copy-done.4, bf16[1,16,1,48,128]{4,3,2,1,0:T(8,128)(2,1)} %collective-permute-done), kind=kLoop, calls=%fused_computation.33 | loop fusion | flops 1179648 | bytes 2359296 | tf_op jit(solution)/shard_map/squeeze | solution.py:94
  33.9 0.3 fusion.22
  34.8 0.3 fusion.25
  35.1 0.5 fusion.26
  35.6 0.5 fusion.27
  36.1 1.0 %fusion.28 = (bf16[16,4,48,1152]{3,2,1,0:T(8,128)(2,1)S(1)}, bf16[16,4,48,1152]{3,2,1,0:T(8,128)(2,1)S(1)}, bf16[16,4,48,1152]{3,2,1,0:T(8,128)(2,1)S(1)}) fusion(bf16[16,4,48,1152]{3,2,1,0:T(8,128)(2,1)S(1)} %get-tuple-element.23, bf16[16,6,48,128]{3,2,1,0:T(8,128)(2,1)S(1)} %maximum_bitcast_fusion, bf16[16,4,48,1152]{3,2,1,0:T(8,128)(2,1)S(1)} %get-tuple-element.24), kind=kLoop, calls=%fused_computation.62 | loop fusion | bytes 3538944 | tf_op jit(solution)/shard_map/concatenate | solution.py:60
  37.1 0.3 fusion.7
  37.7 0.4 fusion.8
  38.1 0.4 fusion.9
  38.7 0.6 fusion.10
  39.3 0.4 fusion.13
  39.6 0.3 fusion.14
  40.2 0.4 fusion.16
  40.6 0.3 fusion.17
  41.1 0.4 fusion.19
  41.5 2.0 %fusion.49 = f32[16,192,128]{2,1,0:T(8,128)S(1)} fusion(bf16[16,192,1152]{2,1,0:T(8,128)(2,1)S(1)} %bitcast.111, bf16[1152,128,1]{1,0,2:T(8,128)(2,1)S(1)} %bitcast.119), kind=kOutput, calls=%fused_computation.128 | convolution fusion | flops 905969664 | bytes 8945664 | tf_op jit(solution)/shard_map/dot_general | solution.py:61
  43.6 2.2 %fusion.48 = f32[16,192,128]{2,1,0:T(8,128)S(1)} fusion(bf16[16,192,1152]{2,1,0:T(8,128)(2,1)S(1)} %bitcast.112, bf16[1152,128,1]{1,0,2:T(8,128)(2,1)S(1)} %bitcast.118), kind=kOutput, calls=%fused_computation.127 | convolution fusion | flops 905969664 | bytes 8945664 | tf_op jit(solution)/shard_map/dot_general | solution.py:61
  45.8 2.1 %multiply_add_fusion = f32[16,192,128]{2,1,0:T(8,128)S(1)} fusion(f32[16,192,128]{2,1,0:T(8,128)S(1)} %fusion.49, f32[16,192,128]{2,1,0:T(8,128)S(1)} %fusion.48, bf16[16,192,1152]{2,1,0:T(8,128)(2,1)S(1)} %bitcast.110, bf16[1152,128,1]{1,0,2:T(8,128)(2,1)S(1)} %bitcast.120, f32[16]{0:T(128)S(1)} %copy-done.11, f32[16]{0:T(128)S(1)} %copy-done.12, ...), kind=kOutput, calls=%fused_computation.8 | convolution fusion | flops 907935744 | bytes 12091584 | tf_op jit(solution)/shard_map/dot_general | solution.py:61
  47.9 0.9 copy.49
  48.8 0.5 copy-done.3
  49.3 0.4 fusion.29
  49.7 0.4 copy.50
  50.1 1.5 %reshape.247 = bf16[192,2048]{1,0:T(8,128)(2,1)} reshape(bf16[16,1,12,4,4,128]{5,4,3,2,0,1:T(4,128)(2,1)S(1)} %copy.50) | data formatting | bytes 1572864 | tf_op jit(solution)/shard_map/reshape | solution.py:101
  51.6 1.5 %convolution_convert_fusion.1 = bf16[192,64]{0,1:T(8,128)(2,1)S(1)} fusion(bf16[192,2048]{1,0:T(8,128)(2,1)} %reshape.247, bf16[2048,64]{0,1:T(8,128)(2,1)S(1)} %copy-done.6), kind=kOutput, calls=%fused_computation.36 | convolution fusion | flops 50343936 | bytes 1073152 | tf_op jit(solution)/shard_map/dot_general | solution.py:103
  53.5 0.7 reshape.275
  54.2 6.0 %all-to-all-start.1 = ((bf16[16,2,576]{2,1,0:T(2,128)(2,1)}), bf16[16,2,576]{2,1,0:T(2,128)(2,1)S(1)}, u32[]{:S(2)}, u32[]{:S(2)}) async-start(bf16[16,2,576]{2,1,0:T(2,128)(2,1)} %reshape.275), calls=%async_computation.1 | async-start | bytes 81920 | tf_op jit(solution)/shard_map/all_to_all | solution.py:124
  60.3 1.9 %fusion.45 = bf16[3072,288]{0,1:T(8,128)(2,1)} fusion(f32[288]{0:T(512)S(1)} %get-tuple-element.39, f32[288]{0:T(512)S(1)} %copy-done.9, bf16[1,288,3072]{2,1,0:T(8,128)(2,1)S(1)} %copy-done.1), kind=kLoop, calls=%fused_computation.124 | loop fusion | flops 3538944 | bytes 3541248 | tf_op jit(solution)/shard_map/dot_general | solution.py:151
  62.1 4.0 %copy.59 = bf16[3072,288]{1,0:T(8,128)(2,1)} copy(bf16[3072,288]{0,1:T(8,128)(2,1)} %fusion.45) | data formatting | bytes 3538944 | tf_op jit(solution)/shard_map/dot_general | solution.py:151
  66.1 0.8 all-to-all-done.1
  67.2 0.8 multiply_reduce_fusion
  68.3 0.6 copy-done.2
  68.9 1.1 %fusion.35 = f32[16,192,64]{1,2,0:T(8,128)S(1)} fusion(bf16[16,192,288]{2,1,0:T(8,128)(2,1)S(1)} %bitcast.113, f32[288,64]{0,1:T(8,128)S(1)} %get-tuple-element.38, f32[288]{0:T(512)S(1)} %broadcast_multiply_fusion), kind=kOutput, calls=%fused_computation.85 | convolution fusion | flops 113283072 | bytes 2630784 | tf_op jit(solution)/shard_map/dot_general | solution.py:151
  70.6 1.9 %collective-permute-done.2 = f32[2,2,2,193,64]{3,4,2,1,0:T(8,128)S(1)} collective-permute-done((f32[2,2,2,193,64]{3,4,2,1,0:T(8,128)S(1)}, f32[2,2,2,193,64]{3,4,2,1,0:T(8,128)S(1)}, u32[]{:S(2)}, u32[]{:S(2)}) %collective-permute-start.2) | collective-permute-done | bytes 395296 | tf_op jit(solution)/shard_map/ppermute | solution.py:41
  72.6 1.2 %collective-permute-start.3 = (f32[2,2,193,64]{2,3,1,0:T(8,128)S(1)}, f32[2,2,193,64]{2,3,1,0:T(8,128)S(1)}, u32[]{:S(2)}, u32[]{:S(2)}) collective-permute-start(f32[2,2,193,64]{2,3,1,0:T(8,128)S(1)} %dynamic-slice_bitcast_fusion.1), channel_id=1, source_target_pairs={{0,2},{1,3},{2,0},{3,1},{4,6},{5,7},{6,4},{7,5},{8,10},{9,11},{10,... | collective-permute-start | bytes 592904 | tf_op jit(solution)/shard_map/ppermute | solution.py:41
  73.8 7.2 %collective-permute-done.3 = f32[2,2,193,64]{2,3,1,0:T(8,128)S(1)} collective-permute-done((f32[2,2,193,64]{2,3,1,0:T(8,128)S(1)}, f32[2,2,193,64]{2,3,1,0:T(8,128)S(1)}, u32[]{:S(2)}, u32[]{:S(2)}) %collective-permute-start.3) | collective-permute-done | bytes 197664 | tf_op jit(solution)/shard_map/ppermute | solution.py:41
  81.1 1.2 %collective-permute-start.4 = (f32[2,193,64]{1,2,0:T(8,128)S(1)}, f32[2,193,64]{1,2,0:T(8,128)S(1)}, u32[]{:S(2)}, u32[]{:S(2)}) collective-permute-start(f32[2,193,64]{1,2,0:T(8,128)S(1)} %dynamic-slice_bitcast_fusion.2), channel_id=1, source_target_pairs={{0,4},{1,5},{2,6},{3,7},{4,0},{5,1},{6,2},{7,3},{8,12},{9,13},{10,... | collective-permute-start | bytes 296456 | tf_op jit(solution)/shard_map/ppermute | solution.py:41
  82.3 3.8 %collective-permute-done.4 = f32[2,193,64]{1,2,0:T(8,128)S(1)} collective-permute-done((f32[2,193,64]{1,2,0:T(8,128)S(1)}, f32[2,193,64]{1,2,0:T(8,128)S(1)}, u32[]{:S(2)}, u32[]{:S(2)}) %collective-permute-start.4) | collective-permute-done | bytes 98848 | tf_op jit(solution)/shard_map/ppermute | solution.py:41
  86.2 2.1 %collective-permute-start.5 = (f32[193,64]{0,1:T(8,128)S(1)}, f32[193,64]{0,1:T(8,128)S(1)}, u32[]{:S(2)}, u32[]{:S(2)}) collective-permute-start(f32[193,64]{0,1:T(8,128)S(1)} %dynamic-slice_bitcast_fusion.3), channel_id=1, source_target_pairs={{0,8},{1,9},{2,10},{3,11},{4,12},{5,13},{6,14},{7,15},{8,0},{9,1},... | collective-permute-start | bytes 148232 | tf_op jit(solution)/shard_map/ppermute | solution.py:41
  88.3 3.8 %collective-permute-done.5 = f32[193,64]{0,1:T(8,128)S(1)} collective-permute-done((f32[193,64]{0,1:T(8,128)S(1)}, f32[193,64]{0,1:T(8,128)S(1)}, u32[]{:S(2)}, u32[]{:S(2)}) %collective-permute-start.5) | collective-permute-done | bytes 49440 | tf_op jit(solution)/shard_map/ppermute | solution.py:41
  92.1 1.6 %collective-permute-start.6 = (f32[193,64]{0,1:T(8,128)S(1)}, f32[193,64]{0,1:T(8,128)S(1)}, u32[]{:S(2)}, u32[]{:S(2)}) collective-permute-start(f32[193,64]{0,1:T(8,128)S(1)} %bitcast_add_fusion.3), channel_id=1, source_target_pairs={{0,16},{16,0},{1,17},{17,1},{2,18},{18,2},{3,19},{19,3},{4,20},{20... | collective-permute-start | bytes 148232 | tf_op jit(solution)/shard_map/ppermute | solution.py:45
  93.8 0.7 reshape.248
  94.5 1.9 %collective-permute-done.6 = f32[193,64]{0,1:T(8,128)S(1)} collective-permute-done((f32[193,64]{0,1:T(8,128)S(1)}, f32[193,64]{0,1:T(8,128)S(1)}, u32[]{:S(2)}, u32[]{:S(2)}) %collective-permute-start.6) | collective-permute-done | bytes 49440 | tf_op jit(solution)/shard_map/ppermute | solution.py:45
  96.5 0.6 copy.58
  (96 shorter events, 4.9 us)
Async XLA Ops:
  0.6 66.6 %copy-start = (bf16[3072,64]{0,1:T(8,128)(2,1)S(1)}, bf16[3072,64]{0,1:T(8,128)(2,1)}, u32[]{:S(2)}) copy-start(bf16[3072,64]{0,1:T(8,128)(2,1)} %param.21) | copy-start | bytes 1179652
  0.6 27.3 %copy-start.19 = (s32[1,4]{1,0:T(1,128)S(1)}, s32[1,4]{1,0:T(1,128)}, u32[]{:S(2)}) copy-start(s32[1,4]{1,0:T(1,128)} %param.13) | copy-start | bytes 52
  0.7 27.9 %copy-start.1 = (bf16[1,288,3072]{2,1,0:T(8,128)(2,1)S(1)}, bf16[1,288,3072]{2,1,0:T(8,128)(2,1)}, u32[]{:S(2)}) copy-start(bf16[1,288,3072]{2,1,0:T(8,128)(2,1)} %param.18) | copy-start | bytes 5308420
  2.6 29.6 %collective-permute-start = (bf16[1,16,1,48,128]{4,3,2,1,0:T(8,128)(2,1)}, bf16[1,16,1,48,128]{4,3,2,1,0:T(8,128)(2,1)}, u32[]{:S(2)}, u32[]{:S(2)}) collective-permute-start(bf16[1,16,1,48,128]{4,3,2,1,0:T(8,128)(2,1)} %get-tuple-element.32), channel_id=1, source_target_pairs={{0,1},{1,2},{2,3},{3,4},{4,5},{5,6},{6,7},{7,8},{8,9},{9,10},{10,1... | collective-permute-start | bytes 589832 | tf_op jit(solution)/shard_map/ppermute | solution.py:18
  5.7 26.6 %collective-permute-start.1 = (bf16[1,16,1,48,128]{4,3,2,1,0:T(8,128)(2,1)}, bf16[1,16,1,48,128]{4,3,2,1,0:T(8,128)(2,1)}, u32[]{:S(2)}, u32[]{:S(2)}) collective-permute-start(bf16[1,16,1,48,128]{4,3,2,1,0:T(8,128)(2,1)} %get-tuple-element.33), channel_id=1, source_target_pairs={{1,0},{2,1},{3,2},{4,3},{5,4},{6,5},{7,6},{8,7},{9,8},{10,9},{11,1... | collective-permute-start | bytes 589832 | tf_op jit(solution)/shard_map/ppermute | solution.py:20
  7.9 16.8 %copy-start.23 = (s32[16]{0:T(128)}, s32[16]{0:T(128)S(1)}, u32[]{:S(2)}) copy-start(s32[16]{0:T(128)S(1)} %convert_reduce_fusion.2) | copy-start | bytes 196
  10.9 13.8 %copy-start.15 = (s32[192]{0:T(256)}, s32[192]{0:T(256)S(1)}, u32[]{:S(2)}) copy-start(s32[192]{0:T(256)S(1)} %add_add_fusion) | copy-start | bytes 2308
  12.0 18.7 %all-to-all-start = ((bf16[16,1,18]{2,1,0:T(2,128)(2,1)}), bf16[16,1,18]{2,1,0:T(2,128)(2,1)S(1)}, u32[]{:S(2)}, u32[]{:S(2)}) async-start(bf16[16,1,18]{2,1,0:T(2,128)(2,1)} %all_to_all.12), calls=%async_computation | async-start | bytes 16384 | tf_op jit(solution)/shard_map/all_to_all | solution.py:125
  21.3 8.8 %copy-start.17 = (s32[1,4]{1,0:T(1,128)S(1)}, s32[1,4]{1,0:T(1,128)}, u32[]{:S(2)}) copy-start(s32[1,4]{1,0:T(1,128)} %param.12) | copy-start | bytes 52
  21.3 8.8 %copy-start.18 = (s32[1,4]{1,0:T(1,128)S(1)}, s32[1,4]{1,0:T(1,128)}, u32[]{:S(2)}) copy-start(s32[1,4]{1,0:T(1,128)} %param.14) | copy-start | bytes 52
  21.3 8.8 %copy-start.20 = (s32[1,4]{1,0:T(1,128)S(1)}, s32[1,4]{1,0:T(1,128)}, u32[]{:S(2)}) copy-start(s32[1,4]{1,0:T(1,128)} %param.13) | copy-start | bytes 52
  21.3 11.0 %copy-start.4 = (bf16[1,16,4,48,128]{4,3,2,1,0:T(8,128)(2,1)S(1)}, bf16[1,16,4,48,128]{4,3,2,1,0:T(8,128)(2,1)}, u32[]{:S(2)}) copy-start(bf16[1,16,4,48,128]{4,3,2,1,0:T(8,128)(2,1)} %param.11) | copy-start | bytes 2359300
  28.9 1.8 %copy-start.8 = (f32[288]{0:T(512)}, f32[288]{0:T(512)S(1)}, u32[]{:S(2)}) copy-start(f32[288]{0:T(512)S(1)} %broadcast_multiply_fusion.1) | copy-start | bytes 3460
  43.5 2.3 %copy-start.5 = (bf16[1,3,3,128,128]{4,3,2,1,0:T(8,128)(2,1)S(1)}, bf16[1,3,3,128,128]{4,3,2,1,0:T(8,128)(2,1)}, u32[]{:S(2)}) copy-start(bf16[1,3,3,128,128]{4,3,2,1,0:T(8,128)(2,1)} %get-tuple-element.29) | copy-start | bytes 884740
  43.5 2.3 %copy-start.10 = (f32[16]{0:T(128)S(1)}, f32[16]{0:T(128)}, u32[]{:S(2)}) copy-start(f32[16]{0:T(128)} %get-tuple-element.34) | copy-start | bytes 196
  43.5 2.3 %copy-start.11 = (f32[16]{0:T(128)S(1)}, f32[16]{0:T(128)}, u32[]{:S(2)}) copy-start(f32[16]{0:T(128)} %get-tuple-element.35) | copy-start | bytes 196
  43.5 2.3 %copy-start.12 = (f32[16]{0:T(128)S(1)}, f32[16]{0:T(128)}, u32[]{:S(2)}) copy-start(f32[16]{0:T(128)} %get-tuple-element.36) | copy-start | bytes 196
  47.9 1.4 %copy-start.3 = (f32[1,16,4,48,128]{4,1,3,2,0:T(8,128)S(1)}, f32[1,16,4,48,128]{4,1,3,2,0:T(8,128)}, u32[]{:S(2)}) copy-start(f32[1,16,4,48,128]{4,1,3,2,0:T(8,128)} %copy.48) | copy-start | bytes 4718596
  49.3 2.3 %copy-start.6 = (bf16[2048,64]{0,1:T(8,128)(2,1)S(1)}, bf16[2048,64]{0,1:T(8,128)(2,1)}, u32[]{:S(2)}) copy-start(bf16[2048,64]{0,1:T(8,128)(2,1)} %param.17) | copy-start | bytes 786436
  49.3 3.8 %copy-start.16 = (s32[192]{0:T(256)S(1)}, s32[192]{0:T(256)}, u32[]{:S(2)}) copy-start(s32[192]{0:T(256)} %copy-done.15) | copy-start | bytes 2308
  49.3 10.9 %copy-start.9 = (f32[288]{0:T(512)S(1)}, f32[288]{0:T(512)}, u32[]{:S(2)}) copy-start(f32[288]{0:T(512)} %copy-done.8) | copy-start | bytes 3460
  54.2 12.7 %all-to-all-start.1 = ((bf16[16,2,576]{2,1,0:T(2,128)(2,1)}), bf16[16,2,576]{2,1,0:T(2,128)(2,1)S(1)}, u32[]{:S(2)}, u32[]{:S(2)}) async-start(bf16[16,2,576]{2,1,0:T(2,128)(2,1)} %reshape.275), calls=%async_computation.1 | async-start | bytes 81920 | tf_op jit(solution)/shard_map/all_to_all | solution.py:124
  60.2 7.0 %copy-start.21 = (f32[1,288,64]{1,2,0:T(8,128)S(1)}, f32[1,288,64]{1,2,0:T(8,128)}, u32[]{:S(2)}) copy-start(f32[1,288,64]{1,2,0:T(8,128)} %param.19) | copy-start | bytes 221188
  60.3 7.0 %copy-start.22 = (f32[1,288,64]{1,2,0:T(8,128)S(1)}, f32[1,288,64]{1,2,0:T(8,128)}, u32[]{:S(2)}) copy-start(f32[1,288,64]{1,2,0:T(8,128)} %param.20) | copy-start | bytes 221188
  62.1 5.9 %copy-start.13 = (f32[4]{0:T(128)S(1)}, f32[4]{0:T(128)}, u32[]{:S(2)}) copy-start(f32[4]{0:T(128)} %fusion.43) | copy-start | bytes 52
  62.1 6.0 %copy-start.14 = (f32[4]{0:T(128)S(1)}, f32[4]{0:T(128)}, u32[]{:S(2)}) copy-start(f32[4]{0:T(128)} %iota_add_fusion) | copy-start | bytes 52
  67.2 1.7 %copy-start.2 = (bf16[3072,288]{1,0:T(8,128)(2,1)S(1)}, bf16[3072,288]{1,0:T(8,128)(2,1)}, u32[]{:S(2)}) copy-start(bf16[3072,288]{1,0:T(8,128)(2,1)} %copy.59) | copy-start | bytes 5308420
  70.5 2.0 %collective-permute-start.2 = (f32[2,2,2,193,64]{3,4,2,1,0:T(8,128)S(1)}, f32[2,2,2,193,64]{3,4,2,1,0:T(8,128)S(1)}, u32[]{:S(2)}, u32[]{:S(2)}) collective-permute-start(f32[2,2,2,193,64]{3,4,2,1,0:T(8,128)S(1)} %dynamic-slice_bitcast_fusion), channel_id=1, source_target_pairs={{0,1},{1,0},{2,3},{3,2},{4,5},{5,4},{6,7},{7,6},{8,9},{9,8},{10,11... | collective-permute-start | bytes 1185800 | tf_op jit(solution)/shard_map/ppermute | solution.py:41
  72.6 8.4 %collective-permute-start.3 = (f32[2,2,193,64]{2,3,1,0:T(8,128)S(1)}, f32[2,2,193,64]{2,3,1,0:T(8,128)S(1)}, u32[]{:S(2)}, u32[]{:S(2)}) collective-permute-start(f32[2,2,193,64]{2,3,1,0:T(8,128)S(1)} %dynamic-slice_bitcast_fusion.1), channel_id=1, source_target_pairs={{0,2},{1,3},{2,0},{3,1},{4,6},{5,7},{6,4},{7,5},{8,10},{9,11},{10,... | collective-permute-start | bytes 592904 | tf_op jit(solution)/shard_map/ppermute | solution.py:41
  81.1 5.0 %collective-permute-start.4 = (f32[2,193,64]{1,2,0:T(8,128)S(1)}, f32[2,193,64]{1,2,0:T(8,128)S(1)}, u32[]{:S(2)}, u32[]{:S(2)}) collective-permute-start(f32[2,193,64]{1,2,0:T(8,128)S(1)} %dynamic-slice_bitcast_fusion.2), channel_id=1, source_target_pairs={{0,4},{1,5},{2,6},{3,7},{4,0},{5,1},{6,2},{7,3},{8,12},{9,13},{10,... | collective-permute-start | bytes 296456 | tf_op jit(solution)/shard_map/ppermute | solution.py:41
  86.2 5.9 %collective-permute-start.5 = (f32[193,64]{0,1:T(8,128)S(1)}, f32[193,64]{0,1:T(8,128)S(1)}, u32[]{:S(2)}, u32[]{:S(2)}) collective-permute-start(f32[193,64]{0,1:T(8,128)S(1)} %dynamic-slice_bitcast_fusion.3), channel_id=1, source_target_pairs={{0,8},{1,9},{2,10},{3,11},{4,12},{5,13},{6,14},{7,15},{8,0},{9,1},... | collective-permute-start | bytes 148232 | tf_op jit(solution)/shard_map/ppermute | solution.py:41
  92.1 4.3 %collective-permute-start.6 = (f32[193,64]{0,1:T(8,128)S(1)}, f32[193,64]{0,1:T(8,128)S(1)}, u32[]{:S(2)}, u32[]{:S(2)}) collective-permute-start(f32[193,64]{0,1:T(8,128)S(1)} %bitcast_add_fusion.3), channel_id=1, source_target_pairs={{0,16},{16,0},{1,17},{17,1},{2,18},{18,2},{3,19},{19,3},{4,20},{20... | collective-permute-start | bytes 148232 | tf_op jit(solution)/shard_map/ppermute | solution.py:45
  96.4 0.7 copy-start.7

commit v2 on v1

--- a/solution.py
+++ b/solution.py
@@ -24,45 +24,46 @@
     return cells
 
 
-def tree_reduce(grad_part, loss_row, nseq, ndp):
-    rows = grad_part.shape[0] // nseq
+def causal_conv(rimmed, conv_weight, keep):
+    nframes = rimmed.shape[0]
+    chans = rimmed.shape[-1]
+    padded = jnp.pad(rimmed, ((0, 0), (0, 0), (1, 1), (0, 0)))
+    kernel = jnp.transpose(conv_weight, (1, 2, 3, 0, 4)).reshape(3, 3, chans, 3 * chans)
+    each = lax.conv_general_dilated(
+        padded,
+        kernel,
+        (1, 1),
+        "VALID",
+        dimension_numbers=("NHWC", "HWIO", "NHWC"),
+        preferred_element_type=jnp.float32,
+    )
+    total = each[..., :chans]
+    for lag in (1, 2):
+        part = each[: nframes - lag, ..., lag * chans : (lag + 1) * chans]
+        part = jnp.pad(part, ((lag, 0), (0, 0), (0, 0), (0, 0)))
+        total = total + part * keep[lag][:, None, None, None]
+    return total
+
+
+def tree_reduce(grad_t, loss_line, nseq, ndp):
+    rows = grad_t.shape[1] // nseq
     nbits = nseq.bit_length() - 1
     assert 1 << nbits == nseq and ndp & (ndp - 1) == 0
-    blocks = grad_part.reshape(nseq, rows, LAT)
-    extra = jnp.broadcast_to(loss_row[None, None, :], (nseq, 1, LAT))
-    x = jnp.concatenate([blocks, extra], axis=1).reshape((2,) * nbits + (rows + 1, LAT))
+    x = jnp.concatenate([grad_t, loss_line[None, :]], axis=0)
+    x = x.reshape((x.shape[0],) + (2,) * nbits + (rows,))
     me = lax.axis_index("seq")
     left = list(range(nbits - 1, -1, -1))
     for k in range(nbits):
-        axis = left.index(k)
+        axis = left.index(k) + 1
         bit = (me >> k) & 1
         keep = lax.dynamic_index_in_dim(x, bit, axis, keepdims=False)
         send = lax.dynamic_index_in_dim(x, 1 - bit, axis, keepdims=False)
         x = keep + lax.ppermute(send, "seq", [(i, i ^ (1 << k)) for i in range(nseq)])
-        left.pop(axis)
-    x = x.reshape(rows + 1, LAT)
+        left.pop(axis - 1)
+    x = x.reshape(-1, rows)
     for k in range(ndp.bit_length() - 1):
         x = x + lax.ppermute(x, "dp", [(i, i ^ (1 << k)) for i in range(ndp)])
     return x
-
-
-def conv_rows(padded, kernel, keep, first, count):
-    nframes = keep.shape[1]
-    width = padded.shape[2] - 2
-    chans = padded.shape[3]
-    total = jnp.zeros((nframes, count * width, chans), jnp.float32)
-    for lag in range(3):
-        pieces = [
-            padded[2 - lag : 2 - lag + nframes, first + i : first + i + count, j : j + width, :]
-            for i in range(3)
-            for j in range(3)
-        ]
-        columns = jnp.concatenate(pieces, axis=-1).reshape(-1, 9 * chans)
-        part = jnp.dot(
-            columns, kernel[lag].reshape(9 * chans, chans), preferred_element_type=jnp.float32
-        )
-        total = total + part.reshape(nframes, count * width, chans) * keep[lag][:, None, None]
-    return total.reshape(nframes, count, width, chans)
 
 
 def per_device(
@@ -92,18 +93,21 @@
     starts = jnp.sum(clip_hot * (ends - counts)[None, :], axis=1)
     keep = jnp.stack([(index - lag >= starts).astype(jnp.float32) for lag in range(3)])
     rimmed = with_halo(frames, (("seq", 2),), 1)[0]
-    outer_pad = jnp.pad(rimmed, ((2, 0), (0, 0), (1, 1), (0, 0)))
-    conv = conv_rows(outer_pad, conv_weight, keep, 0, nrows)
+    conv = causal_conv(rimmed, conv_weight, keep)
     cells = (local.astype(jnp.float32) + jax.nn.silu(conv)).astype(jnp.bfloat16)
-    patches = (
-        cells.reshape(nframes, tok_rows, 4, tok_cols, 4, chans)
-        .transpose(0, 1, 3, 2, 4, 5)
-        .reshape(-1, 16 * chans)
-    )
-    tokens = jnp.dot(patches, w_latent, preferred_element_type=jnp.float32).astype(jnp.bfloat16)
+    tokens = lax.conv_general_dilated(
+        cells,
+        w_latent.reshape(4, 4, chans, LAT),
+        (4, 4),
+        "VALID",
+        dimension_numbers=("NHWC", "HWIO", "NHWC"),
+        preferred_element_type=jnp.float32,
+    ).astype(jnp.bfloat16)
     latent_out = tokens.reshape(1, nframes, tok_rows, tok_cols * LAT)
+    tokens = tokens.reshape(-1, LAT)
     slots = hidden.shape[1]
     capacity = slots // nseq
+    assert capacity <= LAT
     owners = owner_map.reshape(-1)
     owner_hot = (owners[:, None] == jnp.arange(nseq, dtype=jnp.int32)[None, :]).astype(jnp.int32)
     rank = jnp.sum(jnp.cumsum(owner_hot, axis=0) * owner_hot, axis=1) - 1
@@ -118,14 +122,14 @@
     labels = (
         jnp.dot(select, tok_clip.astype(jnp.bfloat16)[:, None], preferred_element_type=jnp.float32)
         .astype(jnp.bfloat16)
-        .reshape(nseq, capacity)
+        .reshape(nseq, 1, capacity)
     )
-    arrived, arrived_tags = (
-        lax.all_to_all(outgoing, "seq", split_axis=0, concat_axis=0, tiled=True),
-        lax.all_to_all(labels, "seq", split_axis=0, concat_axis=0, tiled=True),
+    labels = jnp.pad(labels, ((0, 0), (0, 0), (0, LAT - capacity)))
+    arrived = lax.all_to_all(
+        jnp.concatenate([outgoing, labels], axis=1), "seq", split_axis=0, concat_axis=0, tiled=True
     )
-    x0 = arrived.reshape(slots, LAT).astype(jnp.float32)
-    tag = arrived_tags.reshape(slots).astype(jnp.float32)
+    x0 = arrived[:, :capacity].reshape(slots, LAT).astype(jnp.float32)
+    tag = arrived[:, capacity, :capacity].reshape(slots).astype(jnp.float32)
     kind = clip_group[0].astype(jnp.float32)
     coef = (
         (2.0 * kind - 1.0)
@@ -148,15 +152,17 @@
     err = jnp.sum(diff * diff, axis=1)
     partial_loss = coef * jnp.sum(slot_hot * err[:, None], axis=0)
     dpred = (2.0 * slot_coef[:, None] * diff).astype(jnp.bfloat16)
-    grad_part = lax.dot_general(
-        normed, dpred, (((0,), (0,)), ((), ())), preferred_element_type=jnp.float32
+    grad_t = lax.dot_general(
+        dpred, normed, (((0,), (0,)), ((), ())), preferred_element_type=jnp.float32
     )
     ndp = lax.axis_size("dp")
+    share = grad_t.shape[1] // nseq
+    assert ndp * CLIPS <= share
     place = lax.axis_index("dp") * CLIPS
-    loss_row = lax.dynamic_update_slice(jnp.zeros((LAT,), jnp.float32), partial_loss, (place,))
-    summed = tree_reduce(grad_part, loss_row, nseq, ndp)
-    grad_mine = summed[:-1]
-    clip_loss = lax.dynamic_slice_in_dim(summed[-1], place, CLIPS).reshape(1, CLIPS)
+    loss_row = lax.dynamic_update_slice(jnp.zeros((share,), jnp.float32), partial_loss, (place,))
+    summed = tree_reduce(grad_t, jnp.tile(loss_row, nseq), nseq, ndp)
+    grad_mine = summed[:LAT].T
+    clip_loss = lax.dynamic_slice_in_dim(summed[LAT], place, CLIPS).reshape(1, CLIPS)
     return (latent_out, clip_loss, grad_mine)
 
 

time: 97.8 us -> 74.9 us (0.77)
  local copies, waits for them, and re-layouts: 26.6 us -> 13.1 us
  waiting for transfers between devices: 19.5 us -> 29 us
  starting transfers between devices: 25.1 us -> 15.7 us
  other arithmetic: 14.6 us -> 5.35 us
    conv_general_dilated x0 -> x2, matrix products: none -> 7.97 us  [the longest x1 5.55 us: causal_conv(): lax.conv_general_dilated(padded, kernel, (1, 1), 'VALID', dimension_numbe...]
    dot_general x5 -> x1, matrix products: 8.92 us -> 1.11 us  [per_device(): lax.dot_general(dpred, normed, (((0,), (0,)), ((), ())), preferred_elemen...]
    all_to_all x2 -> x1, starting transfers between devices: 14.6 us -> 8.63 us  [per_device(): lax.all_to_all(jnp.concatenate([outgoing, labels], axis=1), 'seq', split_...]
    all_to_all x2 -> x1, waiting for transfers between devices: 0.79 us -> 6.69 us  [per_device(): lax.all_to_all(jnp.concatenate([outgoing, labels], axis=1), 'seq', split_...]
    unnamed x70 -> x25, local copies, waits for them, and re-layouts: 8.58 us -> 5.13 us
    ppermute x4, waiting for transfers between devices: 16.8 us -> 20.2 us  [tree_reduce(): x = keep + lax.ppermute(send, 'seq', [(i, i ^ 1 << k) for i in range(nseq)])]
    ppermute x4, starting transfers between devices: 4.57 us -> 1.19 us  [tree_reduce(): x = keep + lax.ppermute(send, 'seq', [(i, i ^ 1 << k) for i in range(nseq)])]
    convert_element_type x5 -> x4, local copies, waits for them, and re-layouts: 3.16 us -> 0.24 us  [the longest x2 0.13 us: per_device(): x0 = arrived[:, :capacity].reshape(slots, LAT).astype(jnp.float32)]
  transfers between devices with their start and end apart: 9 -> 8, of which waited for: 6 -> 6; matrix products, arithmetic and copies ran while one was open for 23% -> 8% of each run, Pallas kernels for 0% -> 0%
where the time goes in v2:
time: 74.9 us; the launch traced here: 74.5 us
  waiting for transfers between devices  29 us (39%)
  starting transfers between devices  15.7 us (21%)
  local copies, waits for them, and re-layouts  13.1 us (17%)
  matrix products  10.3 us (14%)
  other arithmetic  5.35 us (7%)
  between operations  1.09 us (1%)
    ppermute x4, waiting for transfers between devices, tree_reduce(): x = keep + lax.ppermute(send, 'seq', [(i, i ^ 1 << k) for i in range(nseq)])  20.2 us
    all_to_all x1, starting transfers between devices, per_device(): lax.all_to_all(jnp.concatenate([outgoing, labels], axis=1), 'seq', split_...  8.63 us
    all_to_all x1, waiting for transfers between devices, per_device(): lax.all_to_all(jnp.concatenate([outgoing, labels], axis=1), 'seq', split_...  6.69 us
    conv_general_dilated x1, matrix products, causal_conv(): lax.conv_general_dilated(padded, kernel, (1, 1), 'VALID', dimension_numbe...  5.55 us
    unnamed x25, local copies, waits for them, and re-layouts  5.13 us
    ppermute x1, starting transfers between devices, with_halo(): lax.ppermute(tail, axis, [(i, (i + 1) % count) for i in range(ends)])  3.06 us
    dot_general x1, local copies, waits for them, and re-layouts, per_device(): lax.dot_general(dpred, normed, (((0,), (0,)), ((), ())), preferred_elemen...  2.87 us
    conv_general_dilated x1, matrix products, per_device(): lax.conv_general_dilated(cells, w_latent.reshape(4, 4, chans, LAT), (4, 4...  2.42 us
  transfers between devices with their start and end apart: 8, of which 6 were waited for; matrix products, arithmetic and copies ran while one was open for 8% of the time, Pallas kernels for 0%

profile of v2, /device:TPU:0, one launch (start us, length us, event | category | flops | bytes accessed | tf_op | source)
XLA Modules:
  0.0 74.5 jit_solution(8676123405139931236)
XLA Ops:
  0.6 0.0 copy-start
  0.7 1.7 %copy.50 = bf16[1,16,4,48,128]{4,1,3,2,0:T(8,128)(2,1)S(1)} copy(bf16[1,16,4,48,128]{4,3,2,1,0:T(8,128)(2,1)} %param.11) | data formatting | bytes 1572864 | tf_op args[0]
  2.4 0.0 copy-start.3
  2.4 0.8 %fusion.38 = (bf16[1,16,1,48,128]{4,1,3,2,0:T(8,128)(2,1)}, bf16[1,16,1,48,128]{4,1,3,2,0:T(8,128)(2,1)}) fusion(bf16[1,16,4,48,128]{4,1,3,2,0:T(8,128)(2,1)S(1)} %copy.50), kind=kLoop, calls=%fused_computation.101 | loop fusion | bytes 786432 | tf_op jit(solution)/shard_map/slice | solution.py:15
  3.2 3.1 %collective-permute-start = (bf16[1,16,1,48,128]{4,1,3,2,0:T(8,128)(2,1)}, bf16[1,16,1,48,128]{4,1,3,2,0:T(8,128)(2,1)}, u32[]{:S(2)}, u32[]{:S(2)}) collective-permute-start(bf16[1,16,1,48,128]{4,1,3,2,0:T(8,128)(2,1)} %get-tuple-element.7), channel_id=1, source_target_pairs={{0,1},{1,2},{2,3},{3,4},{4,5},{5,6},{6,7},{7,8},{8,9},{9,10},{10,1... | collective-permute-start | bytes 589832 | tf_op jit(solution)/shard_map/ppermute | solution.py:18
  6.2 1.3 %collective-permute-start.1 = (bf16[1,16,1,48,128]{4,1,3,2,0:T(8,128)(2,1)}, bf16[1,16,1,48,128]{4,1,3,2,0:T(8,128)(2,1)}, u32[]{:S(2)}, u32[]{:S(2)}) collective-permute-start(bf16[1,16,1,48,128]{4,1,3,2,0:T(8,128)(2,1)} %get-tuple-element.8), channel_id=1, source_target_pairs={{1,0},{2,1},{3,2},{4,3},{5,4},{6,5},{7,6},{8,7},{9,8},{10,9},{11,1... | collective-permute-start | bytes 589832 | tf_op jit(solution)/shard_map/ppermute | solution.py:20
  7.5 2.3 %copy.54 = bf16[3,3,3,128,128]{3,4,0,2,1:T(8,128)(2,1)} copy(bf16[3,3,3,128,128]{4,3,2,1,0:T(8,128)(2,1)} %param.16) | data formatting | bytes 1769472 | tf_op args[5]
  9.8 0.2 reduce-window.10
  10.0 0.1 convert_reduce_fusion.1
  10.1 0.1 select_reduce_fusion
  10.2 0.2 reshape.141
  10.4 0.6 reduce-window.11
  11.0 0.2 slice_reduce_fusion
  11.2 0.1 bitcast_bitcast_fusion
  11.3 0.1 broadcast_in_dim.2
  11.4 0.1 reshape.153
  11.5 0.2 convolution_reduce_fusion
  11.7 0.1 reshape.157
  11.9 0.3 convert_reduce_fusion
  12.2 0.6 fusion.3
  12.9 5.6 %fusion.7 = f32[16,4,48,384]{3,0,2,1:T(8,128)S(1)} fusion(bf16[3,3,128,384]{2,3,1,0:T(8,128)(2,1)} %bitcast.111, bf16[1,16,1,48,128]{4,1,3,2,0:T(8,128)(2,1)} %collective-permute-done.1, bf16[1,16,4,48,128]{4,1,3,2,0:T(8,128)(2,1)S(1)} %copy.50, bf16[1,16,1,48,128]{4,1,3,2,0:T(8,128)(2,1)} %collective-permute-done), kind=kOutput, calls=%fused_computation.14 | convolution fusion | flops 2683699200 | bytes 6782976 | tf_op jit(solution)/shard_map/conv_general_dilated | solution.py:32
  18.4 0.1 slice.51
  18.5 0.1 slice.52
  18.7 2.4 %convolution_convert_fusion.1 = bf16[16,1,12,64]{3,0,2,1:T(8,128)(2,1)S(1)} fusion(f32[16,4,48,384]{3,0,2,1:T(8,128)S(1)} %fusion.7, f32[14,4,48,128]{3,0,2,1:T(8,128)S(1)} %slice.52, f32[15,4,48,128]{3,0,2,1:T(8,128)S(1)} %slice.51, f32[16]{0:T(128)S(1)} %get-tuple-element.16, f32[16]{0:T(128)S(1)} %get-tuple-element.15, ...), kind=kOutput, calls=%fused_computation.23 | convolution fusion | flops 54669312 | bytes 5792768 | tf_op jit(solution)/shard_map/conv_general_dilated | solution.py:98
  21.1 0.2 convolution_convert_fusion
  21.4 0.1 copy.60
  21.6 0.7 reshape.167
  22.3 8.6 %all-to-all-start = ((bf16[16,2,608]{2,1,0:T(2,128)(2,1)}), bf16[16,2,608]{2,1,0:T(2,128)(2,1)S(1)}, u32[]{:S(2)}, u32[]{:S(2)}) async-start(bf16[16,2,608]{2,1,0:T(2,128)(2,1)} %reshape.167), calls=%async_computation | async-start | bytes 81920 | tf_op jit(solution)/shard_map/all_to_all | solution.py:128
  31.0 6.7 %all-to-all-done = bf16[16,2,608]{2,1,0:T(2,128)(2,1)S(1)} async-done(((bf16[16,2,608]{2,1,0:T(2,128)(2,1)}), bf16[16,2,608]{2,1,0:T(2,128)(2,1)S(1)}, u32[]{:S(2)}, u32[]{:S(2)}) %all-to-all-start) | async-done | bytes 38944 | tf_op jit(solution)/shard_map/all_to_all | solution.py:128
  37.7 0.1 reshape.168
  37.9 0.1 reshape.151
  38.0 0.1 copy.62
  38.1 0.1 fusion.29
  38.2 0.0 copy-start.7
  38.2 0.0 copy-start.8
  38.2 1.9 %fusion.36 = bf16[3072,288]{0,1:T(8,128)(2,1)} fusion(f32[288]{0:T(512)S(1)} %get-tuple-element.19, f32[288]{0:T(512)S(1)} %broadcast_multiply_fusion, bf16[1,288,3072]{2,1,0:T(8,128)(2,1)S(1)} %copy-done.1), kind=kLoop, calls=%fused_computation.100 | loop fusion | flops 3538944 | bytes 3541248 | tf_op jit(solution)/shard_map/dot_general | solution.py:155
  40.1 0.8 %multiply_reduce_fusion = (f32[288]{0:T(512)S(1)}, f32[288,64]{0,1:T(8,128)S(1)}) fusion(f32[288,64]{0,1:T(8,128)S(1)} %copy.62, f32[1,288,64]{1,2,0:T(8,128)S(1)} %copy-done.7, f32[288]{0:T(512)S(1)} %get-tuple-element.20, f32[1,288,64]{1,2,0:T(8,128)S(1)} %copy-done.8, f32[288]{0:T(512)S(1)} %fusion.29, bf16[3072,64]{0,1:T(8,128)(2,1)S(1)} %copy-done, ...), kind=kOutput, calls=%fused_computation.45 | convolution fusion | flops 116913888 | bytes 2463360 | tf_op jit(solution)/shard_map/dot_general | solution.py:149
  40.9 0.2 fusion.30
  41.1 2.9 %copy.67 = bf16[3072,288]{1,0:T(8,128)(2,1)S(1)} copy(bf16[3072,288]{0,1:T(8,128)(2,1)} %fusion.36) | data formatting | bytes 3538944 | tf_op jit(solution)/shard_map/dot_general | solution.py:155
  44.0 1.1 %fusion.23 = f32[64,2,2,2,2,192]{5,0,4,3,2,1:T(8,128)S(1)} fusion(bf16[2,2,2,2,192,288]{5,4,3,2,1,0:T(8,128)(2,1)S(1)} %bitcast.110, f32[288,64]{0,1:T(8,128)S(1)} %get-tuple-element.18, f32[288]{0:T(512)S(1)} %broadcast_multiply_fusion.1), kind=kOutput, calls=%fused_computation.51 | convolution fusion | flops 113283072 | bytes 2630784 | tf_op jit(solution)/shard_map/dot_general | solution.py:155
  45.1 0.2 bitcast_dynamic-update-slice_fusion
  45.3 0.1 fusion.14
  45.5 0.3 copy.92
  45.8 0.1 collective-permute-start.2
  45.8 1.9 %collective-permute-done.2 = f32[65,2,2,2,192]{4,3,2,1,0:T(2,128)S(1)} collective-permute-done((f32[65,2,2,2,192]{4,3,2,1,0:T(2,128)S(1)}, f32[65,2,2,2,192]{4,3,2,1,0:T(2,128)S(1)}, u32[]{:S(2)}, u32[]{:S(2)}) %collective-permute-start.2) | collective-permute-done | bytes 399392 | tf_op jit(solution)/shard_map/ppermute | solution.py:61
  47.7 0.4 bitcast_add_fusion
  48.1 0.5 constant_dynamic-slice_fusion.6
  48.6 0.1 copy.93
  48.7 0.4 collective-permute-start.3
  49.1 8.1 %collective-permute-done.3 = f32[65,2,2,192]{3,2,1,0:T(2,128)S(1)} collective-permute-done((f32[65,2,2,192]{3,2,1,0:T(2,128)S(1)}, f32[65,2,2,192]{3,2,1,0:T(2,128)S(1)}, u32[]{:S(2)}, u32[]{:S(2)}) %collective-permute-start.3) | collective-permute-done | bytes 199712 | tf_op jit(solution)/shard_map/ppermute | solution.py:61
  57.2 0.2 bitcast_add_fusion.1
  57.4 0.2 constant_dynamic-slice_fusion.4
  57.7 0.1 copy.94
  57.8 0.4 collective-permute-start.4
  58.1 4.7 %collective-permute-done.4 = f32[65,2,192]{2,1,0:T(2,128)S(1)} collective-permute-done((f32[65,2,192]{2,1,0:T(2,128)S(1)}, f32[65,2,192]{2,1,0:T(2,128)S(1)}, u32[]{:S(2)}, u32[]{:S(2)}) %collective-permute-start.4) | collective-permute-done | bytes 99872 | tf_op jit(solution)/shard_map/ppermute | solution.py:61
  62.8 0.1 bitcast_add_fusion.2
  62.9 0.1 constant_dynamic-slice_fusion.2
  63.0 0.4 collective-permute-start.5
  63.5 5.4 %collective-permute-done.5 = f32[65,192]{1,0:T(8,128)S(1)} collective-permute-done((f32[65,192]{1,0:T(8,128)S(1)}, f32[65,192]{1,0:T(8,128)S(1)}, u32[]{:S(2)}, u32[]{:S(2)}) %collective-permute-start.5) | collective-permute-done | bytes 49952 | tf_op jit(solution)/shard_map/ppermute | solution.py:61
  68.9 1.6 %collective-permute-start.6 = (f32[65,192]{1,0:T(8,128)S(1)}, f32[65,192]{1,0:T(8,128)S(1)}, u32[]{:S(2)}, u32[]{:S(2)}) collective-permute-start(f32[65,192]{1,0:T(8,128)S(1)} %bitcast_add_fusion.3), channel_id=1, source_target_pairs={{0,16},{16,0},{1,17},{17,1},{2,18},{18,2},{3,19},{19,3},{4,20},{20... | collective-permute-start | bytes 149768 | tf_op jit(solution)/shard_map/ppermute | solution.py:65
  70.5 0.7 reshape.142
  71.2 2.1 %collective-permute-done.6 = f32[65,192]{1,0:T(8,128)S(1)} collective-permute-done((f32[65,192]{1,0:T(8,128)S(1)}, f32[65,192]{1,0:T(8,128)S(1)}, u32[]{:S(2)}, u32[]{:S(2)}) %collective-permute-start.6) | collective-permute-done | bytes 49952 | tf_op jit(solution)/shard_map/ppermute | solution.py:65
  73.3 0.6 slice_bitcast_fusion
  74.0 0.6 constant_dynamic-slice_fusion
  (44 shorter events, 0.4 us)
Async XLA Ops:
  0.6 39.5 %copy-start = (bf16[3072,64]{0,1:T(8,128)(2,1)S(1)}, bf16[3072,64]{0,1:T(8,128)(2,1)}, u32[]{:S(2)}) copy-start(bf16[3072,64]{0,1:T(8,128)(2,1)} %param.21) | copy-start | bytes 1179652
  0.6 9.2 %copy-start.4 = (s32[1,4]{1,0:T(1,128)S(1)}, s32[1,4]{1,0:T(1,128)}, u32[]{:S(2)}) copy-start(s32[1,4]{1,0:T(1,128)} %param.12) | copy-start | bytes 52
  0.7 9.5 %copy-start.2 = (bf16[2048,64]{0,1:T(8,128)(2,1)S(1)}, bf16[2048,64]{0,1:T(8,128)(2,1)}, u32[]{:S(2)}) copy-start(bf16[2048,64]{0,1:T(8,128)(2,1)} %param.17) | copy-start | bytes 786436
  2.4 8.0 %copy-start.3 = (s32[1,1,192,1]{2,3,1,0:T(1,128)S(1)}, s32[1,1,192,1]{2,3,1,0:T(1,128)}, u32[]{:S(2)}) copy-start(s32[1,1,192,1]{2,3,1,0:T(1,128)} %param.15) | copy-start | bytes 2308
  2.4 9.4 %copy-start.1 = (bf16[1,288,3072]{2,1,0:T(8,128)(2,1)S(1)}, bf16[1,288,3072]{2,1,0:T(8,128)(2,1)}, u32[]{:S(2)}) copy-start(bf16[1,288,3072]{2,1,0:T(8,128)(2,1)} %param.18) | copy-start | bytes 5308420
  3.2 9.7 %collective-permute-start = (bf16[1,16,1,48,128]{4,1,3,2,0:T(8,128)(2,1)}, bf16[1,16,1,48,128]{4,1,3,2,0:T(8,128)(2,1)}, u32[]{:S(2)}, u32[]{:S(2)}) collective-permute-start(bf16[1,16,1,48,128]{4,1,3,2,0:T(8,128)(2,1)} %get-tuple-element.7), channel_id=1, source_target_pairs={{0,1},{1,2},{2,3},{3,4},{4,5},{5,6},{6,7},{7,8},{8,9},{9,10},{10,1... | collective-permute-start | bytes 589832 | tf_op jit(solution)/shard_map/ppermute | solution.py:18
  6.2 6.6 %collective-permute-start.1 = (bf16[1,16,1,48,128]{4,1,3,2,0:T(8,128)(2,1)}, bf16[1,16,1,48,128]{4,1,3,2,0:T(8,128)(2,1)}, u32[]{:S(2)}, u32[]{:S(2)}) collective-permute-start(bf16[1,16,1,48,128]{4,1,3,2,0:T(8,128)(2,1)} %get-tuple-element.8), channel_id=1, source_target_pairs={{1,0},{2,1},{3,2},{4,3},{5,4},{6,5},{7,6},{8,7},{9,8},{10,9},{11,1... | collective-permute-start | bytes 589832 | tf_op jit(solution)/shard_map/ppermute | solution.py:20
  11.8 1.0 %copy-start.5 = (s32[1,4]{1,0:T(1,128)S(1)}, s32[1,4]{1,0:T(1,128)}, u32[]{:S(2)}) copy-start(s32[1,4]{1,0:T(1,128)} %param.14) | copy-start | bytes 52
  11.8 1.0 %copy-start.6 = (s32[1,4]{1,0:T(1,128)S(1)}, s32[1,4]{1,0:T(1,128)}, u32[]{:S(2)}) copy-start(s32[1,4]{1,0:T(1,128)} %param.13) | copy-start | bytes 52
  22.3 15.3 %all-to-all-start = ((bf16[16,2,608]{2,1,0:T(2,128)(2,1)}), bf16[16,2,608]{2,1,0:T(2,128)(2,1)S(1)}, u32[]{:S(2)}, u32[]{:S(2)}) async-start(bf16[16,2,608]{2,1,0:T(2,128)(2,1)} %reshape.167), calls=%async_computation | async-start | bytes 81920 | tf_op jit(solution)/shard_map/all_to_all | solution.py:128
  38.2 1.9 %copy-start.7 = (f32[1,288,64]{1,2,0:T(8,128)S(1)}, f32[1,288,64]{1,2,0:T(8,128)}, u32[]{:S(2)}) copy-start(f32[1,288,64]{1,2,0:T(8,128)} %param.19) | copy-start | bytes 221188
  38.2 1.9 %copy-start.8 = (f32[1,288,64]{1,2,0:T(8,128)S(1)}, f32[1,288,64]{1,2,0:T(8,128)}, u32[]{:S(2)}) copy-start(f32[1,288,64]{1,2,0:T(8,128)} %param.20) | copy-start | bytes 221188
  45.8 2.0 %collective-permute-start.2 = (f32[65,2,2,2,192]{4,3,2,1,0:T(2,128)S(1)}, f32[65,2,2,2,192]{4,3,2,1,0:T(2,128)S(1)}, u32[]{:S(2)}, u32[]{:S(2)}) collective-permute-start(f32[65,2,2,2,192]{4,3,2,1,0:T(2,128)S(1)} %bitcast.112), channel_id=1, source_target_pairs={{0,1},{1,0},{2,3},{3,2},{4,5},{5,4},{6,7},{7,6},{8,9},{9,8},{10,11... | collective-permute-start | bytes 1198088 | tf_op jit(solution)/shard_map/ppermute | solution.py:61
  48.7 8.5 %collective-permute-start.3 = (f32[65,2,2,192]{3,2,1,0:T(2,128)S(1)}, f32[65,2,2,192]{3,2,1,0:T(2,128)S(1)}, u32[]{:S(2)}, u32[]{:S(2)}) collective-permute-start(f32[65,2,2,192]{3,2,1,0:T(2,128)S(1)} %bitcast.113), channel_id=1, source_target_pairs={{0,2},{1,3},{2,0},{3,1},{4,6},{5,7},{6,4},{7,5},{8,10},{9,11},{10,... | collective-permute-start | bytes 599048 | tf_op jit(solution)/shard_map/ppermute | solution.py:61
  57.8 5.1 %collective-permute-start.4 = (f32[65,2,192]{2,1,0:T(2,128)S(1)}, f32[65,2,192]{2,1,0:T(2,128)S(1)}, u32[]{:S(2)}, u32[]{:S(2)}) collective-permute-start(f32[65,2,192]{2,1,0:T(2,128)S(1)} %bitcast.114), channel_id=1, source_target_pairs={{0,4},{1,5},{2,6},{3,7},{4,0},{5,1},{6,2},{7,3},{8,12},{9,13},{10,... | collective-permute-start | bytes 299528 | tf_op jit(solution)/shard_map/ppermute | solution.py:61
  63.0 5.8 %collective-permute-start.5 = (f32[65,192]{1,0:T(8,128)S(1)}, f32[65,192]{1,0:T(8,128)S(1)}, u32[]{:S(2)}, u32[]{:S(2)}) collective-permute-start(f32[65,192]{1,0:T(8,128)S(1)} %bitcast.115), channel_id=1, source_target_pairs={{0,8},{1,9},{2,10},{3,11},{4,12},{5,13},{6,14},{7,15},{8,0},{9,1},... | collective-permute-start | bytes 149768 | tf_op jit(solution)/shard_map/ppermute | solution.py:61
  68.9 4.4 %collective-permute-start.6 = (f32[65,192]{1,0:T(8,128)S(1)}, f32[65,192]{1,0:T(8,128)S(1)}, u32[]{:S(2)}, u32[]{:S(2)}) collective-permute-start(f32[65,192]{1,0:T(8,128)S(1)} %bitcast_add_fusion.3), channel_id=1, source_target_pairs={{0,16},{16,0},{1,17},{17,1},{2,18},{18,2},{3,19},{19,3},{4,20},{20... | collective-permute-start | bytes 149768 | tf_op jit(solution)/shard_map/ppermute | solution.py:65

commit v3 on v2

--- a/solution.py
+++ b/solution.py
@@ -1,6 +1,8 @@
 import jax
 import jax.numpy as jnp
 from jax import lax
+from jax.experimental import pallas as pl
+from jax.experimental.pallas import tpu as pltpu
 from jax.sharding import PartitionSpec as P
 
 LAT = 64
@@ -26,23 +28,48 @@
 
 def causal_conv(rimmed, conv_weight, keep):
     nframes = rimmed.shape[0]
-    chans = rimmed.shape[-1]
     padded = jnp.pad(rimmed, ((0, 0), (0, 0), (1, 1), (0, 0)))
-    kernel = jnp.transpose(conv_weight, (1, 2, 3, 0, 4)).reshape(3, 3, chans, 3 * chans)
-    each = lax.conv_general_dilated(
-        padded,
-        kernel,
-        (1, 1),
-        "VALID",
-        dimension_numbers=("NHWC", "HWIO", "NHWC"),
-        preferred_element_type=jnp.float32,
-    )
-    total = each[..., :chans]
-    for lag in (1, 2):
-        part = each[: nframes - lag, ..., lag * chans : (lag + 1) * chans]
-        part = jnp.pad(part, ((lag, 0), (0, 0), (0, 0), (0, 0)))
-        total = total + part * keep[lag][:, None, None, None]
+    total = None
+    for lag in range(3):
+        part = lax.conv_general_dilated(
+            padded[: nframes - lag],
+            conv_weight[lag],
+            (1, 1),
+            "VALID",
+            dimension_numbers=("NHWC", "HWIO", "NHWC"),
+            preferred_element_type=jnp.float32,
+        )
+        if lag == 0:
+            total = part
+        else:
+            part = jnp.pad(part, ((lag, 0), (0, 0), (0, 0), (0, 0)))
+            total = total + part * keep[lag][:, None, None, None]
     return total
+
+
+def _grad_kernel(dpt_ref, normed_ref, out_ref):
+    out_ref[...] = jnp.dot(dpt_ref[...], normed_ref[...], preferred_element_type=jnp.float32)
+
+
+def grad_matmul(dpt, normed):
+    lat, slots = dpt.shape
+    feats = normed.shape[1]
+    tile = 512 if feats % 512 == 0 else feats
+    return pl.pallas_call(
+        _grad_kernel,
+        out_shape=jax.ShapeDtypeStruct((lat, feats), jnp.float32),
+        grid=(feats // tile,),
+        in_specs=[
+            pl.BlockSpec((lat, slots), lambda i: (0, 0)),
+            pl.BlockSpec((slots, tile), lambda i: (0, i)),
+        ],
+        out_specs=pl.BlockSpec((lat, tile), lambda i: (0, i)),
+        cost_estimate=pl.CostEstimate(
+            flops=2 * lat * slots * feats,
+            bytes_accessed=2 * lat * slots + 2 * slots * feats + 4 * lat * feats,
+            transcendentals=0,
+        ),
+    )(dpt, normed)
 
 
 def tree_reduce(grad_t, loss_line, nseq, ndp):
@@ -152,9 +179,7 @@
     err = jnp.sum(diff * diff, axis=1)
     partial_loss = coef * jnp.sum(slot_hot * err[:, None], axis=0)
     dpred = (2.0 * slot_coef[:, None] * diff).astype(jnp.bfloat16)
-    grad_t = lax.dot_general(
-        dpred, normed, (((0,), (0,)), ((), ())), preferred_element_type=jnp.float32
-    )
+    grad_t = grad_matmul(dpred.T, normed)
     ndp = lax.axis_size("dp")
     share = grad_t.shape[1] // nseq
     assert ndp * CLIPS <= share

time: 74.9 us -> 81.6 us (1.089)
  Pallas kernels: 0 us -> 4.87 us
  local copies, waits for them, and re-layouts: 13.1 us -> 9.97 us
  matrix products: 10.3 us -> 13 us
  other arithmetic: 5.35 us -> 7.5 us
    pallas_call x0 -> x1, Pallas kernels: none -> 4.87 us  [grad_matmul(): pl.pallas_call(_grad_kernel, out_shape=jax.ShapeDtypeStruct((lat, feats),...]
    conv_general_dilated x1, matrix products: 2.42 us -> 5.4 us  [per_device(): lax.conv_general_dilated(cells, w_latent.reshape(4, 4, chans, LAT), (4, 4...]
    dot_general x1 -> x0, local copies, waits for them, and re-layouts: 2.87 us -> none  [per_device(): lax.dot_general(dpred, normed, (((0,), (0,)), ((), ())), preferred_elemen...]
    concatenate x1 -> x2, local copies, waits for them, and re-layouts: 0.01 us -> 2.09 us  [tree_reduce(): x = jnp.concatenate([grad_t, loss_line[None, :]], axis=0)]
    dot_general x1 -> x0, other arithmetic: 1.88 us -> none  [per_device(): lax.dot_general(dpred, normed, (((0,), (0,)), ((), ())), preferred_elemen...]
    squeeze x0 -> x1, other arithmetic: none -> 1.79 us  [per_device(): rimmed = with_halo(frames, (('seq', 2),), 1)[0]]
    unnamed x25 -> x29, local copies, waits for them, and re-layouts: 5.13 us -> 3.44 us
    dot_general x1 -> x0, matrix products: 1.11 us -> none  [per_device(): lax.dot_general(dpred, normed, (((0,), (0,)), ((), ())), preferred_elemen...]
  transfers between devices with their start and end apart: 8 -> 8, of which waited for: 6 -> 6; matrix products, arithmetic and copies ran while one was open for 8% -> 5% of each run, Pallas kernels for 0% -> 0%
where the time goes in v3:
time: 81.6 us; the launch traced here: 81.1 us
  waiting for transfers between devices  29 us (36%)
  starting transfers between devices  15.7 us (19%)
  matrix products  13 us (16%)
  local copies, waits for them, and re-layouts  9.97 us (12%)
  other arithmetic  7.5 us (9%)
  Pallas kernels  4.87 us (6%)
  between operations  1.11 us (1%)
    ppermute x4, waiting for transfers between devices, tree_reduce(): x = keep + lax.ppermute(send, 'seq', [(i, i ^ 1 << k) for i in range(nseq)])  20.2 us
    all_to_all x1, starting transfers between devices, per_device(): lax.all_to_all(jnp.concatenate([outgoing, labels], axis=1), 'seq', split_...  8.63 us
    all_to_all x1, waiting for transfers between devices, per_device(): lax.all_to_all(jnp.concatenate([outgoing, labels], axis=1), 'seq', split_...  6.68 us
    conv_general_dilated x2, matrix products, causal_conv(): lax.conv_general_dilated(padded[:nframes - lag], conv_weight[lag], (1, 1)...  6.4 us
    conv_general_dilated x1, matrix products, per_device(): lax.conv_general_dilated(cells, w_latent.reshape(4, 4, chans, LAT), (4, 4...  5.4 us
    pallas_call x1, Pallas kernels, grad_matmul(): pl.pallas_call(_grad_kernel, out_shape=jax.ShapeDtypeStruct((lat, feats),...  4.87 us
    unnamed x29, local copies, waits for them, and re-layouts  3.44 us
    ppermute x1, starting transfers between devices, with_halo(): lax.ppermute(tail, axis, [(i, (i + 1) % count) for i in range(ends)])  3.07 us
  transfers between devices with their start and end apart: 8, of which 6 were waited for; matrix products, arithmetic and copies ran while one was open for 5% of the time, Pallas kernels for 0%

profile of v3, /device:TPU:0, one launch (start us, length us, event | category | flops | bytes accessed | tf_op | source)
XLA Modules:
  0.0 81.1 jit_solution(5061389090275406870)
XLA Ops:
  0.6 0.0 copy-start
  0.7 0.0 copy-start.2
  0.7 1.8 %copy.33 = bf16[1,16,4,48,128]{4,1,3,2,0:T(8,128)(2,1)S(1)} copy(bf16[1,16,4,48,128]{4,3,2,1,0:T(8,128)(2,1)} %param.11) | data formatting | bytes 1572864 | tf_op args[0]
  2.5 0.8 fusion.47
  3.3 3.1 %collective-permute-start = (bf16[1,16,1,48,128]{4,1,3,2,0:T(8,128)(2,1)}, bf16[1,16,1,48,128]{4,1,3,2,0:T(8,128)(2,1)}, u32[]{:S(2)}, u32[]{:S(2)}) collective-permute-start(bf16[1,16,1,48,128]{4,1,3,2,0:T(8,128)(2,1)} %get-tuple-element.7), channel_id=1, source_target_pairs={{0,1},{1,2},{2,3},{3,4},{4,5},{5,6},{6,7},{7,8},{8,9},{9,10},{10,1... | collective-permute-start | bytes 589832 | tf_op jit(solution)/shard_map/ppermute | solution.py:20
  6.3 1.3 %collective-permute-start.1 = (bf16[1,16,1,48,128]{4,1,3,2,0:T(8,128)(2,1)}, bf16[1,16,1,48,128]{4,1,3,2,0:T(8,128)(2,1)}, u32[]{:S(2)}, u32[]{:S(2)}) collective-permute-start(bf16[1,16,1,48,128]{4,1,3,2,0:T(8,128)(2,1)} %get-tuple-element.8), channel_id=1, source_target_pairs={{1,0},{2,1},{3,2},{4,3},{5,4},{6,5},{7,6},{8,7},{9,8},{10,9},{11,1... | collective-permute-start | bytes 589832 | tf_op jit(solution)/shard_map/ppermute | solution.py:22
  7.6 0.2 reduce-window.10
  7.8 0.1 convert_reduce_fusion.1
  7.9 0.1 select_reduce_fusion
  8.0 0.2 reshape.136
  8.2 0.6 reduce-window.11
  8.8 0.2 slice_reduce_fusion
  9.0 0.1 bitcast_bitcast_fusion
  9.2 0.1 broadcast_in_dim.2
  9.2 0.1 reshape.148
  9.3 0.2 convolution_reduce_fusion
  9.5 0.1 reshape.151
  9.7 0.0 copy-start.3
  9.7 0.3 convert_reduce_fusion
  10.0 0.6 fusion.3
  10.6 0.5 copy-done.3
  11.1 0.7 fusion.4.normed_ref
  11.9 1.8 %maximum_bitcast_fusion = bf16[16,6,48,128]{3,0,2,1:T(8,128)(2,1)S(1)} fusion(bf16[1,16,1,48,128]{4,1,3,2,0:T(8,128)(2,1)} %collective-permute-done.1, bf16[1,16,4,48,128]{4,1,3,2,0:T(8,128)(2,1)S(1)} %copy.33, bf16[1,16,1,48,128]{4,1,3,2,0:T(8,128)(2,1)} %collective-permute-done), kind=kLoop, calls=%fused_computation.16 | loop fusion | flops 1179648 | bytes 2359296 | tf_op jit(solution)/shard_map/squeeze | solution.py:122
  13.7 0.1 copy-done.11
  13.8 3.2 %fusion.7 = f32[14,4,48,128]{3,0,2,1:T(8,128)} fusion(bf16[16,6,48,128]{3,0,2,1:T(8,128)(2,1)S(1)} %maximum_bitcast_fusion, bf16[3,3,3,128,128]{4,3,2,1,0:T(8,128)(2,1)S(1)} %copy-done.11), kind=kOutput, calls=%fused_computation.12 | convolution fusion | flops 792723456 | bytes 2850816 | tf_op jit(solution)/shard_map/conv_general_dilated | solution.py:34
  17.0 3.2 %fusion.9 = f32[15,4,48,128]{3,0,2,1:T(8,128)} fusion(bf16[16,6,48,128]{3,0,2,1:T(8,128)(2,1)S(1)} %maximum_bitcast_fusion, bf16[3,3,3,128,128]{4,3,2,1,0:T(8,128)(2,1)S(1)} %copy-done.11), kind=kOutput, calls=%fused_computation.14 | convolution fusion | flops 849346560 | bytes 2949120 | tf_op jit(solution)/shard_map/conv_general_dilated | solution.py:34
  20.2 5.4 %fusion.11 = bf16[16,1,12,64]{3,0,2,1:T(8,128)(2,1)S(1)} fusion(f32[14,4,48,128]{3,0,2,1:T(8,128)} %fusion.7, f32[15,4,48,128]{3,0,2,1:T(8,128)} %fusion.9, f32[16]{0:T(128)S(1)} %get-tuple-element.14, f32[16]{0:T(128)S(1)} %get-tuple-element.13, bf16[3,3,3,128,128]{4,3,2,1,0:T(8,128)(2,1)} %param.16, bf16[4,4,128,64]{2,1,0,3:T(4,128)(2,1)S(1)} %reshape.136, ...), kind=kOutput, calls=%fused_computation.18 | convolution fusion | flops 951595008 | bytes 5693568 | tf_op jit(solution)/shard_map/conv_general_dilated | solution.py:125
  25.7 0.2 convolution_convert_fusion
  25.9 0.1 copy.42
  26.2 0.7 reshape.161
  26.9 8.6 %all-to-all-start = ((bf16[16,2,608]{2,1,0:T(2,128)(2,1)}), bf16[16,2,608]{2,1,0:T(2,128)(2,1)S(1)}, u32[]{:S(2)}, u32[]{:S(2)}) async-start(bf16[16,2,608]{2,1,0:T(2,128)(2,1)} %reshape.161), calls=%async_computation | async-start | bytes 81920 | tf_op jit(solution)/shard_map/all_to_all | solution.py:155
  35.5 6.7 %all-to-all-done = bf16[16,2,608]{2,1,0:T(2,128)(2,1)S(1)} async-done(((bf16[16,2,608]{2,1,0:T(2,128)(2,1)}), bf16[16,2,608]{2,1,0:T(2,128)(2,1)S(1)}, u32[]{:S(2)}, u32[]{:S(2)}) %all-to-all-start) | async-done | bytes 38944 | tf_op jit(solution)/shard_map/all_to_all | solution.py:155
  42.2 0.1 reshape.162
  42.4 0.1 reshape.146
  42.5 0.1 fusion.39
  42.6 0.1 copy.44
  42.8 0.7 multiply_reduce_fusion
  43.5 0.2 fusion.38
  43.7 0.6 fusion.35.dpt_ref
  44.4 4.9 %shard_map.130 = f32[64,3072]{1,0:T(8,128)} custom-call(bf16[64,288]{1,0:T(8,128)(2,1)} %fusion.35.dpt_ref, bf16[288,3072]{1,0:T(8,128)(2,1)} %copy-done.1), custom_call_target="tpu_custom_call" | custom-call | flops 113246208 | bytes 2592768 | tf_op jit(solution)/shard_map/pallas_call | solution.py:58
  49.2 2.1 %concatenate.16 = f32[64,2,2,2,2,192]{5,4,3,2,1,0:T(2,128)S(1)} reshape(f32[64,3072]{1,0:T(8,128)} %shard_map.130) | data formatting | bytes 1572864 | tf_op jit(solution)/shard_map/concatenate | solution.py:79
  51.3 0.1 bitcast_dynamic-update-slice_fusion
  51.4 1.2 %fusion.19 = (f32[65,2,2,2,1,192]{5,4,3,2,1,0:T(1,128)S(1)}, f32[65,2,2,2,1,192]{5,4,3,2,1,0:T(1,128)S(1)}) fusion(s32[]{:T(128)S(6)} %select_n.33, f32[1,2,2,2,2,192]{5,4,3,2,1,0:T(2,128)S(1)} %concatenate.17, f32[64,2,2,2,2,192]{5,4,3,2,1,0:T(2,128)S(1)} %concatenate.16, s32[]{:T(128)S(6)} %select_n.34), kind=kLoop, calls=%fused_computation.30 | loop fusion | flops 199680 | bytes 1597448 | tf_op jit(solution)/shard_map/concatenate | solution.py:79
  52.6 0.3 copy.67
  52.9 0.1 collective-permute-start.2
  53.0 1.9 %collective-permute-done.2 = f32[65,2,2,2,192]{4,2,1,0,3:T(2,128)S(1)} collective-permute-done((f32[65,2,2,2,192]{4,2,1,0,3:T(2,128)S(1)}, f32[65,2,2,2,192]{4,2,1,0,3:T(2,128)S(1)}, u32[]{:S(2)}, u32[]{:S(2)}) %collective-permute-start.2) | collective-permute-done | bytes 399392 | tf_op jit(solution)/shard_map/ppermute | solution.py:88
  54.9 0.4 bitcast_add_fusion
  55.3 0.1 dynamic-slice_bitcast_fusion
  55.4 0.4 collective-permute-start.3
  55.7 8.1 %collective-permute-done.3 = f32[65,2,2,192]{3,2,1,0:T(2,128)S(1)} collective-permute-done((f32[65,2,2,192]{3,2,1,0:T(2,128)S(1)}, f32[65,2,2,192]{3,2,1,0:T(2,128)S(1)}, u32[]{:S(2)}, u32[]{:S(2)}) %collective-permute-start.3) | collective-permute-done | bytes 199712 | tf_op jit(solution)/shard_map/ppermute | solution.py:88
  63.9 0.1 bitcast_add_fusion.1
  64.0 0.2 constant_dynamic-slice_fusion.4
  64.3 0.1 copy.68
  64.3 0.3 collective-permute-start.4
  64.7 4.7 %collective-permute-done.4 = f32[65,2,192]{2,1,0:T(2,128)S(1)} collective-permute-done((f32[65,2,192]{2,1,0:T(2,128)S(1)}, f32[65,2,192]{2,1,0:T(2,128)S(1)}, u32[]{:S(2)}, u32[]{:S(2)}) %collective-permute-start.4) | collective-permute-done | bytes 99872 | tf_op jit(solution)/shard_map/ppermute | solution.py:88
  69.4 0.1 bitcast_add_fusion.2
  69.5 0.1 constant_dynamic-slice_fusion.2
  69.6 0.4 collective-permute-start.5
  70.0 5.4 %collective-permute-done.5 = f32[65,192]{1,0:T(8,128)S(1)} collective-permute-done((f32[65,192]{1,0:T(8,128)S(1)}, f32[65,192]{1,0:T(8,128)S(1)}, u32[]{:S(2)}, u32[]{:S(2)}) %collective-permute-start.5) | collective-permute-done | bytes 49952 | tf_op jit(solution)/shard_map/ppermute | solution.py:88
  75.5 1.6 %collective-permute-start.6 = (f32[65,192]{1,0:T(8,128)S(1)}, f32[65,192]{1,0:T(8,128)S(1)}, u32[]{:S(2)}, u32[]{:S(2)}) collective-permute-start(f32[65,192]{1,0:T(8,128)S(1)} %bitcast_add_fusion.3), channel_id=1, source_target_pairs={{0,16},{16,0},{1,17},{17,1},{2,18},{18,2},{3,19},{19,3},{4,20},{20... | collective-permute-start | bytes 149768 | tf_op jit(solution)/shard_map/ppermute | solution.py:92
  77.0 0.7 reshape.137
  77.7 2.2 %collective-permute-done.6 = f32[65,192]{1,0:T(8,128)S(1)} collective-permute-done((f32[65,192]{1,0:T(8,128)S(1)}, f32[65,192]{1,0:T(8,128)S(1)}, u32[]{:S(2)}, u32[]{:S(2)}) %collective-permute-start.6) | collective-permute-done | bytes 49952 | tf_op jit(solution)/shard_map/ppermute | solution.py:92
  79.9 0.6 slice_bitcast_fusion
  80.5 0.6 constant_dynamic-slice_fusion
  (50 shorter events, 0.4 us)
Async XLA Ops:
  0.6 42.1 %copy-start = (bf16[3072,64]{0,1:T(8,128)(2,1)S(1)}, bf16[3072,64]{0,1:T(8,128)(2,1)}, u32[]{:S(2)}) copy-start(bf16[3072,64]{0,1:T(8,128)(2,1)} %param.21) | copy-start | bytes 1179652
  0.6 7.0 %copy-start.8 = (s32[1,4]{1,0:T(1,128)S(1)}, s32[1,4]{1,0:T(1,128)}, u32[]{:S(2)}) copy-start(s32[1,4]{1,0:T(1,128)} %param.12) | copy-start | bytes 52
  0.7 7.4 %copy-start.4 = (bf16[2048,64]{0,1:T(8,128)(2,1)S(1)}, bf16[2048,64]{0,1:T(8,128)(2,1)}, u32[]{:S(2)}) copy-start(bf16[2048,64]{0,1:T(8,128)(2,1)} %param.17) | copy-start | bytes 786436
  0.7 7.5 %copy-start.7 = (s32[1,1,192,1]{2,3,1,0:T(1,128)S(1)}, s32[1,1,192,1]{2,3,1,0:T(1,128)}, u32[]{:S(2)}) copy-start(s32[1,1,192,1]{2,3,1,0:T(1,128)} %param.15) | copy-start | bytes 2308
  0.7 9.0 %copy-start.2 = (bf16[1,288,3072]{2,1,0:T(8,128)(2,1)S(1)}, bf16[1,288,3072]{2,1,0:T(8,128)(2,1)}, u32[]{:S(2)}) copy-start(bf16[1,288,3072]{2,1,0:T(8,128)(2,1)} %param.18) | copy-start | bytes 5308420
  3.3 8.6 %collective-permute-start = (bf16[1,16,1,48,128]{4,1,3,2,0:T(8,128)(2,1)}, bf16[1,16,1,48,128]{4,1,3,2,0:T(8,128)(2,1)}, u32[]{:S(2)}, u32[]{:S(2)}) collective-permute-start(bf16[1,16,1,48,128]{4,1,3,2,0:T(8,128)(2,1)} %get-tuple-element.7), channel_id=1, source_target_pairs={{0,1},{1,2},{2,3},{3,4},{4,5},{5,6},{6,7},{7,8},{8,9},{9,10},{10,1... | collective-permute-start | bytes 589832 | tf_op jit(solution)/shard_map/ppermute | solution.py:20
  6.3 5.6 %collective-permute-start.1 = (bf16[1,16,1,48,128]{4,1,3,2,0:T(8,128)(2,1)}, bf16[1,16,1,48,128]{4,1,3,2,0:T(8,128)(2,1)}, u32[]{:S(2)}, u32[]{:S(2)}) collective-permute-start(bf16[1,16,1,48,128]{4,1,3,2,0:T(8,128)(2,1)} %get-tuple-element.8), channel_id=1, source_target_pairs={{1,0},{2,1},{3,2},{4,3},{5,4},{6,5},{7,6},{8,7},{9,8},{10,9},{11,1... | collective-permute-start | bytes 589832 | tf_op jit(solution)/shard_map/ppermute | solution.py:22
  9.7 1.5 %copy-start.3 = (bf16[1,288,3072]{2,1,0:T(8,128)(2,1)S(1)}, bf16[1,288,3072]{2,1,0:T(8,128)(2,1)}, u32[]{:S(2)}) copy-start(bf16[1,288,3072]{2,1,0:T(8,128)(2,1)} %param.18) | copy-start | bytes 5308420
  11.1 0.7 copy-start.9
  11.1 0.7 copy-start.10
  11.8 30.9 %copy-start.1 = (bf16[288,3072]{1,0:T(8,128)(2,1)}, bf16[288,3072]{1,0:T(8,128)(2,1)S(1)}, u32[]{:S(2)}) copy-start(bf16[288,3072]{1,0:T(8,128)(2,1)S(1)} %fusion.4.normed_ref) | copy-start | bytes 5308420
  11.9 2.0 %copy-start.11 = (bf16[3,3,3,128,128]{4,3,2,1,0:T(8,128)(2,1)S(1)}, bf16[3,3,3,128,128]{4,3,2,1,0:T(8,128)(2,1)}, u32[]{:S(2)}) copy-start(bf16[3,3,3,128,128]{4,3,2,1,0:T(8,128)(2,1)} %param.16) | copy-start | bytes 2654212
  25.6 17.1 %copy-start.5 = (f32[1,288,64]{1,2,0:T(8,128)S(1)}, f32[1,288,64]{1,2,0:T(8,128)}, u32[]{:S(2)}) copy-start(f32[1,288,64]{1,2,0:T(8,128)} %param.19) | copy-start | bytes 221188
  25.7 17.1 %copy-start.6 = (f32[1,288,64]{1,2,0:T(8,128)S(1)}, f32[1,288,64]{1,2,0:T(8,128)}, u32[]{:S(2)}) copy-start(f32[1,288,64]{1,2,0:T(8,128)} %param.20) | copy-start | bytes 221188
  26.9 15.3 %all-to-all-start = ((bf16[16,2,608]{2,1,0:T(2,128)(2,1)}), bf16[16,2,608]{2,1,0:T(2,128)(2,1)S(1)}, u32[]{:S(2)}, u32[]{:S(2)}) async-start(bf16[16,2,608]{2,1,0:T(2,128)(2,1)} %reshape.161), calls=%async_computation | async-start | bytes 81920 | tf_op jit(solution)/shard_map/all_to_all | solution.py:155
  52.9 2.0 %collective-permute-start.2 = (f32[65,2,2,2,192]{4,2,1,0,3:T(2,128)S(1)}, f32[65,2,2,2,192]{4,2,1,0,3:T(2,128)S(1)}, u32[]{:S(2)}, u32[]{:S(2)}) collective-permute-start(f32[65,2,2,2,192]{4,2,1,0,3:T(2,128)S(1)} %bitcast.107), channel_id=1, source_target_pairs={{0,1},{1,0},{2,3},{3,2},{4,5},{5,4},{6,7},{7,6},{8,9},{9,8},{10,11... | collective-permute-start | bytes 1198088 | tf_op jit(solution)/shard_map/ppermute | solution.py:88
  55.4 8.5 %collective-permute-start.3 = (f32[65,2,2,192]{3,2,1,0:T(2,128)S(1)}, f32[65,2,2,192]{3,2,1,0:T(2,128)S(1)}, u32[]{:S(2)}, u32[]{:S(2)}) collective-permute-start(f32[65,2,2,192]{3,2,1,0:T(2,128)S(1)} %dynamic-slice_bitcast_fusion), channel_id=1, source_target_pairs={{0,2},{1,3},{2,0},{3,1},{4,6},{5,7},{6,4},{7,5},{8,10},{9,11},{10,... | collective-permute-start | bytes 599048 | tf_op jit(solution)/shard_map/ppermute | solution.py:88
  64.3 5.1 %collective-permute-start.4 = (f32[65,2,192]{2,1,0:T(2,128)S(1)}, f32[65,2,192]{2,1,0:T(2,128)S(1)}, u32[]{:S(2)}, u32[]{:S(2)}) collective-permute-start(f32[65,2,192]{2,1,0:T(2,128)S(1)} %bitcast.108), channel_id=1, source_target_pairs={{0,4},{1,5},{2,6},{3,7},{4,0},{5,1},{6,2},{7,3},{8,12},{9,13},{10,... | collective-permute-start | bytes 299528 | tf_op jit(solution)/shard_map/ppermute | solution.py:88
  69.6 5.8 %collective-permute-start.5 = (f32[65,192]{1,0:T(8,128)S(1)}, f32[65,192]{1,0:T(8,128)S(1)}, u32[]{:S(2)}, u32[]{:S(2)}) collective-permute-start(f32[65,192]{1,0:T(8,128)S(1)} %bitcast.109), channel_id=1, source_target_pairs={{0,8},{1,9},{2,10},{3,11},{4,12},{5,13},{6,14},{7,15},{8,0},{9,1},... | collective-permute-start | bytes 149768 | tf_op jit(solution)/shard_map/ppermute | solution.py:88
  75.5 4.4 %collective-permute-start.6 = (f32[65,192]{1,0:T(8,128)S(1)}, f32[65,192]{1,0:T(8,128)S(1)}, u32[]{:S(2)}, u32[]{:S(2)}) collective-permute-start(f32[65,192]{1,0:T(8,128)S(1)} %bitcast_add_fusion.3), channel_id=1, source_target_pairs={{0,16},{16,0},{1,17},{17,1},{2,18},{18,2},{3,19},{19,3},{4,20},{20... | collective-permute-start | bytes 149768 | tf_op jit(solution)/shard_map/ppermute | solution.py:92

commit v4 on v2

--- a/solution.py
+++ b/solution.py
@@ -1,6 +1,7 @@
 import jax
 import jax.numpy as jnp
 from jax import lax
+from jax.experimental import pallas as pl
 from jax.sharding import PartitionSpec as P
 
 LAT = 64
@@ -45,22 +46,50 @@
     return total
 
 
-def tree_reduce(grad_t, loss_line, nseq, ndp):
-    rows = grad_t.shape[1] // nseq
+def _grad_kernel(normed_ref, dpred_ref, out_ref):
+    out_ref[...] = lax.dot_general(
+        normed_ref[...], dpred_ref[...], (((0,), (0,)), ((), ())), preferred_element_type=jnp.float32
+    )
+
+
+def grad_matmul(normed, dpred):
+    slots, feats = normed.shape
+    lat = dpred.shape[1]
+    tile = 512 if feats % 512 == 0 else feats
+    return pl.pallas_call(
+        _grad_kernel,
+        out_shape=jax.ShapeDtypeStruct((feats, lat), jnp.float32),
+        grid=(feats // tile,),
+        in_specs=[
+            pl.BlockSpec((slots, tile), lambda i: (0, i)),
+            pl.BlockSpec((slots, lat), lambda i: (0, 0)),
+        ],
+        out_specs=pl.BlockSpec((tile, lat), lambda i: (i, 0)),
+        cost_estimate=pl.CostEstimate(
+            flops=2 * lat * slots * feats,
+            bytes_accessed=2 * lat * slots + 2 * slots * feats + 4 * lat * feats,
+            transcendentals=0,
+        ),
+    )(normed, dpred)
+
+
+def tree_reduce(grad_part, loss_row, nseq, ndp):
+    rows = grad_part.shape[0] // nseq
     nbits = nseq.bit_length() - 1
     assert 1 << nbits == nseq and ndp & (ndp - 1) == 0
-    x = jnp.concatenate([grad_t, loss_line[None, :]], axis=0)
-    x = x.reshape((x.shape[0],) + (2,) * nbits + (rows,))
+    blocks = grad_part.reshape(nseq, rows, LAT)
+    extra = jnp.broadcast_to(loss_row[None, None, :], (nseq, 1, LAT))
+    x = jnp.concatenate([blocks, extra], axis=1).reshape((2,) * nbits + (rows + 1, LAT))
     me = lax.axis_index("seq")
     left = list(range(nbits - 1, -1, -1))
     for k in range(nbits):
-        axis = left.index(k) + 1
+        axis = left.index(k)
         bit = (me >> k) & 1
         keep = lax.dynamic_index_in_dim(x, bit, axis, keepdims=False)
         send = lax.dynamic_index_in_dim(x, 1 - bit, axis, keepdims=False)
         x = keep + lax.ppermute(send, "seq", [(i, i ^ (1 << k)) for i in range(nseq)])
-        left.pop(axis - 1)
-    x = x.reshape(-1, rows)
+        left.pop(axis)
+    x = x.reshape(rows + 1, LAT)
     for k in range(ndp.bit_length() - 1):
         x = x + lax.ppermute(x, "dp", [(i, i ^ (1 << k)) for i in range(ndp)])
     return x
@@ -152,17 +181,14 @@
     err = jnp.sum(diff * diff, axis=1)
     partial_loss = coef * jnp.sum(slot_hot * err[:, None], axis=0)
     dpred = (2.0 * slot_coef[:, None] * diff).astype(jnp.bfloat16)
-    grad_t = lax.dot_general(
-        dpred, normed, (((0,), (0,)), ((), ())), preferred_element_type=jnp.float32
-    )
+    grad_part = grad_matmul(normed, dpred)
     ndp = lax.axis_size("dp")
-    share = grad_t.shape[1] // nseq
-    assert ndp * CLIPS <= share
+    assert ndp * CLIPS <= LAT
     place = lax.axis_index("dp") * CLIPS
-    loss_row = lax.dynamic_update_slice(jnp.zeros((share,), jnp.float32), partial_loss, (place,))
-    summed = tree_reduce(grad_t, jnp.tile(loss_row, nseq), nseq, ndp)
-    grad_mine = summed[:LAT].T
-    clip_loss = lax.dynamic_slice_in_dim(summed[LAT], place, CLIPS).reshape(1, CLIPS)
+    loss_row = lax.dynamic_update_slice(jnp.zeros((LAT,), jnp.float32), partial_loss, (place,))
+    summed = tree_reduce(grad_part, loss_row, nseq, ndp)
+    grad_mine = summed[:-1]
+    clip_loss = lax.dynamic_slice_in_dim(summed[-1], place, CLIPS).reshape(1, CLIPS)
     return (latent_out, clip_loss, grad_mine)
 
 

time: 74.9 us -> 76.6 us (1.023)
  Pallas kernels: 0 us -> 5.36 us
  local copies, waits for them, and re-layouts: 13.1 us -> 10.8 us
  matrix products: 10.3 us -> 9.1 us
    pallas_call x0 -> x1, Pallas kernels: none -> 5.36 us  [grad_matmul(): pl.pallas_call(_grad_kernel, out_shape=jax.ShapeDtypeStruct((feats, lat),...]
    dot_general x1 -> x0, local copies, waits for them, and re-layouts: 2.87 us -> none  [per_device(): lax.dot_general(dpred, normed, (((0,), (0,)), ((), ())), preferred_elemen...]
    unnamed x25 -> x29, local copies, waits for them, and re-layouts: 5.13 us -> 7.42 us
    dot_general x1 -> x0, other arithmetic: 1.88 us -> none  [per_device(): lax.dot_general(dpred, normed, (((0,), (0,)), ((), ())), preferred_elemen...]
    convert_element_type x0 -> x2, other arithmetic: none -> 1.42 us  [the longest x1 0.73 us: per_device(): dpred = (2.0 * slot_coef[:, None] * diff).astype(jnp.bfloat16)]
    concatenate x1, other arithmetic: 0.12 us -> 1.51 us  [tree_reduce(): jnp.concatenate([blocks, extra], axis=1)]
    dot_general x1 -> x0, matrix products: 1.11 us -> none  [per_device(): lax.dot_general(dpred, normed, (((0,), (0,)), ((), ())), preferred_elemen...]
  transfers between devices with their start and end apart: 8 -> 8, of which waited for: 6 -> 6; matrix products, arithmetic and copies ran while one was open for 8% -> 11% of each run, Pallas kernels for 0% -> 0%
where the time goes in v4:
time: 76.6 us; the launch traced here: 76 us
  waiting for transfers between devices  28.3 us (37%)
  starting transfers between devices  15.7 us (20%)
  local copies, waits for them, and re-layouts  10.8 us (14%)
  matrix products  9.1 us (12%)
  other arithmetic  5.62 us (7%)
  Pallas kernels  5.36 us (7%)
  between operations  1.08 us (1%)
    ppermute x4, waiting for transfers between devices, tree_reduce(): x = keep + lax.ppermute(send, 'seq', [(i, i ^ 1 << k) for i in range(nseq)])  19.6 us
    all_to_all x1, starting transfers between devices, per_device(): lax.all_to_all(jnp.concatenate([outgoing, labels], axis=1), 'seq', split_...  8.64 us
    unnamed x29, local copies, waits for them, and re-layouts  7.42 us
    all_to_all x1, waiting for transfers between devices, per_device(): lax.all_to_all(jnp.concatenate([outgoing, labels], axis=1), 'seq', split_...  6.69 us
    conv_general_dilated x1, matrix products, causal_conv(): lax.conv_general_dilated(padded, kernel, (1, 1), 'VALID', dimension_numbe...  5.55 us
    pallas_call x1, Pallas kernels, grad_matmul(): pl.pallas_call(_grad_kernel, out_shape=jax.ShapeDtypeStruct((feats, lat),...  5.36 us
    ppermute x1, starting transfers between devices, with_halo(): lax.ppermute(tail, axis, [(i, (i + 1) % count) for i in range(ends)])  3.07 us
    conv_general_dilated x1, matrix products, per_device(): lax.conv_general_dilated(cells, w_latent.reshape(4, 4, chans, LAT), (4, 4...  2.42 us
  transfers between devices with their start and end apart: 8, of which 6 were waited for; matrix products, arithmetic and copies ran while one was open for 11% of the time, Pallas kernels for 0%

profile of v4, /device:TPU:0, one launch (start us, length us, event | category | flops | bytes accessed | tf_op | source)
XLA Modules:
  0.0 76.0 jit_solution(9717746607052084286)
XLA Ops:
  0.6 0.0 copy-start
  0.6 1.7 %copy.42 = bf16[1,16,4,48,128]{4,1,3,2,0:T(8,128)(2,1)S(1)} copy(bf16[1,16,4,48,128]{4,3,2,1,0:T(8,128)(2,1)} %param.11) | data formatting | bytes 1572864 | tf_op args[0]
  2.3 0.0 copy-start.8
  2.4 0.0 copy-start.4
  2.4 0.0 copy-start.7
  2.4 0.0 copy-start.2
  2.4 0.8 %fusion.33 = (bf16[1,16,1,48,128]{4,1,3,2,0:T(8,128)(2,1)}, bf16[1,16,1,48,128]{4,1,3,2,0:T(8,128)(2,1)}) fusion(bf16[1,16,4,48,128]{4,1,3,2,0:T(8,128)(2,1)S(1)} %copy.42), kind=kLoop, calls=%fused_computation.89 | loop fusion | bytes 786432 | tf_op jit(solution)/shard_map/slice | solution.py:16
  3.2 3.1 %collective-permute-start = (bf16[1,16,1,48,128]{4,1,3,2,0:T(8,128)(2,1)}, bf16[1,16,1,48,128]{4,1,3,2,0:T(8,128)(2,1)}, u32[]{:S(2)}, u32[]{:S(2)}) collective-permute-start(bf16[1,16,1,48,128]{4,1,3,2,0:T(8,128)(2,1)} %get-tuple-element.16), channel_id=1, source_target_pairs={{0,1},{1,2},{2,3},{3,4},{4,5},{5,6},{6,7},{7,8},{8,9},{9,10},{10,1... | collective-permute-start | bytes 589832 | tf_op jit(solution)/shard_map/ppermute | solution.py:19
  6.2 1.3 %collective-permute-start.1 = (bf16[1,16,1,48,128]{4,1,3,2,0:T(8,128)(2,1)}, bf16[1,16,1,48,128]{4,1,3,2,0:T(8,128)(2,1)}, u32[]{:S(2)}, u32[]{:S(2)}) collective-permute-start(bf16[1,16,1,48,128]{4,1,3,2,0:T(8,128)(2,1)} %get-tuple-element.17), channel_id=1, source_target_pairs={{1,0},{2,1},{3,2},{4,3},{5,4},{6,5},{7,6},{8,7},{9,8},{10,9},{11,1... | collective-permute-start | bytes 589832 | tf_op jit(solution)/shard_map/ppermute | solution.py:21
  7.5 2.3 %copy.46 = bf16[3,3,3,128,128]{3,4,0,2,1:T(8,128)(2,1)} copy(bf16[3,3,3,128,128]{4,3,2,1,0:T(8,128)(2,1)} %param.16) | data formatting | bytes 1769472 | tf_op args[5]
  9.8 0.2 reduce-window.10
  10.0 0.1 convert_reduce_fusion.1
  10.1 0.1 select_reduce_fusion
  10.2 0.2 reshape.183
  10.4 0.6 reduce-window.11
  11.0 0.2 slice_reduce_fusion
  11.2 0.1 bitcast_bitcast_fusion
  11.3 0.1 broadcast_in_dim.6
  11.4 0.1 reshape.196
  11.5 0.2 convolution_reduce_fusion
  11.7 0.1 reshape.199
  11.8 0.0 copy-start.3
  11.8 0.3 convert_reduce_fusion
  12.2 0.6 fusion.3
  12.8 0.5 copy-done.3
  13.3 0.7 fusion.4.normed_ref
  14.0 0.2 copy-done.6
  14.2 0.1 copy.54
  14.3 1.1 %copy.55 = f32[1,288,64]{2,1,0:T(8,128)S(1)} copy(f32[1,288,64]{1,2,0:T(8,128)} %param.19) | data formatting | bytes 147456 | tf_op args[8]
  15.5 5.6 %fusion.7 = f32[16,4,48,384]{3,0,2,1:T(8,128)S(1)} fusion(bf16[3,3,128,384]{2,3,1,0:T(8,128)(2,1)} %bitcast.88, bf16[1,16,1,48,128]{4,1,3,2,0:T(8,128)(2,1)} %collective-permute-done.1, bf16[1,16,4,48,128]{4,1,3,2,0:T(8,128)(2,1)S(1)} %copy.42, bf16[1,16,1,48,128]{4,1,3,2,0:T(8,128)(2,1)} %collective-permute-done), kind=kOutput, calls=%fused_computation.16 | convolution fusion | flops 2683699200 | bytes 6782976 | tf_op jit(solution)/shard_map/conv_general_dilated | solution.py:33
  21.1 0.1 slice.51
  21.2 0.1 slice.52
  21.3 2.4 %convolution_convert_fusion.1 = bf16[16,1,12,64]{3,0,2,1:T(8,128)(2,1)S(1)} fusion(f32[16,4,48,384]{3,0,2,1:T(8,128)S(1)} %fusion.7, f32[14,4,48,128]{3,0,2,1:T(8,128)S(1)} %slice.52, f32[15,4,48,128]{3,0,2,1:T(8,128)S(1)} %slice.51, f32[16]{0:T(128)S(1)} %get-tuple-element.19, f32[16]{0:T(128)S(1)} %get-tuple-element.18, ...), kind=kOutput, calls=%fused_computation.23 | convolution fusion | flops 54669312 | bytes 5792768 | tf_op jit(solution)/shard_map/conv_general_dilated | solution.py:127
  23.8 0.2 convolution_convert_fusion
  24.0 0.1 copy.52
  24.2 0.7 reshape.209
  25.0 8.6 %all-to-all-start = ((bf16[16,2,608]{2,1,0:T(2,128)(2,1)}), bf16[16,2,608]{2,1,0:T(2,128)(2,1)S(1)}, u32[]{:S(2)}, u32[]{:S(2)}) async-start(bf16[16,2,608]{2,1,0:T(2,128)(2,1)} %reshape.209), calls=%async_computation | async-start | bytes 81920 | tf_op jit(solution)/shard_map/all_to_all | solution.py:157
  33.6 6.7 %all-to-all-done = bf16[16,2,608]{2,1,0:T(2,128)(2,1)S(1)} async-done(((bf16[16,2,608]{2,1,0:T(2,128)(2,1)}), bf16[16,2,608]{2,1,0:T(2,128)(2,1)S(1)}, u32[]{:S(2)}, u32[]{:S(2)}) %all-to-all-start) | async-done | bytes 38944 | tf_op jit(solution)/shard_map/all_to_all | solution.py:157
  40.3 0.1 reshape.210
  40.5 0.1 reshape.193
  40.6 0.1 fusion.25
  40.7 0.7 multiply_reduce_fusion
  41.4 0.2 fusion.26
  41.6 0.7 multiply_convert_fusion.dpred_ref
  42.4 5.4 %shard_map.130 = f32[3072,64]{1,0:T(8,128)} custom-call(bf16[288,3072]{1,0:T(8,128)(2,1)} %copy-done.1, bf16[288,64]{1,0:T(8,128)(2,1)} %multiply_convert_fusion.dpred_ref), custom_call_target="tpu_custom_call" | custom-call | flops 113246208 | bytes 2592768 | tf_op jit(solution)/shard_map/pallas_call | solution.py:59
  47.7 0.1 multiply_dynamic-update-slice_fusion
  47.8 1.5 %fusion.13 = (f32[2,2,2,1,193,64]{5,4,3,2,1,0:T(8,128)S(1)}, f32[2,2,2,1,193,64]{5,4,3,2,1,0:T(8,128)S(1)}) fusion(s32[]{:T(128)S(6)} %select_n.33, f32[2,2,2,2,192,64]{5,4,3,2,1,0:T(8,128)} %bitcast.87, f32[2,2,2,2,1,64]{5,4,3,2,1,0:T(1,128)S(1)} %broadcast_in_dim.8, s32[]{:T(128)S(6)} %select_n.34), kind=kLoop, calls=%fused_computation.26 | loop fusion | flops 197632 | bytes 1581064 | tf_op jit(solution)/shard_map/concatenate | solution.py:82
  49.3 0.3 copy.58
  49.7 0.1 collective-permute-start.2
  49.8 0.3 copy.57
  50.1 1.6 %collective-permute-done.2 = f32[2,2,2,193,64]{3,4,2,1,0:T(8,128)S(1)} collective-permute-done((f32[2,2,2,193,64]{3,4,2,1,0:T(8,128)S(1)}, f32[2,2,2,193,64]{3,4,2,1,0:T(8,128)S(1)}, u32[]{:S(2)}, u32[]{:S(2)}) %collective-permute-start.2) | collective-permute-done | bytes 395296 | tf_op jit(solution)/shard_map/ppermute | solution.py:90
  51.6 0.1 bitcast_add_fusion
  51.8 0.4 collective-permute-start.3
  52.1 8.1 %collective-permute-done.3 = f32[2,2,193,64]{2,3,1,0:T(8,128)S(1)} collective-permute-done((f32[2,2,193,64]{2,3,1,0:T(8,128)S(1)}, f32[2,2,193,64]{2,3,1,0:T(8,128)S(1)}, u32[]{:S(2)}, u32[]{:S(2)}) %collective-permute-start.3) | collective-permute-done | bytes 197664 | tf_op jit(solution)/shard_map/ppermute | solution.py:90
  60.2 0.4 collective-permute-start.4
  60.6 4.7 %collective-permute-done.4 = f32[2,193,64]{1,2,0:T(8,128)S(1)} collective-permute-done((f32[2,193,64]{1,2,0:T(8,128)S(1)}, f32[2,193,64]{1,2,0:T(8,128)S(1)}, u32[]{:S(2)}, u32[]{:S(2)}) %collective-permute-start.4) | collective-permute-done | bytes 98848 | tf_op jit(solution)/shard_map/ppermute | solution.py:90
  65.3 0.4 collective-permute-start.5
  65.7 5.2 %collective-permute-done.5 = f32[193,64]{0,1:T(8,128)S(1)} collective-permute-done((f32[193,64]{0,1:T(8,128)S(1)}, f32[193,64]{0,1:T(8,128)S(1)}, u32[]{:S(2)}, u32[]{:S(2)}) %collective-permute-start.5) | collective-permute-done | bytes 49440 | tf_op jit(solution)/shard_map/ppermute | solution.py:90
  71.0 1.6 %collective-permute-start.6 = (f32[193,64]{0,1:T(8,128)S(1)}, f32[193,64]{0,1:T(8,128)S(1)}, u32[]{:S(2)}, u32[]{:S(2)}) collective-permute-start(f32[193,64]{0,1:T(8,128)S(1)} %bitcast_add_fusion.3), channel_id=1, source_target_pairs={{0,16},{16,0},{1,17},{17,1},{2,18},{18,2},{3,19},{19,3},{4,20},{20... | collective-permute-start | bytes 148232 | tf_op jit(solution)/shard_map/ppermute | solution.py:94
  72.5 0.7 reshape.184
  73.2 2.1 %collective-permute-done.6 = f32[193,64]{0,1:T(8,128)S(1)} collective-permute-done((f32[193,64]{0,1:T(8,128)S(1)}, f32[193,64]{0,1:T(8,128)S(1)}, u32[]{:S(2)}, u32[]{:S(2)}) %collective-permute-start.6) | collective-permute-done | bytes 49440 | tf_op jit(solution)/shard_map/ppermute | solution.py:94
  75.3 0.0 copy-start.5
  75.3 0.1 slice.57
  75.4 0.6 copy.59
  (48 shorter events, 0.5 us)
Async XLA Ops:
  0.6 40.1 %copy-start = (bf16[3072,64]{0,1:T(8,128)(2,1)S(1)}, bf16[3072,64]{0,1:T(8,128)(2,1)}, u32[]{:S(2)}) copy-start(bf16[3072,64]{0,1:T(8,128)(2,1)} %param.21) | copy-start | bytes 1179652
  2.3 7.5 %copy-start.8 = (s32[1,4]{1,0:T(1,128)S(1)}, s32[1,4]{1,0:T(1,128)}, u32[]{:S(2)}) copy-start(s32[1,4]{1,0:T(1,128)} %param.12) | copy-start | bytes 52
  2.4 7.8 %copy-start.4 = (bf16[2048,64]{0,1:T(8,128)(2,1)S(1)}, bf16[2048,64]{0,1:T(8,128)(2,1)}, u32[]{:S(2)}) copy-start(bf16[2048,64]{0,1:T(8,128)(2,1)} %param.17) | copy-start | bytes 786436
  2.4 8.0 %copy-start.7 = (s32[1,1,192,1]{2,3,1,0:T(1,128)S(1)}, s32[1,1,192,1]{2,3,1,0:T(1,128)}, u32[]{:S(2)}) copy-start(s32[1,1,192,1]{2,3,1,0:T(1,128)} %param.15) | copy-start | bytes 2308
  2.4 9.4 %copy-start.2 = (bf16[1,288,3072]{2,1,0:T(8,128)(2,1)S(1)}, bf16[1,288,3072]{2,1,0:T(8,128)(2,1)}, u32[]{:S(2)}) copy-start(bf16[1,288,3072]{2,1,0:T(8,128)(2,1)} %param.18) | copy-start | bytes 5308420
  3.2 12.3 %collective-permute-start = (bf16[1,16,1,48,128]{4,1,3,2,0:T(8,128)(2,1)}, bf16[1,16,1,48,128]{4,1,3,2,0:T(8,128)(2,1)}, u32[]{:S(2)}, u32[]{:S(2)}) collective-permute-start(bf16[1,16,1,48,128]{4,1,3,2,0:T(8,128)(2,1)} %get-tuple-element.16), channel_id=1, source_target_pairs={{0,1},{1,2},{2,3},{3,4},{4,5},{5,6},{6,7},{7,8},{8,9},{9,10},{10,1... | collective-permute-start | bytes 589832 | tf_op jit(solution)/shard_map/ppermute | solution.py:19
  6.2 9.3 %collective-permute-start.1 = (bf16[1,16,1,48,128]{4,1,3,2,0:T(8,128)(2,1)}, bf16[1,16,1,48,128]{4,1,3,2,0:T(8,128)(2,1)}, u32[]{:S(2)}, u32[]{:S(2)}) collective-permute-start(bf16[1,16,1,48,128]{4,1,3,2,0:T(8,128)(2,1)} %get-tuple-element.17), channel_id=1, source_target_pairs={{1,0},{2,1},{3,2},{4,3},{5,4},{6,5},{7,6},{8,7},{9,8},{10,9},{11,1... | collective-permute-start | bytes 589832 | tf_op jit(solution)/shard_map/ppermute | solution.py:21
  11.8 1.5 %copy-start.3 = (bf16[1,288,3072]{2,1,0:T(8,128)(2,1)S(1)}, bf16[1,288,3072]{2,1,0:T(8,128)(2,1)}, u32[]{:S(2)}) copy-start(bf16[1,288,3072]{2,1,0:T(8,128)(2,1)} %param.18) | copy-start | bytes 5308420
  13.3 0.9 %copy-start.6 = (f32[1,288,64]{1,2,0:T(8,128)S(1)}, f32[1,288,64]{1,2,0:T(8,128)}, u32[]{:S(2)}) copy-start(f32[1,288,64]{1,2,0:T(8,128)} %param.20) | copy-start | bytes 221188
  13.3 2.1 %copy-start.9 = (s32[1,4]{1,0:T(1,128)S(1)}, s32[1,4]{1,0:T(1,128)}, u32[]{:S(2)}) copy-start(s32[1,4]{1,0:T(1,128)} %param.14) | copy-start | bytes 52
  13.3 2.1 %copy-start.10 = (s32[1,4]{1,0:T(1,128)S(1)}, s32[1,4]{1,0:T(1,128)}, u32[]{:S(2)}) copy-start(s32[1,4]{1,0:T(1,128)} %param.13) | copy-start | bytes 52
  14.2 26.5 %copy-start.1 = (bf16[288,3072]{1,0:T(8,128)(2,1)}, bf16[288,3072]{1,0:T(8,128)(2,1)S(1)}, u32[]{:S(2)}) copy-start(bf16[288,3072]{1,0:T(8,128)(2,1)S(1)} %fusion.4.normed_ref) | copy-start | bytes 5308420
  25.0 15.3 %all-to-all-start = ((bf16[16,2,608]{2,1,0:T(2,128)(2,1)}), bf16[16,2,608]{2,1,0:T(2,128)(2,1)S(1)}, u32[]{:S(2)}, u32[]{:S(2)}) async-start(bf16[16,2,608]{2,1,0:T(2,128)(2,1)} %reshape.209), calls=%async_computation | async-start | bytes 81920 | tf_op jit(solution)/shard_map/all_to_all | solution.py:157
  49.7 2.0 %collective-permute-start.2 = (f32[2,2,2,193,64]{3,4,2,1,0:T(8,128)S(1)}, f32[2,2,2,193,64]{3,4,2,1,0:T(8,128)S(1)}, u32[]{:S(2)}, u32[]{:S(2)}) collective-permute-start(f32[2,2,2,193,64]{3,4,2,1,0:T(8,128)S(1)} %bitcast.89), channel_id=1, source_target_pairs={{0,1},{1,0},{2,3},{3,2},{4,5},{5,4},{6,7},{7,6},{8,9},{9,8},{10,11... | collective-permute-start | bytes 1185800 | tf_op jit(solution)/shard_map/ppermute | solution.py:90
  51.8 8.4 %collective-permute-start.3 = (f32[2,2,193,64]{2,3,1,0:T(8,128)S(1)}, f32[2,2,193,64]{2,3,1,0:T(8,128)S(1)}, u32[]{:S(2)}, u32[]{:S(2)}) collective-permute-start(f32[2,2,193,64]{2,3,1,0:T(8,128)S(1)} %dynamic-slice_bitcast_fusion), channel_id=1, source_target_pairs={{0,2},{1,3},{2,0},{3,1},{4,6},{5,7},{6,4},{7,5},{8,10},{9,11},{10,... | collective-permute-start | bytes 592904 | tf_op jit(solution)/shard_map/ppermute | solution.py:90
  60.2 5.0 %collective-permute-start.4 = (f32[2,193,64]{1,2,0:T(8,128)S(1)}, f32[2,193,64]{1,2,0:T(8,128)S(1)}, u32[]{:S(2)}, u32[]{:S(2)}) collective-permute-start(f32[2,193,64]{1,2,0:T(8,128)S(1)} %dynamic-slice_bitcast_fusion.1), channel_id=1, source_target_pairs={{0,4},{1,5},{2,6},{3,7},{4,0},{5,1},{6,2},{7,3},{8,12},{9,13},{10,... | collective-permute-start | bytes 296456 | tf_op jit(solution)/shard_map/ppermute | solution.py:90
  65.3 5.7 %collective-permute-start.5 = (f32[193,64]{0,1:T(8,128)S(1)}, f32[193,64]{0,1:T(8,128)S(1)}, u32[]{:S(2)}, u32[]{:S(2)}) collective-permute-start(f32[193,64]{0,1:T(8,128)S(1)} %dynamic-slice_bitcast_fusion.2), channel_id=1, source_target_pairs={{0,8},{1,9},{2,10},{3,11},{4,12},{5,13},{6,14},{7,15},{8,0},{9,1},... | collective-permute-start | bytes 148232 | tf_op jit(solution)/shard_map/ppermute | solution.py:90
  71.0 4.3 %collective-permute-start.6 = (f32[193,64]{0,1:T(8,128)S(1)}, f32[193,64]{0,1:T(8,128)S(1)}, u32[]{:S(2)}, u32[]{:S(2)}) collective-permute-start(f32[193,64]{0,1:T(8,128)S(1)} %bitcast_add_fusion.3), channel_id=1, source_target_pairs={{0,16},{16,0},{1,17},{17,1},{2,18},{18,2},{3,19},{19,3},{4,20},{20... | collective-permute-start | bytes 148232 | tf_op jit(solution)/shard_map/ppermute | solution.py:94
  75.3 0.7 copy-start.5

commit v5 on v2

--- a/solution.py
+++ b/solution.py
@@ -49,17 +49,22 @@
     rows = grad_t.shape[1] // nseq
     nbits = nseq.bit_length() - 1
     assert 1 << nbits == nseq and ndp & (ndp - 1) == 0
+    groups = [1, 2] + [1] * (nbits - 3) if nbits >= 3 else [1] * nbits
     x = jnp.concatenate([grad_t, loss_line[None, :]], axis=0)
-    x = x.reshape((x.shape[0],) + (2,) * nbits + (rows,))
+    x = x.reshape(x.shape[0], nseq, rows)
     me = lax.axis_index("seq")
-    left = list(range(nbits - 1, -1, -1))
-    for k in range(nbits):
-        axis = left.index(k) + 1
-        bit = (me >> k) & 1
-        keep = lax.dynamic_index_in_dim(x, bit, axis, keepdims=False)
-        send = lax.dynamic_index_in_dim(x, 1 - bit, axis, keepdims=False)
-        x = keep + lax.ppermute(send, "seq", [(i, i ^ (1 << k)) for i in range(nseq)])
-        left.pop(axis - 1)
+    low = 0
+    for width in groups:
+        ways = 1 << width
+        x = x.reshape(x.shape[0], x.shape[1] // ways, ways, rows)
+        digit = (me >> low) & (ways - 1)
+        total = lax.dynamic_index_in_dim(x, digit, 2, keepdims=False)
+        for step in range(1, ways):
+            send = lax.dynamic_index_in_dim(x, digit ^ step, 2, keepdims=False)
+            pairs = [(i, i ^ (step << low)) for i in range(nseq)]
+            total = total + lax.ppermute(send, "seq", pairs)
+        x = total
+        low += width
     x = x.reshape(-1, rows)
     for k in range(ndp.bit_length() - 1):
         x = x + lax.ppermute(x, "dp", [(i, i ^ (1 << k)) for i in range(ndp)])

time: 74.9 us -> 70.3 us (0.939)
  waiting for transfers between devices: 29 us -> 22 us
  starting transfers between devices: 15.7 us -> 18.7 us
    ppermute x4 -> x5, waiting for transfers between devices: 20.2 us -> 13.1 us  [tree_reduce(): total = total + lax.ppermute(send, 'seq', pairs)]
    ppermute x4 -> x5, starting transfers between devices: 1.19 us -> 4.17 us  [tree_reduce(): total = total + lax.ppermute(send, 'seq', pairs)]
    unnamed x25 -> x26, local copies, waits for them, and re-layouts: 5.13 us -> 5.13 us
  transfers between devices with their start and end apart: 8 -> 9, of which waited for: 6 -> 7; matrix products, arithmetic and copies ran while one was open for 8% -> 9% of each run, Pallas kernels for 0% -> 0%
where the time goes in v5:
time: 70.3 us; the launch traced here: 69.9 us
  waiting for transfers between devices  22 us (31%)
  starting transfers between devices  18.7 us (27%)
  local copies, waits for them, and re-layouts  12.8 us (18%)
  matrix products  10.3 us (15%)
  other arithmetic  4.97 us (7%)
  between operations  1.1 us (2%)
    ppermute x5, waiting for transfers between devices, tree_reduce(): total = total + lax.ppermute(send, 'seq', pairs)  13.1 us
    all_to_all x1, starting transfers between devices, per_device(): lax.all_to_all(jnp.concatenate([outgoing, labels], axis=1), 'seq', split_...  8.63 us
    all_to_all x1, waiting for transfers between devices, per_device(): lax.all_to_all(jnp.concatenate([outgoing, labels], axis=1), 'seq', split_...  6.69 us
    conv_general_dilated x1, matrix products, causal_conv(): lax.conv_general_dilated(padded, kernel, (1, 1), 'VALID', dimension_numbe...  5.56 us
    unnamed x26, local copies, waits for them, and re-layouts  5.13 us
    ppermute x5, starting transfers between devices, tree_reduce(): total = total + lax.ppermute(send, 'seq', pairs)  4.17 us
    ppermute x1, starting transfers between devices, with_halo(): lax.ppermute(tail, axis, [(i, (i + 1) % count) for i in range(ends)])  3.06 us
    dot_general x1, local copies, waits for them, and re-layouts, per_device(): lax.dot_general(dpred, normed, (((0,), (0,)), ((), ())), preferred_elemen...  2.87 us
  transfers between devices with their start and end apart: 9, of which 7 were waited for; matrix products, arithmetic and copies ran while one was open for 9% of the time, Pallas kernels for 0%

profile of v5, /device:TPU:0, one launch (start us, length us, event | category | flops | bytes accessed | tf_op | source)
XLA Modules:
  0.0 69.9 jit_solution(17475180925072396295)
XLA Ops:
  0.6 0.0 copy-start
  0.7 1.7 %copy.50 = bf16[1,16,4,48,128]{4,1,3,2,0:T(8,128)(2,1)S(1)} copy(bf16[1,16,4,48,128]{4,3,2,1,0:T(8,128)(2,1)} %param.11) | data formatting | bytes 1572864 | tf_op args[0]
  2.4 0.8 %fusion.41 = (bf16[1,16,1,48,128]{4,1,3,2,0:T(8,128)(2,1)}, bf16[1,16,1,48,128]{4,1,3,2,0:T(8,128)(2,1)}) fusion(bf16[1,16,4,48,128]{4,1,3,2,0:T(8,128)(2,1)S(1)} %copy.50), kind=kLoop, calls=%fused_computation.103 | loop fusion | bytes 786432 | tf_op jit(solution)/shard_map/slice | solution.py:15
  3.2 3.1 %collective-permute-start = (bf16[1,16,1,48,128]{4,1,3,2,0:T(8,128)(2,1)}, bf16[1,16,1,48,128]{4,1,3,2,0:T(8,128)(2,1)}, u32[]{:S(2)}, u32[]{:S(2)}) collective-permute-start(bf16[1,16,1,48,128]{4,1,3,2,0:T(8,128)(2,1)} %get-tuple-element.7), channel_id=1, source_target_pairs={{0,1},{1,2},{2,3},{3,4},{4,5},{5,6},{6,7},{7,8},{8,9},{9,10},{10,1... | collective-permute-start | bytes 589832 | tf_op jit(solution)/shard_map/ppermute | solution.py:18
  6.2 1.3 %collective-permute-start.1 = (bf16[1,16,1,48,128]{4,1,3,2,0:T(8,128)(2,1)}, bf16[1,16,1,48,128]{4,1,3,2,0:T(8,128)(2,1)}, u32[]{:S(2)}, u32[]{:S(2)}) collective-permute-start(bf16[1,16,1,48,128]{4,1,3,2,0:T(8,128)(2,1)} %get-tuple-element.8), channel_id=1, source_target_pairs={{1,0},{2,1},{3,2},{4,3},{5,4},{6,5},{7,6},{8,7},{9,8},{10,9},{11,1... | collective-permute-start | bytes 589832 | tf_op jit(solution)/shard_map/ppermute | solution.py:20
  7.5 2.3 %copy.54 = bf16[3,3,3,128,128]{3,4,0,2,1:T(8,128)(2,1)} copy(bf16[3,3,3,128,128]{4,3,2,1,0:T(8,128)(2,1)} %param.16) | data formatting | bytes 1769472 | tf_op args[5]
  9.8 0.2 reduce-window.10
  10.0 0.1 convert_reduce_fusion.1
  10.1 0.1 select_reduce_fusion
  10.2 0.2 reshape.151
  10.4 0.6 reduce-window.11
  11.0 0.2 slice_reduce_fusion
  11.2 0.1 bitcast_bitcast_fusion
  11.3 0.1 broadcast_in_dim.2
  11.4 0.1 reshape.165
  11.5 0.2 convolution_reduce_fusion
  11.7 0.1 reshape.169
  11.9 0.3 convert_reduce_fusion
  12.2 0.6 fusion.3
  12.9 5.6 %fusion.7 = f32[16,4,48,384]{3,0,2,1:T(8,128)S(1)} fusion(bf16[3,3,128,384]{2,3,1,0:T(8,128)(2,1)} %bitcast.116, bf16[1,16,1,48,128]{4,1,3,2,0:T(8,128)(2,1)} %collective-permute-done.1, bf16[1,16,4,48,128]{4,1,3,2,0:T(8,128)(2,1)S(1)} %copy.50, bf16[1,16,1,48,128]{4,1,3,2,0:T(8,128)(2,1)} %collective-permute-done), kind=kOutput, calls=%fused_computation.14 | convolution fusion | flops 2683699200 | bytes 6782976 | tf_op jit(solution)/shard_map/conv_general_dilated | solution.py:32
  18.4 0.1 slice.51
  18.6 0.1 slice.52
  18.7 2.4 %convolution_convert_fusion.1 = bf16[16,1,12,64]{3,0,2,1:T(8,128)(2,1)S(1)} fusion(f32[16,4,48,384]{3,0,2,1:T(8,128)S(1)} %fusion.7, f32[14,4,48,128]{3,0,2,1:T(8,128)S(1)} %slice.52, f32[15,4,48,128]{3,0,2,1:T(8,128)S(1)} %slice.51, f32[16]{0:T(128)S(1)} %get-tuple-element.14, f32[16]{0:T(128)S(1)} %get-tuple-element.13, ...), kind=kOutput, calls=%fused_computation.23 | convolution fusion | flops 54669312 | bytes 5792768 | tf_op jit(solution)/shard_map/conv_general_dilated | solution.py:103
  21.2 0.2 convolution_convert_fusion
  21.4 0.1 copy.60
  21.6 0.7 %reshape.179 = bf16[16,2,608]{2,1,0:T(2,128)(2,1)} reshape(bf16[16,19,64]{2,1,0:T(8,128)(2,1)S(1)} %fusion.21) | data formatting | bytes 77824
  22.3 8.6 %all-to-all-start = ((bf16[16,2,608]{2,1,0:T(2,128)(2,1)}), bf16[16,2,608]{2,1,0:T(2,128)(2,1)S(1)}, u32[]{:S(2)}, u32[]{:S(2)}) async-start(bf16[16,2,608]{2,1,0:T(2,128)(2,1)} %reshape.179), calls=%async_computation | async-start | bytes 81920 | tf_op jit(solution)/shard_map/all_to_all | solution.py:133
  31.0 6.7 %all-to-all-done = bf16[16,2,608]{2,1,0:T(2,128)(2,1)S(1)} async-done(((bf16[16,2,608]{2,1,0:T(2,128)(2,1)}), bf16[16,2,608]{2,1,0:T(2,128)(2,1)S(1)}, u32[]{:S(2)}, u32[]{:S(2)}) %all-to-all-start) | async-done | bytes 38944 | tf_op jit(solution)/shard_map/all_to_all | solution.py:133
  37.7 0.1 reshape.180
  37.9 0.1 reshape.163
  38.0 0.1 copy.62
  38.1 0.1 fusion.31
  38.2 1.9 %fusion.39 = bf16[3072,288]{0,1:T(8,128)(2,1)} fusion(f32[288]{0:T(512)S(1)} %get-tuple-element.17, f32[288]{0:T(512)S(1)} %broadcast_multiply_fusion, bf16[1,288,3072]{2,1,0:T(8,128)(2,1)S(1)} %copy-done.1), kind=kLoop, calls=%fused_computation.102 | loop fusion | flops 3538944 | bytes 3541248 | tf_op jit(solution)/shard_map/dot_general | solution.py:160
  40.1 0.8 %multiply_reduce_fusion = (f32[288]{0:T(512)S(1)}, f32[288,64]{0,1:T(8,128)S(1)}) fusion(f32[288,64]{0,1:T(8,128)S(1)} %copy.62, f32[1,288,64]{1,2,0:T(8,128)S(1)} %copy-done.7, f32[288]{0:T(512)S(1)} %get-tuple-element.18, f32[1,288,64]{1,2,0:T(8,128)S(1)} %copy-done.8, f32[288]{0:T(512)S(1)} %fusion.31, bf16[3072,64]{0,1:T(8,128)(2,1)S(1)} %copy-done, ...), kind=kOutput, calls=%fused_computation.47 | convolution fusion | flops 116913888 | bytes 2463360 | tf_op jit(solution)/shard_map/dot_general | solution.py:154
  40.9 0.2 fusion.32
  41.1 2.9 %copy.67 = bf16[3072,288]{1,0:T(8,128)(2,1)S(1)} copy(bf16[3072,288]{0,1:T(8,128)(2,1)} %fusion.39) | data formatting | bytes 3538944 | tf_op jit(solution)/shard_map/dot_general | solution.py:160
  44.0 1.1 %fusion.25 = f32[64,8,2,192]{3,0,2,1:T(8,128)S(1)} fusion(bf16[8,2,192,288]{3,2,1,0:T(8,128)(2,1)S(1)} %bitcast.115, f32[288,64]{0,1:T(8,128)S(1)} %get-tuple-element.16, f32[288]{0:T(512)S(1)} %broadcast_multiply_fusion.1), kind=kOutput, calls=%fused_computation.53 | convolution fusion | flops 113283072 | bytes 2630784 | tf_op jit(solution)/shard_map/dot_general | solution.py:160
  45.1 0.1 bitcast_dynamic-update-slice_fusion
  45.2 0.1 fusion.14
  45.3 0.2 copy.92
  45.5 0.1 collective-permute-start.2
  45.6 1.9 %collective-permute-done.2 = f32[65,8,192]{2,1,0:T(8,128)S(1)} collective-permute-done((f32[65,8,192]{2,1,0:T(8,128)S(1)}, f32[65,8,192]{2,1,0:T(8,128)S(1)}, u32[]{:S(2)}, u32[]{:S(2)}) %collective-permute-start.2) | collective-permute-done | bytes 399392 | tf_op jit(solution)/shard_map/ppermute | solution.py:65
  47.5 0.2 bitcast_add_fusion
  47.7 0.2 reshape.159
  47.9 0.5 constant_dynamic-slice_fusion.5
  48.3 0.1 copy.95
  48.4 0.4 collective-permute-start.3
  48.8 0.1 copy.94
  48.8 0.7 collective-permute-start.4
  49.5 0.1 copy.93
  49.6 2.6 %collective-permute-start.5 = (f32[65,2,192]{2,1,0:T(2,128)S(1)}, f32[65,2,192]{2,1,0:T(2,128)S(1)}, u32[]{:S(2)}, u32[]{:S(2)}) collective-permute-start(f32[65,2,192]{2,1,0:T(2,128)S(1)} %bitcast.120), channel_id=1, source_target_pairs={{0,6},{1,7},{2,4},{3,5},{4,2},{5,3},{6,0},{7,1},{8,14},{9,15},{10,... | collective-permute-start | bytes 299528 | tf_op jit(solution)/shard_map/ppermute | solution.py:65
  52.2 1.8 %collective-permute-done.3 = f32[65,2,192]{2,1,0:T(2,128)S(1)} collective-permute-done((f32[65,2,192]{2,1,0:T(2,128)S(1)}, f32[65,2,192]{2,1,0:T(2,128)S(1)}, u32[]{:S(2)}, u32[]{:S(2)}) %collective-permute-start.3) | collective-permute-done | bytes 99872 | tf_op jit(solution)/shard_map/ppermute | solution.py:65
  54.1 1.3 %collective-permute-done.4 = f32[65,2,192]{2,1,0:T(2,128)S(1)} collective-permute-done((f32[65,2,192]{2,1,0:T(2,128)S(1)}, f32[65,2,192]{2,1,0:T(2,128)S(1)}, u32[]{:S(2)}, u32[]{:S(2)}) %collective-permute-start.4) | collective-permute-done | bytes 99872 | tf_op jit(solution)/shard_map/ppermute | solution.py:65
  55.3 2.9 %collective-permute-done.5 = f32[65,2,192]{2,1,0:T(2,128)S(1)} collective-permute-done((f32[65,2,192]{2,1,0:T(2,128)S(1)}, f32[65,2,192]{2,1,0:T(2,128)S(1)}, u32[]{:S(2)}, u32[]{:S(2)}) %collective-permute-start.5) | collective-permute-done | bytes 99872 | tf_op jit(solution)/shard_map/ppermute | solution.py:65
  58.2 0.1 fusion.20
  58.4 0.1 constant_dynamic-slice_fusion.1
  58.4 0.4 collective-permute-start.6
  58.9 5.3 %collective-permute-done.6 = f32[65,1,192]{2,1,0:T(1,128)S(1)} collective-permute-done((f32[65,1,192]{2,1,0:T(1,128)S(1)}, f32[65,1,192]{2,1,0:T(1,128)S(1)}, u32[]{:S(2)}, u32[]{:S(2)}) %collective-permute-start.6) | collective-permute-done | bytes 49952 | tf_op jit(solution)/shard_map/ppermute | solution.py:65
  64.1 0.1 dynamic-slice_add_fusion
  64.2 1.6 %collective-permute-start.7 = (f32[65,192]{1,0:T(8,128)S(1)}, f32[65,192]{1,0:T(8,128)S(1)}, u32[]{:S(2)}, u32[]{:S(2)}) collective-permute-start(f32[65,192]{1,0:T(8,128)S(1)} %bitcast.121), channel_id=1, source_target_pairs={{0,16},{16,0},{1,17},{17,1},{2,18},{18,2},{3,19},{19,3},{4,20},{20... | collective-permute-start | bytes 149768 | tf_op jit(solution)/shard_map/ppermute | solution.py:70
  65.8 0.7 %reshape.152 = bf16[1,16,1,768]{3,1,2,0:T(8,128)(2,1)} reshape(bf16[16,1,12,64]{3,2,0,1:T(8,128)(2,1)S(1)} %copy.56) | data formatting | bytes 49152 | tf_op jit(solution)/shard_map/reshape | solution.py:111
  66.5 2.2 %collective-permute-done.7 = f32[65,192]{1,0:T(8,128)S(1)} collective-permute-done((f32[65,192]{1,0:T(8,128)S(1)}, f32[65,192]{1,0:T(8,128)S(1)}, u32[]{:S(2)}, u32[]{:S(2)}) %collective-permute-start.7) | collective-permute-done | bytes 49952 | tf_op jit(solution)/shard_map/ppermute | solution.py:70
  68.7 0.6 slice_bitcast_fusion
  69.3 0.6 constant_dynamic-slice_fusion
  (46 shorter events, 0.4 us)
Async XLA Ops:
  0.6 39.5 %copy-start = (bf16[3072,64]{0,1:T(8,128)(2,1)S(1)}, bf16[3072,64]{0,1:T(8,128)(2,1)}, u32[]{:S(2)}) copy-start(bf16[3072,64]{0,1:T(8,128)(2,1)} %param.21) | copy-start | bytes 1179652
  0.6 9.2 %copy-start.4 = (s32[1,4]{1,0:T(1,128)S(1)}, s32[1,4]{1,0:T(1,128)}, u32[]{:S(2)}) copy-start(s32[1,4]{1,0:T(1,128)} %param.12) | copy-start | bytes 52
  0.7 9.5 %copy-start.2 = (bf16[2048,64]{0,1:T(8,128)(2,1)S(1)}, bf16[2048,64]{0,1:T(8,128)(2,1)}, u32[]{:S(2)}) copy-start(bf16[2048,64]{0,1:T(8,128)(2,1)} %param.17) | copy-start | bytes 786436
  2.4 8.0 %copy-start.3 = (s32[1,1,192,1]{2,3,1,0:T(1,128)S(1)}, s32[1,1,192,1]{2,3,1,0:T(1,128)}, u32[]{:S(2)}) copy-start(s32[1,1,192,1]{2,3,1,0:T(1,128)} %param.15) | copy-start | bytes 2308
  2.4 9.4 %copy-start.1 = (bf16[1,288,3072]{2,1,0:T(8,128)(2,1)S(1)}, bf16[1,288,3072]{2,1,0:T(8,128)(2,1)}, u32[]{:S(2)}) copy-start(bf16[1,288,3072]{2,1,0:T(8,128)(2,1)} %param.18) | copy-start | bytes 5308420
  3.2 9.7 %collective-permute-start = (bf16[1,16,1,48,128]{4,1,3,2,0:T(8,128)(2,1)}, bf16[1,16,1,48,128]{4,1,3,2,0:T(8,128)(2,1)}, u32[]{:S(2)}, u32[]{:S(2)}) collective-permute-start(bf16[1,16,1,48,128]{4,1,3,2,0:T(8,128)(2,1)} %get-tuple-element.7), channel_id=1, source_target_pairs={{0,1},{1,2},{2,3},{3,4},{4,5},{5,6},{6,7},{7,8},{8,9},{9,10},{10,1... | collective-permute-start | bytes 589832 | tf_op jit(solution)/shard_map/ppermute | solution.py:18
  6.2 6.6 %collective-permute-start.1 = (bf16[1,16,1,48,128]{4,1,3,2,0:T(8,128)(2,1)}, bf16[1,16,1,48,128]{4,1,3,2,0:T(8,128)(2,1)}, u32[]{:S(2)}, u32[]{:S(2)}) collective-permute-start(bf16[1,16,1,48,128]{4,1,3,2,0:T(8,128)(2,1)} %get-tuple-element.8), channel_id=1, source_target_pairs={{1,0},{2,1},{3,2},{4,3},{5,4},{6,5},{7,6},{8,7},{9,8},{10,9},{11,1... | collective-permute-start | bytes 589832 | tf_op jit(solution)/shard_map/ppermute | solution.py:20
  11.8 1.0 %copy-start.5 = (s32[1,4]{1,0:T(1,128)S(1)}, s32[1,4]{1,0:T(1,128)}, u32[]{:S(2)}) copy-start(s32[1,4]{1,0:T(1,128)} %param.14) | copy-start | bytes 52
  11.8 1.0 %copy-start.6 = (s32[1,4]{1,0:T(1,128)S(1)}, s32[1,4]{1,0:T(1,128)}, u32[]{:S(2)}) copy-start(s32[1,4]{1,0:T(1,128)} %param.13) | copy-start | bytes 52
  22.3 15.3 %all-to-all-start = ((bf16[16,2,608]{2,1,0:T(2,128)(2,1)}), bf16[16,2,608]{2,1,0:T(2,128)(2,1)S(1)}, u32[]{:S(2)}, u32[]{:S(2)}) async-start(bf16[16,2,608]{2,1,0:T(2,128)(2,1)} %reshape.179), calls=%async_computation | async-start | bytes 81920 | tf_op jit(solution)/shard_map/all_to_all | solution.py:133
  38.2 1.9 %copy-start.7 = (f32[1,288,64]{1,2,0:T(8,128)S(1)}, f32[1,288,64]{1,2,0:T(8,128)}, u32[]{:S(2)}) copy-start(f32[1,288,64]{1,2,0:T(8,128)} %param.19) | copy-start | bytes 221188
  38.2 1.9 %copy-start.8 = (f32[1,288,64]{1,2,0:T(8,128)S(1)}, f32[1,288,64]{1,2,0:T(8,128)}, u32[]{:S(2)}) copy-start(f32[1,288,64]{1,2,0:T(8,128)} %param.20) | copy-start | bytes 221188
  45.5 2.0 %collective-permute-start.2 = (f32[65,8,192]{2,1,0:T(8,128)S(1)}, f32[65,8,192]{2,1,0:T(8,128)S(1)}, u32[]{:S(2)}, u32[]{:S(2)}) collective-permute-start(f32[65,8,192]{2,1,0:T(8,128)S(1)} %bitcast.117), channel_id=1, source_target_pairs={{0,1},{1,0},{2,3},{3,2},{4,5},{5,4},{6,7},{7,6},{8,9},{9,8},{10,11... | collective-permute-start | bytes 1198088 | tf_op jit(solution)/shard_map/ppermute | solution.py:65
  48.4 5.6 %collective-permute-start.3 = (f32[65,2,192]{2,1,0:T(2,128)S(1)}, f32[65,2,192]{2,1,0:T(2,128)S(1)}, u32[]{:S(2)}, u32[]{:S(2)}) collective-permute-start(f32[65,2,192]{2,1,0:T(2,128)S(1)} %bitcast.118), channel_id=1, source_target_pairs={{0,2},{1,3},{2,0},{3,1},{4,6},{5,7},{6,4},{7,5},{8,10},{9,11},{10,... | collective-permute-start | bytes 299528 | tf_op jit(solution)/shard_map/ppermute | solution.py:65
  48.8 6.5 %collective-permute-start.4 = (f32[65,2,192]{2,1,0:T(2,128)S(1)}, f32[65,2,192]{2,1,0:T(2,128)S(1)}, u32[]{:S(2)}, u32[]{:S(2)}) collective-permute-start(f32[65,2,192]{2,1,0:T(2,128)S(1)} %bitcast.119), channel_id=1, source_target_pairs={{0,4},{1,5},{2,6},{3,7},{4,0},{5,1},{6,2},{7,3},{8,12},{9,13},{10,... | collective-permute-start | bytes 299528 | tf_op jit(solution)/shard_map/ppermute | solution.py:65
  49.6 8.6 %collective-permute-start.5 = (f32[65,2,192]{2,1,0:T(2,128)S(1)}, f32[65,2,192]{2,1,0:T(2,128)S(1)}, u32[]{:S(2)}, u32[]{:S(2)}) collective-permute-start(f32[65,2,192]{2,1,0:T(2,128)S(1)} %bitcast.120), channel_id=1, source_target_pairs={{0,6},{1,7},{2,4},{3,5},{4,2},{5,3},{6,0},{7,1},{8,14},{9,15},{10,... | collective-permute-start | bytes 299528 | tf_op jit(solution)/shard_map/ppermute | solution.py:65
  58.4 5.7 %collective-permute-start.6 = (f32[65,1,192]{2,1,0:T(1,128)S(1)}, f32[65,1,192]{2,1,0:T(1,128)S(1)}, u32[]{:S(2)}, u32[]{:S(2)}) collective-permute-start(f32[65,1,192]{2,1,0:T(1,128)S(1)} %constant_dynamic-slice_fusion.1), channel_id=1, source_target_pairs={{0,8},{1,9},{2,10},{3,11},{4,12},{5,13},{6,14},{7,15},{8,0},{9,1},... | collective-permute-start | bytes 149768 | tf_op jit(solution)/shard_map/ppermute | solution.py:65
  64.2 4.4 %collective-permute-start.7 = (f32[65,192]{1,0:T(8,128)S(1)}, f32[65,192]{1,0:T(8,128)S(1)}, u32[]{:S(2)}, u32[]{:S(2)}) collective-permute-start(f32[65,192]{1,0:T(8,128)S(1)} %bitcast.121), channel_id=1, source_target_pairs={{0,16},{16,0},{1,17},{17,1},{2,18},{18,2},{3,19},{19,3},{4,20},{20... | collective-permute-start | bytes 149768 | tf_op jit(solution)/shard_map/ppermute | solution.py:70

commit v6 on v5

--- a/solution.py
+++ b/solution.py
@@ -28,21 +28,20 @@
     nframes = rimmed.shape[0]
     chans = rimmed.shape[-1]
     padded = jnp.pad(rimmed, ((0, 0), (0, 0), (1, 1), (0, 0)))
-    kernel = jnp.transpose(conv_weight, (1, 2, 3, 0, 4)).reshape(3, 3, chans, 3 * chans)
-    each = lax.conv_general_dilated(
-        padded,
+    lagged = []
+    for lag in range(3):
+        part = jnp.pad(padded[: nframes - lag], ((lag, 0), (0, 0), (0, 0), (0, 0)))
+        lagged.append(jnp.where(keep[lag][:, None, None, None] > 0, part, jnp.zeros_like(part)))
+    stacked = jnp.concatenate(lagged, axis=-1)
+    kernel = jnp.transpose(conv_weight, (1, 2, 0, 3, 4)).reshape(3, 3, 3 * chans, chans)
+    return lax.conv_general_dilated(
+        stacked,
         kernel,
         (1, 1),
         "VALID",
         dimension_numbers=("NHWC", "HWIO", "NHWC"),
         preferred_element_type=jnp.float32,
     )
-    total = each[..., :chans]
-    for lag in (1, 2):
-        part = each[: nframes - lag, ..., lag * chans : (lag + 1) * chans]
-        part = jnp.pad(part, ((lag, 0), (0, 0), (0, 0), (0, 0)))
-        total = total + part * keep[lag][:, None, None, None]
-    return total
 
 
 def tree_reduce(grad_t, loss_line, nseq, ndp):

time: 70.3 us -> 77.4 us (1.10)
  other arithmetic: 4.97 us -> 8.81 us
  local copies, waits for them, and re-layouts: 12.8 us -> 15.5 us
    conv_general_dilated x1, matrix products: 2.42 us -> 8.59 us  [per_device(): lax.conv_general_dilated(cells, w_latent.reshape(4, 4, chans, LAT), (4, 4...]
    conv_general_dilated x1 -> x0, matrix products: 5.56 us -> none  [causal_conv(): lax.conv_general_dilated(padded, kernel, (1, 1), 'VALID', dimension_numbe...]
    select_n x0 -> x2, other arithmetic: none -> 2.77 us  [causal_conv(): jnp.where(keep[lag][:, None, None, None] > 0, part, jnp.zeros_like(part))]
    dot_general x1, local copies, waits for them, and re-layouts: 2.87 us -> 4.03 us  [per_device(): lax.dot_general(dpred, normed, (((0,), (0,)), ((), ())), preferred_elemen...]
    squeeze x0 -> x1, other arithmetic: none -> 1.07 us  [per_device(): rimmed = with_halo(frames, (('seq', 2),), 1)[0]]
    unnamed x26 -> x28, local copies, waits for them, and re-layouts: 5.13 us -> 5.7 us
  transfers between devices with their start and end apart: 9 -> 9, of which waited for: 7 -> 7; matrix products, arithmetic and copies ran while one was open for 9% -> 16% of each run, Pallas kernels for 0% -> 0%
where the time goes in v6:
time: 77.4 us; the launch traced here: 76.9 us
  waiting for transfers between devices  22 us (28%)
  starting transfers between devices  18.7 us (24%)
  local copies, waits for them, and re-layouts  15.5 us (20%)
  matrix products  10.9 us (14%)
  other arithmetic  8.81 us (11%)
  between operations  1.08 us (1%)
    ppermute x5, waiting for transfers between devices, tree_reduce(): total = total + lax.ppermute(send, 'seq', pairs)  13.1 us
    all_to_all x1, starting transfers between devices, per_device(): lax.all_to_all(jnp.concatenate([outgoing, labels], axis=1), 'seq', split_...  9.29 us
    conv_general_dilated x1, matrix products, per_device(): lax.conv_general_dilated(cells, w_latent.reshape(4, 4, chans, LAT), (4, 4...  8.59 us
    all_to_all x1, waiting for transfers between devices, per_device(): lax.all_to_all(jnp.concatenate([outgoing, labels], axis=1), 'seq', split_...  6.68 us
    unnamed x28, local copies, waits for them, and re-layouts  5.7 us
    ppermute x5, starting transfers between devices, tree_reduce(): total = total + lax.ppermute(send, 'seq', pairs)  4.17 us
    dot_general x1, local copies, waits for them, and re-layouts, per_device(): lax.dot_general(dpred, normed, (((0,), (0,)), ((), ())), preferred_elemen...  4.03 us
    select_n x2, other arithmetic, causal_conv(): jnp.where(keep[lag][:, None, None, None] > 0, part, jnp.zeros_like(part))  2.77 us
  transfers between devices with their start and end apart: 9, of which 7 were waited for; matrix products, arithmetic and copies ran while one was open for 16% of the time, Pallas kernels for 0%

profile of v6, /device:TPU:0, one launch (start us, length us, event | category | flops | bytes accessed | tf_op | source)
XLA Modules:
  0.0 76.9 jit_solution(3242141460603962799)
XLA Ops:
  0.7 1.7 %copy.50 = bf16[1,16,4,48,128]{4,1,3,2,0:T(8,128)(2,1)S(1)} copy(bf16[1,16,4,48,128]{4,3,2,1,0:T(8,128)(2,1)} %param.11) | data formatting | bytes 1572864 | tf_op args[0]
  2.4 0.8 fusion.49
  3.2 2.4 %collective-permute-start = (bf16[1,16,1,48,128]{4,1,3,2,0:T(8,128)(2,1)}, bf16[1,16,1,48,128]{4,1,3,2,0:T(8,128)(2,1)S(1)}, u32[]{:S(2)}, u32[]{:S(2)}) collective-permute-start(bf16[1,16,1,48,128]{4,1,3,2,0:T(8,128)(2,1)} %get-tuple-element.7), channel_id=1, source_target_pairs={{0,1},{1,2},{2,3},{3,4},{4,5},{5,6},{6,7},{7,8},{8,9},{9,10},{10,1... | collective-permute-start | bytes 589832 | tf_op jit(solution)/shard_map/ppermute | solution.py:18
  5.6 1.3 %collective-permute-start.1 = (bf16[1,16,1,48,128]{4,1,3,2,0:T(8,128)(2,1)}, bf16[1,16,1,48,128]{4,1,3,2,0:T(8,128)(2,1)}, u32[]{:S(2)}, u32[]{:S(2)}) collective-permute-start(bf16[1,16,1,48,128]{4,1,3,2,0:T(8,128)(2,1)} %get-tuple-element.8), channel_id=1, source_target_pairs={{1,0},{2,1},{3,2},{4,3},{5,4},{6,5},{7,6},{8,7},{9,8},{10,9},{11,1... | collective-permute-start | bytes 589832 | tf_op jit(solution)/shard_map/ppermute | solution.py:20
  6.9 0.2 reduce-window.10
  7.1 0.1 convert_reduce_fusion.1
  7.2 0.1 select_reduce_fusion
  7.3 2.2 %copy.54 = bf16[3,3,3,128,128]{4,3,0,2,1:T(8,128)(2,1)} copy(bf16[3,3,3,128,128]{4,3,2,1,0:T(8,128)(2,1)} %param.16) | data formatting | bytes 1769472 | tf_op args[5]
  9.5 0.9 %reshape.164 = bf16[4,4,128,64]{2,1,0,3:T(4,128)(2,1)} reshape(bf16[2048,64]{0,1:T(8,128)(2,1)S(1)} %copy-done.3) | data formatting | bytes 524288 | tf_op jit(solution)/shard_map/reshape | solution.py:104
  10.4 0.6 reduce-window.11
  11.0 0.2 slice_reduce_fusion
  11.2 0.1 bitcast_bitcast_fusion
  11.3 0.1 broadcast_in_dim.23
  11.4 0.1 reshape.178
  11.5 0.2 convolution_reduce_fusion
  11.7 0.1 reshape.182
  11.8 0.3 convert_reduce_fusion
  12.1 0.6 fusion.9
  12.8 1.9 %fusion.47 = bf16[3072,288]{0,1:T(8,128)(2,1)} fusion(f32[288]{0:T(512)S(1)} %add_rsqrt_fusion, f32[288]{0:T(512)S(1)} %broadcast_multiply_fusion, bf16[1,288,3072]{2,1,0:T(8,128)(2,1)S(1)} %copy-done.1), kind=kLoop, calls=%fused_computation.111 | loop fusion | flops 3538944 | bytes 3541248 | tf_op jit(solution)/shard_map/dot_general | solution.py:159
  14.6 4.0 %copy.67 = bf16[3072,288]{1,0:T(8,128)(2,1)} copy(bf16[3072,288]{0,1:T(8,128)(2,1)} %fusion.47) | data formatting | bytes 3538944 | tf_op jit(solution)/shard_map/dot_general | solution.py:159
  18.7 1.1 %maximum_bitcast_fusion = bf16[16,6,48,128]{3,0,2,1:T(8,128)(2,1)S(1)} fusion(bf16[1,16,1,48,128]{4,1,3,2,0:T(8,128)(2,1)} %collective-permute-done.1, bf16[1,16,4,48,128]{4,1,3,2,0:T(8,128)(2,1)S(1)} %copy.50, bf16[1,16,1,48,128]{4,1,3,2,0:T(8,128)(2,1)S(1)} %collective-permute-done), kind=kLoop, calls=%fused_computation.20 | loop fusion | flops 1179648 | bytes 2359296 | tf_op jit(solution)/shard_map/squeeze | solution.py:99
  19.8 0.2 pad_slice_fusion
  20.0 0.2 pad_slice_fusion.1
  20.2 0.2 broadcast_select_fusion
  20.4 2.6 %pad_select_fusion = (bf16[16,6,50,128]{3,0,2,1:T(8,128)(2,1)}, bf16[16,6,50,128]{3,0,2,1:T(8,128)(2,1)}) fusion(bf16[14,6,50,128]{3,0,2,1:T(8,128)(2,1)S(1)} %pad_slice_fusion, pred[16]{0:T(512)(128)(4,1)S(1)} %get-tuple-element.14, bf16[15,6,50,128]{3,0,2,1:T(8,128)(2,1)S(1)} %pad_slice_fusion.1, pred[16]{0:T(512)(128)(4,1)S(1)} %get-tuple-element.15), kind=kLoop, calls=%fused_computation.17 | loop fusion | flops 1228800 | bytes 4684832 | tf_op jit(solution)/shard_map/jit(_where)/select_n | solution.py:34
  23.0 8.6 %convolution_convert_fusion.1 = bf16[16,1,12,64]{3,0,2,1:T(8,128)(2,1)S(1)} fusion(bf16[3,3,384,128]{3,2,1,0:T(8,128)(2,1)} %bitcast.117, bf16[16,6,50,128]{3,0,2,1:T(8,128)(2,1)} %get-tuple-element.18, bf16[16,6,50,128]{3,0,2,1:T(8,128)(2,1)} %get-tuple-element.19, bf16[16,6,50,128]{3,0,2,1:T(8,128)(2,1)S(1)} %broadcast_select_fusion, ...), kind=kOutput, calls=%fused_computation.25 | convolution fusion | flops 2782064640 | bytes 5644288 | tf_op jit(solution)/shard_map/conv_general_dilated | solution.py:102
  31.7 0.2 convolution_convert_fusion
  31.9 0.1 copy.60
  32.1 0.7 reshape.192
  32.8 9.3 %all-to-all-start = ((bf16[16,2,608]{2,1,0:T(2,128)(2,1)}), bf16[16,2,608]{2,1,0:T(2,128)(2,1)S(1)}, u32[]{:S(2)}, u32[]{:S(2)}) async-start(bf16[16,2,608]{2,1,0:T(2,128)(2,1)} %reshape.192), calls=%async_computation | async-start | bytes 81920 | tf_op jit(solution)/shard_map/all_to_all | solution.py:132
  42.2 6.7 %all-to-all-done = bf16[16,2,608]{2,1,0:T(2,128)(2,1)S(1)} async-done(((bf16[16,2,608]{2,1,0:T(2,128)(2,1)}), bf16[16,2,608]{2,1,0:T(2,128)(2,1)S(1)}, u32[]{:S(2)}, u32[]{:S(2)}) %all-to-all-start) | async-done | bytes 38944 | tf_op jit(solution)/shard_map/all_to_all | solution.py:132
  48.8 0.1 reshape.193
  49.0 0.1 reshape.176
  49.1 0.1 fusion.36
  49.2 0.1 copy.62
  49.4 0.8 %multiply_reduce_fusion = (f32[288]{0:T(512)S(1)}, f32[288,64]{0,1:T(8,128)S(1)}) fusion(f32[288,64]{0,1:T(8,128)S(1)} %copy.62, f32[1,288,64]{1,2,0:T(8,128)S(1)} %copy-done.8, f32[288]{0:T(512)S(1)} %broadcast_subtract_fusion, f32[1,288,64]{1,2,0:T(8,128)S(1)} %copy-done.9, f32[288]{0:T(512)S(1)} %fusion.36, bf16[3072,64]{0,1:T(8,128)(2,1)S(1)} %copy-done, ...), kind=kOutput, calls=%fused_computation.53 | convolution fusion | flops 116913888 | bytes 2463360 | tf_op jit(solution)/shard_map/dot_general | solution.py:153
  50.2 0.2 fusion.37
  50.4 0.6 copy-done.2
  51.1 1.1 %fusion.30 = f32[64,8,2,192]{3,0,2,1:T(8,128)S(1)} fusion(bf16[8,2,192,288]{3,2,1,0:T(8,128)(2,1)S(1)} %bitcast.116, f32[288,64]{0,1:T(8,128)S(1)} %get-tuple-element.17, f32[288]{0:T(512)S(1)} %broadcast_multiply_fusion.1), kind=kOutput, calls=%fused_computation.59 | convolution fusion | flops 113283072 | bytes 2630784 | tf_op jit(solution)/shard_map/dot_general | solution.py:159
  52.2 0.1 bitcast_dynamic-update-slice_fusion
  52.3 0.1 fusion.19
  52.4 0.2 copy.92
  52.6 0.1 collective-permute-start.2
  52.7 1.9 %collective-permute-done.2 = f32[65,8,192]{2,1,0:T(8,128)S(1)} collective-permute-done((f32[65,8,192]{2,1,0:T(8,128)S(1)}, f32[65,8,192]{2,1,0:T(8,128)S(1)}, u32[]{:S(2)}, u32[]{:S(2)}) %collective-permute-start.2) | collective-permute-done | bytes 399392 | tf_op jit(solution)/shard_map/ppermute | solution.py:64
  54.6 0.2 bitcast_add_fusion
  54.8 0.2 reshape.172
  54.9 0.5 constant_dynamic-slice_fusion.5
  55.4 0.1 copy.95
  55.5 0.4 collective-permute-start.3
  55.8 0.1 copy.94
  55.9 0.7 collective-permute-start.4
  56.7 2.6 %collective-permute-start.5 = (f32[65,2,192]{2,1,0:T(2,128)S(1)}, f32[65,2,192]{2,1,0:T(2,128)S(1)}, u32[]{:S(2)}, u32[]{:S(2)}) collective-permute-start(f32[65,2,192]{2,1,0:T(2,128)S(1)} %bitcast.121), channel_id=1, source_target_pairs={{0,6},{1,7},{2,4},{3,5},{4,2},{5,3},{6,0},{7,1},{8,14},{9,15},{10,... | collective-permute-start | bytes 299528 | tf_op jit(solution)/shard_map/ppermute | solution.py:64
  59.3 1.8 %collective-permute-done.3 = f32[65,2,192]{2,1,0:T(2,128)S(1)} collective-permute-done((f32[65,2,192]{2,1,0:T(2,128)S(1)}, f32[65,2,192]{2,1,0:T(2,128)S(1)}, u32[]{:S(2)}, u32[]{:S(2)}) %collective-permute-start.3) | collective-permute-done | bytes 99872 | tf_op jit(solution)/shard_map/ppermute | solution.py:64
  61.1 1.3 %collective-permute-done.4 = f32[65,2,192]{2,1,0:T(2,128)S(1)} collective-permute-done((f32[65,2,192]{2,1,0:T(2,128)S(1)}, f32[65,2,192]{2,1,0:T(2,128)S(1)}, u32[]{:S(2)}, u32[]{:S(2)}) %collective-permute-start.4) | collective-permute-done | bytes 99872 | tf_op jit(solution)/shard_map/ppermute | solution.py:64
  62.4 2.9 %collective-permute-done.5 = f32[65,2,192]{2,1,0:T(2,128)S(1)} collective-permute-done((f32[65,2,192]{2,1,0:T(2,128)S(1)}, f32[65,2,192]{2,1,0:T(2,128)S(1)}, u32[]{:S(2)}, u32[]{:S(2)}) %collective-permute-start.5) | collective-permute-done | bytes 99872 | tf_op jit(solution)/shard_map/ppermute | solution.py:64
  65.3 0.1 fusion.25
  65.5 0.4 collective-permute-start.6
  65.9 5.3 %collective-permute-done.6 = f32[65,1,192]{2,1,0:T(1,128)S(1)} collective-permute-done((f32[65,1,192]{2,1,0:T(1,128)S(1)}, f32[65,1,192]{2,1,0:T(1,128)S(1)}, u32[]{:S(2)}, u32[]{:S(2)}) %collective-permute-start.6) | collective-permute-done | bytes 49952 | tf_op jit(solution)/shard_map/ppermute | solution.py:64
  71.2 0.1 dynamic-slice_add_fusion
  71.3 1.6 %collective-permute-start.7 = (f32[65,192]{1,0:T(8,128)S(1)}, f32[65,192]{1,0:T(8,128)S(1)}, u32[]{:S(2)}, u32[]{:S(2)}) collective-permute-start(f32[65,192]{1,0:T(8,128)S(1)} %bitcast.122), channel_id=1, source_target_pairs={{0,16},{16,0},{1,17},{17,1},{2,18},{18,2},{3,19},{19,3},{4,20},{20... | collective-permute-start | bytes 149768 | tf_op jit(solution)/shard_map/ppermute | solution.py:69
  72.9 0.7 reshape.165
  73.6 2.2 %collective-permute-done.7 = f32[65,192]{1,0:T(8,128)S(1)} collective-permute-done((f32[65,192]{1,0:T(8,128)S(1)}, f32[65,192]{1,0:T(8,128)S(1)}, u32[]{:S(2)}, u32[]{:S(2)}) %collective-permute-start.7) | collective-permute-done | bytes 49952 | tf_op jit(solution)/shard_map/ppermute | solution.py:69
  75.7 0.6 slice_bitcast_fusion
  76.4 0.6 constant_dynamic-slice_fusion
  (51 shorter events, 0.6 us)
Async XLA Ops:
  0.6 48.7 %copy-start = (bf16[3072,64]{0,1:T(8,128)(2,1)S(1)}, bf16[3072,64]{0,1:T(8,128)(2,1)}, u32[]{:S(2)}) copy-start(bf16[3072,64]{0,1:T(8,128)(2,1)} %param.21) | copy-start | bytes 1179652
  0.6 6.2 %copy-start.5 = (s32[1,4]{1,0:T(1,128)S(1)}, s32[1,4]{1,0:T(1,128)}, u32[]{:S(2)}) copy-start(s32[1,4]{1,0:T(1,128)} %param.12) | copy-start | bytes 52
  2.4 7.1 %copy-start.3 = (bf16[2048,64]{0,1:T(8,128)(2,1)S(1)}, bf16[2048,64]{0,1:T(8,128)(2,1)}, u32[]{:S(2)}) copy-start(bf16[2048,64]{0,1:T(8,128)(2,1)} %param.17) | copy-start | bytes 786436
  2.4 8.0 %copy-start.4 = (s32[1,1,192,1]{2,3,1,0:T(1,128)S(1)}, s32[1,1,192,1]{2,3,1,0:T(1,128)}, u32[]{:S(2)}) copy-start(s32[1,1,192,1]{2,3,1,0:T(1,128)} %param.15) | copy-start | bytes 2308
  2.4 9.4 %copy-start.1 = (bf16[1,288,3072]{2,1,0:T(8,128)(2,1)S(1)}, bf16[1,288,3072]{2,1,0:T(8,128)(2,1)}, u32[]{:S(2)}) copy-start(bf16[1,288,3072]{2,1,0:T(8,128)(2,1)} %param.18) | copy-start | bytes 5308420
  3.2 15.5 %collective-permute-start = (bf16[1,16,1,48,128]{4,1,3,2,0:T(8,128)(2,1)}, bf16[1,16,1,48,128]{4,1,3,2,0:T(8,128)(2,1)S(1)}, u32[]{:S(2)}, u32[]{:S(2)}) collective-permute-start(bf16[1,16,1,48,128]{4,1,3,2,0:T(8,128)(2,1)} %get-tuple-element.7), channel_id=1, source_target_pairs={{0,1},{1,2},{2,3},{3,4},{4,5},{5,6},{6,7},{7,8},{8,9},{9,10},{10,1... | collective-permute-start | bytes 589832 | tf_op jit(solution)/shard_map/ppermute | solution.py:18
  5.6 13.1 %collective-permute-start.1 = (bf16[1,16,1,48,128]{4,1,3,2,0:T(8,128)(2,1)}, bf16[1,16,1,48,128]{4,1,3,2,0:T(8,128)(2,1)}, u32[]{:S(2)}, u32[]{:S(2)}) collective-permute-start(bf16[1,16,1,48,128]{4,1,3,2,0:T(8,128)(2,1)} %get-tuple-element.8), channel_id=1, source_target_pairs={{1,0},{2,1},{3,2},{4,3},{5,4},{6,5},{7,6},{8,7},{9,8},{10,9},{11,1... | collective-permute-start | bytes 589832 | tf_op jit(solution)/shard_map/ppermute | solution.py:20
  14.6 4.0 %copy-start.6 = (s32[1,4]{1,0:T(1,128)S(1)}, s32[1,4]{1,0:T(1,128)}, u32[]{:S(2)}) copy-start(s32[1,4]{1,0:T(1,128)} %param.14) | copy-start | bytes 52
  14.6 4.0 %copy-start.7 = (s32[1,4]{1,0:T(1,128)S(1)}, s32[1,4]{1,0:T(1,128)}, u32[]{:S(2)}) copy-start(s32[1,4]{1,0:T(1,128)} %param.13) | copy-start | bytes 52
  31.6 17.8 %copy-start.8 = (f32[1,288,64]{1,2,0:T(8,128)S(1)}, f32[1,288,64]{1,2,0:T(8,128)}, u32[]{:S(2)}) copy-start(f32[1,288,64]{1,2,0:T(8,128)} %param.19) | copy-start | bytes 221188
  31.6 17.8 %copy-start.9 = (f32[1,288,64]{1,2,0:T(8,128)S(1)}, f32[1,288,64]{1,2,0:T(8,128)}, u32[]{:S(2)}) copy-start(f32[1,288,64]{1,2,0:T(8,128)} %param.20) | copy-start | bytes 221188
  32.8 16.0 %all-to-all-start = ((bf16[16,2,608]{2,1,0:T(2,128)(2,1)}), bf16[16,2,608]{2,1,0:T(2,128)(2,1)S(1)}, u32[]{:S(2)}, u32[]{:S(2)}) async-start(bf16[16,2,608]{2,1,0:T(2,128)(2,1)} %reshape.192), calls=%async_computation | async-start | bytes 81920 | tf_op jit(solution)/shard_map/all_to_all | solution.py:132
  49.4 1.7 %copy-start.2 = (bf16[3072,288]{1,0:T(8,128)(2,1)S(1)}, bf16[3072,288]{1,0:T(8,128)(2,1)}, u32[]{:S(2)}) copy-start(bf16[3072,288]{1,0:T(8,128)(2,1)} %copy.67) | copy-start | bytes 5308420
  52.6 2.0 %collective-permute-start.2 = (f32[65,8,192]{2,1,0:T(8,128)S(1)}, f32[65,8,192]{2,1,0:T(8,128)S(1)}, u32[]{:S(2)}, u32[]{:S(2)}) collective-permute-start(f32[65,8,192]{2,1,0:T(8,128)S(1)} %bitcast.118), channel_id=1, source_target_pairs={{0,1},{1,0},{2,3},{3,2},{4,5},{5,4},{6,7},{7,6},{8,9},{9,8},{10,11... | collective-permute-start | bytes 1198088 | tf_op jit(solution)/shard_map/ppermute | solution.py:64
  55.5 5.6 %collective-permute-start.3 = (f32[65,2,192]{2,1,0:T(2,128)S(1)}, f32[65,2,192]{2,1,0:T(2,128)S(1)}, u32[]{:S(2)}, u32[]{:S(2)}) collective-permute-start(f32[65,2,192]{2,1,0:T(2,128)S(1)} %bitcast.119), channel_id=1, source_target_pairs={{0,2},{1,3},{2,0},{3,1},{4,6},{5,7},{6,4},{7,5},{8,10},{9,11},{10,... | collective-permute-start | bytes 299528 | tf_op jit(solution)/shard_map/ppermute | solution.py:64
  55.9 6.5 %collective-permute-start.4 = (f32[65,2,192]{2,1,0:T(2,128)S(1)}, f32[65,2,192]{2,1,0:T(2,128)S(1)}, u32[]{:S(2)}, u32[]{:S(2)}) collective-permute-start(f32[65,2,192]{2,1,0:T(2,128)S(1)} %bitcast.120), channel_id=1, source_target_pairs={{0,4},{1,5},{2,6},{3,7},{4,0},{5,1},{6,2},{7,3},{8,12},{9,13},{10,... | collective-permute-start | bytes 299528 | tf_op jit(solution)/shard_map/ppermute | solution.py:64
  56.7 8.6 %collective-permute-start.5 = (f32[65,2,192]{2,1,0:T(2,128)S(1)}, f32[65,2,192]{2,1,0:T(2,128)S(1)}, u32[]{:S(2)}, u32[]{:S(2)}) collective-permute-start(f32[65,2,192]{2,1,0:T(2,128)S(1)} %bitcast.121), channel_id=1, source_target_pairs={{0,6},{1,7},{2,4},{3,5},{4,2},{5,3},{6,0},{7,1},{8,14},{9,15},{10,... | collective-permute-start | bytes 299528 | tf_op jit(solution)/shard_map/ppermute | solution.py:64
  65.5 5.7 %collective-permute-start.6 = (f32[65,1,192]{2,1,0:T(1,128)S(1)}, f32[65,1,192]{2,1,0:T(1,128)S(1)}, u32[]{:S(2)}, u32[]{:S(2)}) collective-permute-start(f32[65,1,192]{2,1,0:T(1,128)S(1)} %constant_dynamic-slice_fusion.1), channel_id=1, source_target_pairs={{0,8},{1,9},{2,10},{3,11},{4,12},{5,13},{6,14},{7,15},{8,0},{9,1},... | collective-permute-start | bytes 149768 | tf_op jit(solution)/shard_map/ppermute | solution.py:64
  71.3 4.4 %collective-permute-start.7 = (f32[65,192]{1,0:T(8,128)S(1)}, f32[65,192]{1,0:T(8,128)S(1)}, u32[]{:S(2)}, u32[]{:S(2)}) collective-permute-start(f32[65,192]{1,0:T(8,128)S(1)} %bitcast.122), channel_id=1, source_target_pairs={{0,16},{16,0},{1,17},{17,1},{2,18},{18,2},{3,19},{19,3},{4,20},{20... | collective-permute-start | bytes 149768 | tf_op jit(solution)/shard_map/ppermute | solution.py:69

commit v7 on v5

--- a/solution.py
+++ b/solution.py
@@ -45,27 +45,26 @@
     return total
 
 
-def tree_reduce(grad_t, loss_line, nseq, ndp):
-    rows = grad_t.shape[1] // nseq
+def tree_reduce(blocks, nseq, ndp):
     nbits = nseq.bit_length() - 1
     assert 1 << nbits == nseq and ndp & (ndp - 1) == 0
     groups = [1, 2] + [1] * (nbits - 3) if nbits >= 3 else [1] * nbits
-    x = jnp.concatenate([grad_t, loss_line[None, :]], axis=0)
-    x = x.reshape(x.shape[0], nseq, rows)
+    x = blocks
+    tail = x.shape[1:]
     me = lax.axis_index("seq")
     low = 0
     for width in groups:
         ways = 1 << width
-        x = x.reshape(x.shape[0], x.shape[1] // ways, ways, rows)
+        x = x.reshape((x.shape[0] // ways, ways) + tail)
         digit = (me >> low) & (ways - 1)
-        total = lax.dynamic_index_in_dim(x, digit, 2, keepdims=False)
+        total = lax.dynamic_index_in_dim(x, digit, 1, keepdims=False)
         for step in range(1, ways):
-            send = lax.dynamic_index_in_dim(x, digit ^ step, 2, keepdims=False)
+            send = lax.dynamic_index_in_dim(x, digit ^ step, 1, keepdims=False)
             pairs = [(i, i ^ (step << low)) for i in range(nseq)]
             total = total + lax.ppermute(send, "seq", pairs)
         x = total
         low += width
-    x = x.reshape(-1, rows)
+    x = x.reshape(tail)
     for k in range(ndp.bit_length() - 1):
         x = x + lax.ppermute(x, "dp", [(i, i ^ (1 << k)) for i in range(ndp)])
     return x
@@ -162,12 +161,16 @@
     )
     ndp = lax.axis_size("dp")
     share = grad_t.shape[1] // nseq
-    assert ndp * CLIPS <= share
+    lanes = 128
+    dense = LAT * share // lanes
+    assert ndp * CLIPS <= lanes and dense * lanes == LAT * share
     place = lax.axis_index("dp") * CLIPS
-    loss_row = lax.dynamic_update_slice(jnp.zeros((share,), jnp.float32), partial_loss, (place,))
-    summed = tree_reduce(grad_t, jnp.tile(loss_row, nseq), nseq, ndp)
-    grad_mine = summed[:LAT].T
-    clip_loss = lax.dynamic_slice_in_dim(summed[LAT], place, CLIPS).reshape(1, CLIPS)
+    blocks = grad_t.reshape(LAT, nseq, share).transpose(1, 0, 2).reshape(nseq, dense, lanes)
+    loss_row = lax.dynamic_update_slice(jnp.zeros((lanes,), jnp.float32), partial_loss, (place,))
+    loss_rows = jnp.broadcast_to(loss_row[None, None, :], (nseq, 1, lanes))
+    summed = tree_reduce(jnp.concatenate([blocks, loss_rows], axis=1), nseq, ndp)
+    grad_mine = summed[:dense].reshape(LAT, share).T
+    clip_loss = lax.dynamic_slice_in_dim(summed[dense], place, CLIPS).reshape(1, CLIPS)
     return (latent_out, clip_loss, grad_mine)
 
 

time: 70.3 us -> 70.2 us (level)
  waiting for transfers between devices: 22 us -> 20 us
  local copies, waits for them, and re-layouts: 12.8 us -> 14.1 us
  matrix products: 10.3 us -> 11.3 us
    ppermute x5, waiting for transfers between devices: 13.1 us -> 11.3 us  [tree_reduce(): total = total + lax.ppermute(send, 'seq', pairs)]
    concatenate x1, local copies, waits for them, and re-layouts: 0.01 us -> 1.76 us  [per_device(): jnp.concatenate([blocks, loss_rows], axis=1)]
    dot_general x1, matrix products: 1.11 us -> 2.11 us  [per_device(): lax.dot_general(dpred, normed, (((0,), (0,)), ((), ())), preferred_elemen...]
    unnamed x26 -> x23, local copies, waits for them, and re-layouts: 5.13 us -> 4.92 us
  transfers between devices with their start and end apart: 9 -> 9, of which waited for: 7 -> 7; matrix products, arithmetic and copies ran while one was open for 9% -> 8% of each run, Pallas kernels for 0% -> 0%
where the time goes in v7:
time: 70.2 us; the launch traced here: 69.7 us
  waiting for transfers between devices  20 us (28%)
  starting transfers between devices  18.6 us (26%)
  local copies, waits for them, and re-layouts  14.1 us (20%)
  matrix products  11.3 us (16%)
  other arithmetic  4.75 us (7%)
  between operations  1.1 us (2%)
    ppermute x5, waiting for transfers between devices, tree_reduce(): total = total + lax.ppermute(send, 'seq', pairs)  11.3 us
    all_to_all x1, starting transfers between devices, per_device(): lax.all_to_all(jnp.concatenate([outgoing, labels], axis=1), 'seq', split_...  8.63 us
    all_to_all x1, waiting for transfers between devices, per_device(): lax.all_to_all(jnp.concatenate([outgoing, labels], axis=1), 'seq', split_...  6.69 us
    conv_general_dilated x1, matrix products, causal_conv(): lax.conv_general_dilated(padded, kernel, (1, 1), 'VALID', dimension_numbe...  5.56 us
    unnamed x23, local copies, waits for them, and re-layouts  4.92 us
    ppermute x5, starting transfers between devices, tree_reduce(): total = total + lax.ppermute(send, 'seq', pairs)  4.03 us
    ppermute x1, starting transfers between devices, with_halo(): lax.ppermute(tail, axis, [(i, (i + 1) % count) for i in range(ends)])  3.06 us
    dot_general x1, local copies, waits for them, and re-layouts, per_device(): lax.dot_general(dpred, normed, (((0,), (0,)), ((), ())), preferred_elemen...  2.87 us
  transfers between devices with their start and end apart: 9, of which 7 were waited for; matrix products, arithmetic and copies ran while one was open for 8% of the time, Pallas kernels for 0%

profile of v7, /device:TPU:0, one launch (start us, length us, event | category | flops | bytes accessed | tf_op | source)
XLA Modules:
  0.0 69.7 jit_solution(9644912150398506645)
XLA Ops:
  0.6 0.0 copy-start
  0.7 1.7 %copy.52 = bf16[1,16,4,48,128]{4,1,3,2,0:T(8,128)(2,1)S(1)} copy(bf16[1,16,4,48,128]{4,3,2,1,0:T(8,128)(2,1)} %param.11) | data formatting | bytes 1572864 | tf_op args[0]
  2.4 0.0 copy-start.3
  2.4 0.0 copy-start.1
  2.4 0.8 %fusion.39 = (bf16[1,16,1,48,128]{4,1,3,2,0:T(8,128)(2,1)}, bf16[1,16,1,48,128]{4,1,3,2,0:T(8,128)(2,1)}) fusion(bf16[1,16,4,48,128]{4,1,3,2,0:T(8,128)(2,1)S(1)} %copy.52), kind=kLoop, calls=%fused_computation.97 | loop fusion | bytes 786432 | tf_op jit(solution)/shard_map/slice | solution.py:15
  3.2 3.1 %collective-permute-start = (bf16[1,16,1,48,128]{4,1,3,2,0:T(8,128)(2,1)}, bf16[1,16,1,48,128]{4,1,3,2,0:T(8,128)(2,1)}, u32[]{:S(2)}, u32[]{:S(2)}) collective-permute-start(bf16[1,16,1,48,128]{4,1,3,2,0:T(8,128)(2,1)} %get-tuple-element.7), channel_id=1, source_target_pairs={{0,1},{1,2},{2,3},{3,4},{4,5},{5,6},{6,7},{7,8},{8,9},{9,10},{10,1... | collective-permute-start | bytes 589832 | tf_op jit(solution)/shard_map/ppermute | solution.py:18
  6.2 1.3 %collective-permute-start.1 = (bf16[1,16,1,48,128]{4,1,3,2,0:T(8,128)(2,1)}, bf16[1,16,1,48,128]{4,1,3,2,0:T(8,128)(2,1)}, u32[]{:S(2)}, u32[]{:S(2)}) collective-permute-start(bf16[1,16,1,48,128]{4,1,3,2,0:T(8,128)(2,1)} %get-tuple-element.8), channel_id=1, source_target_pairs={{1,0},{2,1},{3,2},{4,3},{5,4},{6,5},{7,6},{8,7},{9,8},{10,9},{11,1... | collective-permute-start | bytes 589832 | tf_op jit(solution)/shard_map/ppermute | solution.py:20
  7.5 2.3 %copy.56 = bf16[3,3,3,128,128]{3,4,0,2,1:T(8,128)(2,1)} copy(bf16[3,3,3,128,128]{4,3,2,1,0:T(8,128)(2,1)} %param.16) | data formatting | bytes 1769472 | tf_op args[5]
  9.8 0.2 reduce-window.10
  10.0 0.1 convert_reduce_fusion.1
  10.1 0.1 select_reduce_fusion
  10.2 0.2 reshape.199
  10.4 0.6 reduce-window.11
  11.0 0.2 slice_reduce_fusion
  11.2 0.1 bitcast_bitcast_fusion
  11.3 0.1 broadcast_in_dim.6
  11.4 0.1 reshape.215
  11.5 0.2 convolution_reduce_fusion
  11.7 0.1 reshape.219
  11.8 0.0 copy-start.6
  11.9 0.3 convert_reduce_fusion
  12.2 0.6 fusion.3
  12.9 5.6 %fusion.7 = f32[16,4,48,384]{3,0,2,1:T(8,128)S(1)} fusion(bf16[3,3,128,384]{2,3,1,0:T(8,128)(2,1)} %bitcast.101, bf16[1,16,1,48,128]{4,1,3,2,0:T(8,128)(2,1)} %collective-permute-done.1, bf16[1,16,4,48,128]{4,1,3,2,0:T(8,128)(2,1)S(1)} %copy.52, bf16[1,16,1,48,128]{4,1,3,2,0:T(8,128)(2,1)} %collective-permute-done), kind=kOutput, calls=%fused_computation.15 | convolution fusion | flops 2683699200 | bytes 6782976 | tf_op jit(solution)/shard_map/conv_general_dilated | solution.py:32
  18.4 0.1 slice.51
  18.6 0.1 slice.52
  18.7 2.4 %convolution_convert_fusion.1 = bf16[16,1,12,64]{3,0,2,1:T(8,128)(2,1)S(1)} fusion(f32[16,4,48,384]{3,0,2,1:T(8,128)S(1)} %fusion.7, f32[14,4,48,128]{3,0,2,1:T(8,128)S(1)} %slice.52, f32[15,4,48,128]{3,0,2,1:T(8,128)S(1)} %slice.51, f32[16]{0:T(128)S(1)} %get-tuple-element.14, f32[16]{0:T(128)S(1)} %get-tuple-element.13, ...), kind=kOutput, calls=%fused_computation.22 | convolution fusion | flops 54669312 | bytes 5792768 | tf_op jit(solution)/shard_map/conv_general_dilated | solution.py:102
  21.2 0.2 convolution_convert_fusion
  21.4 0.1 copy.62
  21.6 0.7 %reshape.229 = bf16[16,2,608]{2,1,0:T(2,128)(2,1)} reshape(bf16[16,19,64]{2,1,0:T(8,128)(2,1)S(1)} %fusion.19) | data formatting | bytes 77824
  22.3 8.6 %all-to-all-start = ((bf16[16,2,608]{2,1,0:T(2,128)(2,1)}), bf16[16,2,608]{2,1,0:T(2,128)(2,1)S(1)}, u32[]{:S(2)}, u32[]{:S(2)}) async-start(bf16[16,2,608]{2,1,0:T(2,128)(2,1)} %reshape.229), calls=%async_computation | async-start | bytes 81920 | tf_op jit(solution)/shard_map/all_to_all | solution.py:132
  31.0 6.7 %all-to-all-done = bf16[16,2,608]{2,1,0:T(2,128)(2,1)S(1)} async-done(((bf16[16,2,608]{2,1,0:T(2,128)(2,1)}), bf16[16,2,608]{2,1,0:T(2,128)(2,1)S(1)}, u32[]{:S(2)}, u32[]{:S(2)}) %all-to-all-start) | async-done | bytes 38944 | tf_op jit(solution)/shard_map/all_to_all | solution.py:132
  37.7 0.1 reshape.230
  37.9 0.1 reshape.212
  38.0 0.1 copy.64
  38.1 0.1 fusion.28
  38.2 0.0 copy-start.7
  38.2 1.9 %fusion.37 = bf16[3072,288]{0,1:T(8,128)(2,1)} fusion(f32[288]{0:T(512)S(1)} %get-tuple-element.17, f32[288]{0:T(512)S(1)} %broadcast_multiply_fusion, bf16[1,288,3072]{2,1,0:T(8,128)(2,1)S(1)} %copy-done.1), kind=kLoop, calls=%fused_computation.96 | loop fusion | flops 3538944 | bytes 3541248 | tf_op jit(solution)/shard_map/dot_general | solution.py:159
  40.1 0.8 %multiply_reduce_fusion = (f32[288]{0:T(512)S(1)}, f32[288,64]{0,1:T(8,128)S(1)}) fusion(f32[288,64]{0,1:T(8,128)S(1)} %copy.64, f32[1,288,64]{1,2,0:T(8,128)S(1)} %copy-done.7, f32[288]{0:T(512)S(1)} %get-tuple-element.18, f32[1,288,64]{1,2,0:T(8,128)S(1)} %copy-done.8, f32[288]{0:T(512)S(1)} %fusion.28, bf16[3072,64]{0,1:T(8,128)(2,1)S(1)} %copy-done, ...), kind=kOutput, calls=%fused_computation.43 | convolution fusion | flops 116913888 | bytes 2463360 | tf_op jit(solution)/shard_map/dot_general | solution.py:153
  40.9 0.2 fusion.29
  41.1 2.9 %copy.68 = bf16[3072,288]{1,0:T(8,128)(2,1)S(1)} copy(bf16[3072,288]{0,1:T(8,128)(2,1)} %fusion.37) | data formatting | bytes 3538944 | tf_op jit(solution)/shard_map/dot_general | solution.py:159
  44.0 2.1 %convolution_bitcast_fusion = f32[16,64,192]{2,1,0:T(8,128)} fusion(bf16[16,192,288]{2,1,0:T(8,128)(2,1)S(1)} %bitcast.99, f32[288,64]{0,1:T(8,128)S(1)} %get-tuple-element.16, f32[288]{0:T(512)S(1)} %broadcast_multiply_fusion.1), kind=kOutput, calls=%fused_computation.11 | convolution fusion | flops 113283072 | bytes 2630784 | tf_op jit(solution)/shard_map/dot_general | solution.py:159
  46.1 1.8 %concatenate.14 = f32[8,2,96,128]{3,2,1,0:T(8,128)S(1)} reshape(f32[16,64,192]{2,1,0:T(8,128)} %convolution_bitcast_fusion) | data formatting | bytes 1572864 | tf_op jit(solution)/shard_map/concatenate | solution.py:171
  47.9 0.1 multiply_dynamic-update-slice_fusion
  48.0 0.1 fusion.14
  48.0 0.1 copy.85
  48.1 0.1 collective-permute-start.2
  48.2 1.7 %collective-permute-done.2 = f32[8,97,128]{2,0,1:T(8,128)S(1)} collective-permute-done((f32[8,97,128]{2,0,1:T(8,128)S(1)}, f32[8,97,128]{2,0,1:T(8,128)S(1)}, u32[]{:S(2)}, u32[]{:S(2)}) %collective-permute-start.2) | collective-permute-done | bytes 397344 | tf_op jit(solution)/shard_map/ppermute | solution.py:64
  49.9 0.1 bitcast_add_fusion
  50.0 0.3 constant_dynamic-slice_fusion.4
  50.4 0.4 collective-permute-start.3
  50.7 0.6 collective-permute-start.4
  51.3 2.6 %collective-permute-start.5 = (f32[2,97,128]{2,0,1:T(2,128)S(1)}, f32[2,97,128]{2,0,1:T(2,128)S(1)}, u32[]{:S(2)}, u32[]{:S(2)}) collective-permute-start(f32[2,97,128]{2,0,1:T(2,128)S(1)} %bitcast.104), channel_id=1, source_target_pairs={{0,6},{1,7},{2,4},{3,5},{4,2},{5,3},{6,0},{7,1},{8,14},{9,15},{10,... | collective-permute-start | bytes 297992 | tf_op jit(solution)/shard_map/ppermute | solution.py:64
  53.9 1.4 %collective-permute-done.3 = f32[2,97,128]{2,0,1:T(2,128)S(1)} collective-permute-done((f32[2,97,128]{2,0,1:T(2,128)S(1)}, f32[2,97,128]{2,0,1:T(2,128)S(1)}, u32[]{:S(2)}, u32[]{:S(2)}) %collective-permute-start.3) | collective-permute-done | bytes 99360 | tf_op jit(solution)/shard_map/ppermute | solution.py:64
  55.3 1.1 %collective-permute-done.4 = f32[2,97,128]{2,0,1:T(2,128)S(1)} collective-permute-done((f32[2,97,128]{2,0,1:T(2,128)S(1)}, f32[2,97,128]{2,0,1:T(2,128)S(1)}, u32[]{:S(2)}, u32[]{:S(2)}) %collective-permute-start.4) | collective-permute-done | bytes 99360 | tf_op jit(solution)/shard_map/ppermute | solution.py:64
  56.4 2.2 %collective-permute-done.5 = f32[2,97,128]{2,0,1:T(2,128)S(1)} collective-permute-done((f32[2,97,128]{2,0,1:T(2,128)S(1)}, f32[2,97,128]{2,0,1:T(2,128)S(1)}, u32[]{:S(2)}, u32[]{:S(2)}) %collective-permute-start.5) | collective-permute-done | bytes 99360 | tf_op jit(solution)/shard_map/ppermute | solution.py:64
  58.6 0.1 add_add_fusion
  58.8 0.4 collective-permute-start.6
  59.2 5.0 %collective-permute-done.6 = f32[1,97,128]{2,0,1:T(1,128)S(1)} collective-permute-done((f32[1,97,128]{2,0,1:T(1,128)S(1)}, f32[1,97,128]{2,0,1:T(1,128)S(1)}, u32[]{:S(2)}, u32[]{:S(2)}) %collective-permute-start.6) | collective-permute-done | bytes 49696 | tf_op jit(solution)/shard_map/ppermute | solution.py:64
  64.1 0.1 dynamic-slice_add_fusion
  64.2 1.6 %collective-permute-start.7 = (f32[97,128]{1,0:T(8,128)S(1)}, f32[97,128]{1,0:T(8,128)S(1)}, u32[]{:S(2)}, u32[]{:S(2)}) collective-permute-start(f32[97,128]{1,0:T(8,128)S(1)} %bitcast.108), channel_id=1, source_target_pairs={{0,16},{16,0},{1,17},{17,1},{2,18},{18,2},{3,19},{19,3},{4,20},{20... | collective-permute-start | bytes 149000 | tf_op jit(solution)/shard_map/ppermute | solution.py:69
  65.8 0.7 %reshape.200 = bf16[1,16,1,768]{3,1,2,0:T(8,128)(2,1)} reshape(bf16[16,1,12,64]{3,2,0,1:T(8,128)(2,1)S(1)} %copy.58) | data formatting | bytes 49152 | tf_op jit(solution)/shard_map/reshape | solution.py:110
  66.5 1.9 %collective-permute-done.7 = f32[97,128]{1,0:T(8,128)S(1)} collective-permute-done((f32[97,128]{1,0:T(8,128)S(1)}, f32[97,128]{1,0:T(8,128)S(1)}, u32[]{:S(2)}, u32[]{:S(2)}) %collective-permute-start.7) | collective-permute-done | bytes 49696 | tf_op jit(solution)/shard_map/ppermute | solution.py:69
  68.4 0.7 %reshape.209 = f32[64,192]{1,0:T(8,128)} reshape(f32[96,128]{1,0:T(8,128)S(1)} %slice.58) | data formatting | bytes 98304 | tf_op jit(solution)/shard_map/reshape | solution.py:172
  69.2 0.6 constant_dynamic-slice_fusion
  (44 shorter events, 0.5 us)
Async XLA Ops:
  0.6 39.5 %copy-start = (bf16[3072,64]{0,1:T(8,128)(2,1)S(1)}, bf16[3072,64]{0,1:T(8,128)(2,1)}, u32[]{:S(2)}) copy-start(bf16[3072,64]{0,1:T(8,128)(2,1)} %param.21) | copy-start | bytes 1179652
  0.6 9.2 %copy-start.4 = (s32[1,4]{1,0:T(1,128)S(1)}, s32[1,4]{1,0:T(1,128)}, u32[]{:S(2)}) copy-start(s32[1,4]{1,0:T(1,128)} %param.12) | copy-start | bytes 52
  0.7 9.5 %copy-start.2 = (bf16[2048,64]{0,1:T(8,128)(2,1)S(1)}, bf16[2048,64]{0,1:T(8,128)(2,1)}, u32[]{:S(2)}) copy-start(bf16[2048,64]{0,1:T(8,128)(2,1)} %param.17) | copy-start | bytes 786436
  2.4 8.0 %copy-start.3 = (s32[1,1,192,1]{2,3,1,0:T(1,128)S(1)}, s32[1,1,192,1]{2,3,1,0:T(1,128)}, u32[]{:S(2)}) copy-start(s32[1,1,192,1]{2,3,1,0:T(1,128)} %param.15) | copy-start | bytes 2308
  2.4 9.4 %copy-start.1 = (bf16[1,288,3072]{2,1,0:T(8,128)(2,1)S(1)}, bf16[1,288,3072]{2,1,0:T(8,128)(2,1)}, u32[]{:S(2)}) copy-start(bf16[1,288,3072]{2,1,0:T(8,128)(2,1)} %param.18) | copy-start | bytes 5308420
  3.2 9.7 %collective-permute-start = (bf16[1,16,1,48,128]{4,1,3,2,0:T(8,128)(2,1)}, bf16[1,16,1,48,128]{4,1,3,2,0:T(8,128)(2,1)}, u32[]{:S(2)}, u32[]{:S(2)}) collective-permute-start(bf16[1,16,1,48,128]{4,1,3,2,0:T(8,128)(2,1)} %get-tuple-element.7), channel_id=1, source_target_pairs={{0,1},{1,2},{2,3},{3,4},{4,5},{5,6},{6,7},{7,8},{8,9},{9,10},{10,1... | collective-permute-start | bytes 589832 | tf_op jit(solution)/shard_map/ppermute | solution.py:18
  6.2 6.6 %collective-permute-start.1 = (bf16[1,16,1,48,128]{4,1,3,2,0:T(8,128)(2,1)}, bf16[1,16,1,48,128]{4,1,3,2,0:T(8,128)(2,1)}, u32[]{:S(2)}, u32[]{:S(2)}) collective-permute-start(bf16[1,16,1,48,128]{4,1,3,2,0:T(8,128)(2,1)} %get-tuple-element.8), channel_id=1, source_target_pairs={{1,0},{2,1},{3,2},{4,3},{5,4},{6,5},{7,6},{8,7},{9,8},{10,9},{11,1... | collective-permute-start | bytes 589832 | tf_op jit(solution)/shard_map/ppermute | solution.py:20
  11.8 1.0 %copy-start.5 = (s32[1,4]{1,0:T(1,128)S(1)}, s32[1,4]{1,0:T(1,128)}, u32[]{:S(2)}) copy-start(s32[1,4]{1,0:T(1,128)} %param.14) | copy-start | bytes 52
  11.8 1.0 %copy-start.6 = (s32[1,4]{1,0:T(1,128)S(1)}, s32[1,4]{1,0:T(1,128)}, u32[]{:S(2)}) copy-start(s32[1,4]{1,0:T(1,128)} %param.13) | copy-start | bytes 52
  22.3 15.3 %all-to-all-start = ((bf16[16,2,608]{2,1,0:T(2,128)(2,1)}), bf16[16,2,608]{2,1,0:T(2,128)(2,1)S(1)}, u32[]{:S(2)}, u32[]{:S(2)}) async-start(bf16[16,2,608]{2,1,0:T(2,128)(2,1)} %reshape.229), calls=%async_computation | async-start | bytes 81920 | tf_op jit(solution)/shard_map/all_to_all | solution.py:132
  38.2 1.9 %copy-start.7 = (f32[1,288,64]{1,2,0:T(8,128)S(1)}, f32[1,288,64]{1,2,0:T(8,128)}, u32[]{:S(2)}) copy-start(f32[1,288,64]{1,2,0:T(8,128)} %param.19) | copy-start | bytes 221188
  38.2 1.9 %copy-start.8 = (f32[1,288,64]{1,2,0:T(8,128)S(1)}, f32[1,288,64]{1,2,0:T(8,128)}, u32[]{:S(2)}) copy-start(f32[1,288,64]{1,2,0:T(8,128)} %param.20) | copy-start | bytes 221188
  48.1 1.8 %collective-permute-start.2 = (f32[8,97,128]{2,0,1:T(8,128)S(1)}, f32[8,97,128]{2,0,1:T(8,128)S(1)}, u32[]{:S(2)}, u32[]{:S(2)}) collective-permute-start(f32[8,97,128]{2,0,1:T(8,128)S(1)} %bitcast.102), channel_id=1, source_target_pairs={{0,1},{1,0},{2,3},{3,2},{4,5},{5,4},{6,7},{7,6},{8,9},{9,8},{10,11... | collective-permute-start | bytes 1191944 | tf_op jit(solution)/shard_map/ppermute | solution.py:64
  50.4 4.9 %collective-permute-start.3 = (f32[2,97,128]{2,0,1:T(2,128)S(1)}, f32[2,97,128]{2,0,1:T(2,128)S(1)}, u32[]{:S(2)}, u32[]{:S(2)}) collective-permute-start(f32[2,97,128]{2,0,1:T(2,128)S(1)} %bitcast.106), channel_id=1, source_target_pairs={{0,2},{1,3},{2,0},{3,1},{4,6},{5,7},{6,4},{7,5},{8,10},{9,11},{10,... | collective-permute-start | bytes 297992 | tf_op jit(solution)/shard_map/ppermute | solution.py:64
  50.7 5.7 %collective-permute-start.4 = (f32[2,97,128]{2,0,1:T(2,128)S(1)}, f32[2,97,128]{2,0,1:T(2,128)S(1)}, u32[]{:S(2)}, u32[]{:S(2)}) collective-permute-start(f32[2,97,128]{2,0,1:T(2,128)S(1)} %bitcast.105), channel_id=1, source_target_pairs={{0,4},{1,5},{2,6},{3,7},{4,0},{5,1},{6,2},{7,3},{8,12},{9,13},{10,... | collective-permute-start | bytes 297992 | tf_op jit(solution)/shard_map/ppermute | solution.py:64
  51.3 7.3 %collective-permute-start.5 = (f32[2,97,128]{2,0,1:T(2,128)S(1)}, f32[2,97,128]{2,0,1:T(2,128)S(1)}, u32[]{:S(2)}, u32[]{:S(2)}) collective-permute-start(f32[2,97,128]{2,0,1:T(2,128)S(1)} %bitcast.104), channel_id=1, source_target_pairs={{0,6},{1,7},{2,4},{3,5},{4,2},{5,3},{6,0},{7,1},{8,14},{9,15},{10,... | collective-permute-start | bytes 297992 | tf_op jit(solution)/shard_map/ppermute | solution.py:64
  58.8 5.4 %collective-permute-start.6 = (f32[1,97,128]{2,0,1:T(1,128)S(1)}, f32[1,97,128]{2,0,1:T(1,128)S(1)}, u32[]{:S(2)}, u32[]{:S(2)}) collective-permute-start(f32[1,97,128]{2,0,1:T(1,128)S(1)} %constant_dynamic-slice_fusion.1), channel_id=1, source_target_pairs={{0,8},{1,9},{2,10},{3,11},{4,12},{5,13},{6,14},{7,15},{8,0},{9,1},... | collective-permute-start | bytes 149000 | tf_op jit(solution)/shard_map/ppermute | solution.py:64
  64.2 4.2 %collective-permute-start.7 = (f32[97,128]{1,0:T(8,128)S(1)}, f32[97,128]{1,0:T(8,128)S(1)}, u32[]{:S(2)}, u32[]{:S(2)}) collective-permute-start(f32[97,128]{1,0:T(8,128)S(1)} %bitcast.108), channel_id=1, source_target_pairs={{0,16},{16,0},{1,17},{17,1},{2,18},{18,2},{3,19},{19,3},{4,20},{20... | collective-permute-start | bytes 149000 | tf_op jit(solution)/shard_map/ppermute | solution.py:69

commit v8 on v7

--- a/solution.py
+++ b/solution.py
@@ -45,14 +45,27 @@
     return total
 
 
-def tree_reduce(blocks, nseq, ndp):
+def tree_reduce(grad_t, loss_row, nseq, ndp):
     nbits = nseq.bit_length() - 1
-    assert 1 << nbits == nseq and ndp & (ndp - 1) == 0
-    groups = [1, 2] + [1] * (nbits - 3) if nbits >= 3 else [1] * nbits
-    x = blocks
+    assert nbits >= 1 and 1 << nbits == nseq and ndp & (ndp - 1) == 0
+    groups = [2] + [1] * (nbits - 3) if nbits >= 3 else [1] * (nbits - 1)
+    lat = grad_t.shape[0]
+    share = grad_t.shape[1] // nseq
+    lanes = loss_row.shape[0]
+    dense = lat * share // lanes
+    me = lax.axis_index("seq")
+    halves = grad_t.reshape(lat, nseq // 2, 2, share)
+    loss_rows = jnp.broadcast_to(loss_row[None, None, :], (nseq // 2, 1, lanes))
+
+    def half(bit):
+        part = lax.dynamic_index_in_dim(halves, bit, 2, keepdims=False)
+        part = part.transpose(1, 0, 2).reshape(nseq // 2, dense, lanes)
+        return jnp.concatenate([part, loss_rows], axis=1)
+
+    bit = me & 1
+    x = half(bit) + lax.ppermute(half(1 - bit), "seq", [(i, i ^ 1) for i in range(nseq)])
     tail = x.shape[1:]
-    me = lax.axis_index("seq")
-    low = 0
+    low = 1
     for width in groups:
         ways = 1 << width
         x = x.reshape((x.shape[0] // ways, ways) + tail)
@@ -165,10 +178,8 @@
     dense = LAT * share // lanes
     assert ndp * CLIPS <= lanes and dense * lanes == LAT * share
     place = lax.axis_index("dp") * CLIPS
-    blocks = grad_t.reshape(LAT, nseq, share).transpose(1, 0, 2).reshape(nseq, dense, lanes)
     loss_row = lax.dynamic_update_slice(jnp.zeros((lanes,), jnp.float32), partial_loss, (place,))
-    loss_rows = jnp.broadcast_to(loss_row[None, None, :], (nseq, 1, lanes))
-    summed = tree_reduce(jnp.concatenate([blocks, loss_rows], axis=1), nseq, ndp)
+    summed = tree_reduce(grad_t, loss_row, nseq, ndp)
     grad_mine = summed[:dense].reshape(LAT, share).T
     clip_loss = lax.dynamic_slice_in_dim(summed[dense], place, CLIPS).reshape(1, CLIPS)
     return (latent_out, clip_loss, grad_mine)

time: 70.2 us -> 67.7 us (0.964)
  local copies, waits for them, and re-layouts: 14.1 us -> 12.9 us
  matrix products: 11.3 us -> 10.3 us
    concatenate x1 -> x0, local copies, waits for them, and re-layouts: 1.76 us -> none  [per_device(): jnp.concatenate([blocks, loss_rows], axis=1)]
    ppermute x5 -> x4, waiting for transfers between devices: 11.3 us -> 9.64 us  [tree_reduce(): total = total + lax.ppermute(send, 'seq', pairs)]
    ppermute x0 -> x1, waiting for transfers between devices: none -> 1.45 us  [tree_reduce(): lax.ppermute(half(1 - bit), 'seq', [(i, i ^ 1) for i in range(nseq)])]
    dot_general x1, matrix products: 2.11 us -> 1.11 us  [per_device(): lax.dot_general(dpred, normed, (((0,), (0,)), ((), ())), preferred_elemen...]
    ppermute x5 -> x4, starting transfers between devices: 4.03 us -> 3.96 us  [tree_reduce(): total = total + lax.ppermute(send, 'seq', pairs)]
  transfers between devices with their start and end apart: 9 -> 9, of which waited for: 7 -> 7; matrix products, arithmetic and copies ran while one was open for 8% -> 9% of each run, Pallas kernels for 0% -> 0%
where the time goes in v8:
time: 67.7 us; the launch traced here: 67.3 us
  waiting for transfers between devices  19.7 us (29%)
  starting transfers between devices  18.6 us (27%)
  local copies, waits for them, and re-layouts  12.9 us (19%)
  matrix products  10.3 us (15%)
  other arithmetic  4.68 us (7%)
  between operations  1.1 us (2%)
    ppermute x4, waiting for transfers between devices, tree_reduce(): total = total + lax.ppermute(send, 'seq', pairs)  9.64 us
    all_to_all x1, starting transfers between devices, per_device(): lax.all_to_all(jnp.concatenate([outgoing, labels], axis=1), 'seq', split_...  8.63 us
    all_to_all x1, waiting for transfers between devices, per_device(): lax.all_to_all(jnp.concatenate([outgoing, labels], axis=1), 'seq', split_...  6.69 us
    conv_general_dilated x1, matrix products, causal_conv(): lax.conv_general_dilated(padded, kernel, (1, 1), 'VALID', dimension_numbe...  5.56 us
    unnamed x23, local copies, waits for them, and re-layouts  4.92 us
    ppermute x4, starting transfers between devices, tree_reduce(): total = total + lax.ppermute(send, 'seq', pairs)  3.96 us
    ppermute x1, starting transfers between devices, with_halo(): lax.ppermute(tail, axis, [(i, (i + 1) % count) for i in range(ends)])  3.06 us
    dot_general x1, local copies, waits for them, and re-layouts, per_device(): lax.dot_general(dpred, normed, (((0,), (0,)), ((), ())), preferred_elemen...  2.87 us
  transfers between devices with their start and end apart: 9, of which 7 were waited for; matrix products, arithmetic and copies ran while one was open for 9% of the time, Pallas kernels for 0%

profile of v8, /device:TPU:0, one launch (start us, length us, event | category | flops | bytes accessed | tf_op | source)
XLA Modules:
  0.0 67.3 jit_solution(17234809089735742085)
XLA Ops:
  0.6 0.0 copy-start
  0.7 1.7 %copy.49 = bf16[1,16,4,48,128]{4,1,3,2,0:T(8,128)(2,1)S(1)} copy(bf16[1,16,4,48,128]{4,3,2,1,0:T(8,128)(2,1)} %param.11) | data formatting | bytes 1572864 | tf_op args[0]
  2.4 0.0 copy-start.3
  2.4 0.0 copy-start.1
  2.4 0.8 %fusion.39 = (bf16[1,16,1,48,128]{4,1,3,2,0:T(8,128)(2,1)}, bf16[1,16,1,48,128]{4,1,3,2,0:T(8,128)(2,1)}) fusion(bf16[1,16,4,48,128]{4,1,3,2,0:T(8,128)(2,1)S(1)} %copy.49), kind=kLoop, calls=%fused_computation.94 | loop fusion | bytes 786432 | tf_op jit(solution)/shard_map/slice | solution.py:15
  3.2 3.1 %collective-permute-start = (bf16[1,16,1,48,128]{4,1,3,2,0:T(8,128)(2,1)}, bf16[1,16,1,48,128]{4,1,3,2,0:T(8,128)(2,1)}, u32[]{:S(2)}, u32[]{:S(2)}) collective-permute-start(bf16[1,16,1,48,128]{4,1,3,2,0:T(8,128)(2,1)} %get-tuple-element.7), channel_id=1, source_target_pairs={{0,1},{1,2},{2,3},{3,4},{4,5},{5,6},{6,7},{7,8},{8,9},{9,10},{10,1... | collective-permute-start | bytes 589832 | tf_op jit(solution)/shard_map/ppermute | solution.py:18
  6.2 1.3 %collective-permute-start.1 = (bf16[1,16,1,48,128]{4,1,3,2,0:T(8,128)(2,1)}, bf16[1,16,1,48,128]{4,1,3,2,0:T(8,128)(2,1)}, u32[]{:S(2)}, u32[]{:S(2)}) collective-permute-start(bf16[1,16,1,48,128]{4,1,3,2,0:T(8,128)(2,1)} %get-tuple-element.8), channel_id=1, source_target_pairs={{1,0},{2,1},{3,2},{4,3},{5,4},{6,5},{7,6},{8,7},{9,8},{10,9},{11,1... | collective-permute-start | bytes 589832 | tf_op jit(solution)/shard_map/ppermute | solution.py:20
  7.5 2.3 %copy.53 = bf16[3,3,3,128,128]{3,4,0,2,1:T(8,128)(2,1)} copy(bf16[3,3,3,128,128]{4,3,2,1,0:T(8,128)(2,1)} %param.16) | data formatting | bytes 1769472 | tf_op args[5]
  9.8 0.2 reduce-window.10
  10.0 0.1 convert_reduce_fusion.1
  10.1 0.1 select_reduce_fusion
  10.2 0.2 reshape.198
  10.4 0.6 reduce-window.11
  11.0 0.2 slice_reduce_fusion
  11.2 0.1 bitcast_bitcast_fusion
  11.3 0.1 broadcast_in_dim.6
  11.4 0.1 reshape.216
  11.5 0.2 convolution_reduce_fusion
  11.7 0.1 reshape.220
  11.8 0.3 convert_reduce_fusion
  12.2 0.6 fusion.3
  12.9 5.6 %fusion.7 = f32[16,4,48,384]{3,0,2,1:T(8,128)S(1)} fusion(bf16[3,3,128,384]{2,3,1,0:T(8,128)(2,1)} %bitcast.104, bf16[1,16,1,48,128]{4,1,3,2,0:T(8,128)(2,1)} %collective-permute-done.1, bf16[1,16,4,48,128]{4,1,3,2,0:T(8,128)(2,1)S(1)} %copy.49, bf16[1,16,1,48,128]{4,1,3,2,0:T(8,128)(2,1)} %collective-permute-done), kind=kOutput, calls=%fused_computation.12 | convolution fusion | flops 2683699200 | bytes 6782976 | tf_op jit(solution)/shard_map/conv_general_dilated | solution.py:32
  18.4 0.1 slice.51
  18.5 0.1 slice.52
  18.7 2.4 %convolution_convert_fusion.1 = bf16[16,1,12,64]{3,0,2,1:T(8,128)(2,1)S(1)} fusion(f32[16,4,48,384]{3,0,2,1:T(8,128)S(1)} %fusion.7, f32[14,4,48,128]{3,0,2,1:T(8,128)S(1)} %slice.52, f32[15,4,48,128]{3,0,2,1:T(8,128)S(1)} %slice.51, f32[16]{0:T(128)S(1)} %get-tuple-element.14, f32[16]{0:T(128)S(1)} %get-tuple-element.13, ...), kind=kOutput, calls=%fused_computation.19 | convolution fusion | flops 54669312 | bytes 5792768 | tf_op jit(solution)/shard_map/conv_general_dilated | solution.py:115
  21.2 0.2 convolution_convert_fusion
  21.4 0.1 copy.59
  21.6 0.7 %reshape.230 = bf16[16,2,608]{2,1,0:T(2,128)(2,1)} reshape(bf16[16,19,64]{2,1,0:T(8,128)(2,1)S(1)} %fusion.18) | data formatting | bytes 77824
  22.3 8.6 %all-to-all-start = ((bf16[16,2,608]{2,1,0:T(2,128)(2,1)}), bf16[16,2,608]{2,1,0:T(2,128)(2,1)S(1)}, u32[]{:S(2)}, u32[]{:S(2)}) async-start(bf16[16,2,608]{2,1,0:T(2,128)(2,1)} %reshape.230), calls=%async_computation | async-start | bytes 81920 | tf_op jit(solution)/shard_map/all_to_all | solution.py:145
  31.0 6.7 %all-to-all-done = bf16[16,2,608]{2,1,0:T(2,128)(2,1)S(1)} async-done(((bf16[16,2,608]{2,1,0:T(2,128)(2,1)}), bf16[16,2,608]{2,1,0:T(2,128)(2,1)S(1)}, u32[]{:S(2)}, u32[]{:S(2)}) %all-to-all-start) | async-done | bytes 38944 | tf_op jit(solution)/shard_map/all_to_all | solution.py:145
  37.7 0.1 reshape.231
  37.9 0.1 reshape.213
  38.0 0.1 copy.61
  38.1 0.1 fusion.28
  38.2 0.0 copy-start.7
  38.2 0.0 copy-start.8
  38.2 1.9 %fusion.37 = bf16[3072,288]{0,1:T(8,128)(2,1)} fusion(f32[288]{0:T(512)S(1)} %get-tuple-element.17, f32[288]{0:T(512)S(1)} %broadcast_multiply_fusion, bf16[1,288,3072]{2,1,0:T(8,128)(2,1)S(1)} %copy-done.1), kind=kLoop, calls=%fused_computation.93 | loop fusion | flops 3538944 | bytes 3541248 | tf_op jit(solution)/shard_map/dot_general | solution.py:172
  40.1 0.8 %multiply_reduce_fusion = (f32[288]{0:T(512)S(1)}, f32[288,64]{0,1:T(8,128)S(1)}) fusion(f32[288,64]{0,1:T(8,128)S(1)} %copy.61, f32[1,288,64]{1,2,0:T(8,128)S(1)} %copy-done.7, f32[288]{0:T(512)S(1)} %get-tuple-element.18, f32[1,288,64]{1,2,0:T(8,128)S(1)} %copy-done.8, f32[288]{0:T(512)S(1)} %fusion.28, bf16[3072,64]{0,1:T(8,128)(2,1)S(1)} %copy-done, ...), kind=kOutput, calls=%fused_computation.39 | convolution fusion | flops 116913888 | bytes 2463360 | tf_op jit(solution)/shard_map/dot_general | solution.py:166
  40.9 0.2 fusion.27
  41.1 2.9 %copy.65 = bf16[3072,288]{1,0:T(8,128)(2,1)S(1)} copy(bf16[3072,288]{0,1:T(8,128)(2,1)} %fusion.37) | data formatting | bytes 3538944 | tf_op jit(solution)/shard_map/dot_general | solution.py:172
  44.0 1.1 %fusion.22 = f32[64,8,2,192]{3,0,2,1:T(8,128)S(1)} fusion(bf16[8,2,192,288]{3,2,1,0:T(8,128)(2,1)S(1)} %bitcast.102, f32[288,64]{0,1:T(8,128)S(1)} %get-tuple-element.16, f32[288]{0:T(512)S(1)} %broadcast_multiply_fusion.1), kind=kOutput, calls=%fused_computation.44 | convolution fusion | flops 113283072 | bytes 2630784 | tf_op jit(solution)/shard_map/dot_general | solution.py:172
  45.1 0.1 dynamic-slice_bitcast_fusion.1
  45.2 0.3 reshape.207
  45.5 0.1 multiply_dynamic-update-slice_fusion
  45.6 0.1 collective-permute-start.2
  45.7 0.3 reshape.206
  46.0 1.4 %collective-permute-done.2 = f32[8,97,128]{2,1,0:T(8,128)S(1)} collective-permute-done((f32[8,97,128]{2,1,0:T(8,128)S(1)}, f32[8,97,128]{2,1,0:T(8,128)S(1)}, u32[]{:S(2)}, u32[]{:S(2)}) %collective-permute-start.2) | collective-permute-done | bytes 397344 | tf_op jit(solution)/shard_map/ppermute | solution.py:66
  47.5 0.1 copy.63
  47.6 0.3 constant_dynamic-slice_fusion.4
  47.9 0.4 collective-permute-start.3
  48.3 0.6 collective-permute-start.4
  48.9 2.6 %collective-permute-start.5 = (f32[2,97,128]{2,0,1:T(2,128)S(1)}, f32[2,97,128]{2,0,1:T(2,128)S(1)}, u32[]{:S(2)}, u32[]{:S(2)}) collective-permute-start(f32[2,97,128]{2,0,1:T(2,128)S(1)} %bitcast.106), channel_id=1, source_target_pairs={{0,6},{1,7},{2,4},{3,5},{4,2},{5,3},{6,0},{7,1},{8,14},{9,15},{10,... | collective-permute-start | bytes 297992 | tf_op jit(solution)/shard_map/ppermute | solution.py:77
  51.5 1.4 %collective-permute-done.3 = f32[2,97,128]{2,0,1:T(2,128)S(1)} collective-permute-done((f32[2,97,128]{2,0,1:T(2,128)S(1)}, f32[2,97,128]{2,0,1:T(2,128)S(1)}, u32[]{:S(2)}, u32[]{:S(2)}) %collective-permute-start.3) | collective-permute-done | bytes 99360 | tf_op jit(solution)/shard_map/ppermute | solution.py:77
  52.9 1.1 %collective-permute-done.4 = f32[2,97,128]{2,0,1:T(2,128)S(1)} collective-permute-done((f32[2,97,128]{2,0,1:T(2,128)S(1)}, f32[2,97,128]{2,0,1:T(2,128)S(1)}, u32[]{:S(2)}, u32[]{:S(2)}) %collective-permute-start.4) | collective-permute-done | bytes 99360 | tf_op jit(solution)/shard_map/ppermute | solution.py:77
  54.0 2.2 %collective-permute-done.5 = f32[2,97,128]{2,0,1:T(2,128)S(1)} collective-permute-done((f32[2,97,128]{2,0,1:T(2,128)S(1)}, f32[2,97,128]{2,0,1:T(2,128)S(1)}, u32[]{:S(2)}, u32[]{:S(2)}) %collective-permute-start.5) | collective-permute-done | bytes 99360 | tf_op jit(solution)/shard_map/ppermute | solution.py:77
  56.2 0.1 add_add_fusion
  56.3 0.4 collective-permute-start.6
  56.7 5.0 %collective-permute-done.6 = f32[1,97,128]{2,0,1:T(1,128)S(1)} collective-permute-done((f32[1,97,128]{2,0,1:T(1,128)S(1)}, f32[1,97,128]{2,0,1:T(1,128)S(1)}, u32[]{:S(2)}, u32[]{:S(2)}) %collective-permute-start.6) | collective-permute-done | bytes 49696 | tf_op jit(solution)/shard_map/ppermute | solution.py:77
  61.7 0.1 dynamic-slice_add_fusion
  61.8 1.6 %collective-permute-start.7 = (f32[97,128]{1,0:T(8,128)S(1)}, f32[97,128]{1,0:T(8,128)S(1)}, u32[]{:S(2)}, u32[]{:S(2)}) collective-permute-start(f32[97,128]{1,0:T(8,128)S(1)} %bitcast.110), channel_id=1, source_target_pairs={{0,16},{16,0},{1,17},{17,1},{2,18},{18,2},{3,19},{19,3},{4,20},{20... | collective-permute-start | bytes 149000 | tf_op jit(solution)/shard_map/ppermute | solution.py:82
  63.3 0.7 %reshape.199 = bf16[1,16,1,768]{3,1,2,0:T(8,128)(2,1)} reshape(bf16[16,1,12,64]{3,2,0,1:T(8,128)(2,1)S(1)} %copy.55) | data formatting | bytes 49152 | tf_op jit(solution)/shard_map/reshape | solution.py:123
  64.0 1.9 %collective-permute-done.7 = f32[97,128]{1,0:T(8,128)S(1)} collective-permute-done((f32[97,128]{1,0:T(8,128)S(1)}, f32[97,128]{1,0:T(8,128)S(1)}, u32[]{:S(2)}, u32[]{:S(2)}) %collective-permute-start.7) | collective-permute-done | bytes 49696 | tf_op jit(solution)/shard_map/ppermute | solution.py:82
  66.0 0.7 %reshape.210 = f32[64,192]{1,0:T(8,128)} reshape(f32[96,128]{1,0:T(8,128)S(1)} %slice.58) | data formatting | bytes 98304 | tf_op jit(solution)/shard_map/reshape | solution.py:183
  66.7 0.6 constant_dynamic-slice_fusion
  (46 shorter events, 0.5 us)
Async XLA Ops:
  0.6 39.5 %copy-start = (bf16[3072,64]{0,1:T(8,128)(2,1)S(1)}, bf16[3072,64]{0,1:T(8,128)(2,1)}, u32[]{:S(2)}) copy-start(bf16[3072,64]{0,1:T(8,128)(2,1)} %param.21) | copy-start | bytes 1179652
  0.6 9.2 %copy-start.4 = (s32[1,4]{1,0:T(1,128)S(1)}, s32[1,4]{1,0:T(1,128)}, u32[]{:S(2)}) copy-start(s32[1,4]{1,0:T(1,128)} %param.12) | copy-start | bytes 52
  0.7 9.5 %copy-start.2 = (bf16[2048,64]{0,1:T(8,128)(2,1)S(1)}, bf16[2048,64]{0,1:T(8,128)(2,1)}, u32[]{:S(2)}) copy-start(bf16[2048,64]{0,1:T(8,128)(2,1)} %param.17) | copy-start | bytes 786436
  2.4 8.0 %copy-start.3 = (s32[1,1,192,1]{2,3,1,0:T(1,128)S(1)}, s32[1,1,192,1]{2,3,1,0:T(1,128)}, u32[]{:S(2)}) copy-start(s32[1,1,192,1]{2,3,1,0:T(1,128)} %param.15) | copy-start | bytes 2308
  2.4 9.4 %copy-start.1 = (bf16[1,288,3072]{2,1,0:T(8,128)(2,1)S(1)}, bf16[1,288,3072]{2,1,0:T(8,128)(2,1)}, u32[]{:S(2)}) copy-start(bf16[1,288,3072]{2,1,0:T(8,128)(2,1)} %param.18) | copy-start | bytes 5308420
  3.2 9.7 %collective-permute-start = (bf16[1,16,1,48,128]{4,1,3,2,0:T(8,128)(2,1)}, bf16[1,16,1,48,128]{4,1,3,2,0:T(8,128)(2,1)}, u32[]{:S(2)}, u32[]{:S(2)}) collective-permute-start(bf16[1,16,1,48,128]{4,1,3,2,0:T(8,128)(2,1)} %get-tuple-element.7), channel_id=1, source_target_pairs={{0,1},{1,2},{2,3},{3,4},{4,5},{5,6},{6,7},{7,8},{8,9},{9,10},{10,1... | collective-permute-start | bytes 589832 | tf_op jit(solution)/shard_map/ppermute | solution.py:18
  6.2 6.6 %collective-permute-start.1 = (bf16[1,16,1,48,128]{4,1,3,2,0:T(8,128)(2,1)}, bf16[1,16,1,48,128]{4,1,3,2,0:T(8,128)(2,1)}, u32[]{:S(2)}, u32[]{:S(2)}) collective-permute-start(bf16[1,16,1,48,128]{4,1,3,2,0:T(8,128)(2,1)} %get-tuple-element.8), channel_id=1, source_target_pairs={{1,0},{2,1},{3,2},{4,3},{5,4},{6,5},{7,6},{8,7},{9,8},{10,9},{11,1... | collective-permute-start | bytes 589832 | tf_op jit(solution)/shard_map/ppermute | solution.py:20
  11.8 1.0 %copy-start.5 = (s32[1,4]{1,0:T(1,128)S(1)}, s32[1,4]{1,0:T(1,128)}, u32[]{:S(2)}) copy-start(s32[1,4]{1,0:T(1,128)} %param.14) | copy-start | bytes 52
  11.8 1.0 %copy-start.6 = (s32[1,4]{1,0:T(1,128)S(1)}, s32[1,4]{1,0:T(1,128)}, u32[]{:S(2)}) copy-start(s32[1,4]{1,0:T(1,128)} %param.13) | copy-start | bytes 52
  22.3 15.3 %all-to-all-start = ((bf16[16,2,608]{2,1,0:T(2,128)(2,1)}), bf16[16,2,608]{2,1,0:T(2,128)(2,1)S(1)}, u32[]{:S(2)}, u32[]{:S(2)}) async-start(bf16[16,2,608]{2,1,0:T(2,128)(2,1)} %reshape.230), calls=%async_computation | async-start | bytes 81920 | tf_op jit(solution)/shard_map/all_to_all | solution.py:145
  38.2 1.9 %copy-start.7 = (f32[1,288,64]{1,2,0:T(8,128)S(1)}, f32[1,288,64]{1,2,0:T(8,128)}, u32[]{:S(2)}) copy-start(f32[1,288,64]{1,2,0:T(8,128)} %param.19) | copy-start | bytes 221188
  38.2 1.9 %copy-start.8 = (f32[1,288,64]{1,2,0:T(8,128)S(1)}, f32[1,288,64]{1,2,0:T(8,128)}, u32[]{:S(2)}) copy-start(f32[1,288,64]{1,2,0:T(8,128)} %param.20) | copy-start | bytes 221188
  45.6 1.8 %collective-permute-start.2 = (f32[8,97,128]{2,1,0:T(8,128)S(1)}, f32[8,97,128]{2,1,0:T(8,128)S(1)}, u32[]{:S(2)}, u32[]{:S(2)}) collective-permute-start(f32[8,97,128]{2,1,0:T(8,128)S(1)} %pad_maximum_fusion), channel_id=1, source_target_pairs={{0,1},{1,0},{2,3},{3,2},{4,5},{5,4},{6,7},{7,6},{8,9},{9,8},{10,11... | collective-permute-start | bytes 1191944 | tf_op jit(solution)/shard_map/ppermute | solution.py:66
  47.9 4.9 %collective-permute-start.3 = (f32[2,97,128]{2,0,1:T(2,128)S(1)}, f32[2,97,128]{2,0,1:T(2,128)S(1)}, u32[]{:S(2)}, u32[]{:S(2)}) collective-permute-start(f32[2,97,128]{2,0,1:T(2,128)S(1)} %bitcast.108), channel_id=1, source_target_pairs={{0,2},{1,3},{2,0},{3,1},{4,6},{5,7},{6,4},{7,5},{8,10},{9,11},{10,... | collective-permute-start | bytes 297992 | tf_op jit(solution)/shard_map/ppermute | solution.py:77
  48.3 5.7 %collective-permute-start.4 = (f32[2,97,128]{2,0,1:T(2,128)S(1)}, f32[2,97,128]{2,0,1:T(2,128)S(1)}, u32[]{:S(2)}, u32[]{:S(2)}) collective-permute-start(f32[2,97,128]{2,0,1:T(2,128)S(1)} %bitcast.107), channel_id=1, source_target_pairs={{0,4},{1,5},{2,6},{3,7},{4,0},{5,1},{6,2},{7,3},{8,12},{9,13},{10,... | collective-permute-start | bytes 297992 | tf_op jit(solution)/shard_map/ppermute | solution.py:77
  48.9 7.3 %collective-permute-start.5 = (f32[2,97,128]{2,0,1:T(2,128)S(1)}, f32[2,97,128]{2,0,1:T(2,128)S(1)}, u32[]{:S(2)}, u32[]{:S(2)}) collective-permute-start(f32[2,97,128]{2,0,1:T(2,128)S(1)} %bitcast.106), channel_id=1, source_target_pairs={{0,6},{1,7},{2,4},{3,5},{4,2},{5,3},{6,0},{7,1},{8,14},{9,15},{10,... | collective-permute-start | bytes 297992 | tf_op jit(solution)/shard_map/ppermute | solution.py:77
  56.3 5.4 %collective-permute-start.6 = (f32[1,97,128]{2,0,1:T(1,128)S(1)}, f32[1,97,128]{2,0,1:T(1,128)S(1)}, u32[]{:S(2)}, u32[]{:S(2)}) collective-permute-start(f32[1,97,128]{2,0,1:T(1,128)S(1)} %constant_dynamic-slice_fusion.1), channel_id=1, source_target_pairs={{0,8},{1,9},{2,10},{3,11},{4,12},{5,13},{6,14},{7,15},{8,0},{9,1},... | collective-permute-start | bytes 149000 | tf_op jit(solution)/shard_map/ppermute | solution.py:77
  61.8 4.2 %collective-permute-start.7 = (f32[97,128]{1,0:T(8,128)S(1)}, f32[97,128]{1,0:T(8,128)S(1)}, u32[]{:S(2)}, u32[]{:S(2)}) collective-permute-start(f32[97,128]{1,0:T(8,128)S(1)} %bitcast.110), channel_id=1, source_target_pairs={{0,16},{16,0},{1,17},{17,1},{2,18},{18,2},{3,19},{19,3},{4,20},{20... | collective-permute-start | bytes 149000 | tf_op jit(solution)/shard_map/ppermute | solution.py:82

commit v9 on v8

--- a/solution.py
+++ b/solution.py
@@ -169,8 +169,10 @@
     err = jnp.sum(diff * diff, axis=1)
     partial_loss = coef * jnp.sum(slot_hot * err[:, None], axis=0)
     dpred = (2.0 * slot_coef[:, None] * diff).astype(jnp.bfloat16)
+    states_t = hidden[0].T.astype(jnp.float32)
+    normed_t = ((states_t - mean.T) * lax.rsqrt(var.T + 1e-06)).astype(jnp.bfloat16)
     grad_t = lax.dot_general(
-        dpred, normed, (((0,), (0,)), ((), ())), preferred_element_type=jnp.float32
+        dpred, normed_t, (((0,), (1,)), ((), ())), preferred_element_type=jnp.float32
     )
     ndp = lax.axis_size("dp")
     share = grad_t.shape[1] // nseq

time: 67.7 us -> 65.6 us (0.969)
  other arithmetic: 4.68 us -> 3.49 us
    dot_general x1 -> x0, local copies, waits for them, and re-layouts: 2.87 us -> none  [per_device(): lax.dot_general(dpred, normed, (((0,), (0,)), ((), ())), preferred_elemen...]
    dot_general x1 -> x0, other arithmetic: 1.88 us -> none  [per_device(): lax.dot_general(dpred, normed, (((0,), (0,)), ((), ())), preferred_elemen...]
    dynamic_slice x0 -> x3, local copies, waits for them, and re-layouts: none -> 1.42 us  [half(): part = lax.dynamic_index_in_dim(halves, bit, 2, keepdims=False)]
    reshape x0 -> x1, local copies, waits for them, and re-layouts: none -> 0.99 us  [tree_reduce(): halves = grad_t.reshape(lat, nseq // 2, 2, share)]
    convert_element_type x0 -> x1, other arithmetic: none -> 0.68 us  [per_device(): normed = (centred * lax.rsqrt(var + 1e-06)).astype(jnp.bfloat16)]
    unnamed x23 -> x25, local copies, waits for them, and re-layouts: 4.92 us -> 5.43 us
  transfers between devices with their start and end apart: 9 -> 9, of which waited for: 7 -> 7; matrix products, arithmetic and copies ran while one was open for 9% -> 11% of each run, Pallas kernels for 0% -> 0%
where the time goes in v9:
time: 65.6 us; the launch traced here: 65.3 us
  waiting for transfers between devices  19.5 us (30%)
  starting transfers between devices  18.6 us (28%)
  local copies, waits for them, and re-layouts  12.9 us (20%)
  matrix products  9.64 us (15%)
  other arithmetic  3.49 us (5%)
  between operations  1.14 us (2%)
    ppermute x4, waiting for transfers between devices, tree_reduce(): total = total + lax.ppermute(send, 'seq', pairs)  9.64 us
    all_to_all x1, starting transfers between devices, per_device(): lax.all_to_all(jnp.concatenate([outgoing, labels], axis=1), 'seq', split_...  8.64 us
    all_to_all x1, waiting for transfers between devices, per_device(): lax.all_to_all(jnp.concatenate([outgoing, labels], axis=1), 'seq', split_...  6.68 us
    conv_general_dilated x1, matrix products, causal_conv(): lax.conv_general_dilated(padded, kernel, (1, 1), 'VALID', dimension_numbe...  5.56 us
    unnamed x25, local copies, waits for them, and re-layouts  5.43 us
    ppermute x4, starting transfers between devices, tree_reduce(): total = total + lax.ppermute(send, 'seq', pairs)  3.96 us
    ppermute x1, starting transfers between devices, with_halo(): lax.ppermute(tail, axis, [(i, (i + 1) % count) for i in range(ends)])  3.06 us
    conv_general_dilated x1, matrix products, per_device(): lax.conv_general_dilated(cells, w_latent.reshape(4, 4, chans, LAT), (4, 4...  2.42 us
  transfers between devices with their start and end apart: 9, of which 7 were waited for; matrix products, arithmetic and copies ran while one was open for 11% of the time, Pallas kernels for 0%

profile of v9, /device:TPU:0, one launch (start us, length us, event | category | flops | bytes accessed | tf_op | source)
XLA Modules:
  0.0 65.3 jit_solution(8746114913175249255)
XLA Ops:
  0.6 0.0 copy-start
  0.7 1.7 %copy.51 = bf16[1,16,4,48,128]{4,1,3,2,0:T(8,128)(2,1)S(1)} copy(bf16[1,16,4,48,128]{4,3,2,1,0:T(8,128)(2,1)} %param.11) | data formatting | bytes 1572864 | tf_op args[0]
  2.4 0.0 copy-start.6
  2.4 0.8 %fusion.35 = (bf16[1,16,1,48,128]{4,1,3,2,0:T(8,128)(2,1)}, bf16[1,16,1,48,128]{4,1,3,2,0:T(8,128)(2,1)}) fusion(bf16[1,16,4,48,128]{4,1,3,2,0:T(8,128)(2,1)S(1)} %copy.51), kind=kLoop, calls=%fused_computation.94 | loop fusion | bytes 786432 | tf_op jit(solution)/shard_map/slice | solution.py:15
  3.2 3.1 %collective-permute-start = (bf16[1,16,1,48,128]{4,1,3,2,0:T(8,128)(2,1)}, bf16[1,16,1,48,128]{4,1,3,2,0:T(8,128)(2,1)}, u32[]{:S(2)}, u32[]{:S(2)}) collective-permute-start(bf16[1,16,1,48,128]{4,1,3,2,0:T(8,128)(2,1)} %get-tuple-element.7), channel_id=1, source_target_pairs={{0,1},{1,2},{2,3},{3,4},{4,5},{5,6},{6,7},{7,8},{8,9},{9,10},{10,1... | collective-permute-start | bytes 589832 | tf_op jit(solution)/shard_map/ppermute | solution.py:18
  6.2 1.3 %collective-permute-start.1 = (bf16[1,16,1,48,128]{4,1,3,2,0:T(8,128)(2,1)}, bf16[1,16,1,48,128]{4,1,3,2,0:T(8,128)(2,1)}, u32[]{:S(2)}, u32[]{:S(2)}) collective-permute-start(bf16[1,16,1,48,128]{4,1,3,2,0:T(8,128)(2,1)} %get-tuple-element.8), channel_id=1, source_target_pairs={{1,0},{2,1},{3,2},{4,3},{5,4},{6,5},{7,6},{8,7},{9,8},{10,9},{11,1... | collective-permute-start | bytes 589832 | tf_op jit(solution)/shard_map/ppermute | solution.py:20
  7.5 2.3 %copy.55 = bf16[3,3,3,128,128]{3,4,0,2,1:T(8,128)(2,1)} copy(bf16[3,3,3,128,128]{4,3,2,1,0:T(8,128)(2,1)} %param.16) | data formatting | bytes 1769472 | tf_op args[5]
  9.8 0.2 reduce-window.10
  10.0 0.1 convert_reduce_fusion.1
  10.1 0.1 select_reduce_fusion
  10.2 0.2 reshape.213
  10.4 0.6 reduce-window.11
  11.0 0.2 slice_reduce_fusion
  11.2 0.1 bitcast_bitcast_fusion
  11.3 0.1 broadcast_in_dim.6
  11.4 0.1 reshape.233
  11.5 0.2 convolution_reduce_fusion
  11.7 0.1 reshape.236
  11.8 0.3 convert_reduce_fusion
  12.2 0.6 fusion.3
  12.8 0.5 copy-done.2
  13.3 0.7 %fusion.4 = bf16[288,3072]{1,0:T(8,128)(2,1)S(1)} fusion(bf16[1,288,3072]{2,1,0:T(8,128)(2,1)S(1)} %copy-done.2, f32[288]{0:T(512)S(1)} %add_rsqrt_fusion, f32[288]{0:T(512)S(1)} %broadcast_multiply_fusion), kind=kLoop, calls=%fused_computation.6 | loop fusion | flops 3538944 | bytes 3541248 | tf_op jit(solution)/shard_map/convert_element_type | solution.py:165
  14.1 5.6 %fusion.7 = f32[16,4,48,384]{3,0,2,1:T(8,128)S(1)} fusion(bf16[3,3,128,384]{2,3,1,0:T(8,128)(2,1)} %bitcast.95, bf16[1,16,1,48,128]{4,1,3,2,0:T(8,128)(2,1)} %collective-permute-done.1, bf16[1,16,4,48,128]{4,1,3,2,0:T(8,128)(2,1)S(1)} %copy.51, bf16[1,16,1,48,128]{4,1,3,2,0:T(8,128)(2,1)} %collective-permute-done), kind=kOutput, calls=%fused_computation.12 | convolution fusion | flops 2683699200 | bytes 6782976 | tf_op jit(solution)/shard_map/conv_general_dilated | solution.py:32
  19.6 0.1 slice.51
  19.8 0.1 slice.52
  19.9 2.4 %convolution_convert_fusion.1 = bf16[16,1,12,64]{3,0,2,1:T(8,128)(2,1)S(1)} fusion(f32[16,4,48,384]{3,0,2,1:T(8,128)S(1)} %fusion.7, f32[14,4,48,128]{3,0,2,1:T(8,128)S(1)} %slice.52, f32[15,4,48,128]{3,0,2,1:T(8,128)S(1)} %slice.51, f32[16]{0:T(128)S(1)} %get-tuple-element.14, f32[16]{0:T(128)S(1)} %get-tuple-element.13, ...), kind=kOutput, calls=%fused_computation.19 | convolution fusion | flops 54669312 | bytes 5792768 | tf_op jit(solution)/shard_map/conv_general_dilated | solution.py:115
  22.4 0.2 convolution_convert_fusion
  22.6 0.1 copy.61
  22.8 0.7 %reshape.246 = bf16[16,2,608]{2,1,0:T(2,128)(2,1)} reshape(bf16[16,19,64]{2,1,0:T(8,128)(2,1)S(1)} %fusion.18) | data formatting | bytes 77824
  23.5 8.6 %all-to-all-start = ((bf16[16,2,608]{2,1,0:T(2,128)(2,1)}), bf16[16,2,608]{2,1,0:T(2,128)(2,1)S(1)}, u32[]{:S(2)}, u32[]{:S(2)}) async-start(bf16[16,2,608]{2,1,0:T(2,128)(2,1)} %reshape.246), calls=%async_computation | async-start | bytes 81920 | tf_op jit(solution)/shard_map/all_to_all | solution.py:145
  32.2 6.7 %all-to-all-done = bf16[16,2,608]{2,1,0:T(2,128)(2,1)S(1)} async-done(((bf16[16,2,608]{2,1,0:T(2,128)(2,1)}), bf16[16,2,608]{2,1,0:T(2,128)(2,1)S(1)}, u32[]{:S(2)}, u32[]{:S(2)}) %all-to-all-start) | async-done | bytes 38944 | tf_op jit(solution)/shard_map/all_to_all | solution.py:145
  38.9 0.1 reshape.247
  39.1 0.1 reshape.229
  39.2 0.1 fusion.26
  39.3 0.1 copy.63
  39.4 0.7 %multiply_reduce_fusion = (f32[288]{0:T(512)S(1)}, f32[288,64]{0,1:T(8,128)S(1)}) fusion(f32[288,64]{0,1:T(8,128)S(1)} %copy.63, f32[1,288,64]{1,2,0:T(8,128)S(1)} %copy-done.4, f32[288]{0:T(512)S(1)} %broadcast_subtract_fusion, f32[1,288,64]{1,2,0:T(8,128)S(1)} %copy-done.5, f32[288]{0:T(512)S(1)} %fusion.26, bf16[288,3072]{1,0:T(8,128)(2,1)S(1)} %fusion.4, ...), kind=kOutput, calls=%fused_computation.39 | convolution fusion | flops 113374944 | bytes 2461056 | tf_op jit(solution)/shard_map/dot_general | solution.py:166
  40.2 0.2 fusion.25
  40.4 0.5 fusion.21
  40.9 1.0 %reshape.221 = f32[64,8,2,192]{3,2,1,0:T(2,128)S(1)} reshape(f32[64,3072]{1,0:T(8,128)S(1)} %fusion.21) | data formatting | bytes 1572864 | tf_op jit(solution)/shard_map/reshape | solution.py:57
  41.9 1.1 %constant_dynamic-slice_fusion.7 = (f32[64,8,1,192]{3,2,1,0:T(1,128)S(1)}, f32[64,8,1,192]{3,2,1,0:T(1,128)S(1)}) fusion(f32[64,8,2,192]{3,2,1,0:T(2,128)S(1)} %reshape.221, s32[]{:T(128)S(6)} %select_n.31, s32[]{:T(128)S(6)} %select_n.33), kind=kLoop, calls=%fused_computation.69 | loop fusion | bytes 1572872 | tf_op jit(solution)/shard_map/jit(dynamic_index_in_dim)/dynamic_slice | solution.py:61
  43.0 0.2 copy.83
  43.1 0.3 reshape.223
  43.4 0.1 multiply_dynamic-update-slice_fusion
  43.6 0.1 collective-permute-start.2
  43.7 0.2 copy.84
  43.9 0.3 reshape.222
  44.2 1.3 %collective-permute-done.2 = f32[8,97,128]{2,1,0:T(8,128)S(1)} collective-permute-done((f32[8,97,128]{2,1,0:T(8,128)S(1)}, f32[8,97,128]{2,1,0:T(8,128)S(1)}, u32[]{:S(2)}, u32[]{:S(2)}) %collective-permute-start.2) | collective-permute-done | bytes 397344 | tf_op jit(solution)/shard_map/ppermute | solution.py:66
  45.5 0.1 copy.66
  45.6 0.3 constant_dynamic-slice_fusion.4
  45.9 0.4 collective-permute-start.3
  46.3 0.6 collective-permute-start.4
  46.9 2.6 %collective-permute-start.5 = (f32[2,97,128]{2,0,1:T(2,128)S(1)}, f32[2,97,128]{2,0,1:T(2,128)S(1)}, u32[]{:S(2)}, u32[]{:S(2)}) collective-permute-start(f32[2,97,128]{2,0,1:T(2,128)S(1)} %bitcast.97), channel_id=1, source_target_pairs={{0,6},{1,7},{2,4},{3,5},{4,2},{5,3},{6,0},{7,1},{8,14},{9,15},{10,... | collective-permute-start | bytes 297992 | tf_op jit(solution)/shard_map/ppermute | solution.py:77
  49.5 1.4 %collective-permute-done.3 = f32[2,97,128]{2,0,1:T(2,128)S(1)} collective-permute-done((f32[2,97,128]{2,0,1:T(2,128)S(1)}, f32[2,97,128]{2,0,1:T(2,128)S(1)}, u32[]{:S(2)}, u32[]{:S(2)}) %collective-permute-start.3) | collective-permute-done | bytes 99360 | tf_op jit(solution)/shard_map/ppermute | solution.py:77
  50.8 1.1 %collective-permute-done.4 = f32[2,97,128]{2,0,1:T(2,128)S(1)} collective-permute-done((f32[2,97,128]{2,0,1:T(2,128)S(1)}, f32[2,97,128]{2,0,1:T(2,128)S(1)}, u32[]{:S(2)}, u32[]{:S(2)}) %collective-permute-start.4) | collective-permute-done | bytes 99360 | tf_op jit(solution)/shard_map/ppermute | solution.py:77
  51.9 2.2 %collective-permute-done.5 = f32[2,97,128]{2,0,1:T(2,128)S(1)} collective-permute-done((f32[2,97,128]{2,0,1:T(2,128)S(1)}, f32[2,97,128]{2,0,1:T(2,128)S(1)}, u32[]{:S(2)}, u32[]{:S(2)}) %collective-permute-start.5) | collective-permute-done | bytes 99360 | tf_op jit(solution)/shard_map/ppermute | solution.py:77
  54.2 0.1 add_add_fusion
  54.3 0.4 collective-permute-start.6
  54.7 5.0 %collective-permute-done.6 = f32[1,97,128]{2,0,1:T(1,128)S(1)} collective-permute-done((f32[1,97,128]{2,0,1:T(1,128)S(1)}, f32[1,97,128]{2,0,1:T(1,128)S(1)}, u32[]{:S(2)}, u32[]{:S(2)}) %collective-permute-start.6) | collective-permute-done | bytes 49696 | tf_op jit(solution)/shard_map/ppermute | solution.py:77
  59.7 0.1 dynamic-slice_add_fusion
  59.8 1.6 %collective-permute-start.7 = (f32[97,128]{1,0:T(8,128)S(1)}, f32[97,128]{1,0:T(8,128)S(1)}, u32[]{:S(2)}, u32[]{:S(2)}) collective-permute-start(f32[97,128]{1,0:T(8,128)S(1)} %bitcast.101), channel_id=1, source_target_pairs={{0,16},{16,0},{1,17},{17,1},{2,18},{18,2},{3,19},{19,3},{4,20},{20... | collective-permute-start | bytes 149000 | tf_op jit(solution)/shard_map/ppermute | solution.py:82
  61.3 0.7 %reshape.214 = bf16[1,16,1,768]{3,1,2,0:T(8,128)(2,1)} reshape(bf16[16,1,12,64]{3,2,0,1:T(8,128)(2,1)S(1)} %copy.57) | data formatting | bytes 49152 | tf_op jit(solution)/shard_map/reshape | solution.py:123
  62.0 1.9 %collective-permute-done.7 = f32[97,128]{1,0:T(8,128)S(1)} collective-permute-done((f32[97,128]{1,0:T(8,128)S(1)}, f32[97,128]{1,0:T(8,128)S(1)}, u32[]{:S(2)}, u32[]{:S(2)}) %collective-permute-start.7) | collective-permute-done | bytes 49696 | tf_op jit(solution)/shard_map/ppermute | solution.py:82
  64.0 0.7 %reshape.226 = f32[64,192]{1,0:T(8,128)} reshape(f32[96,128]{1,0:T(8,128)S(1)} %slice.58) | data formatting | bytes 98304 | tf_op jit(solution)/shard_map/reshape | solution.py:185
  64.7 0.6 constant_dynamic-slice_fusion
  (51 shorter events, 0.5 us)
Async XLA Ops:
  0.6 38.8 %copy-start = (bf16[3072,64]{0,1:T(8,128)(2,1)S(1)}, bf16[3072,64]{0,1:T(8,128)(2,1)}, u32[]{:S(2)}) copy-start(bf16[3072,64]{0,1:T(8,128)(2,1)} %param.21) | copy-start | bytes 1179652
  0.6 9.2 %copy-start.7 = (s32[1,4]{1,0:T(1,128)S(1)}, s32[1,4]{1,0:T(1,128)}, u32[]{:S(2)}) copy-start(s32[1,4]{1,0:T(1,128)} %param.12) | copy-start | bytes 52
  0.7 9.5 %copy-start.3 = (bf16[2048,64]{0,1:T(8,128)(2,1)S(1)}, bf16[2048,64]{0,1:T(8,128)(2,1)}, u32[]{:S(2)}) copy-start(bf16[2048,64]{0,1:T(8,128)(2,1)} %param.17) | copy-start | bytes 786436
  2.4 8.0 %copy-start.6 = (s32[1,1,192,1]{2,3,1,0:T(1,128)S(1)}, s32[1,1,192,1]{2,3,1,0:T(1,128)}, u32[]{:S(2)}) copy-start(s32[1,1,192,1]{2,3,1,0:T(1,128)} %param.15) | copy-start | bytes 2308
  2.4 9.4 %copy-start.1 = (bf16[1,288,3072]{2,1,0:T(8,128)(2,1)S(1)}, bf16[1,288,3072]{2,1,0:T(8,128)(2,1)}, u32[]{:S(2)}) copy-start(bf16[1,288,3072]{2,1,0:T(8,128)(2,1)} %param.18) | copy-start | bytes 5308420
  3.2 10.9 %collective-permute-start = (bf16[1,16,1,48,128]{4,1,3,2,0:T(8,128)(2,1)}, bf16[1,16,1,48,128]{4,1,3,2,0:T(8,128)(2,1)}, u32[]{:S(2)}, u32[]{:S(2)}) collective-permute-start(bf16[1,16,1,48,128]{4,1,3,2,0:T(8,128)(2,1)} %get-tuple-element.7), channel_id=1, source_target_pairs={{0,1},{1,2},{2,3},{3,4},{4,5},{5,6},{6,7},{7,8},{8,9},{9,10},{10,1... | collective-permute-start | bytes 589832 | tf_op jit(solution)/shard_map/ppermute | solution.py:18
  6.2 7.8 %collective-permute-start.1 = (bf16[1,16,1,48,128]{4,1,3,2,0:T(8,128)(2,1)}, bf16[1,16,1,48,128]{4,1,3,2,0:T(8,128)(2,1)}, u32[]{:S(2)}, u32[]{:S(2)}) collective-permute-start(bf16[1,16,1,48,128]{4,1,3,2,0:T(8,128)(2,1)} %get-tuple-element.8), channel_id=1, source_target_pairs={{1,0},{2,1},{3,2},{4,3},{5,4},{6,5},{7,6},{8,7},{9,8},{10,9},{11,1... | collective-permute-start | bytes 589832 | tf_op jit(solution)/shard_map/ppermute | solution.py:20
  11.8 1.5 %copy-start.2 = (bf16[1,288,3072]{2,1,0:T(8,128)(2,1)S(1)}, bf16[1,288,3072]{2,1,0:T(8,128)(2,1)}, u32[]{:S(2)}) copy-start(bf16[1,288,3072]{2,1,0:T(8,128)(2,1)} %param.18) | copy-start | bytes 5308420
  13.3 0.7 %copy-start.8 = (s32[1,4]{1,0:T(1,128)S(1)}, s32[1,4]{1,0:T(1,128)}, u32[]{:S(2)}) copy-start(s32[1,4]{1,0:T(1,128)} %param.14) | copy-start | bytes 52
  13.3 0.7 %copy-start.9 = (s32[1,4]{1,0:T(1,128)S(1)}, s32[1,4]{1,0:T(1,128)}, u32[]{:S(2)}) copy-start(s32[1,4]{1,0:T(1,128)} %param.13) | copy-start | bytes 52
  22.3 17.1 %copy-start.4 = (f32[1,288,64]{1,2,0:T(8,128)S(1)}, f32[1,288,64]{1,2,0:T(8,128)}, u32[]{:S(2)}) copy-start(f32[1,288,64]{1,2,0:T(8,128)} %param.19) | copy-start | bytes 221188
  22.3 17.1 %copy-start.5 = (f32[1,288,64]{1,2,0:T(8,128)S(1)}, f32[1,288,64]{1,2,0:T(8,128)}, u32[]{:S(2)}) copy-start(f32[1,288,64]{1,2,0:T(8,128)} %param.20) | copy-start | bytes 221188
  23.5 15.3 %all-to-all-start = ((bf16[16,2,608]{2,1,0:T(2,128)(2,1)}), bf16[16,2,608]{2,1,0:T(2,128)(2,1)S(1)}, u32[]{:S(2)}, u32[]{:S(2)}) async-start(bf16[16,2,608]{2,1,0:T(2,128)(2,1)} %reshape.246), calls=%async_computation | async-start | bytes 81920 | tf_op jit(solution)/shard_map/all_to_all | solution.py:145
  43.6 1.8 %collective-permute-start.2 = (f32[8,97,128]{2,1,0:T(8,128)S(1)}, f32[8,97,128]{2,1,0:T(8,128)S(1)}, u32[]{:S(2)}, u32[]{:S(2)}) collective-permute-start(f32[8,97,128]{2,1,0:T(8,128)S(1)} %pad_maximum_fusion), channel_id=1, source_target_pairs={{0,1},{1,0},{2,3},{3,2},{4,5},{5,4},{6,7},{7,6},{8,9},{9,8},{10,11... | collective-permute-start | bytes 1191944 | tf_op jit(solution)/shard_map/ppermute | solution.py:66
  45.9 4.9 %collective-permute-start.3 = (f32[2,97,128]{2,0,1:T(2,128)S(1)}, f32[2,97,128]{2,0,1:T(2,128)S(1)}, u32[]{:S(2)}, u32[]{:S(2)}) collective-permute-start(f32[2,97,128]{2,0,1:T(2,128)S(1)} %bitcast.99), channel_id=1, source_target_pairs={{0,2},{1,3},{2,0},{3,1},{4,6},{5,7},{6,4},{7,5},{8,10},{9,11},{10,... | collective-permute-start | bytes 297992 | tf_op jit(solution)/shard_map/ppermute | solution.py:77
  46.3 5.7 %collective-permute-start.4 = (f32[2,97,128]{2,0,1:T(2,128)S(1)}, f32[2,97,128]{2,0,1:T(2,128)S(1)}, u32[]{:S(2)}, u32[]{:S(2)}) collective-permute-start(f32[2,97,128]{2,0,1:T(2,128)S(1)} %bitcast.98), channel_id=1, source_target_pairs={{0,4},{1,5},{2,6},{3,7},{4,0},{5,1},{6,2},{7,3},{8,12},{9,13},{10,... | collective-permute-start | bytes 297992 | tf_op jit(solution)/shard_map/ppermute | solution.py:77
  46.9 7.3 %collective-permute-start.5 = (f32[2,97,128]{2,0,1:T(2,128)S(1)}, f32[2,97,128]{2,0,1:T(2,128)S(1)}, u32[]{:S(2)}, u32[]{:S(2)}) collective-permute-start(f32[2,97,128]{2,0,1:T(2,128)S(1)} %bitcast.97), channel_id=1, source_target_pairs={{0,6},{1,7},{2,4},{3,5},{4,2},{5,3},{6,0},{7,1},{8,14},{9,15},{10,... | collective-permute-start | bytes 297992 | tf_op jit(solution)/shard_map/ppermute | solution.py:77
  54.3 5.4 %collective-permute-start.6 = (f32[1,97,128]{2,0,1:T(1,128)S(1)}, f32[1,97,128]{2,0,1:T(1,128)S(1)}, u32[]{:S(2)}, u32[]{:S(2)}) collective-permute-start(f32[1,97,128]{2,0,1:T(1,128)S(1)} %constant_dynamic-slice_fusion.1), channel_id=1, source_target_pairs={{0,8},{1,9},{2,10},{3,11},{4,12},{5,13},{6,14},{7,15},{8,0},{9,1},... | collective-permute-start | bytes 149000 | tf_op jit(solution)/shard_map/ppermute | solution.py:77
  59.8 4.2 %collective-permute-start.7 = (f32[97,128]{1,0:T(8,128)S(1)}, f32[97,128]{1,0:T(8,128)S(1)}, u32[]{:S(2)}, u32[]{:S(2)}) collective-permute-start(f32[97,128]{1,0:T(8,128)S(1)} %bitcast.101), channel_id=1, source_target_pairs={{0,16},{16,0},{1,17},{17,1},{2,18},{18,2},{3,19},{19,3},{4,20},{20... | collective-permute-start | bytes 149000 | tf_op jit(solution)/shard_map/ppermute | solution.py:82

commit v10 on v9

--- a/solution.py
+++ b/solution.py
@@ -97,8 +97,7 @@
     w_out,
 ):
     nseq = lax.axis_size("seq")
-    local = frames[0]
-    nframes, nrows, width, chans = local.shape
+    nframes, nrows, width, chans = frames.shape[1:]
     tok_rows = nrows // 4
     tok_cols = width // 4
     per_frame = nrows * nseq // 4 * tok_cols
@@ -109,9 +108,18 @@
     clip_hot = (clip_of[:, None] == jnp.arange(CLIPS, dtype=jnp.int32)[None, :]).astype(jnp.int32)
     starts = jnp.sum(clip_hot * (ends - counts)[None, :], axis=1)
     keep = jnp.stack([(index - lag >= starts).astype(jnp.float32) for lag in range(3)])
+    slots = hidden.shape[1]
+    capacity = slots // nseq
+    assert capacity <= LAT
+    owners = owner_map.reshape(-1)
+    owner_hot = (owners[:, None] == jnp.arange(nseq, dtype=jnp.int32)[None, :]).astype(jnp.int32)
+    rank = jnp.sum(jnp.cumsum(owner_hot, axis=0) * owner_hot, axis=1) - 1
+    dest = owners * capacity + rank
+    select = (dest[None, :] == jnp.arange(slots, dtype=jnp.int32)[:, None]).astype(jnp.bfloat16)
+    frames, select, keep, conv_weight = lax.optimization_barrier((frames, select, keep, conv_weight))
     rimmed = with_halo(frames, (("seq", 2),), 1)[0]
     conv = causal_conv(rimmed, conv_weight, keep)
-    cells = (local.astype(jnp.float32) + jax.nn.silu(conv)).astype(jnp.bfloat16)
+    cells = (frames[0].astype(jnp.float32) + jax.nn.silu(conv)).astype(jnp.bfloat16)
     tokens = lax.conv_general_dilated(
         cells,
         w_latent.reshape(4, 4, chans, LAT),
@@ -122,14 +130,6 @@
     ).astype(jnp.bfloat16)
     latent_out = tokens.reshape(1, nframes, tok_rows, tok_cols * LAT)
     tokens = tokens.reshape(-1, LAT)
-    slots = hidden.shape[1]
-    capacity = slots // nseq
-    assert capacity <= LAT
-    owners = owner_map.reshape(-1)
-    owner_hot = (owners[:, None] == jnp.arange(nseq, dtype=jnp.int32)[None, :]).astype(jnp.int32)
-    rank = jnp.sum(jnp.cumsum(owner_hot, axis=0) * owner_hot, axis=1) - 1
-    dest = owners * capacity + rank
-    select = (dest[None, :] == jnp.arange(slots, dtype=jnp.int32)[:, None]).astype(jnp.bfloat16)
     tok_clip = jnp.repeat(clip_of, tok_rows * tok_cols).astype(jnp.float32) + 1.0
     outgoing = (
         jnp.dot(select, tokens, preferred_element_type=jnp.float32)

time: 65.6 us -> 73.7 us (1.12)
  other arithmetic: 3.49 us -> 8.08 us
  local copies, waits for them, and re-layouts: 12.9 us -> 16.3 us
    optimization_barrier x0 -> x2, local copies, waits for them, and re-layouts: none -> 3.95 us  [per_device(): lax.optimization_barrier((frames, select, keep, conv_weight))]
    unnamed x25 -> x31, local copies, waits for them, and re-layouts: 5.43 us -> 2.26 us
    another operation x5 -> x6, other arithmetic: 0.88 us -> 2.17 us
    mul x0 -> x1, local copies, waits for them, and re-layouts: none -> 1.27 us  [causal_conv(): total = total + part * keep[lag][:, None, None, None]]
  transfers between devices with their start and end apart: 9 -> 9, of which waited for: 7 -> 7; matrix products, arithmetic and copies ran while one was open for 11% -> 12% of each run, Pallas kernels for 0% -> 0%
where the time goes in v10:
time: 73.7 us; the launch traced here: 73.2 us
  waiting for transfers between devices  19.5 us (26%)
  starting transfers between devices  18.6 us (25%)
  local copies, waits for them, and re-layouts  16.3 us (22%)
  matrix products  9.64 us (13%)
  other arithmetic  8.08 us (11%)
  between operations  1.13 us (2%)
    ppermute x4, waiting for transfers between devices, tree_reduce(): total = total + lax.ppermute(send, 'seq', pairs)  9.64 us
    all_to_all x1, starting transfers between devices, per_device(): lax.all_to_all(jnp.concatenate([outgoing, labels], axis=1), 'seq', split_...  8.63 us
    all_to_all x1, waiting for transfers between devices, per_device(): lax.all_to_all(jnp.concatenate([outgoing, labels], axis=1), 'seq', split_...  6.68 us
    conv_general_dilated x1, matrix products, causal_conv(): lax.conv_general_dilated(padded, kernel, (1, 1), 'VALID', dimension_numbe...  5.56 us
    ppermute x4, starting transfers between devices, tree_reduce(): total = total + lax.ppermute(send, 'seq', pairs)  3.96 us
    optimization_barrier x2, local copies, waits for them, and re-layouts, per_device(): lax.optimization_barrier((frames, select, keep, conv_weight))  3.95 us
    ppermute x1, starting transfers between devices, with_halo(): lax.ppermute(tail, axis, [(i, (i + 1) % count) for i in range(ends)])  3.06 us
    conv_general_dilated x1, matrix products, per_device(): lax.conv_general_dilated(cells, w_latent.reshape(4, 4, chans, LAT), (4, 4...  2.42 us
  transfers between devices with their start and end apart: 9, of which 7 were waited for; matrix products, arithmetic and copies ran while one was open for 12% of the time, Pallas kernels for 0%

profile of v10, /device:TPU:0, one launch (start us, length us, event | category | flops | bytes accessed | tf_op | source)
XLA Modules:
  0.0 73.2 jit_solution(4435537187992354918)
XLA Ops:
  0.6 0.9 %reduce-window.14 = s32[4,1]{0,1:T(1,128)S(1)} reduce-window(s32[4,1]{0,1:T(1,128)} %bitcast.115, s32[]{:T(128)} %constant.80.clone.1), window={size=4x1 pad=3_0x0_0}, to_apply=%region_3.4 | reduce-window | flops 12 | bytes 36 | tf_op jit(solution)/shard_map/reduce-window.2
  1.5 0.7 fusion.27
  2.4 0.7 iota_compare_fusion.2
  3.1 0.6 reduce-window.10
  3.6 0.2 slice_reduce_fusion
  4.0 0.7 fusion.22
  4.7 0.7 add_add_fusion.1
  5.4 0.6 add_convert_fusion
  6.0 1.7 %copy.53 = bf16[1,16,4,48,128]{4,1,3,2,0:T(8,128)(2,1)S(1)} copy(bf16[1,16,4,48,128]{4,3,2,1,0:T(8,128)(2,1)} %param.11) | data formatting | bytes 1572864 | tf_op jit(solution)/shard_map/optimization_barrier | solution.py:119
  7.7 0.7 fusion.34
  8.4 3.1 %collective-permute-start = (bf16[1,16,1,48,128]{4,1,3,2,0:T(8,128)(2,1)}, bf16[1,16,1,48,128]{4,1,3,2,0:T(8,128)(2,1)}, u32[]{:S(2)}, u32[]{:S(2)}) collective-permute-start(bf16[1,16,1,48,128]{4,1,3,2,0:T(8,128)(2,1)} %get-tuple-element.15), channel_id=1, source_target_pairs={{0,1},{1,2},{2,3},{3,4},{4,5},{5,6},{6,7},{7,8},{8,9},{9,10},{10,1... | collective-permute-start | bytes 589832 | tf_op jit(solution)/shard_map/ppermute | solution.py:18
  11.4 1.3 %collective-permute-start.1 = (bf16[1,16,1,48,128]{4,1,3,2,0:T(8,128)(2,1)S(1)}, bf16[1,16,1,48,128]{4,1,3,2,0:T(8,128)(2,1)}, u32[]{:S(2)}, u32[]{:S(2)}) collective-permute-start(bf16[1,16,1,48,128]{4,1,3,2,0:T(8,128)(2,1)S(1)} %get-tuple-element.16), channel_id=1, source_target_pairs={{1,0},{2,1},{3,2},{4,3},{5,4},{6,5},{7,6},{8,7},{9,8},{10,9},{11,1... | collective-permute-start | bytes 589832 | tf_op jit(solution)/shard_map/ppermute | solution.py:20
  12.7 0.6 add_convert_fusion.1
  13.3 2.3 %copy.57 = bf16[3,3,3,128,128]{3,4,0,2,1:T(8,128)(2,1)} copy(bf16[3,3,3,128,128]{4,3,2,1,0:T(8,128)(2,1)} %param.16) | data formatting | bytes 1769472 | tf_op jit(solution)/shard_map/optimization_barrier | solution.py:119
  15.6 1.3 %slice_bitcast_fusion.1 = (f32[16]{0:T(128)}, f32[16]{0:T(128)}) fusion(f32[3,16]{1,0:T(4,128)} %add_convert_fusion), kind=kLoop, calls=%fused_computation.90 | loop fusion | bytes 256 | tf_op jit(solution)/shard_map/mul | solution.py:44
  16.9 0.9 %reshape.250 = bf16[4,4,128,64]{2,1,0,3:T(4,128)(2,1)} reshape(bf16[2048,64]{0,1:T(8,128)(2,1)S(1)} %copy-done.3) | data formatting | bytes 524288 | tf_op jit(solution)/shard_map/reshape | solution.py:125
  17.7 0.7 %broadcast_in_dim.6 = bf16[16,12]{1,0:T(8,128)(2,1)S(1)} broadcast(bf16[16]{0:T(256)(128)(2,1)} %add_convert_fusion.1), dimensions={0} | broadcast | bytes 416 | tf_op jit(solution)/shard_map/broadcast_in_dim | solution.py:133
  18.5 0.1 reshape.267
  18.6 0.2 convolution_reduce_fusion
  18.8 0.1 reshape.270
  18.9 0.3 convert_reduce_fusion
  19.2 0.6 fusion.3
  19.9 0.5 copy-done.2
  20.4 0.7 fusion.4
  21.1 5.6 %fusion.7 = f32[16,4,48,384]{3,0,2,1:T(8,128)S(1)} fusion(bf16[3,3,128,384]{2,3,1,0:T(8,128)(2,1)} %bitcast.105, bf16[1,16,1,48,128]{4,1,3,2,0:T(8,128)(2,1)} %collective-permute-done.1, bf16[1,16,4,48,128]{4,1,3,2,0:T(8,128)(2,1)S(1)} %copy.53, bf16[1,16,1,48,128]{4,1,3,2,0:T(8,128)(2,1)} %collective-permute-done), kind=kOutput, calls=%fused_computation.12 | convolution fusion | flops 2683699200 | bytes 6782976 | tf_op jit(solution)/shard_map/conv_general_dilated | solution.py:32
  26.7 0.1 slice.61
  26.9 0.1 slice.62
  27.0 0.8 %copy-done.4 = bf16[4,4,128,64]{2,1,0,3:T(4,128)(2,1)S(1)} copy-done((bf16[4,4,128,64]{2,1,0,3:T(4,128)(2,1)S(1)}, bf16[4,4,128,64]{2,1,0,3:T(4,128)(2,1)}, u32[]{:S(2)}) %copy-start.4) | copy-done | bytes 262168
  27.8 2.4 %convolution_convert_fusion.1 = bf16[16,1,12,64]{3,0,2,1:T(8,128)(2,1)S(1)} fusion(f32[16,4,48,384]{3,0,2,1:T(8,128)S(1)} %fusion.7, f32[14,4,48,128]{3,0,2,1:T(8,128)S(1)} %slice.62, f32[15,4,48,128]{3,0,2,1:T(8,128)S(1)} %slice.61, f32[16]{0:T(128)S(1)} %copy-done.11, f32[16]{0:T(128)S(1)} %copy-done.10, bf16[4,4,128,64]{2,1,0,3:T(4,128)(2,1)S(1)} %copy-done.4, ...), kind=kOutput, calls=%fused_computation.19 | convolution fusion | flops 54669312 | bytes 5792768 | tf_op jit(solution)/shard_map/conv_general_dilated | solution.py:123
  30.3 0.2 convolution_convert_fusion
  30.5 0.1 copy.61
  30.7 0.7 %reshape.280 = bf16[16,2,608]{2,1,0:T(2,128)(2,1)} reshape(bf16[16,19,64]{2,1,0:T(8,128)(2,1)S(1)} %fusion.17) | data formatting | bytes 77824
  31.5 8.6 %all-to-all-start = ((bf16[16,2,608]{2,1,0:T(2,128)(2,1)}), bf16[16,2,608]{2,1,0:T(2,128)(2,1)S(1)}, u32[]{:S(2)}, u32[]{:S(2)}) async-start(bf16[16,2,608]{2,1,0:T(2,128)(2,1)} %reshape.280), calls=%async_computation | async-start | bytes 81920 | tf_op jit(solution)/shard_map/all_to_all | solution.py:145
  40.1 6.7 %all-to-all-done = bf16[16,2,608]{2,1,0:T(2,128)(2,1)S(1)} async-done(((bf16[16,2,608]{2,1,0:T(2,128)(2,1)}), bf16[16,2,608]{2,1,0:T(2,128)(2,1)S(1)}, u32[]{:S(2)}, u32[]{:S(2)}) %all-to-all-start) | async-done | bytes 38944 | tf_op jit(solution)/shard_map/all_to_all | solution.py:145
  46.8 0.1 reshape.281
  47.0 0.1 copy.63
  47.1 0.1 reshape.263
  47.2 0.1 fusion.25
  47.3 0.7 %multiply_reduce_fusion = (f32[288]{0:T(512)S(1)}, f32[288,64]{0,1:T(8,128)S(1)}) fusion(f32[288,64]{0,1:T(8,128)S(1)} %copy.63, f32[1,288,64]{1,2,0:T(8,128)S(1)} %copy-done.5, f32[288]{0:T(512)S(1)} %broadcast_subtract_fusion, f32[1,288,64]{1,2,0:T(8,128)S(1)} %copy-done.6, f32[288]{0:T(512)S(1)} %fusion.25, bf16[288,3072]{1,0:T(8,128)(2,1)S(1)} %fusion.4, ...), kind=kOutput, calls=%fused_computation.38 | convolution fusion | flops 113374944 | bytes 2461056 | tf_op jit(solution)/shard_map/dot_general | solution.py:166
  48.1 0.2 fusion.24
  48.3 0.5 fusion.20
  48.8 1.0 %reshape.255 = f32[64,8,2,192]{3,2,1,0:T(2,128)S(1)} reshape(f32[64,3072]{1,0:T(8,128)S(1)} %fusion.20) | data formatting | bytes 1572864 | tf_op jit(solution)/shard_map/reshape | solution.py:57
  49.8 1.1 %constant_dynamic-slice_fusion.7 = (f32[64,8,1,192]{3,2,1,0:T(1,128)S(1)}, f32[64,8,1,192]{3,2,1,0:T(1,128)S(1)}) fusion(f32[64,8,2,192]{3,2,1,0:T(2,128)S(1)} %reshape.255, s32[]{:T(128)S(6)} %select_n.31, s32[]{:T(128)S(6)} %select_n.33), kind=kLoop, calls=%fused_computation.68 | loop fusion | bytes 1572872 | tf_op jit(solution)/shard_map/jit(dynamic_index_in_dim)/dynamic_slice | solution.py:61
  50.9 0.2 copy.83
  51.1 0.3 reshape.257
  51.4 0.1 multiply_dynamic-update-slice_fusion
  51.6 0.2 copy.84
  51.8 0.3 reshape.256
  52.1 1.3 %collective-permute-done.2 = f32[8,97,128]{2,1,0:T(8,128)S(1)} collective-permute-done((f32[8,97,128]{2,1,0:T(8,128)S(1)}, f32[8,97,128]{2,1,0:T(8,128)S(1)}, u32[]{:S(2)}, u32[]{:S(2)}) %collective-permute-start.2) | collective-permute-done | bytes 397344 | tf_op jit(solution)/shard_map/ppermute | solution.py:66
  53.5 0.3 constant_dynamic-slice_fusion.4
  53.8 0.4 collective-permute-start.3
  54.2 0.6 collective-permute-start.4
  54.8 2.6 %collective-permute-start.5 = (f32[2,97,128]{2,0,1:T(2,128)S(1)}, f32[2,97,128]{2,0,1:T(2,128)S(1)}, u32[]{:S(2)}, u32[]{:S(2)}) collective-permute-start(f32[2,97,128]{2,0,1:T(2,128)S(1)} %bitcast.107), channel_id=1, source_target_pairs={{0,6},{1,7},{2,4},{3,5},{4,2},{5,3},{6,0},{7,1},{8,14},{9,15},{10,... | collective-permute-start | bytes 297992 | tf_op jit(solution)/shard_map/ppermute | solution.py:77
  57.4 1.4 %collective-permute-done.3 = f32[2,97,128]{2,0,1:T(2,128)S(1)} collective-permute-done((f32[2,97,128]{2,0,1:T(2,128)S(1)}, f32[2,97,128]{2,0,1:T(2,128)S(1)}, u32[]{:S(2)}, u32[]{:S(2)}) %collective-permute-start.3) | collective-permute-done | bytes 99360 | tf_op jit(solution)/shard_map/ppermute | solution.py:77
  58.8 1.1 %collective-permute-done.4 = f32[2,97,128]{2,0,1:T(2,128)S(1)} collective-permute-done((f32[2,97,128]{2,0,1:T(2,128)S(1)}, f32[2,97,128]{2,0,1:T(2,128)S(1)}, u32[]{:S(2)}, u32[]{:S(2)}) %collective-permute-start.4) | collective-permute-done | bytes 99360 | tf_op jit(solution)/shard_map/ppermute | solution.py:77
  59.9 2.2 %collective-permute-done.5 = f32[2,97,128]{2,0,1:T(2,128)S(1)} collective-permute-done((f32[2,97,128]{2,0,1:T(2,128)S(1)}, f32[2,97,128]{2,0,1:T(2,128)S(1)}, u32[]{:S(2)}, u32[]{:S(2)}) %collective-permute-start.5) | collective-permute-done | bytes 99360 | tf_op jit(solution)/shard_map/ppermute | solution.py:77
  62.1 0.1 add_add_fusion
  62.2 0.4 collective-permute-start.6
  62.6 5.0 %collective-permute-done.6 = f32[1,97,128]{2,0,1:T(1,128)S(1)} collective-permute-done((f32[1,97,128]{2,0,1:T(1,128)S(1)}, f32[1,97,128]{2,0,1:T(1,128)S(1)}, u32[]{:S(2)}, u32[]{:S(2)}) %collective-permute-start.6) | collective-permute-done | bytes 49696 | tf_op jit(solution)/shard_map/ppermute | solution.py:77
  67.7 1.6 %collective-permute-start.7 = (f32[97,128]{1,0:T(8,128)S(1)}, f32[97,128]{1,0:T(8,128)S(1)}, u32[]{:S(2)}, u32[]{:S(2)}) collective-permute-start(f32[97,128]{1,0:T(8,128)S(1)} %bitcast.111), channel_id=1, source_target_pairs={{0,16},{16,0},{1,17},{17,1},{2,18},{18,2},{3,19},{19,3},{4,20},{20... | collective-permute-start | bytes 149000 | tf_op jit(solution)/shard_map/ppermute | solution.py:82
  69.2 0.7 reshape.251
  69.9 1.9 %collective-permute-done.7 = f32[97,128]{1,0:T(8,128)S(1)} collective-permute-done((f32[97,128]{1,0:T(8,128)S(1)}, f32[97,128]{1,0:T(8,128)S(1)}, u32[]{:S(2)}, u32[]{:S(2)}) %collective-permute-start.7) | collective-permute-done | bytes 49696 | tf_op jit(solution)/shard_map/ppermute | solution.py:82
  71.9 0.7 reshape.260
  72.6 0.6 constant_dynamic-slice_fusion
  (62 shorter events, 1.0 us)
Async XLA Ops:
  0.6 46.7 %copy-start = (bf16[3072,64]{0,1:T(8,128)(2,1)S(1)}, bf16[3072,64]{0,1:T(8,128)(2,1)}, u32[]{:S(2)}) copy-start(bf16[3072,64]{0,1:T(8,128)(2,1)} %param.21) | copy-start | bytes 1179652
  2.3 0.8 %copy-start.12 = (s32[16]{0:T(128)}, s32[16]{0:T(128)S(1)}, u32[]{:S(2)}) copy-start(s32[16]{0:T(128)S(1)} %convert_reduce_fusion.1) | copy-start | bytes 196
  3.9 8.9 %copy-start.13 = (s32[16]{0:T(128)S(1)}, s32[16]{0:T(128)}, u32[]{:S(2)}) copy-start(s32[16]{0:T(128)} %copy-done.12) | copy-start | bytes 196
  6.0 10.9 %copy-start.3 = (bf16[2048,64]{0,1:T(8,128)(2,1)S(1)}, bf16[2048,64]{0,1:T(8,128)(2,1)}, u32[]{:S(2)}) copy-start(bf16[2048,64]{0,1:T(8,128)(2,1)} %param.17) | copy-start | bytes 786436
  7.7 11.2 %copy-start.1 = (bf16[1,288,3072]{2,1,0:T(8,128)(2,1)S(1)}, bf16[1,288,3072]{2,1,0:T(8,128)(2,1)}, u32[]{:S(2)}) copy-start(bf16[1,288,3072]{2,1,0:T(8,128)(2,1)} %param.18) | copy-start | bytes 5308420
  8.4 12.7 %collective-permute-start = (bf16[1,16,1,48,128]{4,1,3,2,0:T(8,128)(2,1)}, bf16[1,16,1,48,128]{4,1,3,2,0:T(8,128)(2,1)}, u32[]{:S(2)}, u32[]{:S(2)}) collective-permute-start(bf16[1,16,1,48,128]{4,1,3,2,0:T(8,128)(2,1)} %get-tuple-element.15), channel_id=1, source_target_pairs={{0,1},{1,2},{2,3},{3,4},{4,5},{5,6},{6,7},{7,8},{8,9},{9,10},{10,1... | collective-permute-start | bytes 589832 | tf_op jit(solution)/shard_map/ppermute | solution.py:18
  11.4 9.7 %collective-permute-start.1 = (bf16[1,16,1,48,128]{4,1,3,2,0:T(8,128)(2,1)S(1)}, bf16[1,16,1,48,128]{4,1,3,2,0:T(8,128)(2,1)}, u32[]{:S(2)}, u32[]{:S(2)}) collective-permute-start(bf16[1,16,1,48,128]{4,1,3,2,0:T(8,128)(2,1)S(1)} %get-tuple-element.16), channel_id=1, source_target_pairs={{1,0},{2,1},{3,2},{4,3},{5,4},{6,5},{7,6},{8,7},{9,8},{10,9},{11,1... | collective-permute-start | bytes 589832 | tf_op jit(solution)/shard_map/ppermute | solution.py:20
  18.9 1.5 %copy-start.2 = (bf16[1,288,3072]{2,1,0:T(8,128)(2,1)S(1)}, bf16[1,288,3072]{2,1,0:T(8,128)(2,1)}, u32[]{:S(2)}) copy-start(bf16[1,288,3072]{2,1,0:T(8,128)(2,1)} %param.18) | copy-start | bytes 5308420
  20.4 0.7 copy-start.7
  20.4 0.7 copy-start.8
  20.4 0.7 copy-start.9
  26.8 1.0 %copy-start.4 = (bf16[4,4,128,64]{2,1,0,3:T(4,128)(2,1)S(1)}, bf16[4,4,128,64]{2,1,0,3:T(4,128)(2,1)}, u32[]{:S(2)}) copy-start(bf16[4,4,128,64]{2,1,0,3:T(4,128)(2,1)} %reshape.250) | copy-start | bytes 786436
  26.8 0.9 %copy-start.10 = (f32[16]{0:T(128)S(1)}, f32[16]{0:T(128)}, u32[]{:S(2)}) copy-start(f32[16]{0:T(128)} %get-tuple-element.21) | copy-start | bytes 196
  26.8 0.9 %copy-start.11 = (f32[16]{0:T(128)S(1)}, f32[16]{0:T(128)}, u32[]{:S(2)}) copy-start(f32[16]{0:T(128)} %get-tuple-element.22) | copy-start | bytes 196
  30.2 17.1 %copy-start.5 = (f32[1,288,64]{1,2,0:T(8,128)S(1)}, f32[1,288,64]{1,2,0:T(8,128)}, u32[]{:S(2)}) copy-start(f32[1,288,64]{1,2,0:T(8,128)} %param.19) | copy-start | bytes 221188
  30.2 17.1 %copy-start.6 = (f32[1,288,64]{1,2,0:T(8,128)S(1)}, f32[1,288,64]{1,2,0:T(8,128)}, u32[]{:S(2)}) copy-start(f32[1,288,64]{1,2,0:T(8,128)} %param.20) | copy-start | bytes 221188
  31.5 15.3 %all-to-all-start = ((bf16[16,2,608]{2,1,0:T(2,128)(2,1)}), bf16[16,2,608]{2,1,0:T(2,128)(2,1)S(1)}, u32[]{:S(2)}, u32[]{:S(2)}) async-start(bf16[16,2,608]{2,1,0:T(2,128)(2,1)} %reshape.280), calls=%async_computation | async-start | bytes 81920 | tf_op jit(solution)/shard_map/all_to_all | solution.py:145
  51.5 1.8 %collective-permute-start.2 = (f32[8,97,128]{2,1,0:T(8,128)S(1)}, f32[8,97,128]{2,1,0:T(8,128)S(1)}, u32[]{:S(2)}, u32[]{:S(2)}) collective-permute-start(f32[8,97,128]{2,1,0:T(8,128)S(1)} %pad_maximum_fusion), channel_id=1, source_target_pairs={{0,1},{1,0},{2,3},{3,2},{4,5},{5,4},{6,7},{7,6},{8,9},{9,8},{10,11... | collective-permute-start | bytes 1191944 | tf_op jit(solution)/shard_map/ppermute | solution.py:66
  53.8 4.9 %collective-permute-start.3 = (f32[2,97,128]{2,0,1:T(2,128)S(1)}, f32[2,97,128]{2,0,1:T(2,128)S(1)}, u32[]{:S(2)}, u32[]{:S(2)}) collective-permute-start(f32[2,97,128]{2,0,1:T(2,128)S(1)} %bitcast.109), channel_id=1, source_target_pairs={{0,2},{1,3},{2,0},{3,1},{4,6},{5,7},{6,4},{7,5},{8,10},{9,11},{10,... | collective-permute-start | bytes 297992 | tf_op jit(solution)/shard_map/ppermute | solution.py:77
  54.2 5.7 %collective-permute-start.4 = (f32[2,97,128]{2,0,1:T(2,128)S(1)}, f32[2,97,128]{2,0,1:T(2,128)S(1)}, u32[]{:S(2)}, u32[]{:S(2)}) collective-permute-start(f32[2,97,128]{2,0,1:T(2,128)S(1)} %bitcast.108), channel_id=1, source_target_pairs={{0,4},{1,5},{2,6},{3,7},{4,0},{5,1},{6,2},{7,3},{8,12},{9,13},{10,... | collective-permute-start | bytes 297992 | tf_op jit(solution)/shard_map/ppermute | solution.py:77
  54.8 7.3 %collective-permute-start.5 = (f32[2,97,128]{2,0,1:T(2,128)S(1)}, f32[2,97,128]{2,0,1:T(2,128)S(1)}, u32[]{:S(2)}, u32[]{:S(2)}) collective-permute-start(f32[2,97,128]{2,0,1:T(2,128)S(1)} %bitcast.107), channel_id=1, source_target_pairs={{0,6},{1,7},{2,4},{3,5},{4,2},{5,3},{6,0},{7,1},{8,14},{9,15},{10,... | collective-permute-start | bytes 297992 | tf_op jit(solution)/shard_map/ppermute | solution.py:77
  62.2 5.4 %collective-permute-start.6 = (f32[1,97,128]{2,0,1:T(1,128)S(1)}, f32[1,97,128]{2,0,1:T(1,128)S(1)}, u32[]{:S(2)}, u32[]{:S(2)}) collective-permute-start(f32[1,97,128]{2,0,1:T(1,128)S(1)} %constant_dynamic-slice_fusion.1), channel_id=1, source_target_pairs={{0,8},{1,9},{2,10},{3,11},{4,12},{5,13},{6,14},{7,15},{8,0},{9,1},... | collective-permute-start | bytes 149000 | tf_op jit(solution)/shard_map/ppermute | solution.py:77
  67.7 4.2 %collective-permute-start.7 = (f32[97,128]{1,0:T(8,128)S(1)}, f32[97,128]{1,0:T(8,128)S(1)}, u32[]{:S(2)}, u32[]{:S(2)}) collective-permute-start(f32[97,128]{1,0:T(8,128)S(1)} %bitcast.111), channel_id=1, source_target_pairs={{0,16},{16,0},{1,17},{17,1},{2,18},{18,2},{3,19},{19,3},{4,20},{20... | collective-permute-start | bytes 149000 | tf_op jit(solution)/shard_map/ppermute | solution.py:82

commit v11 on v9

--- a/solution.py
+++ b/solution.py
@@ -49,12 +49,11 @@
     nbits = nseq.bit_length() - 1
     assert nbits >= 1 and 1 << nbits == nseq and ndp & (ndp - 1) == 0
     groups = [2] + [1] * (nbits - 3) if nbits >= 3 else [1] * (nbits - 1)
-    lat = grad_t.shape[0]
-    share = grad_t.shape[1] // nseq
+    lat, _, _, share = grad_t.shape
     lanes = loss_row.shape[0]
     dense = lat * share // lanes
     me = lax.axis_index("seq")
-    halves = grad_t.reshape(lat, nseq // 2, 2, share)
+    halves = grad_t
     loss_rows = jnp.broadcast_to(loss_row[None, None, :], (nseq // 2, 1, lanes))
 
     def half(bit):
@@ -127,7 +126,10 @@
     assert capacity <= LAT
     owners = owner_map.reshape(-1)
     owner_hot = (owners[:, None] == jnp.arange(nseq, dtype=jnp.int32)[None, :]).astype(jnp.int32)
-    rank = jnp.sum(jnp.cumsum(owner_hot, axis=0) * owner_hot, axis=1) - 1
+    ntok = owners.shape[0]
+    upto = (jnp.arange(ntok)[:, None] >= jnp.arange(ntok)[None, :]).astype(jnp.bfloat16)
+    running = jnp.dot(upto, owner_hot.astype(jnp.bfloat16), preferred_element_type=jnp.float32)
+    rank = jnp.sum(running * owner_hot.astype(jnp.float32), axis=1).astype(jnp.int32) - 1
     dest = owners * capacity + rank
     select = (dest[None, :] == jnp.arange(slots, dtype=jnp.int32)[:, None]).astype(jnp.bfloat16)
     tok_clip = jnp.repeat(clip_of, tok_rows * tok_cols).astype(jnp.float32) + 1.0
@@ -171,11 +173,14 @@
     dpred = (2.0 * slot_coef[:, None] * diff).astype(jnp.bfloat16)
     states_t = hidden[0].T.astype(jnp.float32)
     normed_t = ((states_t - mean.T) * lax.rsqrt(var.T + 1e-06)).astype(jnp.bfloat16)
+    share = normed_t.shape[0] // nseq
     grad_t = lax.dot_general(
-        dpred, normed_t, (((0,), (1,)), ((), ())), preferred_element_type=jnp.float32
+        dpred,
+        normed_t.reshape(nseq // 2, 2, share, slots),
+        (((0,), (3,)), ((), ())),
+        preferred_element_type=jnp.float32,
     )
     ndp = lax.axis_size("dp")
-    share = grad_t.shape[1] // nseq
     lanes = 128
     dense = LAT * share // lanes
     assert ndp * CLIPS <= lanes and dense * lanes == LAT * share

time: 65.6 us -> 67.1 us (1.023)
  matrix products: 9.64 us -> 10.5 us
    reshape x1, local copies, waits for them, and re-layouts: 0.99 us -> 2.87 us  [per_device(): normed_t.reshape(nseq // 2, 2, share, slots)]
    dynamic_slice x3 -> x0, local copies, waits for them, and re-layouts: 1.42 us -> none  [half(): part = lax.dynamic_index_in_dim(halves, bit, 2, keepdims=False)]
    convert_element_type x1, other arithmetic: 0.68 us -> 1.88 us  [per_device(): ((states_t - mean.T) * lax.rsqrt(var.T + 1e-06)).astype(jnp.bfloat16)]
    dot_general x1 -> x2, matrix products: 0.5 us -> 1.28 us  [the longest x1 1.12 us: per_device(): lax.dot_general(dpred, normed_t.reshape(nseq // 2, 2, share, slots), (((0...]
    another operation x5 -> x1, other arithmetic: 0.88 us -> 0.18 us
    unnamed x25 -> x23, local copies, waits for them, and re-layouts: 5.43 us -> 4.92 us
  transfers between devices with their start and end apart: 9 -> 9, of which waited for: 7 -> 7; matrix products, arithmetic and copies ran while one was open for 11% -> 8% of each run, Pallas kernels for 0% -> 0%
where the time goes in v11:
time: 67.1 us; the launch traced here: 66.7 us
  waiting for transfers between devices  19.7 us (29%)
  starting transfers between devices  18.7 us (28%)
  local copies, waits for them, and re-layouts  12.8 us (19%)
  matrix products  10.5 us (16%)
  other arithmetic  3.94 us (6%)
  between operations  1.09 us (2%)
    ppermute x4, waiting for transfers between devices, tree_reduce(): total = total + lax.ppermute(send, 'seq', pairs)  9.64 us
    all_to_all x1, starting transfers between devices, per_device(): lax.all_to_all(jnp.concatenate([outgoing, labels], axis=1), 'seq', split_...  8.82 us
    all_to_all x1, waiting for transfers between devices, per_device(): lax.all_to_all(jnp.concatenate([outgoing, labels], axis=1), 'seq', split_...  6.69 us
    conv_general_dilated x1, matrix products, causal_conv(): lax.conv_general_dilated(padded, kernel, (1, 1), 'VALID', dimension_numbe...  5.56 us
    unnamed x23, local copies, waits for them, and re-layouts  4.92 us
    ppermute x4, starting transfers between devices, tree_reduce(): total = total + lax.ppermute(send, 'seq', pairs)  3.96 us
    ppermute x1, starting transfers between devices, with_halo(): lax.ppermute(tail, axis, [(i, (i + 1) % count) for i in range(ends)])  3.06 us
    reshape x1, local copies, waits for them, and re-layouts, per_device(): normed_t.reshape(nseq // 2, 2, share, slots)  2.87 us
  transfers between devices with their start and end apart: 9, of which 7 were waited for; matrix products, arithmetic and copies ran while one was open for 8% of the time, Pallas kernels for 0%

profile of v11, /device:TPU:0, one launch (start us, length us, event | category | flops | bytes accessed | tf_op | source)
XLA Modules:
  0.0 66.7 jit_solution(9204498047638879953)
XLA Ops:
  0.6 0.0 copy-start
  0.7 1.7 %copy.45 = bf16[1,16,4,48,128]{4,1,3,2,0:T(8,128)(2,1)S(1)} copy(bf16[1,16,4,48,128]{4,3,2,1,0:T(8,128)(2,1)} %param.11) | data formatting | bytes 1572864 | tf_op args[0]
  2.4 0.0 copy-start.3
  2.4 0.0 copy-start.1
  2.4 0.8 %fusion.40 = (bf16[1,16,1,48,128]{4,1,3,2,0:T(8,128)(2,1)}, bf16[1,16,1,48,128]{4,1,3,2,0:T(8,128)(2,1)}) fusion(bf16[1,16,4,48,128]{4,1,3,2,0:T(8,128)(2,1)S(1)} %copy.45), kind=kLoop, calls=%fused_computation.92 | loop fusion | bytes 786432 | tf_op jit(solution)/shard_map/slice | solution.py:15
  3.2 3.1 %collective-permute-start = (bf16[1,16,1,48,128]{4,1,3,2,0:T(8,128)(2,1)}, bf16[1,16,1,48,128]{4,1,3,2,0:T(8,128)(2,1)}, u32[]{:S(2)}, u32[]{:S(2)}) collective-permute-start(bf16[1,16,1,48,128]{4,1,3,2,0:T(8,128)(2,1)} %get-tuple-element.7), channel_id=1, source_target_pairs={{0,1},{1,2},{2,3},{3,4},{4,5},{5,6},{6,7},{7,8},{8,9},{9,10},{10,1... | collective-permute-start | bytes 589832 | tf_op jit(solution)/shard_map/ppermute | solution.py:18
  6.2 1.3 %collective-permute-start.1 = (bf16[1,16,1,48,128]{4,1,3,2,0:T(8,128)(2,1)}, bf16[1,16,1,48,128]{4,1,3,2,0:T(8,128)(2,1)}, u32[]{:S(2)}, u32[]{:S(2)}) collective-permute-start(bf16[1,16,1,48,128]{4,1,3,2,0:T(8,128)(2,1)} %get-tuple-element.8), channel_id=1, source_target_pairs={{1,0},{2,1},{3,2},{4,3},{5,4},{6,5},{7,6},{8,7},{9,8},{10,9},{11,1... | collective-permute-start | bytes 589832 | tf_op jit(solution)/shard_map/ppermute | solution.py:20
  7.5 2.3 %copy.49 = bf16[3,3,3,128,128]{3,4,0,2,1:T(8,128)(2,1)} copy(bf16[3,3,3,128,128]{4,3,2,1,0:T(8,128)(2,1)} %param.16) | data formatting | bytes 1769472 | tf_op args[5]
  9.8 0.2 reduce-window.4
  10.0 0.1 convert_reduce_fusion.1
  10.1 0.1 select_reduce_fusion
  10.2 0.2 reshape.203
  10.4 0.2 fusion.12
  10.6 0.1 broadcast_in_dim.6
  10.6 0.1 reshape.220
  10.7 0.2 convolution_reduce_fusion
  11.0 0.1 reshape.224
  11.1 0.0 copy-start.5
  11.1 0.0 copy-start.6
  11.1 0.3 convert_reduce_fusion
  11.4 0.6 fusion.3
  12.1 5.6 %fusion.7 = f32[16,4,48,384]{3,0,2,1:T(8,128)S(1)} fusion(bf16[3,3,128,384]{2,3,1,0:T(8,128)(2,1)} %bitcast.92, bf16[1,16,1,48,128]{4,1,3,2,0:T(8,128)(2,1)} %collective-permute-done.1, bf16[1,16,4,48,128]{4,1,3,2,0:T(8,128)(2,1)S(1)} %copy.45, bf16[1,16,1,48,128]{4,1,3,2,0:T(8,128)(2,1)} %collective-permute-done), kind=kOutput, calls=%fused_computation.12 | convolution fusion | flops 2683699200 | bytes 6782976 | tf_op jit(solution)/shard_map/conv_general_dilated | solution.py:32
  17.7 0.1 slice.39
  17.8 0.1 slice.40
  17.9 2.4 %convolution_convert_fusion.1 = bf16[16,1,12,64]{3,0,2,1:T(8,128)(2,1)S(1)} fusion(f32[16,4,48,384]{3,0,2,1:T(8,128)S(1)} %fusion.7, f32[14,4,48,128]{3,0,2,1:T(8,128)S(1)} %slice.40, f32[15,4,48,128]{3,0,2,1:T(8,128)S(1)} %slice.39, f32[16]{0:T(128)S(1)} %get-tuple-element.14, f32[16]{0:T(128)S(1)} %get-tuple-element.13, ...), kind=kOutput, calls=%fused_computation.19 | convolution fusion | flops 54669312 | bytes 5792768 | tf_op jit(solution)/shard_map/conv_general_dilated | solution.py:114
  20.4 0.2 convolution_convert_fusion
  20.6 0.1 copy.53
  20.8 0.7 %reshape.233 = bf16[16,2,608]{2,1,0:T(2,128)(2,1)} reshape(bf16[16,19,64]{2,1,0:T(8,128)(2,1)S(1)} %fusion.19) | data formatting | bytes 77824
  21.6 8.8 %all-to-all-start = ((bf16[16,2,608]{2,1,0:T(2,128)(2,1)}), bf16[16,2,608]{2,1,0:T(2,128)(2,1)S(1)}, u32[]{:S(2)}, u32[]{:S(2)}) async-start(bf16[16,2,608]{2,1,0:T(2,128)(2,1)} %reshape.233), calls=%async_computation | async-start | bytes 81920 | tf_op jit(solution)/shard_map/all_to_all | solution.py:147
  30.4 6.7 %all-to-all-done = bf16[16,2,608]{2,1,0:T(2,128)(2,1)S(1)} async-done(((bf16[16,2,608]{2,1,0:T(2,128)(2,1)}), bf16[16,2,608]{2,1,0:T(2,128)(2,1)S(1)}, u32[]{:S(2)}, u32[]{:S(2)}) %all-to-all-start) | async-done | bytes 38944 | tf_op jit(solution)/shard_map/all_to_all | solution.py:147
  37.1 0.1 reshape.234
  37.3 0.1 reshape.216
  37.4 0.1 copy.55
  37.5 0.1 fusion.29
  37.6 0.0 copy-start.7
  37.6 0.0 copy-start.8
  37.6 1.9 %fusion.38 = bf16[3072,288]{0,1:T(8,128)(2,1)} fusion(f32[288]{0:T(512)S(1)} %get-tuple-element.17, f32[288]{0:T(512)S(1)} %broadcast_multiply_fusion, bf16[1,288,3072]{2,1,0:T(8,128)(2,1)S(1)} %copy-done.1), kind=kLoop, calls=%fused_computation.91 | loop fusion | flops 3538944 | bytes 3541248 | tf_op jit(solution)/shard_map/convert_element_type | solution.py:175
  39.5 0.8 %multiply_reduce_fusion = (f32[288]{0:T(512)S(1)}, f32[288,64]{0,1:T(8,128)S(1)}) fusion(f32[288,64]{0,1:T(8,128)S(1)} %copy.55, f32[1,288,64]{1,2,0:T(8,128)S(1)} %copy-done.7, f32[288]{0:T(512)S(1)} %get-tuple-element.18, f32[1,288,64]{1,2,0:T(8,128)S(1)} %copy-done.8, f32[288]{0:T(512)S(1)} %fusion.29, bf16[3072,64]{0,1:T(8,128)(2,1)S(1)} %copy-done, ...), kind=kOutput, calls=%fused_computation.42 | convolution fusion | flops 116913888 | bytes 2463360 | tf_op jit(solution)/shard_map/dot_general | solution.py:168
  40.3 0.2 fusion.28
  40.5 2.9 %copy.59 = bf16[3072,288]{1,0:T(8,128)(2,1)S(1)} copy(bf16[3072,288]{0,1:T(8,128)(2,1)} %fusion.38) | data formatting | bytes 3538944 | tf_op jit(solution)/shard_map/reshape | solution.py:179
  43.4 1.1 %fusion.23 = f32[64,8,2,192]{3,0,2,1:T(8,128)S(1)} fusion(bf16[8,2,192,288]{3,2,1,0:T(8,128)(2,1)S(1)} %bitcast.90, f32[288,64]{0,1:T(8,128)S(1)} %get-tuple-element.16, f32[288]{0:T(512)S(1)} %broadcast_multiply_fusion.1), kind=kOutput, calls=%fused_computation.47 | convolution fusion | flops 113283072 | bytes 2630784 | tf_op jit(solution)/shard_map/dot_general | solution.py:177
  44.5 0.1 dynamic-slice_bitcast_fusion.1
  44.6 0.3 reshape.211
  44.9 0.1 multiply_dynamic-update-slice_fusion
  45.0 0.1 collective-permute-start.2
  45.1 0.3 reshape.210
  45.4 1.4 %collective-permute-done.2 = f32[8,97,128]{2,1,0:T(8,128)S(1)} collective-permute-done((f32[8,97,128]{2,1,0:T(8,128)S(1)}, f32[8,97,128]{2,1,0:T(8,128)S(1)}, u32[]{:S(2)}, u32[]{:S(2)}) %collective-permute-start.2) | collective-permute-done | bytes 397344 | tf_op jit(solution)/shard_map/ppermute | solution.py:65
  46.9 0.1 copy.57
  47.0 0.3 constant_dynamic-slice_fusion.4
  47.4 0.4 collective-permute-start.3
  47.7 0.6 collective-permute-start.4
  48.3 2.6 %collective-permute-start.5 = (f32[2,97,128]{2,0,1:T(2,128)S(1)}, f32[2,97,128]{2,0,1:T(2,128)S(1)}, u32[]{:S(2)}, u32[]{:S(2)}) collective-permute-start(f32[2,97,128]{2,0,1:T(2,128)S(1)} %bitcast.94), channel_id=1, source_target_pairs={{0,6},{1,7},{2,4},{3,5},{4,2},{5,3},{6,0},{7,1},{8,14},{9,15},{10,... | collective-permute-start | bytes 297992 | tf_op jit(solution)/shard_map/ppermute | solution.py:76
  50.9 1.4 %collective-permute-done.3 = f32[2,97,128]{2,0,1:T(2,128)S(1)} collective-permute-done((f32[2,97,128]{2,0,1:T(2,128)S(1)}, f32[2,97,128]{2,0,1:T(2,128)S(1)}, u32[]{:S(2)}, u32[]{:S(2)}) %collective-permute-start.3) | collective-permute-done | bytes 99360 | tf_op jit(solution)/shard_map/ppermute | solution.py:76
  52.3 1.1 %collective-permute-done.4 = f32[2,97,128]{2,0,1:T(2,128)S(1)} collective-permute-done((f32[2,97,128]{2,0,1:T(2,128)S(1)}, f32[2,97,128]{2,0,1:T(2,128)S(1)}, u32[]{:S(2)}, u32[]{:S(2)}) %collective-permute-start.4) | collective-permute-done | bytes 99360 | tf_op jit(solution)/shard_map/ppermute | solution.py:76
  53.4 2.2 %collective-permute-done.5 = f32[2,97,128]{2,0,1:T(2,128)S(1)} collective-permute-done((f32[2,97,128]{2,0,1:T(2,128)S(1)}, f32[2,97,128]{2,0,1:T(2,128)S(1)}, u32[]{:S(2)}, u32[]{:S(2)}) %collective-permute-start.5) | collective-permute-done | bytes 99360 | tf_op jit(solution)/shard_map/ppermute | solution.py:76
  55.6 0.1 add_add_fusion
  55.8 0.4 collective-permute-start.6
  56.2 5.0 %collective-permute-done.6 = f32[1,97,128]{2,0,1:T(1,128)S(1)} collective-permute-done((f32[1,97,128]{2,0,1:T(1,128)S(1)}, f32[1,97,128]{2,0,1:T(1,128)S(1)}, u32[]{:S(2)}, u32[]{:S(2)}) %collective-permute-start.6) | collective-permute-done | bytes 49696 | tf_op jit(solution)/shard_map/ppermute | solution.py:76
  61.1 0.1 dynamic-slice_add_fusion
  61.2 1.6 %collective-permute-start.7 = (f32[97,128]{1,0:T(8,128)S(1)}, f32[97,128]{1,0:T(8,128)S(1)}, u32[]{:S(2)}, u32[]{:S(2)}) collective-permute-start(f32[97,128]{1,0:T(8,128)S(1)} %bitcast.98), channel_id=1, source_target_pairs={{0,16},{16,0},{1,17},{17,1},{2,18},{18,2},{3,19},{19,3},{4,20},{20... | collective-permute-start | bytes 149000 | tf_op jit(solution)/shard_map/ppermute | solution.py:81
  62.8 0.7 %reshape.204 = bf16[1,16,1,768]{3,1,2,0:T(8,128)(2,1)} reshape(bf16[16,1,12,64]{3,2,0,1:T(8,128)(2,1)S(1)} %copy.51) | data formatting | bytes 49152 | tf_op jit(solution)/shard_map/reshape | solution.py:122
  63.5 1.9 %collective-permute-done.7 = f32[97,128]{1,0:T(8,128)S(1)} collective-permute-done((f32[97,128]{1,0:T(8,128)S(1)}, f32[97,128]{1,0:T(8,128)S(1)}, u32[]{:S(2)}, u32[]{:S(2)}) %collective-permute-start.7) | collective-permute-done | bytes 49696 | tf_op jit(solution)/shard_map/ppermute | solution.py:81
  65.4 0.7 %reshape.214 = f32[64,192]{1,0:T(8,128)} reshape(f32[96,128]{1,0:T(8,128)S(1)} %slice.44) | data formatting | bytes 98304 | tf_op jit(solution)/shard_map/reshape | solution.py:190
  66.1 0.6 constant_dynamic-slice_fusion
  (39 shorter events, 0.4 us)
Async XLA Ops:
  0.6 38.9 %copy-start = (bf16[3072,64]{0,1:T(8,128)(2,1)S(1)}, bf16[3072,64]{0,1:T(8,128)(2,1)}, u32[]{:S(2)}) copy-start(bf16[3072,64]{0,1:T(8,128)(2,1)} %param.21) | copy-start | bytes 1179652
  0.6 9.2 %copy-start.4 = (s32[1,4]{1,0:T(1,128)S(1)}, s32[1,4]{1,0:T(1,128)}, u32[]{:S(2)}) copy-start(s32[1,4]{1,0:T(1,128)} %param.12) | copy-start | bytes 52
  0.7 9.5 %copy-start.2 = (bf16[2048,64]{0,1:T(8,128)(2,1)S(1)}, bf16[2048,64]{0,1:T(8,128)(2,1)}, u32[]{:S(2)}) copy-start(bf16[2048,64]{0,1:T(8,128)(2,1)} %param.17) | copy-start | bytes 786436
  2.4 8.0 %copy-start.3 = (s32[1,1,192,1]{2,3,1,0:T(1,128)S(1)}, s32[1,1,192,1]{2,3,1,0:T(1,128)}, u32[]{:S(2)}) copy-start(s32[1,1,192,1]{2,3,1,0:T(1,128)} %param.15) | copy-start | bytes 2308
  2.4 8.7 %copy-start.1 = (bf16[1,288,3072]{2,1,0:T(8,128)(2,1)S(1)}, bf16[1,288,3072]{2,1,0:T(8,128)(2,1)}, u32[]{:S(2)}) copy-start(bf16[1,288,3072]{2,1,0:T(8,128)(2,1)} %param.18) | copy-start | bytes 5308420
  3.2 8.9 %collective-permute-start = (bf16[1,16,1,48,128]{4,1,3,2,0:T(8,128)(2,1)}, bf16[1,16,1,48,128]{4,1,3,2,0:T(8,128)(2,1)}, u32[]{:S(2)}, u32[]{:S(2)}) collective-permute-start(bf16[1,16,1,48,128]{4,1,3,2,0:T(8,128)(2,1)} %get-tuple-element.7), channel_id=1, source_target_pairs={{0,1},{1,2},{2,3},{3,4},{4,5},{5,6},{6,7},{7,8},{8,9},{9,10},{10,1... | collective-permute-start | bytes 589832 | tf_op jit(solution)/shard_map/ppermute | solution.py:18
  6.2 5.9 %collective-permute-start.1 = (bf16[1,16,1,48,128]{4,1,3,2,0:T(8,128)(2,1)}, bf16[1,16,1,48,128]{4,1,3,2,0:T(8,128)(2,1)}, u32[]{:S(2)}, u32[]{:S(2)}) collective-permute-start(bf16[1,16,1,48,128]{4,1,3,2,0:T(8,128)(2,1)} %get-tuple-element.8), channel_id=1, source_target_pairs={{1,0},{2,1},{3,2},{4,3},{5,4},{6,5},{7,6},{8,7},{9,8},{10,9},{11,1... | collective-permute-start | bytes 589832 | tf_op jit(solution)/shard_map/ppermute | solution.py:20
  11.1 1.0 %copy-start.5 = (s32[1,4]{1,0:T(1,128)S(1)}, s32[1,4]{1,0:T(1,128)}, u32[]{:S(2)}) copy-start(s32[1,4]{1,0:T(1,128)} %param.14) | copy-start | bytes 52
  11.1 1.0 %copy-start.6 = (s32[1,4]{1,0:T(1,128)S(1)}, s32[1,4]{1,0:T(1,128)}, u32[]{:S(2)}) copy-start(s32[1,4]{1,0:T(1,128)} %param.13) | copy-start | bytes 52
  21.6 15.5 %all-to-all-start = ((bf16[16,2,608]{2,1,0:T(2,128)(2,1)}), bf16[16,2,608]{2,1,0:T(2,128)(2,1)S(1)}, u32[]{:S(2)}, u32[]{:S(2)}) async-start(bf16[16,2,608]{2,1,0:T(2,128)(2,1)} %reshape.233), calls=%async_computation | async-start | bytes 81920 | tf_op jit(solution)/shard_map/all_to_all | solution.py:147
  37.6 1.9 %copy-start.7 = (f32[1,288,64]{1,2,0:T(8,128)S(1)}, f32[1,288,64]{1,2,0:T(8,128)}, u32[]{:S(2)}) copy-start(f32[1,288,64]{1,2,0:T(8,128)} %param.19) | copy-start | bytes 221188
  37.6 1.9 %copy-start.8 = (f32[1,288,64]{1,2,0:T(8,128)S(1)}, f32[1,288,64]{1,2,0:T(8,128)}, u32[]{:S(2)}) copy-start(f32[1,288,64]{1,2,0:T(8,128)} %param.20) | copy-start | bytes 221188
  45.0 1.8 %collective-permute-start.2 = (f32[8,97,128]{2,1,0:T(8,128)S(1)}, f32[8,97,128]{2,1,0:T(8,128)S(1)}, u32[]{:S(2)}, u32[]{:S(2)}) collective-permute-start(f32[8,97,128]{2,1,0:T(8,128)S(1)} %pad_maximum_fusion), channel_id=1, source_target_pairs={{0,1},{1,0},{2,3},{3,2},{4,5},{5,4},{6,7},{7,6},{8,9},{9,8},{10,11... | collective-permute-start | bytes 1191944 | tf_op jit(solution)/shard_map/ppermute | solution.py:65
  47.4 4.9 %collective-permute-start.3 = (f32[2,97,128]{2,0,1:T(2,128)S(1)}, f32[2,97,128]{2,0,1:T(2,128)S(1)}, u32[]{:S(2)}, u32[]{:S(2)}) collective-permute-start(f32[2,97,128]{2,0,1:T(2,128)S(1)} %bitcast.96), channel_id=1, source_target_pairs={{0,2},{1,3},{2,0},{3,1},{4,6},{5,7},{6,4},{7,5},{8,10},{9,11},{10,... | collective-permute-start | bytes 297992 | tf_op jit(solution)/shard_map/ppermute | solution.py:76
  47.7 5.7 %collective-permute-start.4 = (f32[2,97,128]{2,0,1:T(2,128)S(1)}, f32[2,97,128]{2,0,1:T(2,128)S(1)}, u32[]{:S(2)}, u32[]{:S(2)}) collective-permute-start(f32[2,97,128]{2,0,1:T(2,128)S(1)} %bitcast.95), channel_id=1, source_target_pairs={{0,4},{1,5},{2,6},{3,7},{4,0},{5,1},{6,2},{7,3},{8,12},{9,13},{10,... | collective-permute-start | bytes 297992 | tf_op jit(solution)/shard_map/ppermute | solution.py:76
  48.3 7.3 %collective-permute-start.5 = (f32[2,97,128]{2,0,1:T(2,128)S(1)}, f32[2,97,128]{2,0,1:T(2,128)S(1)}, u32[]{:S(2)}, u32[]{:S(2)}) collective-permute-start(f32[2,97,128]{2,0,1:T(2,128)S(1)} %bitcast.94), channel_id=1, source_target_pairs={{0,6},{1,7},{2,4},{3,5},{4,2},{5,3},{6,0},{7,1},{8,14},{9,15},{10,... | collective-permute-start | bytes 297992 | tf_op jit(solution)/shard_map/ppermute | solution.py:76
  55.8 5.4 %collective-permute-start.6 = (f32[1,97,128]{2,0,1:T(1,128)S(1)}, f32[1,97,128]{2,0,1:T(1,128)S(1)}, u32[]{:S(2)}, u32[]{:S(2)}) collective-permute-start(f32[1,97,128]{2,0,1:T(1,128)S(1)} %constant_dynamic-slice_fusion.1), channel_id=1, source_target_pairs={{0,8},{1,9},{2,10},{3,11},{4,12},{5,13},{6,14},{7,15},{8,0},{9,1},... | collective-permute-start | bytes 149000 | tf_op jit(solution)/shard_map/ppermute | solution.py:76
  61.2 4.2 %collective-permute-start.7 = (f32[97,128]{1,0:T(8,128)S(1)}, f32[97,128]{1,0:T(8,128)S(1)}, u32[]{:S(2)}, u32[]{:S(2)}) collective-permute-start(f32[97,128]{1,0:T(8,128)S(1)} %bitcast.98), channel_id=1, source_target_pairs={{0,16},{16,0},{1,17},{17,1},{2,18},{18,2},{3,19},{19,3},{4,20},{20... | collective-permute-start | bytes 149000 | tf_op jit(solution)/shard_map/ppermute | solution.py:81

commit v12 on v9

--- a/solution.py
+++ b/solution.py
@@ -127,7 +127,10 @@
     assert capacity <= LAT
     owners = owner_map.reshape(-1)
     owner_hot = (owners[:, None] == jnp.arange(nseq, dtype=jnp.int32)[None, :]).astype(jnp.int32)
-    rank = jnp.sum(jnp.cumsum(owner_hot, axis=0) * owner_hot, axis=1) - 1
+    ntok = owners.shape[0]
+    upto = (jnp.arange(ntok)[:, None] >= jnp.arange(ntok)[None, :]).astype(jnp.bfloat16)
+    running = jnp.dot(upto, owner_hot.astype(jnp.bfloat16), preferred_element_type=jnp.float32)
+    rank = jnp.sum(running * owner_hot.astype(jnp.float32), axis=1).astype(jnp.int32) - 1
     dest = owners * capacity + rank
     select = (dest[None, :] == jnp.arange(slots, dtype=jnp.int32)[:, None]).astype(jnp.bfloat16)
     tok_clip = jnp.repeat(clip_of, tok_rows * tok_cols).astype(jnp.float32) + 1.0

time: 65.6 us -> 64.9 us (0.989)
  other arithmetic: 3.49 us -> 2.75 us
    another operation x5 -> x1, other arithmetic: 0.88 us -> 0.18 us
  transfers between devices with their start and end apart: 9 -> 9, of which waited for: 7 -> 7; matrix products, arithmetic and copies ran while one was open for 11% -> 10% of each run, Pallas kernels for 0% -> 0%
where the time goes in v12:
time: 64.9 us; the launch traced here: 64.5 us
  waiting for transfers between devices  19.5 us (30%)
  starting transfers between devices  18.6 us (29%)
  local copies, waits for them, and re-layouts  12.7 us (20%)
  matrix products  9.8 us (15%)
  other arithmetic  2.75 us (4%)
  between operations  1.14 us (2%)
    ppermute x4, waiting for transfers between devices, tree_reduce(): total = total + lax.ppermute(send, 'seq', pairs)  9.64 us
    all_to_all x1, starting transfers between devices, per_device(): lax.all_to_all(jnp.concatenate([outgoing, labels], axis=1), 'seq', split_...  8.64 us
    all_to_all x1, waiting for transfers between devices, per_device(): lax.all_to_all(jnp.concatenate([outgoing, labels], axis=1), 'seq', split_...  6.68 us
    conv_general_dilated x1, matrix products, causal_conv(): lax.conv_general_dilated(padded, kernel, (1, 1), 'VALID', dimension_numbe...  5.55 us
    unnamed x25, local copies, waits for them, and re-layouts  5.43 us
    ppermute x4, starting transfers between devices, tree_reduce(): total = total + lax.ppermute(send, 'seq', pairs)  3.96 us
    ppermute x1, starting transfers between devices, with_halo(): lax.ppermute(tail, axis, [(i, (i + 1) % count) for i in range(ends)])  3.06 us
    conv_general_dilated x1, matrix products, per_device(): lax.conv_general_dilated(cells, w_latent.reshape(4, 4, chans, LAT), (4, 4...  2.42 us
  transfers between devices with their start and end apart: 9, of which 7 were waited for; matrix products, arithmetic and copies ran while one was open for 10% of the time, Pallas kernels for 0%

profile of v12, /device:TPU:0, one launch (start us, length us, event | category | flops | bytes accessed | tf_op | source)
XLA Modules:
  0.0 64.5 jit_solution(2770916990581380223)
XLA Ops:
  0.6 0.0 copy-start
  0.7 1.7 %copy.47 = bf16[1,16,4,48,128]{4,1,3,2,0:T(8,128)(2,1)S(1)} copy(bf16[1,16,4,48,128]{4,3,2,1,0:T(8,128)(2,1)} %param.11) | data formatting | bytes 1572864 | tf_op args[0]
  2.4 0.0 copy-start.6
  2.4 0.0 copy-start.1
  2.4 0.8 %fusion.36 = (bf16[1,16,1,48,128]{4,1,3,2,0:T(8,128)(2,1)}, bf16[1,16,1,48,128]{4,1,3,2,0:T(8,128)(2,1)}) fusion(bf16[1,16,4,48,128]{4,1,3,2,0:T(8,128)(2,1)S(1)} %copy.47), kind=kLoop, calls=%fused_computation.92 | loop fusion | bytes 786432 | tf_op jit(solution)/shard_map/slice | solution.py:15
  3.2 3.1 %collective-permute-start = (bf16[1,16,1,48,128]{4,1,3,2,0:T(8,128)(2,1)}, bf16[1,16,1,48,128]{4,1,3,2,0:T(8,128)(2,1)}, u32[]{:S(2)}, u32[]{:S(2)}) collective-permute-start(bf16[1,16,1,48,128]{4,1,3,2,0:T(8,128)(2,1)} %get-tuple-element.7), channel_id=1, source_target_pairs={{0,1},{1,2},{2,3},{3,4},{4,5},{5,6},{6,7},{7,8},{8,9},{9,10},{10,1... | collective-permute-start | bytes 589832 | tf_op jit(solution)/shard_map/ppermute | solution.py:18
  6.2 1.3 %collective-permute-start.1 = (bf16[1,16,1,48,128]{4,1,3,2,0:T(8,128)(2,1)}, bf16[1,16,1,48,128]{4,1,3,2,0:T(8,128)(2,1)}, u32[]{:S(2)}, u32[]{:S(2)}) collective-permute-start(bf16[1,16,1,48,128]{4,1,3,2,0:T(8,128)(2,1)} %get-tuple-element.8), channel_id=1, source_target_pairs={{1,0},{2,1},{3,2},{4,3},{5,4},{6,5},{7,6},{8,7},{9,8},{10,9},{11,1... | collective-permute-start | bytes 589832 | tf_op jit(solution)/shard_map/ppermute | solution.py:20
  7.5 2.3 %copy.51 = bf16[3,3,3,128,128]{3,4,0,2,1:T(8,128)(2,1)} copy(bf16[3,3,3,128,128]{4,3,2,1,0:T(8,128)(2,1)} %param.16) | data formatting | bytes 1769472 | tf_op args[5]
  9.8 0.2 reduce-window.4
  10.0 0.1 convert_reduce_fusion.1
  10.1 0.1 select_reduce_fusion
  10.2 0.2 reshape.203
  10.4 0.2 fusion.12
  10.6 0.1 broadcast_in_dim.6
  10.6 0.1 reshape.220
  10.7 0.2 convolution_reduce_fusion
  11.0 0.1 reshape.223
  11.1 0.3 convert_reduce_fusion
  11.4 0.6 fusion.3
  12.0 0.5 copy-done.2
  12.5 0.7 %fusion.4 = bf16[288,3072]{1,0:T(8,128)(2,1)S(1)} fusion(bf16[1,288,3072]{2,1,0:T(8,128)(2,1)S(1)} %copy-done.2, f32[288]{0:T(512)S(1)} %add_rsqrt_fusion, f32[288]{0:T(512)S(1)} %broadcast_multiply_fusion), kind=kLoop, calls=%fused_computation.6 | loop fusion | flops 3538944 | bytes 3541248 | tf_op jit(solution)/shard_map/convert_element_type | solution.py:168
  13.3 5.6 %fusion.7 = f32[16,4,48,384]{3,0,2,1:T(8,128)S(1)} fusion(bf16[3,3,128,384]{2,3,1,0:T(8,128)(2,1)} %bitcast.83, bf16[1,16,1,48,128]{4,1,3,2,0:T(8,128)(2,1)} %collective-permute-done.1, bf16[1,16,4,48,128]{4,1,3,2,0:T(8,128)(2,1)S(1)} %copy.47, bf16[1,16,1,48,128]{4,1,3,2,0:T(8,128)(2,1)} %collective-permute-done), kind=kOutput, calls=%fused_computation.12 | convolution fusion | flops 2683699200 | bytes 6782976 | tf_op jit(solution)/shard_map/conv_general_dilated | solution.py:32
  18.9 0.1 slice.39
  19.0 0.1 slice.40
  19.1 2.4 %convolution_convert_fusion.1 = bf16[16,1,12,64]{3,0,2,1:T(8,128)(2,1)S(1)} fusion(f32[16,4,48,384]{3,0,2,1:T(8,128)S(1)} %fusion.7, f32[14,4,48,128]{3,0,2,1:T(8,128)S(1)} %slice.40, f32[15,4,48,128]{3,0,2,1:T(8,128)S(1)} %slice.39, f32[16]{0:T(128)S(1)} %get-tuple-element.14, f32[16]{0:T(128)S(1)} %get-tuple-element.13, ...), kind=kOutput, calls=%fused_computation.19 | convolution fusion | flops 54669312 | bytes 5792768 | tf_op jit(solution)/shard_map/conv_general_dilated | solution.py:115
  21.5 0.0 copy-start.4
  21.6 0.2 convolution_convert_fusion
  21.8 0.1 copy.55
  22.0 0.7 %reshape.232 = bf16[16,2,608]{2,1,0:T(2,128)(2,1)} reshape(bf16[16,19,64]{2,1,0:T(8,128)(2,1)S(1)} %fusion.19) | data formatting | bytes 77824
  22.8 8.6 %all-to-all-start = ((bf16[16,2,608]{2,1,0:T(2,128)(2,1)}), bf16[16,2,608]{2,1,0:T(2,128)(2,1)S(1)}, u32[]{:S(2)}, u32[]{:S(2)}) async-start(bf16[16,2,608]{2,1,0:T(2,128)(2,1)} %reshape.232), calls=%async_computation | async-start | bytes 81920 | tf_op jit(solution)/shard_map/all_to_all | solution.py:148
  31.4 6.7 %all-to-all-done = bf16[16,2,608]{2,1,0:T(2,128)(2,1)S(1)} async-done(((bf16[16,2,608]{2,1,0:T(2,128)(2,1)}), bf16[16,2,608]{2,1,0:T(2,128)(2,1)S(1)}, u32[]{:S(2)}, u32[]{:S(2)}) %all-to-all-start) | async-done | bytes 38944 | tf_op jit(solution)/shard_map/all_to_all | solution.py:148
  38.1 0.1 reshape.233
  38.3 0.1 reshape.216
  38.4 0.1 fusion.27
  38.5 0.1 copy.57
  38.7 0.7 %multiply_reduce_fusion = (f32[288]{0:T(512)S(1)}, f32[288,64]{0,1:T(8,128)S(1)}) fusion(f32[288,64]{0,1:T(8,128)S(1)} %copy.57, f32[1,288,64]{1,2,0:T(8,128)S(1)} %copy-done.4, f32[288]{0:T(512)S(1)} %broadcast_subtract_fusion, f32[1,288,64]{1,2,0:T(8,128)S(1)} %copy-done.5, f32[288]{0:T(512)S(1)} %fusion.27, bf16[288,3072]{1,0:T(8,128)(2,1)S(1)} %fusion.4, ...), kind=kOutput, calls=%fused_computation.42 | convolution fusion | flops 113374944 | bytes 2461056 | tf_op jit(solution)/shard_map/dot_general | solution.py:169
  39.4 0.2 fusion.26
  39.6 0.5 fusion.22
  40.1 1.0 %reshape.209 = f32[64,8,2,192]{3,2,1,0:T(2,128)S(1)} reshape(f32[64,3072]{1,0:T(8,128)S(1)} %fusion.22) | data formatting | bytes 1572864 | tf_op jit(solution)/shard_map/reshape | solution.py:57
  41.1 1.1 %constant_dynamic-slice_fusion.7 = (f32[64,8,1,192]{3,2,1,0:T(1,128)S(1)}, f32[64,8,1,192]{3,2,1,0:T(1,128)S(1)}) fusion(f32[64,8,2,192]{3,2,1,0:T(2,128)S(1)} %reshape.209, s32[]{:T(128)S(6)} %select_n.31, s32[]{:T(128)S(6)} %select_n.33), kind=kLoop, calls=%fused_computation.67 | loop fusion | bytes 1572872 | tf_op jit(solution)/shard_map/jit(dynamic_index_in_dim)/dynamic_slice | solution.py:61
  42.2 0.2 copy.73
  42.4 0.3 reshape.211
  42.7 0.1 multiply_dynamic-update-slice_fusion
  42.8 0.1 collective-permute-start.2
  42.9 0.2 copy.74
  43.1 0.3 reshape.210
  43.4 1.3 %collective-permute-done.2 = f32[8,97,128]{2,1,0:T(8,128)S(1)} collective-permute-done((f32[8,97,128]{2,1,0:T(8,128)S(1)}, f32[8,97,128]{2,1,0:T(8,128)S(1)}, u32[]{:S(2)}, u32[]{:S(2)}) %collective-permute-start.2) | collective-permute-done | bytes 397344 | tf_op jit(solution)/shard_map/ppermute | solution.py:66
  44.7 0.1 copy.60
  44.8 0.3 constant_dynamic-slice_fusion.4
  45.2 0.4 collective-permute-start.3
  45.5 0.6 collective-permute-start.4
  46.1 2.6 %collective-permute-start.5 = (f32[2,97,128]{2,0,1:T(2,128)S(1)}, f32[2,97,128]{2,0,1:T(2,128)S(1)}, u32[]{:S(2)}, u32[]{:S(2)}) collective-permute-start(f32[2,97,128]{2,0,1:T(2,128)S(1)} %bitcast.85), channel_id=1, source_target_pairs={{0,6},{1,7},{2,4},{3,5},{4,2},{5,3},{6,0},{7,1},{8,14},{9,15},{10,... | collective-permute-start | bytes 297992 | tf_op jit(solution)/shard_map/ppermute | solution.py:77
  48.7 1.4 %collective-permute-done.3 = f32[2,97,128]{2,0,1:T(2,128)S(1)} collective-permute-done((f32[2,97,128]{2,0,1:T(2,128)S(1)}, f32[2,97,128]{2,0,1:T(2,128)S(1)}, u32[]{:S(2)}, u32[]{:S(2)}) %collective-permute-start.3) | collective-permute-done | bytes 99360 | tf_op jit(solution)/shard_map/ppermute | solution.py:77
  50.1 1.1 %collective-permute-done.4 = f32[2,97,128]{2,0,1:T(2,128)S(1)} collective-permute-done((f32[2,97,128]{2,0,1:T(2,128)S(1)}, f32[2,97,128]{2,0,1:T(2,128)S(1)}, u32[]{:S(2)}, u32[]{:S(2)}) %collective-permute-start.4) | collective-permute-done | bytes 99360 | tf_op jit(solution)/shard_map/ppermute | solution.py:77
  51.2 2.2 %collective-permute-done.5 = f32[2,97,128]{2,0,1:T(2,128)S(1)} collective-permute-done((f32[2,97,128]{2,0,1:T(2,128)S(1)}, f32[2,97,128]{2,0,1:T(2,128)S(1)}, u32[]{:S(2)}, u32[]{:S(2)}) %collective-permute-start.5) | collective-permute-done | bytes 99360 | tf_op jit(solution)/shard_map/ppermute | solution.py:77
  53.4 0.1 add_add_fusion
  53.5 0.4 collective-permute-start.6
  53.9 5.0 %collective-permute-done.6 = f32[1,97,128]{2,0,1:T(1,128)S(1)} collective-permute-done((f32[1,97,128]{2,0,1:T(1,128)S(1)}, f32[1,97,128]{2,0,1:T(1,128)S(1)}, u32[]{:S(2)}, u32[]{:S(2)}) %collective-permute-start.6) | collective-permute-done | bytes 49696 | tf_op jit(solution)/shard_map/ppermute | solution.py:77
  58.9 0.1 dynamic-slice_add_fusion
  59.0 1.6 %collective-permute-start.7 = (f32[97,128]{1,0:T(8,128)S(1)}, f32[97,128]{1,0:T(8,128)S(1)}, u32[]{:S(2)}, u32[]{:S(2)}) collective-permute-start(f32[97,128]{1,0:T(8,128)S(1)} %bitcast.89), channel_id=1, source_target_pairs={{0,16},{16,0},{1,17},{17,1},{2,18},{18,2},{3,19},{19,3},{4,20},{20... | collective-permute-start | bytes 149000 | tf_op jit(solution)/shard_map/ppermute | solution.py:82
  60.6 0.7 %reshape.204 = bf16[1,16,1,768]{3,1,2,0:T(8,128)(2,1)} reshape(bf16[16,1,12,64]{3,2,0,1:T(8,128)(2,1)S(1)} %copy.53) | data formatting | bytes 49152 | tf_op jit(solution)/shard_map/reshape | solution.py:123
  61.3 1.9 %collective-permute-done.7 = f32[97,128]{1,0:T(8,128)S(1)} collective-permute-done((f32[97,128]{1,0:T(8,128)S(1)}, f32[97,128]{1,0:T(8,128)S(1)}, u32[]{:S(2)}, u32[]{:S(2)}) %collective-permute-start.7) | collective-permute-done | bytes 49696 | tf_op jit(solution)/shard_map/ppermute | solution.py:82
  63.2 0.7 %reshape.214 = f32[64,192]{1,0:T(8,128)} reshape(f32[96,128]{1,0:T(8,128)S(1)} %slice.44) | data formatting | bytes 98304 | tf_op jit(solution)/shard_map/reshape | solution.py:188
  63.9 0.6 constant_dynamic-slice_fusion
  (44 shorter events, 0.4 us)
Async XLA Ops:
  0.6 38.0 %copy-start = (bf16[3072,64]{0,1:T(8,128)(2,1)S(1)}, bf16[3072,64]{0,1:T(8,128)(2,1)}, u32[]{:S(2)}) copy-start(bf16[3072,64]{0,1:T(8,128)(2,1)} %param.21) | copy-start | bytes 1179652
  0.6 9.2 %copy-start.7 = (s32[1,4]{1,0:T(1,128)S(1)}, s32[1,4]{1,0:T(1,128)}, u32[]{:S(2)}) copy-start(s32[1,4]{1,0:T(1,128)} %param.12) | copy-start | bytes 52
  0.7 9.5 %copy-start.3 = (bf16[2048,64]{0,1:T(8,128)(2,1)S(1)}, bf16[2048,64]{0,1:T(8,128)(2,1)}, u32[]{:S(2)}) copy-start(bf16[2048,64]{0,1:T(8,128)(2,1)} %param.17) | copy-start | bytes 786436
  2.4 8.0 %copy-start.6 = (s32[1,1,192,1]{2,3,1,0:T(1,128)S(1)}, s32[1,1,192,1]{2,3,1,0:T(1,128)}, u32[]{:S(2)}) copy-start(s32[1,1,192,1]{2,3,1,0:T(1,128)} %param.15) | copy-start | bytes 2308
  2.4 8.7 %copy-start.1 = (bf16[1,288,3072]{2,1,0:T(8,128)(2,1)S(1)}, bf16[1,288,3072]{2,1,0:T(8,128)(2,1)}, u32[]{:S(2)}) copy-start(bf16[1,288,3072]{2,1,0:T(8,128)(2,1)} %param.18) | copy-start | bytes 5308420
  3.2 10.1 %collective-permute-start = (bf16[1,16,1,48,128]{4,1,3,2,0:T(8,128)(2,1)}, bf16[1,16,1,48,128]{4,1,3,2,0:T(8,128)(2,1)}, u32[]{:S(2)}, u32[]{:S(2)}) collective-permute-start(bf16[1,16,1,48,128]{4,1,3,2,0:T(8,128)(2,1)} %get-tuple-element.7), channel_id=1, source_target_pairs={{0,1},{1,2},{2,3},{3,4},{4,5},{5,6},{6,7},{7,8},{8,9},{9,10},{10,1... | collective-permute-start | bytes 589832 | tf_op jit(solution)/shard_map/ppermute | solution.py:18
  6.2 7.1 %collective-permute-start.1 = (bf16[1,16,1,48,128]{4,1,3,2,0:T(8,128)(2,1)}, bf16[1,16,1,48,128]{4,1,3,2,0:T(8,128)(2,1)}, u32[]{:S(2)}, u32[]{:S(2)}) collective-permute-start(bf16[1,16,1,48,128]{4,1,3,2,0:T(8,128)(2,1)} %get-tuple-element.8), channel_id=1, source_target_pairs={{1,0},{2,1},{3,2},{4,3},{5,4},{6,5},{7,6},{8,7},{9,8},{10,9},{11,1... | collective-permute-start | bytes 589832 | tf_op jit(solution)/shard_map/ppermute | solution.py:20
  11.1 1.5 %copy-start.2 = (bf16[1,288,3072]{2,1,0:T(8,128)(2,1)S(1)}, bf16[1,288,3072]{2,1,0:T(8,128)(2,1)}, u32[]{:S(2)}) copy-start(bf16[1,288,3072]{2,1,0:T(8,128)(2,1)} %param.18) | copy-start | bytes 5308420
  12.5 0.7 %copy-start.8 = (s32[1,4]{1,0:T(1,128)S(1)}, s32[1,4]{1,0:T(1,128)}, u32[]{:S(2)}) copy-start(s32[1,4]{1,0:T(1,128)} %param.14) | copy-start | bytes 52
  12.5 0.7 %copy-start.9 = (s32[1,4]{1,0:T(1,128)S(1)}, s32[1,4]{1,0:T(1,128)}, u32[]{:S(2)}) copy-start(s32[1,4]{1,0:T(1,128)} %param.13) | copy-start | bytes 52
  21.5 17.1 %copy-start.4 = (f32[1,288,64]{1,2,0:T(8,128)S(1)}, f32[1,288,64]{1,2,0:T(8,128)}, u32[]{:S(2)}) copy-start(f32[1,288,64]{1,2,0:T(8,128)} %param.19) | copy-start | bytes 221188
  21.5 17.1 %copy-start.5 = (f32[1,288,64]{1,2,0:T(8,128)S(1)}, f32[1,288,64]{1,2,0:T(8,128)}, u32[]{:S(2)}) copy-start(f32[1,288,64]{1,2,0:T(8,128)} %param.20) | copy-start | bytes 221188
  22.8 15.3 %all-to-all-start = ((bf16[16,2,608]{2,1,0:T(2,128)(2,1)}), bf16[16,2,608]{2,1,0:T(2,128)(2,1)S(1)}, u32[]{:S(2)}, u32[]{:S(2)}) async-start(bf16[16,2,608]{2,1,0:T(2,128)(2,1)} %reshape.232), calls=%async_computation | async-start | bytes 81920 | tf_op jit(solution)/shard_map/all_to_all | solution.py:148
  42.8 1.8 %collective-permute-start.2 = (f32[8,97,128]{2,1,0:T(8,128)S(1)}, f32[8,97,128]{2,1,0:T(8,128)S(1)}, u32[]{:S(2)}, u32[]{:S(2)}) collective-permute-start(f32[8,97,128]{2,1,0:T(8,128)S(1)} %pad_maximum_fusion), channel_id=1, source_target_pairs={{0,1},{1,0},{2,3},{3,2},{4,5},{5,4},{6,7},{7,6},{8,9},{9,8},{10,11... | collective-permute-start | bytes 1191944 | tf_op jit(solution)/shard_map/ppermute | solution.py:66
  45.2 4.9 %collective-permute-start.3 = (f32[2,97,128]{2,0,1:T(2,128)S(1)}, f32[2,97,128]{2,0,1:T(2,128)S(1)}, u32[]{:S(2)}, u32[]{:S(2)}) collective-permute-start(f32[2,97,128]{2,0,1:T(2,128)S(1)} %bitcast.87), channel_id=1, source_target_pairs={{0,2},{1,3},{2,0},{3,1},{4,6},{5,7},{6,4},{7,5},{8,10},{9,11},{10,... | collective-permute-start | bytes 297992 | tf_op jit(solution)/shard_map/ppermute | solution.py:77
  45.5 5.7 %collective-permute-start.4 = (f32[2,97,128]{2,0,1:T(2,128)S(1)}, f32[2,97,128]{2,0,1:T(2,128)S(1)}, u32[]{:S(2)}, u32[]{:S(2)}) collective-permute-start(f32[2,97,128]{2,0,1:T(2,128)S(1)} %bitcast.86), channel_id=1, source_target_pairs={{0,4},{1,5},{2,6},{3,7},{4,0},{5,1},{6,2},{7,3},{8,12},{9,13},{10,... | collective-permute-start | bytes 297992 | tf_op jit(solution)/shard_map/ppermute | solution.py:77
  46.1 7.3 %collective-permute-start.5 = (f32[2,97,128]{2,0,1:T(2,128)S(1)}, f32[2,97,128]{2,0,1:T(2,128)S(1)}, u32[]{:S(2)}, u32[]{:S(2)}) collective-permute-start(f32[2,97,128]{2,0,1:T(2,128)S(1)} %bitcast.85), channel_id=1, source_target_pairs={{0,6},{1,7},{2,4},{3,5},{4,2},{5,3},{6,0},{7,1},{8,14},{9,15},{10,... | collective-permute-start | bytes 297992 | tf_op jit(solution)/shard_map/ppermute | solution.py:77
  53.5 5.4 %collective-permute-start.6 = (f32[1,97,128]{2,0,1:T(1,128)S(1)}, f32[1,97,128]{2,0,1:T(1,128)S(1)}, u32[]{:S(2)}, u32[]{:S(2)}) collective-permute-start(f32[1,97,128]{2,0,1:T(1,128)S(1)} %constant_dynamic-slice_fusion.1), channel_id=1, source_target_pairs={{0,8},{1,9},{2,10},{3,11},{4,12},{5,13},{6,14},{7,15},{8,0},{9,1},... | collective-permute-start | bytes 149000 | tf_op jit(solution)/shard_map/ppermute | solution.py:77
  59.0 4.2 %collective-permute-start.7 = (f32[97,128]{1,0:T(8,128)S(1)}, f32[97,128]{1,0:T(8,128)S(1)}, u32[]{:S(2)}, u32[]{:S(2)}) collective-permute-start(f32[97,128]{1,0:T(8,128)S(1)} %bitcast.89), channel_id=1, source_target_pairs={{0,16},{16,0},{1,17},{17,1},{2,18},{18,2},{3,19},{19,3},{4,20},{20... | collective-permute-start | bytes 149000 | tf_op jit(solution)/shard_map/ppermute | solution.py:82

commit v13 on v12

--- a/solution.py
+++ b/solution.py
@@ -45,25 +45,24 @@
     return total
 
 
-def tree_reduce(grad_t, loss_row, nseq, ndp):
+def tree_reduce(grad_t, loss_line, nseq, ndp):
     nbits = nseq.bit_length() - 1
     assert nbits >= 1 and 1 << nbits == nseq and ndp & (ndp - 1) == 0
     groups = [2] + [1] * (nbits - 3) if nbits >= 3 else [1] * (nbits - 1)
     lat = grad_t.shape[0]
     share = grad_t.shape[1] // nseq
-    lanes = loss_row.shape[0]
+    lanes = 128
     dense = lat * share // lanes
     me = lax.axis_index("seq")
-    halves = grad_t.reshape(lat, nseq // 2, 2, share)
-    loss_rows = jnp.broadcast_to(loss_row[None, None, :], (nseq // 2, 1, lanes))
-
-    def half(bit):
-        part = lax.dynamic_index_in_dim(halves, bit, 2, keepdims=False)
-        part = part.transpose(1, 0, 2).reshape(nseq // 2, dense, lanes)
-        return jnp.concatenate([part, loss_rows], axis=1)
-
+    x = jnp.concatenate([grad_t, loss_line[None, :]], axis=0).reshape(lat + 1, nseq // 2, 2, share)
     bit = me & 1
-    x = half(bit) + lax.ppermute(half(1 - bit), "seq", [(i, i ^ 1) for i in range(nseq)])
+    keep = lax.dynamic_index_in_dim(x, bit, 2, keepdims=False)
+    send = lax.dynamic_index_in_dim(x, 1 - bit, 2, keepdims=False)
+    x = keep + lax.ppermute(send, "seq", [(i, i ^ 1) for i in range(nseq)])
+    body = x[:lat].transpose(1, 0, 2).reshape(nseq // 2, dense, lanes)
+    loss_rows = x[lat, :, : min(share, lanes)]
+    loss_rows = jnp.pad(loss_rows, ((0, 0), (0, lanes - loss_rows.shape[1])))[:, None, :]
+    x = jnp.concatenate([body, loss_rows], axis=1)
     tail = x.shape[1:]
     low = 1
     for width in groups:
@@ -179,12 +178,11 @@
     )
     ndp = lax.axis_size("dp")
     share = grad_t.shape[1] // nseq
-    lanes = 128
-    dense = LAT * share // lanes
-    assert ndp * CLIPS <= lanes and dense * lanes == LAT * share
+    dense = LAT * share // 128
+    assert ndp * CLIPS <= min(share, 128) and dense * 128 == LAT * share
     place = lax.axis_index("dp") * CLIPS
-    loss_row = lax.dynamic_update_slice(jnp.zeros((lanes,), jnp.float32), partial_loss, (place,))
-    summed = tree_reduce(grad_t, loss_row, nseq, ndp)
+    loss_row = lax.dynamic_update_slice(jnp.zeros((share,), jnp.float32), partial_loss, (place,))
+    summed = tree_reduce(grad_t, jnp.tile(loss_row, nseq), nseq, ndp)
     grad_mine = summed[:dense].reshape(LAT, share).T
     clip_loss = lax.dynamic_slice_in_dim(summed[dense], place, CLIPS).reshape(1, CLIPS)
     return (latent_out, clip_loss, grad_mine)

time: 64.9 us -> 65.1 us (level)
  local copies, waits for them, and re-layouts: 12.7 us -> 10.8 us
  other arithmetic: 2.75 us -> 3.98 us
  waiting for transfers between devices: 19.5 us -> 20.5 us
    dynamic_slice x4 -> x0, local copies, waits for them, and re-layouts: 1.77 us -> none  [the longest x3 1.42 us: half(): part = lax.dynamic_index_in_dim(halves, bit, 2, keepdims=False)]
    reshape x3 -> x0, local copies, waits for them, and re-layouts: 1.55 us -> none  [the longest x1 0.99 us: tree_reduce(): halves = grad_t.reshape(lat, nseq // 2, 2, share)]
    concatenate x0 -> x3, local copies, waits for them, and re-layouts: none -> 1.28 us  [the longest x2 1 us: tree_reduce(): jnp.concatenate([grad_t, loss_line[None, :]], axis=0)]
    concatenate x1, other arithmetic: 0.03 us -> 1.2 us  [tree_reduce(): jnp.concatenate([grad_t, loss_line[None, :]], axis=0)]
  transfers between devices with their start and end apart: 9 -> 9, of which waited for: 7 -> 7; matrix products, arithmetic and copies ran while one was open for 10% -> 9% of each run, Pallas kernels for 0% -> 0%
where the time goes in v13:
time: 65.1 us; the launch traced here: 64.8 us
  waiting for transfers between devices  20.5 us (31%)
  starting transfers between devices  18.6 us (29%)
  local copies, waits for them, and re-layouts  10.8 us (17%)
  matrix products  9.81 us (15%)
  other arithmetic  3.98 us (6%)
  between operations  1.14 us (2%)
    ppermute x4, waiting for transfers between devices, tree_reduce(): total = total + lax.ppermute(send, 'seq', pairs)  9.97 us
    all_to_all x1, starting transfers between devices, per_device(): lax.all_to_all(jnp.concatenate([outgoing, labels], axis=1), 'seq', split_...  8.63 us
    all_to_all x1, waiting for transfers between devices, per_device(): lax.all_to_all(jnp.concatenate([outgoing, labels], axis=1), 'seq', split_...  6.69 us
    conv_general_dilated x1, matrix products, causal_conv(): lax.conv_general_dilated(padded, kernel, (1, 1), 'VALID', dimension_numbe...  5.55 us
    unnamed x25, local copies, waits for them, and re-layouts  5.45 us
    ppermute x4, starting transfers between devices, tree_reduce(): total = total + lax.ppermute(send, 'seq', pairs)  3.96 us
    ppermute x1, starting transfers between devices, with_halo(): lax.ppermute(tail, axis, [(i, (i + 1) % count) for i in range(ends)])  3.06 us
    conv_general_dilated x1, matrix products, per_device(): lax.conv_general_dilated(cells, w_latent.reshape(4, 4, chans, LAT), (4, 4...  2.42 us
  transfers between devices with their start and end apart: 9, of which 7 were waited for; matrix products, arithmetic and copies ran while one was open for 9% of the time, Pallas kernels for 0%

profile of v13, /device:TPU:0, one launch (start us, length us, event | category | flops | bytes accessed | tf_op | source)
XLA Modules:
  0.0 64.8 jit_solution(15716760490620244332)
XLA Ops:
  0.6 0.0 copy-start
  0.6 1.7 %copy.32 = bf16[1,16,4,48,128]{4,1,3,2,0:T(8,128)(2,1)S(1)} copy(bf16[1,16,4,48,128]{4,3,2,1,0:T(8,128)(2,1)} %param.11) | data formatting | bytes 1572864 | tf_op args[0]
  2.3 0.0 copy-start.7
  2.4 0.0 copy-start.3
  2.4 0.0 copy-start.6
  2.4 0.0 copy-start.1
  2.4 0.8 %fusion.46 = (bf16[1,16,1,48,128]{4,1,3,2,0:T(8,128)(2,1)}, bf16[1,16,1,48,128]{4,1,3,2,0:T(8,128)(2,1)}) fusion(bf16[1,16,4,48,128]{4,1,3,2,0:T(8,128)(2,1)S(1)} %copy.32), kind=kLoop, calls=%fused_computation.106 | loop fusion | bytes 786432 | tf_op jit(solution)/shard_map/slice | solution.py:15
  3.2 3.1 %collective-permute-start = (bf16[1,16,1,48,128]{4,1,3,2,0:T(8,128)(2,1)}, bf16[1,16,1,48,128]{4,1,3,2,0:T(8,128)(2,1)}, u32[]{:S(2)}, u32[]{:S(2)}) collective-permute-start(bf16[1,16,1,48,128]{4,1,3,2,0:T(8,128)(2,1)} %get-tuple-element.7), channel_id=1, source_target_pairs={{0,1},{1,2},{2,3},{3,4},{4,5},{5,6},{6,7},{7,8},{8,9},{9,10},{10,1... | collective-permute-start | bytes 589832 | tf_op jit(solution)/shard_map/ppermute | solution.py:18
  6.2 1.3 %collective-permute-start.1 = (bf16[1,16,1,48,128]{4,1,3,2,0:T(8,128)(2,1)}, bf16[1,16,1,48,128]{4,1,3,2,0:T(8,128)(2,1)}, u32[]{:S(2)}, u32[]{:S(2)}) collective-permute-start(bf16[1,16,1,48,128]{4,1,3,2,0:T(8,128)(2,1)} %get-tuple-element.8), channel_id=1, source_target_pairs={{1,0},{2,1},{3,2},{4,3},{5,4},{6,5},{7,6},{8,7},{9,8},{10,9},{11,1... | collective-permute-start | bytes 589832 | tf_op jit(solution)/shard_map/ppermute | solution.py:20
  7.5 2.3 %copy.36 = bf16[3,3,3,128,128]{3,4,0,2,1:T(8,128)(2,1)} copy(bf16[3,3,3,128,128]{4,3,2,1,0:T(8,128)(2,1)} %param.16) | data formatting | bytes 1769472 | tf_op args[5]
  9.8 0.2 reduce-window.4
  10.0 0.1 convert_reduce_fusion.1
  10.1 0.1 select_reduce_fusion
  10.2 0.2 reshape.162
  10.4 0.2 fusion.12
  10.6 0.1 broadcast_in_dim.2
  10.6 0.1 reshape.174
  10.7 0.2 convolution_reduce_fusion
  10.9 0.1 reshape.177
  11.1 0.0 copy-start.2
  11.1 0.3 convert_reduce_fusion
  11.4 0.6 fusion.3
  12.0 0.5 copy-done.2
  12.5 0.7 %fusion.4 = bf16[288,3072]{1,0:T(8,128)(2,1)S(1)} fusion(bf16[1,288,3072]{2,1,0:T(8,128)(2,1)S(1)} %copy-done.2, f32[288]{0:T(512)S(1)} %add_rsqrt_fusion, f32[288]{0:T(512)S(1)} %broadcast_multiply_fusion), kind=kLoop, calls=%fused_computation.6 | loop fusion | flops 3538944 | bytes 3541248 | tf_op jit(solution)/shard_map/convert_element_type | solution.py:167
  13.3 0.0 collective-permute-done
  13.3 5.6 %fusion.7 = f32[16,4,48,384]{3,0,2,1:T(8,128)S(1)} fusion(bf16[3,3,128,384]{2,3,1,0:T(8,128)(2,1)} %bitcast.91, bf16[1,16,1,48,128]{4,1,3,2,0:T(8,128)(2,1)} %collective-permute-done.1, bf16[1,16,4,48,128]{4,1,3,2,0:T(8,128)(2,1)S(1)} %copy.32, bf16[1,16,1,48,128]{4,1,3,2,0:T(8,128)(2,1)} %collective-permute-done), kind=kOutput, calls=%fused_computation.14 | convolution fusion | flops 2683699200 | bytes 6782976 | tf_op jit(solution)/shard_map/conv_general_dilated | solution.py:32
  18.9 0.1 slice.47
  19.0 0.1 slice.48
  19.1 2.4 %convolution_convert_fusion.1 = bf16[16,1,12,64]{3,0,2,1:T(8,128)(2,1)S(1)} fusion(f32[16,4,48,384]{3,0,2,1:T(8,128)S(1)} %fusion.7, f32[14,4,48,128]{3,0,2,1:T(8,128)S(1)} %slice.48, f32[15,4,48,128]{3,0,2,1:T(8,128)S(1)} %slice.47, f32[16]{0:T(128)S(1)} %get-tuple-element.13, f32[16]{0:T(128)S(1)} %get-tuple-element.12, ...), kind=kOutput, calls=%fused_computation.21 | convolution fusion | flops 54669312 | bytes 5792768 | tf_op jit(solution)/shard_map/conv_general_dilated | solution.py:114
  21.5 0.0 copy-start.4
  21.5 0.0 copy-start.5
  21.6 0.2 convolution_convert_fusion
  21.8 0.1 copy.40
  22.0 0.7 %reshape.186 = bf16[16,2,608]{2,1,0:T(2,128)(2,1)} reshape(bf16[16,19,64]{2,1,0:T(8,128)(2,1)S(1)} %fusion.31) | data formatting | bytes 77824
  22.8 8.6 %all-to-all-start = ((bf16[16,2,608]{2,1,0:T(2,128)(2,1)}), bf16[16,2,608]{2,1,0:T(2,128)(2,1)S(1)}, u32[]{:S(2)}, u32[]{:S(2)}) async-start(bf16[16,2,608]{2,1,0:T(2,128)(2,1)} %reshape.186), calls=%async_computation | async-start | bytes 81920 | tf_op jit(solution)/shard_map/all_to_all | solution.py:147
  31.4 6.7 %all-to-all-done = bf16[16,2,608]{2,1,0:T(2,128)(2,1)S(1)} async-done(((bf16[16,2,608]{2,1,0:T(2,128)(2,1)}), bf16[16,2,608]{2,1,0:T(2,128)(2,1)S(1)}, u32[]{:S(2)}, u32[]{:S(2)}) %all-to-all-start) | async-done | bytes 38944 | tf_op jit(solution)/shard_map/all_to_all | solution.py:147
  38.1 0.1 reshape.187
  38.3 0.1 reshape.171
  38.4 0.1 fusion.39
  38.5 0.1 copy.42
  38.7 0.7 %multiply_reduce_fusion = (f32[288]{0:T(512)S(1)}, f32[288,64]{0,1:T(8,128)S(1)}) fusion(f32[288,64]{0,1:T(8,128)S(1)} %copy.42, f32[1,288,64]{1,2,0:T(8,128)S(1)} %copy-done.4, f32[288]{0:T(512)S(1)} %broadcast_subtract_fusion, f32[1,288,64]{1,2,0:T(8,128)S(1)} %copy-done.5, f32[288]{0:T(512)S(1)} %fusion.39, bf16[288,3072]{1,0:T(8,128)(2,1)S(1)} %fusion.4, ...), kind=kOutput, calls=%fused_computation.64 | convolution fusion | flops 113374944 | bytes 2461056 | tf_op jit(solution)/shard_map/dot_general | solution.py:168
  39.4 0.2 fusion.38
  39.6 0.5 fusion.34
  40.1 1.0 %concatenate.24 = f32[64,8,2,192]{3,2,1,0:T(2,128)S(1)} reshape(f32[64,3072]{1,0:T(8,128)S(1)} %fusion.34) | data formatting | bytes 1572864 | tf_op jit(solution)/shard_map/concatenate | solution.py:57
  41.1 0.2 bitcast_dynamic-update-slice_fusion
  41.4 1.2 %fusion.15 = (f32[65,8,1,192]{3,2,1,0:T(1,128)S(1)}, f32[65,8,1,192]{3,2,1,0:T(1,128)S(1)}) fusion(s32[]{:T(128)S(6)} %select_n.34, f32[1,8,2,192]{3,2,1,0:T(2,128)S(1)} %concatenate.25, f32[64,8,2,192]{3,2,1,0:T(2,128)S(1)} %concatenate.24, s32[]{:T(128)S(6)} %select_n.35), kind=kLoop, calls=%fused_computation.32 | loop fusion | flops 199680 | bytes 1597448 | tf_op jit(solution)/shard_map/concatenate | solution.py:57
  42.6 0.1 collective-permute-start.2
  42.7 1.9 %collective-permute-done.2 = f32[65,8,192]{2,1,0:T(8,128)S(1)} collective-permute-done((f32[65,8,192]{2,1,0:T(8,128)S(1)}, f32[65,8,192]{2,1,0:T(8,128)S(1)}, u32[]{:S(2)}, u32[]{:S(2)}) %collective-permute-start.2) | collective-permute-done | bytes 399392 | tf_op jit(solution)/shard_map/ppermute | solution.py:61
  44.6 0.1 bitcast_add_fusion
  44.7 0.2 copy.43
  44.9 0.3 concatenate.27
  45.2 0.4 collective-permute-start.3
  45.6 0.6 collective-permute-start.4
  46.2 2.6 %collective-permute-start.5 = (f32[2,97,128]{2,1,0:T(8,128)S(1)}, f32[2,97,128]{2,1,0:T(8,128)S(1)}, u32[]{:S(2)}, u32[]{:S(2)}) collective-permute-start(f32[2,97,128]{2,1,0:T(8,128)S(1)} %get-tuple-element.11), channel_id=1, source_target_pairs={{0,6},{1,7},{2,4},{3,5},{4,2},{5,3},{6,0},{7,1},{8,14},{9,15},{10,... | collective-permute-start | bytes 297992 | tf_op jit(solution)/shard_map/ppermute | solution.py:76
  48.8 1.5 %collective-permute-done.3 = f32[2,97,128]{2,1,0:T(8,128)S(1)} collective-permute-done((f32[2,97,128]{2,1,0:T(8,128)S(1)}, f32[2,97,128]{2,1,0:T(8,128)S(1)}, u32[]{:S(2)}, u32[]{:S(2)}) %collective-permute-start.3) | collective-permute-done | bytes 99360 | tf_op jit(solution)/shard_map/ppermute | solution.py:76
  50.3 1.1 %collective-permute-done.4 = f32[2,97,128]{2,1,0:T(8,128)S(1)} collective-permute-done((f32[2,97,128]{2,1,0:T(8,128)S(1)}, f32[2,97,128]{2,1,0:T(8,128)S(1)}, u32[]{:S(2)}, u32[]{:S(2)}) %collective-permute-start.4) | collective-permute-done | bytes 99360 | tf_op jit(solution)/shard_map/ppermute | solution.py:76
  51.4 2.3 %collective-permute-done.5 = f32[2,97,128]{2,1,0:T(8,128)S(1)} collective-permute-done((f32[2,97,128]{2,1,0:T(8,128)S(1)}, f32[2,97,128]{2,1,0:T(8,128)S(1)}, u32[]{:S(2)}, u32[]{:S(2)}) %collective-permute-start.5) | collective-permute-done | bytes 99360 | tf_op jit(solution)/shard_map/ppermute | solution.py:76
  53.8 0.4 collective-permute-start.6
  54.2 5.0 %collective-permute-done.6 = f32[1,97,128]{2,1,0:T(8,128)S(1)} collective-permute-done((f32[1,97,128]{2,1,0:T(8,128)S(1)}, f32[1,97,128]{2,1,0:T(8,128)S(1)}, u32[]{:S(2)}, u32[]{:S(2)}) %collective-permute-start.6) | collective-permute-done | bytes 49696 | tf_op jit(solution)/shard_map/ppermute | solution.py:76
  59.2 1.6 %collective-permute-start.7 = (f32[97,128]{1,0:T(8,128)S(1)}, f32[97,128]{1,0:T(8,128)S(1)}, u32[]{:S(2)}, u32[]{:S(2)}) collective-permute-start(f32[97,128]{1,0:T(8,128)S(1)} %add_bitcast_fusion), channel_id=1, source_target_pairs={{0,16},{16,0},{1,17},{17,1},{2,18},{18,2},{3,19},{19,3},{4,20},{20... | collective-permute-start | bytes 149000 | tf_op jit(solution)/shard_map/ppermute | solution.py:81
  60.8 0.7 %reshape.163 = bf16[1,16,1,768]{3,1,2,0:T(8,128)(2,1)} reshape(bf16[16,1,12,64]{3,2,0,1:T(8,128)(2,1)S(1)} %copy.38) | data formatting | bytes 49152 | tf_op jit(solution)/shard_map/reshape | solution.py:122
  61.5 1.9 %collective-permute-done.7 = f32[97,128]{1,0:T(8,128)S(1)} collective-permute-done((f32[97,128]{1,0:T(8,128)S(1)}, f32[97,128]{1,0:T(8,128)S(1)}, u32[]{:S(2)}, u32[]{:S(2)}) %collective-permute-start.7) | collective-permute-done | bytes 49696 | tf_op jit(solution)/shard_map/ppermute | solution.py:81
  63.5 0.7 %reshape.169 = f32[64,192]{1,0:T(8,128)} reshape(f32[96,128]{1,0:T(8,128)S(1)} %slice.54) | data formatting | bytes 98304 | tf_op jit(solution)/shard_map/reshape | solution.py:186
  64.2 0.6 constant_dynamic-slice_fusion
  (42 shorter events, 0.5 us)
Async XLA Ops:
  0.6 38.0 %copy-start = (bf16[3072,64]{0,1:T(8,128)(2,1)S(1)}, bf16[3072,64]{0,1:T(8,128)(2,1)}, u32[]{:S(2)}) copy-start(bf16[3072,64]{0,1:T(8,128)(2,1)} %param.21) | copy-start | bytes 1179652
  2.3 7.5 %copy-start.7 = (s32[1,4]{1,0:T(1,128)S(1)}, s32[1,4]{1,0:T(1,128)}, u32[]{:S(2)}) copy-start(s32[1,4]{1,0:T(1,128)} %param.12) | copy-start | bytes 52
  2.4 7.8 %copy-start.3 = (bf16[2048,64]{0,1:T(8,128)(2,1)S(1)}, bf16[2048,64]{0,1:T(8,128)(2,1)}, u32[]{:S(2)}) copy-start(bf16[2048,64]{0,1:T(8,128)(2,1)} %param.17) | copy-start | bytes 786436
  2.4 8.0 %copy-start.6 = (s32[1,1,192,1]{2,3,1,0:T(1,128)S(1)}, s32[1,1,192,1]{2,3,1,0:T(1,128)}, u32[]{:S(2)}) copy-start(s32[1,1,192,1]{2,3,1,0:T(1,128)} %param.15) | copy-start | bytes 2308
  2.4 8.7 %copy-start.1 = (bf16[1,288,3072]{2,1,0:T(8,128)(2,1)S(1)}, bf16[1,288,3072]{2,1,0:T(8,128)(2,1)}, u32[]{:S(2)}) copy-start(bf16[1,288,3072]{2,1,0:T(8,128)(2,1)} %param.18) | copy-start | bytes 5308420
  3.2 10.1 %collective-permute-start = (bf16[1,16,1,48,128]{4,1,3,2,0:T(8,128)(2,1)}, bf16[1,16,1,48,128]{4,1,3,2,0:T(8,128)(2,1)}, u32[]{:S(2)}, u32[]{:S(2)}) collective-permute-start(bf16[1,16,1,48,128]{4,1,3,2,0:T(8,128)(2,1)} %get-tuple-element.7), channel_id=1, source_target_pairs={{0,1},{1,2},{2,3},{3,4},{4,5},{5,6},{6,7},{7,8},{8,9},{9,10},{10,1... | collective-permute-start | bytes 589832 | tf_op jit(solution)/shard_map/ppermute | solution.py:18
  6.2 7.1 %collective-permute-start.1 = (bf16[1,16,1,48,128]{4,1,3,2,0:T(8,128)(2,1)}, bf16[1,16,1,48,128]{4,1,3,2,0:T(8,128)(2,1)}, u32[]{:S(2)}, u32[]{:S(2)}) collective-permute-start(bf16[1,16,1,48,128]{4,1,3,2,0:T(8,128)(2,1)} %get-tuple-element.8), channel_id=1, source_target_pairs={{1,0},{2,1},{3,2},{4,3},{5,4},{6,5},{7,6},{8,7},{9,8},{10,9},{11,1... | collective-permute-start | bytes 589832 | tf_op jit(solution)/shard_map/ppermute | solution.py:20
  11.1 1.5 %copy-start.2 = (bf16[1,288,3072]{2,1,0:T(8,128)(2,1)S(1)}, bf16[1,288,3072]{2,1,0:T(8,128)(2,1)}, u32[]{:S(2)}) copy-start(bf16[1,288,3072]{2,1,0:T(8,128)(2,1)} %param.18) | copy-start | bytes 5308420
  12.5 0.7 %copy-start.8 = (s32[1,4]{1,0:T(1,128)S(1)}, s32[1,4]{1,0:T(1,128)}, u32[]{:S(2)}) copy-start(s32[1,4]{1,0:T(1,128)} %param.14) | copy-start | bytes 52
  12.5 0.7 %copy-start.9 = (s32[1,4]{1,0:T(1,128)S(1)}, s32[1,4]{1,0:T(1,128)}, u32[]{:S(2)}) copy-start(s32[1,4]{1,0:T(1,128)} %param.13) | copy-start | bytes 52
  21.5 17.1 %copy-start.4 = (f32[1,288,64]{1,2,0:T(8,128)S(1)}, f32[1,288,64]{1,2,0:T(8,128)}, u32[]{:S(2)}) copy-start(f32[1,288,64]{1,2,0:T(8,128)} %param.19) | copy-start | bytes 221188
  21.5 17.1 %copy-start.5 = (f32[1,288,64]{1,2,0:T(8,128)S(1)}, f32[1,288,64]{1,2,0:T(8,128)}, u32[]{:S(2)}) copy-start(f32[1,288,64]{1,2,0:T(8,128)} %param.20) | copy-start | bytes 221188
  22.8 15.3 %all-to-all-start = ((bf16[16,2,608]{2,1,0:T(2,128)(2,1)}), bf16[16,2,608]{2,1,0:T(2,128)(2,1)S(1)}, u32[]{:S(2)}, u32[]{:S(2)}) async-start(bf16[16,2,608]{2,1,0:T(2,128)(2,1)} %reshape.186), calls=%async_computation | async-start | bytes 81920 | tf_op jit(solution)/shard_map/all_to_all | solution.py:147
  42.6 2.0 %collective-permute-start.2 = (f32[65,8,192]{2,1,0:T(8,128)S(1)}, f32[65,8,192]{2,1,0:T(8,128)S(1)}, u32[]{:S(2)}, u32[]{:S(2)}) collective-permute-start(f32[65,8,192]{2,1,0:T(8,128)S(1)} %bitcast.92), channel_id=1, source_target_pairs={{0,1},{1,0},{2,3},{3,2},{4,5},{5,4},{6,7},{7,6},{8,9},{9,8},{10,11... | collective-permute-start | bytes 1198088 | tf_op jit(solution)/shard_map/ppermute | solution.py:61
  45.2 5.1 %collective-permute-start.3 = (f32[2,97,128]{2,1,0:T(8,128)S(1)}, f32[2,97,128]{2,1,0:T(8,128)S(1)}, u32[]{:S(2)}, u32[]{:S(2)}) collective-permute-start(f32[2,97,128]{2,1,0:T(8,128)S(1)} %get-tuple-element.9), channel_id=1, source_target_pairs={{0,2},{1,3},{2,0},{3,1},{4,6},{5,7},{6,4},{7,5},{8,10},{9,11},{10,... | collective-permute-start | bytes 297992 | tf_op jit(solution)/shard_map/ppermute | solution.py:76
  45.6 5.8 %collective-permute-start.4 = (f32[2,97,128]{2,1,0:T(8,128)S(1)}, f32[2,97,128]{2,1,0:T(8,128)S(1)}, u32[]{:S(2)}, u32[]{:S(2)}) collective-permute-start(f32[2,97,128]{2,1,0:T(8,128)S(1)} %get-tuple-element.10), channel_id=1, source_target_pairs={{0,4},{1,5},{2,6},{3,7},{4,0},{5,1},{6,2},{7,3},{8,12},{9,13},{10,... | collective-permute-start | bytes 297992 | tf_op jit(solution)/shard_map/ppermute | solution.py:76
  46.2 7.6 %collective-permute-start.5 = (f32[2,97,128]{2,1,0:T(8,128)S(1)}, f32[2,97,128]{2,1,0:T(8,128)S(1)}, u32[]{:S(2)}, u32[]{:S(2)}) collective-permute-start(f32[2,97,128]{2,1,0:T(8,128)S(1)} %get-tuple-element.11), channel_id=1, source_target_pairs={{0,6},{1,7},{2,4},{3,5},{4,2},{5,3},{6,0},{7,1},{8,14},{9,15},{10,... | collective-permute-start | bytes 297992 | tf_op jit(solution)/shard_map/ppermute | solution.py:76
  53.8 5.4 %collective-permute-start.6 = (f32[1,97,128]{2,1,0:T(8,128)S(1)}, f32[1,97,128]{2,1,0:T(8,128)S(1)}, u32[]{:S(2)}, u32[]{:S(2)}) collective-permute-start(f32[1,97,128]{2,1,0:T(8,128)S(1)} %constant_dynamic-slice_fusion.1), channel_id=1, source_target_pairs={{0,8},{1,9},{2,10},{3,11},{4,12},{5,13},{6,14},{7,15},{8,0},{9,1},... | collective-permute-start | bytes 149000 | tf_op jit(solution)/shard_map/ppermute | solution.py:76
  59.2 4.2 %collective-permute-start.7 = (f32[97,128]{1,0:T(8,128)S(1)}, f32[97,128]{1,0:T(8,128)S(1)}, u32[]{:S(2)}, u32[]{:S(2)}) collective-permute-start(f32[97,128]{1,0:T(8,128)S(1)} %add_bitcast_fusion), channel_id=1, source_target_pairs={{0,16},{16,0},{1,17},{17,1},{2,18},{18,2},{3,19},{19,3},{4,20},{20... | collective-permute-start | bytes 149000 | tf_op jit(solution)/shard_map/ppermute | solution.py:81

commit v14 on v12

--- a/solution.py
+++ b/solution.py
@@ -1,48 +1,57 @@
 import jax
 import jax.numpy as jnp
 from jax import lax
+from jax.experimental import pallas as pl
+from jax.experimental.pallas import tpu as pltpu
 from jax.sharding import PartitionSpec as P
 
 LAT = 64
 CLIPS = 4
 
 
-def with_halo(cells, sides, width):
-    for axis, dim in sides:
-        count = lax.axis_size(axis)
-        ends = count - 1
-        head = lax.slice_in_dim(cells, 0, width, axis=dim)
-        tail = lax.slice_in_dim(cells, cells.shape[dim] - width, cells.shape[dim], axis=dim)
-        cells = jnp.concatenate(
-            [
-                lax.ppermute(tail, axis, [(i, (i + 1) % count) for i in range(ends)]),
-                cells,
-                lax.ppermute(head, axis, [((i + 1) % count, i) for i in range(ends)]),
-            ],
-            axis=dim,
-        )
-    return cells
-
-
-def causal_conv(rimmed, conv_weight, keep):
-    nframes = rimmed.shape[0]
-    chans = rimmed.shape[-1]
-    padded = jnp.pad(rimmed, ((0, 0), (0, 0), (1, 1), (0, 0)))
-    kernel = jnp.transpose(conv_weight, (1, 2, 3, 0, 4)).reshape(3, 3, chans, 3 * chans)
-    each = lax.conv_general_dilated(
-        padded,
-        kernel,
-        (1, 1),
-        "VALID",
-        dimension_numbers=("NHWC", "HWIO", "NHWC"),
-        preferred_element_type=jnp.float32,
-    )
-    total = each[..., :chans]
-    for lag in (1, 2):
-        part = each[: nframes - lag, ..., lag * chans : (lag + 1) * chans]
-        part = jnp.pad(part, ((lag, 0), (0, 0), (0, 0), (0, 0)))
-        total = total + part * keep[lag][:, None, None, None]
-    return total
+def _conv_kernel(keep_ref, frames_ref, top_ref, bottom_ref, w_ref, cells_ref):
+    nframes, nrows, width, chans = frames_ref.shape
+    col = lax.broadcasted_iota(jnp.int32, (nrows + 2, width, chans), 1)
+
+    def slab(g):
+        x = jnp.concatenate([top_ref[g], frames_ref[g], bottom_ref[g]], axis=0).astype(jnp.float32)
+        left = jnp.where(col == 0, 0.0, pltpu.roll(x, 1, 1))
+        right = jnp.where(col == width - 1, 0.0, pltpu.roll(x, width - 1, 1))
+        return jnp.concatenate([left, x, right], axis=-1).astype(jnp.bfloat16)
+
+    def body(f, carry):
+        acc = jnp.zeros((nrows * width, chans), jnp.float32)
+        for lag in range(3):
+            g = jnp.maximum(f - lag, 0)
+            wide = slab(g)
+            part = jnp.zeros((nrows * width, chans), jnp.float32)
+            for i in range(3):
+                rows = wide[i : i + nrows].reshape(nrows * width, 3 * chans)
+                part = part + jnp.dot(rows, w_ref[lag, i], preferred_element_type=jnp.float32)
+            acc = acc + part * keep_ref[lag, f]
+        conv = acc.reshape(nrows, width, chans)
+        out = frames_ref[f].astype(jnp.float32) + conv * jax.nn.sigmoid(conv)
+        cells_ref[f] = out.astype(cells_ref.dtype)
+        return carry
+
+    lax.fori_loop(0, nframes, body, 0)
+
+
+def conv_cells(keep, local, top, bottom, conv_weight):
+    nframes, nrows, width, chans = local.shape
+    w = conv_weight.reshape(3, 3, 3 * chans, chans)
+    vmem = pltpu.VMEM
+    return pl.pallas_call(
+        _conv_kernel,
+        out_shape=jax.ShapeDtypeStruct(local.shape, jnp.bfloat16),
+        in_specs=[pl.BlockSpec(memory_space=pltpu.SMEM)] + [pl.BlockSpec(memory_space=vmem)] * 4,
+        out_specs=pl.BlockSpec(memory_space=vmem),
+        cost_estimate=pl.CostEstimate(
+            flops=2 * 27 * nframes * nrows * width * chans * chans,
+            bytes_accessed=2 * (2 * local.size + top.size + bottom.size + conv_weight.size),
+            transcendentals=nframes * nrows * width * chans,
+        ),
+    )(keep, local, top, bottom, w)
 
 
 def tree_reduce(grad_t, loss_row, nseq, ndp):
@@ -109,9 +118,10 @@
     clip_hot = (clip_of[:, None] == jnp.arange(CLIPS, dtype=jnp.int32)[None, :]).astype(jnp.int32)
     starts = jnp.sum(clip_hot * (ends - counts)[None, :], axis=1)
     keep = jnp.stack([(index - lag >= starts).astype(jnp.float32) for lag in range(3)])
-    rimmed = with_halo(frames, (("seq", 2),), 1)[0]
-    conv = causal_conv(rimmed, conv_weight, keep)
-    cells = (local.astype(jnp.float32) + jax.nn.silu(conv)).astype(jnp.bfloat16)
+    ends_at = nseq - 1
+    top = lax.ppermute(local[:, -1:], "seq", [(i, i + 1) for i in range(ends_at)])
+    bottom = lax.ppermute(local[:, :1], "seq", [(i + 1, i) for i in range(ends_at)])
+    cells = conv_cells(keep, local, top, bottom, conv_weight)
     tokens = lax.conv_general_dilated(
         cells,
         w_latent.reshape(4, 4, chans, LAT),

time: 64.9 us -> 70.7 us (1.089)
  Pallas kernels: 0 us -> 10.8 us
  other arithmetic: 2.75 us -> 8.29 us
  matrix products: 9.8 us -> 4.32 us
  local copies, waits for them, and re-layouts: 12.7 us -> 9.18 us
  waiting for transfers between devices: 19.5 us -> 18.5 us
    pallas_call x0 -> x1, Pallas kernels: none -> 10.8 us  [conv_cells(): pl.pallas_call(_conv_kernel, out_shape=jax.ShapeDtypeStruct(local.shape,...]
    conv_general_dilated x1 -> x0, matrix products: 5.55 us -> none  [causal_conv(): lax.conv_general_dilated(padded, kernel, (1, 1), 'VALID', dimension_numbe...]
    unnamed x25 -> x23, local copies, waits for them, and re-layouts: 5.43 us -> 1.65 us
    reduce_sum x1, other arithmetic: 0.32 us -> 1.84 us  [per_device(): mean = jnp.mean(states, axis=1, keepdims=True)]
    convert_element_type x1, other arithmetic: 0.68 us -> 2.14 us  [per_device(): normed = (centred * lax.rsqrt(var + 1e-06)).astype(jnp.bfloat16)]
    another operation x1 -> x2, other arithmetic: 0.18 us -> 1.42 us
    ppermute x4, waiting for transfers between devices: 9.64 us -> 8.6 us  [tree_reduce(): total = total + lax.ppermute(send, 'seq', pairs)]
    dot_general x1, matrix products: 0.16 us -> 0.93 us  [per_device(): jnp.dot(upto, owner_hot.astype(jnp.bfloat16), preferred_element_type=jnp....]
  transfers between devices with their start and end apart: 9 -> 9, of which waited for: 7 -> 6; matrix products, arithmetic and copies ran while one was open for 10% -> 15% of each run, Pallas kernels for 0% -> 0%
where the time goes in v14:
time: 70.7 us; the launch traced here: 70.3 us
  waiting for transfers between devices  18.5 us (26%)
  starting transfers between devices  18.2 us (26%)
  Pallas kernels  10.8 us (15%)
  local copies, waits for them, and re-layouts  9.18 us (13%)
  other arithmetic  8.29 us (12%)
  matrix products  4.32 us (6%)
  between operations  1.09 us (2%)
    pallas_call x1, Pallas kernels, conv_cells(): pl.pallas_call(_conv_kernel, out_shape=jax.ShapeDtypeStruct(local.shape,...  10.8 us
    ppermute x4, waiting for transfers between devices, tree_reduce(): total = total + lax.ppermute(send, 'seq', pairs)  8.6 us
    all_to_all x1, starting transfers between devices, per_device(): lax.all_to_all(jnp.concatenate([outgoing, labels], axis=1), 'seq', split_...  7.95 us
    all_to_all x1, waiting for transfers between devices, per_device(): lax.all_to_all(jnp.concatenate([outgoing, labels], axis=1), 'seq', split_...  6.69 us
    ppermute x4, starting transfers between devices, tree_reduce(): total = total + lax.ppermute(send, 'seq', pairs)  4.25 us
    ppermute x1, starting transfers between devices, per_device(): lax.ppermute(local[:, -1:], 'seq', [(i, i + 1) for i in range(ends_at)])  3.04 us
    convert_element_type x1, other arithmetic, per_device(): normed = (centred * lax.rsqrt(var + 1e-06)).astype(jnp.bfloat16)  2.14 us
    ppermute x1, waiting for transfers between devices, tree_reduce(): x = x + lax.ppermute(x, 'dp', [(i, i ^ 1 << k) for i in range(ndp)])  1.92 us
  transfers between devices with their start and end apart: 9, of which 6 were waited for; matrix products, arithmetic and copies ran while one was open for 15% of the time, Pallas kernels for 0%

profile of v14, /device:TPU:0, one launch (start us, length us, event | category | flops | bytes accessed | tf_op | source)
XLA Modules:
  0.0 70.3 jit_solution(6694821049680486518)
XLA Ops:
  0.6 0.0 copy-start
  0.6 0.0 copy-start.1
  0.7 1.2 %fusion.25 = (bf16[16,1,48,128]{3,2,1,0:T(8,128)(2,1)S(1)}, bf16[16,1,48,128]{3,2,1,0:T(8,128)(2,1)S(1)}) fusion(bf16[16,4,48,128]{3,2,1,0:T(8,128)(2,1)} %bitcast.79), kind=kLoop, calls=%fused_computation.81 | loop fusion | bytes 786432 | tf_op jit(solution)/shard_map/slice | solution.py:123
  1.9 1.3 %collective-permute-start.1 = (bf16[16,1,48,128]{3,2,1,0:T(8,128)(2,1)S(1)}, bf16[16,1,48,128]{3,2,1,0:T(8,128)(2,1)S(1)}, u32[]{:S(2)}, u32[]{:S(2)}) collective-permute-start(bf16[16,1,48,128]{3,2,1,0:T(8,128)(2,1)S(1)} %get-tuple-element.7), channel_id=1, source_target_pairs={{1,0},{2,1},{3,2},{4,3},{5,4},{6,5},{7,6},{8,7},{9,8},{10,9},{11,1... | collective-permute-start | bytes 589832 | tf_op jit(solution)/shard_map/ppermute | solution.py:123
  3.2 3.0 %collective-permute-start = (bf16[16,1,48,128]{3,2,1,0:T(8,128)(2,1)S(1)}, bf16[16,1,48,128]{3,2,1,0:T(8,128)(2,1)S(1)}, u32[]{:S(2)}, u32[]{:S(2)}) collective-permute-start(bf16[16,1,48,128]{3,2,1,0:T(8,128)(2,1)S(1)} %get-tuple-element.8), channel_id=1, source_target_pairs={{0,1},{1,2},{2,3},{3,4},{4,5},{5,6},{6,7},{7,8},{8,9},{9,10},{10,1... | collective-permute-start | bytes 589832 | tf_op jit(solution)/shard_map/ppermute | solution.py:122
  6.2 0.8 %reduce-window.4 = s32[4,1]{0,1:T(1,128)S(1)} reduce-window(s32[4,1]{0,1:T(1,128)} %bitcast.88, s32[]{:T(128)} %constant.70.clone.1), window={size=4x1 pad=3_0x0_0}, to_apply=%region_0.0 | reduce-window | flops 12 | bytes 36 | tf_op jit(solution)/shard_map/reduce-window
  7.1 0.7 fusion.22
  7.7 0.1 convert_reduce_fusion.1
  7.8 0.1 select_reduce_fusion
  7.9 0.9 %fusion.5 = f32[192]{0:T(256)S(1)} fusion(s32[192]{0:T(256)} %bitcast.86), kind=kOutput, calls=%fused_computation.11 | convolution fusion | flops 1240896 | bytes 1536 | tf_op jit(solution)/shard_map/dot_general | solution.py:142
  8.8 0.7 add_add_fusion.1
  9.5 1.8 %convert_reduce_fusion = f32[288]{0:T(512)S(1)} fusion(bf16[1,288,3072]{2,1,0:T(8,128)(2,1)} %param.18), kind=kLoop, calls=%fused_computation | loop fusion | flops 1769184 | bytes 1770624 | tf_op jit(solution)/shard_map/reduce_sum | solution.py:175
  11.4 0.6 fusion.3
  12.0 0.1 broadcast_in_dim.6
  12.1 0.1 reshape.249
  12.2 0.2 convolution_reduce_fusion
  12.4 0.1 reshape.252
  12.5 0.2 reshape.233
  12.7 0.0 copy-start.5
  12.7 0.0 copy-start.6
  12.7 0.0 copy-start.7
  12.7 2.1 %fusion.4 = bf16[288,3072]{1,0:T(8,128)(2,1)S(1)} fusion(bf16[1,288,3072]{2,1,0:T(8,128)(2,1)} %param.18, f32[288]{0:T(512)S(1)} %add_rsqrt_fusion, f32[288]{0:T(512)S(1)} %broadcast_multiply_fusion), kind=kLoop, calls=%fused_computation.6 | loop fusion | flops 3538944 | bytes 3541248 | tf_op jit(solution)/shard_map/convert_element_type | solution.py:178
  14.9 0.6 add_convert_fusion.keep_ref
  15.5 0.7 copy-done.8
  16.2 0.1 copy-done.9
  16.3 10.8 %shard_map.130 = bf16[16,4,48,128]{3,2,1,0:T(8,128)(2,1)} custom-call(f32[3,16]{1,0:T(4,128)} %add_convert_fusion.keep_ref, bf16[16,4,48,128]{3,2,1,0:T(8,128)(2,1)} %bitcast.80, bf16[16,1,48,128]{3,2,1,0:T(8,128)(2,1)} %copy-done.9, bf16[16,1,48,128]{3,2,1,0:T(8,128)(2,1)} %copy-done.8, bf16[3,3,384,128]{3,2,1,0:T(8,128)(2,1)} %bitcast.89), custom_call_target="tpu_custom_call" | custom-call | flops 2717908992 | bytes 2850816 | tf_op jit(solution)/shard_map/pallas_call | solution.py:44
  27.1 1.7 %convolution_convert_fusion.1 = bf16[16,1,12,64]{3,0,2,1:T(8,128)(2,1)S(1)} fusion(bf16[16,4,48,128]{3,2,1,0:T(8,128)(2,1)} %shard_map.130, bf16[4,4,128,64]{2,1,0,3:T(4,128)(2,1)S(1)} %reshape.233), kind=kOutput, calls=%fused_computation.9 | convolution fusion | flops 50343936 | bytes 1073152 | tf_op jit(solution)/shard_map/conv_general_dilated | solution.py:125
  28.8 0.2 convolution_convert_fusion
  29.1 0.1 copy.40
  29.3 0.7 %reshape.261 = bf16[16,2,608]{2,1,0:T(2,128)(2,1)} reshape(bf16[16,19,64]{2,1,0:T(8,128)(2,1)S(1)} %fusion.12) | data formatting | bytes 77824
  30.0 8.0 %all-to-all-start = ((bf16[16,2,608]{2,1,0:T(2,128)(2,1)}), bf16[16,2,608]{2,1,0:T(2,128)(2,1)S(1)}, u32[]{:S(2)}, u32[]{:S(2)}) async-start(bf16[16,2,608]{2,1,0:T(2,128)(2,1)} %reshape.261), calls=%async_computation | async-start | bytes 81920 | tf_op jit(solution)/shard_map/all_to_all | solution.py:158
  38.0 6.7 %all-to-all-done = bf16[16,2,608]{2,1,0:T(2,128)(2,1)S(1)} async-done(((bf16[16,2,608]{2,1,0:T(2,128)(2,1)}), bf16[16,2,608]{2,1,0:T(2,128)(2,1)S(1)}, u32[]{:S(2)}, u32[]{:S(2)}) %all-to-all-start) | async-done | bytes 38944 | tf_op jit(solution)/shard_map/all_to_all | solution.py:158
  44.7 0.1 reshape.262
  44.9 0.1 reshape.245
  45.0 0.1 fusion.20
  45.1 0.1 copy.42
  45.2 0.7 %multiply_reduce_fusion = (f32[288]{0:T(512)S(1)}, f32[288,64]{0,1:T(8,128)S(1)}) fusion(f32[288,64]{0,1:T(8,128)S(1)} %copy.42, f32[1,288,64]{1,2,0:T(8,128)S(1)} %copy-done.3, f32[288]{0:T(512)S(1)} %broadcast_subtract_fusion, f32[1,288,64]{1,2,0:T(8,128)S(1)} %copy-done.4, f32[288]{0:T(512)S(1)} %fusion.20, bf16[288,3072]{1,0:T(8,128)(2,1)S(1)} %fusion.4, ...), kind=kOutput, calls=%fused_computation.33 | convolution fusion | flops 113374944 | bytes 2461056 | tf_op jit(solution)/shard_map/dot_general | solution.py:179
  46.0 0.2 fusion.19
  46.2 0.5 fusion.15
  46.7 1.0 %reshape.239 = f32[64,8,2,192]{3,2,1,0:T(2,128)S(1)} reshape(f32[64,3072]{1,0:T(8,128)S(1)} %fusion.15) | data formatting | bytes 1572864 | tf_op jit(solution)/shard_map/reshape | solution.py:66
  47.7 1.1 %constant_dynamic-slice_fusion.7 = (f32[64,8,1,192]{3,2,1,0:T(1,128)S(1)}, f32[64,8,1,192]{3,2,1,0:T(1,128)S(1)}) fusion(f32[64,8,2,192]{3,2,1,0:T(2,128)S(1)} %reshape.239, s32[]{:T(128)S(6)} %select_n.31, s32[]{:T(128)S(6)} %select_n.33), kind=kLoop, calls=%fused_computation.58 | loop fusion | bytes 1572872 | tf_op jit(solution)/shard_map/jit(dynamic_index_in_dim)/dynamic_slice | solution.py:70
  48.8 0.2 copy.56
  48.9 0.3 reshape.241
  49.2 0.1 multiply_dynamic-update-slice_fusion
  49.4 0.1 collective-permute-start.2
  49.5 0.2 copy.57
  49.7 0.3 reshape.240
  50.0 1.3 %collective-permute-done.2 = f32[8,97,128]{2,1,0:T(8,128)S(1)} collective-permute-done((f32[8,97,128]{2,1,0:T(8,128)S(1)}, f32[8,97,128]{2,1,0:T(8,128)S(1)}, u32[]{:S(2)}, u32[]{:S(2)}) %collective-permute-start.2) | collective-permute-done | bytes 397344 | tf_op jit(solution)/shard_map/ppermute | solution.py:75
  51.3 0.1 copy.45
  51.4 0.3 constant_dynamic-slice_fusion.4
  51.7 0.4 collective-permute-start.5
  52.1 1.4 %collective-permute-start.3 = (f32[2,97,128]{2,0,1:T(2,128)S(1)}, f32[2,97,128]{2,0,1:T(2,128)S(1)}, u32[]{:S(2)}, u32[]{:S(2)}) collective-permute-start(f32[2,97,128]{2,0,1:T(2,128)S(1)} %bitcast.82), channel_id=1, source_target_pairs={{0,2},{1,3},{2,0},{3,1},{4,6},{5,7},{6,4},{7,5},{8,10},{9,11},{10,... | collective-permute-start | bytes 297992 | tf_op jit(solution)/shard_map/ppermute | solution.py:86
  53.5 1.7 %collective-permute-start.4 = (f32[2,97,128]{2,0,1:T(2,128)S(1)}, f32[2,97,128]{2,0,1:T(2,128)S(1)}, u32[]{:S(2)}, u32[]{:S(2)}) collective-permute-start(f32[2,97,128]{2,0,1:T(2,128)S(1)} %bitcast.81), channel_id=1, source_target_pairs={{0,4},{1,5},{2,6},{3,7},{4,0},{5,1},{6,2},{7,3},{8,12},{9,13},{10,... | collective-permute-start | bytes 297992 | tf_op jit(solution)/shard_map/ppermute | solution.py:86
  55.3 3.1 %collective-permute-done.5 = f32[2,97,128]{2,0,1:T(2,128)S(1)} collective-permute-done((f32[2,97,128]{2,0,1:T(2,128)S(1)}, f32[2,97,128]{2,0,1:T(2,128)S(1)}, u32[]{:S(2)}, u32[]{:S(2)}) %collective-permute-start.5) | collective-permute-done | bytes 99360 | tf_op jit(solution)/shard_map/ppermute | solution.py:86
  58.4 0.4 collective-permute-done.3
  58.9 0.1 add_add_fusion
  59.0 0.7 collective-permute-start.6
  59.7 5.0 %collective-permute-done.6 = f32[1,97,128]{2,0,1:T(1,128)S(1)} collective-permute-done((f32[1,97,128]{2,0,1:T(1,128)S(1)}, f32[1,97,128]{2,0,1:T(1,128)S(1)}, u32[]{:S(2)}, u32[]{:S(2)}) %collective-permute-start.6) | collective-permute-done | bytes 49696 | tf_op jit(solution)/shard_map/ppermute | solution.py:86
  64.7 0.1 dynamic-slice_add_fusion
  64.8 1.6 %collective-permute-start.7 = (f32[97,128]{1,0:T(8,128)S(1)}, f32[97,128]{1,0:T(8,128)S(1)}, u32[]{:S(2)}, u32[]{:S(2)}) collective-permute-start(f32[97,128]{1,0:T(8,128)S(1)} %bitcast.85), channel_id=1, source_target_pairs={{0,16},{16,0},{1,17},{17,1},{2,18},{18,2},{3,19},{19,3},{4,20},{20... | collective-permute-start | bytes 149000 | tf_op jit(solution)/shard_map/ppermute | solution.py:91
  66.4 0.7 %reshape.234 = bf16[1,16,1,768]{3,1,2,0:T(8,128)(2,1)} reshape(bf16[16,1,12,64]{3,2,0,1:T(8,128)(2,1)S(1)} %copy.38) | data formatting | bytes 49152 | tf_op jit(solution)/shard_map/reshape | solution.py:133
  67.1 1.9 %collective-permute-done.7 = f32[97,128]{1,0:T(8,128)S(1)} collective-permute-done((f32[97,128]{1,0:T(8,128)S(1)}, f32[97,128]{1,0:T(8,128)S(1)}, u32[]{:S(2)}, u32[]{:S(2)}) %collective-permute-start.7) | collective-permute-done | bytes 49696 | tf_op jit(solution)/shard_map/ppermute | solution.py:91
  69.0 0.6 constant_dynamic-slice_fusion
  69.6 0.7 %reshape.244 = f32[64,192]{1,0:T(8,128)} reshape(f32[96,128]{1,0:T(8,128)S(1)} %slice.29) | data formatting | bytes 98304 | tf_op jit(solution)/shard_map/reshape | solution.py:198
  (41 shorter events, 0.4 us)
Async XLA Ops:
  0.6 44.6 %copy-start = (bf16[3072,64]{0,1:T(8,128)(2,1)S(1)}, bf16[3072,64]{0,1:T(8,128)(2,1)}, u32[]{:S(2)}) copy-start(bf16[3072,64]{0,1:T(8,128)(2,1)} %param.21) | copy-start | bytes 1179652
  0.6 10.7 %copy-start.1 = (bf16[1,288,3072]{2,1,0:T(8,128)(2,1)S(1)}, bf16[1,288,3072]{2,1,0:T(8,128)(2,1)}, u32[]{:S(2)}) copy-start(bf16[1,288,3072]{2,1,0:T(8,128)(2,1)} %param.18) | copy-start | bytes 5308420
  1.9 13.7 %collective-permute-start.1 = (bf16[16,1,48,128]{3,2,1,0:T(8,128)(2,1)S(1)}, bf16[16,1,48,128]{3,2,1,0:T(8,128)(2,1)S(1)}, u32[]{:S(2)}, u32[]{:S(2)}) collective-permute-start(bf16[16,1,48,128]{3,2,1,0:T(8,128)(2,1)S(1)} %get-tuple-element.7), channel_id=1, source_target_pairs={{1,0},{2,1},{3,2},{4,3},{5,4},{6,5},{7,6},{8,7},{9,8},{10,9},{11,1... | collective-permute-start | bytes 589832 | tf_op jit(solution)/shard_map/ppermute | solution.py:123
  3.2 12.4 %collective-permute-start = (bf16[16,1,48,128]{3,2,1,0:T(8,128)(2,1)S(1)}, bf16[16,1,48,128]{3,2,1,0:T(8,128)(2,1)S(1)}, u32[]{:S(2)}, u32[]{:S(2)}) collective-permute-start(bf16[16,1,48,128]{3,2,1,0:T(8,128)(2,1)S(1)} %get-tuple-element.8), channel_id=1, source_target_pairs={{0,1},{1,2},{2,3},{3,4},{4,5},{5,6},{6,7},{7,8},{8,9},{9,10},{10,1... | collective-permute-start | bytes 589832 | tf_op jit(solution)/shard_map/ppermute | solution.py:122
  9.5 3.0 %copy-start.2 = (bf16[2048,64]{0,1:T(8,128)(2,1)S(1)}, bf16[2048,64]{0,1:T(8,128)(2,1)}, u32[]{:S(2)}) copy-start(bf16[2048,64]{0,1:T(8,128)(2,1)} %param.17) | copy-start | bytes 786436
  12.7 2.2 %copy-start.5 = (s32[1,4]{1,0:T(1,128)S(1)}, s32[1,4]{1,0:T(1,128)}, u32[]{:S(2)}) copy-start(s32[1,4]{1,0:T(1,128)} %param.12) | copy-start | bytes 52
  12.7 2.2 %copy-start.6 = (s32[1,4]{1,0:T(1,128)S(1)}, s32[1,4]{1,0:T(1,128)}, u32[]{:S(2)}) copy-start(s32[1,4]{1,0:T(1,128)} %param.14) | copy-start | bytes 52
  12.7 2.2 %copy-start.7 = (s32[1,4]{1,0:T(1,128)S(1)}, s32[1,4]{1,0:T(1,128)}, u32[]{:S(2)}) copy-start(s32[1,4]{1,0:T(1,128)} %param.13) | copy-start | bytes 52
  15.5 0.7 copy-start.8
  15.5 0.7 %copy-start.9 = (bf16[16,1,48,128]{3,2,1,0:T(8,128)(2,1)}, bf16[16,1,48,128]{3,2,1,0:T(8,128)(2,1)S(1)}, u32[]{:S(2)}) copy-start(bf16[16,1,48,128]{3,2,1,0:T(8,128)(2,1)S(1)} %collective-permute-done.top_ref) | copy-start | bytes 589828
  27.1 18.2 %copy-start.3 = (f32[1,288,64]{1,2,0:T(8,128)S(1)}, f32[1,288,64]{1,2,0:T(8,128)}, u32[]{:S(2)}) copy-start(f32[1,288,64]{1,2,0:T(8,128)} %param.19) | copy-start | bytes 221188
  27.1 18.2 %copy-start.4 = (f32[1,288,64]{1,2,0:T(8,128)S(1)}, f32[1,288,64]{1,2,0:T(8,128)}, u32[]{:S(2)}) copy-start(f32[1,288,64]{1,2,0:T(8,128)} %param.20) | copy-start | bytes 221188
  30.0 14.7 %all-to-all-start = ((bf16[16,2,608]{2,1,0:T(2,128)(2,1)}), bf16[16,2,608]{2,1,0:T(2,128)(2,1)S(1)}, u32[]{:S(2)}, u32[]{:S(2)}) async-start(bf16[16,2,608]{2,1,0:T(2,128)(2,1)} %reshape.261), calls=%async_computation | async-start | bytes 81920 | tf_op jit(solution)/shard_map/all_to_all | solution.py:158
  49.4 1.8 %collective-permute-start.2 = (f32[8,97,128]{2,1,0:T(8,128)S(1)}, f32[8,97,128]{2,1,0:T(8,128)S(1)}, u32[]{:S(2)}, u32[]{:S(2)}) collective-permute-start(f32[8,97,128]{2,1,0:T(8,128)S(1)} %pad_maximum_fusion), channel_id=1, source_target_pairs={{0,1},{1,0},{2,3},{3,2},{4,5},{5,4},{6,7},{7,6},{8,9},{9,8},{10,11... | collective-permute-start | bytes 1191944 | tf_op jit(solution)/shard_map/ppermute | solution.py:75
  51.7 6.7 %collective-permute-start.5 = (f32[2,97,128]{2,0,1:T(2,128)S(1)}, f32[2,97,128]{2,0,1:T(2,128)S(1)}, u32[]{:S(2)}, u32[]{:S(2)}) collective-permute-start(f32[2,97,128]{2,0,1:T(2,128)S(1)} %bitcast.83), channel_id=1, source_target_pairs={{0,6},{1,7},{2,4},{3,5},{4,2},{5,3},{6,0},{7,1},{8,14},{9,15},{10,... | collective-permute-start | bytes 297992 | tf_op jit(solution)/shard_map/ppermute | solution.py:86
  52.1 6.7 %collective-permute-start.3 = (f32[2,97,128]{2,0,1:T(2,128)S(1)}, f32[2,97,128]{2,0,1:T(2,128)S(1)}, u32[]{:S(2)}, u32[]{:S(2)}) collective-permute-start(f32[2,97,128]{2,0,1:T(2,128)S(1)} %bitcast.82), channel_id=1, source_target_pairs={{0,2},{1,3},{2,0},{3,1},{4,6},{5,7},{6,4},{7,5},{8,10},{9,11},{10,... | collective-permute-start | bytes 297992 | tf_op jit(solution)/shard_map/ppermute | solution.py:86
  53.5 5.3 %collective-permute-start.4 = (f32[2,97,128]{2,0,1:T(2,128)S(1)}, f32[2,97,128]{2,0,1:T(2,128)S(1)}, u32[]{:S(2)}, u32[]{:S(2)}) collective-permute-start(f32[2,97,128]{2,0,1:T(2,128)S(1)} %bitcast.81), channel_id=1, source_target_pairs={{0,4},{1,5},{2,6},{3,7},{4,0},{5,1},{6,2},{7,3},{8,12},{9,13},{10,... | collective-permute-start | bytes 297992 | tf_op jit(solution)/shard_map/ppermute | solution.py:86
  59.0 5.7 %collective-permute-start.6 = (f32[1,97,128]{2,0,1:T(1,128)S(1)}, f32[1,97,128]{2,0,1:T(1,128)S(1)}, u32[]{:S(2)}, u32[]{:S(2)}) collective-permute-start(f32[1,97,128]{2,0,1:T(1,128)S(1)} %constant_dynamic-slice_fusion.1), channel_id=1, source_target_pairs={{0,8},{1,9},{2,10},{3,11},{4,12},{5,13},{6,14},{7,15},{8,0},{9,1},... | collective-permute-start | bytes 149000 | tf_op jit(solution)/shard_map/ppermute | solution.py:86
  64.8 4.2 %collective-permute-start.7 = (f32[97,128]{1,0:T(8,128)S(1)}, f32[97,128]{1,0:T(8,128)S(1)}, u32[]{:S(2)}, u32[]{:S(2)}) collective-permute-start(f32[97,128]{1,0:T(8,128)S(1)} %bitcast.85), channel_id=1, source_target_pairs={{0,16},{16,0},{1,17},{17,1},{2,18},{18,2},{3,19},{19,3},{4,20},{20... | collective-permute-start | bytes 149000 | tf_op jit(solution)/shard_map/ppermute | solution.py:91

commit v15 on v12

--- a/solution.py
+++ b/solution.py
@@ -63,7 +63,10 @@
         return jnp.concatenate([part, loss_rows], axis=1)
 
     bit = me & 1
-    x = half(bit) + lax.ppermute(half(1 - bit), "seq", [(i, i ^ 1) for i in range(nseq)])
+    send = half(1 - bit)
+    got = lax.ppermute(send, "seq", [(i, i ^ 1) for i in range(nseq)])
+    halves, send = lax.optimization_barrier((halves, send))
+    x = half(bit) + got
     tail = x.shape[1:]
     low = 1
     for width in groups:

time: 64.9 us -> 64.4 us (level)
    dynamic_slice x3 -> x4, local copies, waits for them, and re-layouts: 1.42 us -> 1.44 us  [half(): part = lax.dynamic_index_in_dim(halves, bit, 2, keepdims=False)]
  transfers between devices with their start and end apart: 9 -> 9, of which waited for: 7 -> 7; matrix products, arithmetic and copies ran while one was open for 10% -> 11% of each run, Pallas kernels for 0% -> 0%
where the time goes in v15:
time: 64.4 us; the launch traced here: 64 us
  waiting for transfers between devices  19 us (30%)
  starting transfers between devices  18.6 us (29%)
  local copies, waits for them, and re-layouts  12.7 us (20%)
  matrix products  9.81 us (15%)
  other arithmetic  2.75 us (4%)
  between operations  1.15 us (2%)
    ppermute x4, waiting for transfers between devices, tree_reduce(): total = total + lax.ppermute(send, 'seq', pairs)  9.64 us
    all_to_all x1, starting transfers between devices, per_device(): lax.all_to_all(jnp.concatenate([outgoing, labels], axis=1), 'seq', split_...  8.64 us
    all_to_all x1, waiting for transfers between devices, per_device(): lax.all_to_all(jnp.concatenate([outgoing, labels], axis=1), 'seq', split_...  6.68 us
    conv_general_dilated x1, matrix products, causal_conv(): lax.conv_general_dilated(padded, kernel, (1, 1), 'VALID', dimension_numbe...  5.56 us
    unnamed x25, local copies, waits for them, and re-layouts  5.43 us
    ppermute x4, starting transfers between devices, tree_reduce(): total = total + lax.ppermute(send, 'seq', pairs)  3.96 us
    ppermute x1, starting transfers between devices, with_halo(): lax.ppermute(tail, axis, [(i, (i + 1) % count) for i in range(ends)])  3.06 us
    conv_general_dilated x1, matrix products, per_device(): lax.conv_general_dilated(cells, w_latent.reshape(4, 4, chans, LAT), (4, 4...  2.42 us
  transfers between devices with their start and end apart: 9, of which 7 were waited for; matrix products, arithmetic and copies ran while one was open for 11% of the time, Pallas kernels for 0%

profile of v15, /device:TPU:0, one launch (start us, length us, event | category | flops | bytes accessed | tf_op | source)
XLA Modules:
  0.0 64.0 jit_solution(6660918191457149720)
XLA Ops:
  0.6 0.0 copy-start
  0.7 1.7 %copy.47 = bf16[1,16,4,48,128]{4,1,3,2,0:T(8,128)(2,1)S(1)} copy(bf16[1,16,4,48,128]{4,3,2,1,0:T(8,128)(2,1)} %param.11) | data formatting | bytes 1572864 | tf_op args[0]
  2.4 0.0 copy-start.6
  2.4 0.8 %fusion.36 = (bf16[1,16,1,48,128]{4,1,3,2,0:T(8,128)(2,1)}, bf16[1,16,1,48,128]{4,1,3,2,0:T(8,128)(2,1)}) fusion(bf16[1,16,4,48,128]{4,1,3,2,0:T(8,128)(2,1)S(1)} %copy.47), kind=kLoop, calls=%fused_computation.92 | loop fusion | bytes 786432 | tf_op jit(solution)/shard_map/slice | solution.py:15
  3.2 3.1 %collective-permute-start = (bf16[1,16,1,48,128]{4,1,3,2,0:T(8,128)(2,1)}, bf16[1,16,1,48,128]{4,1,3,2,0:T(8,128)(2,1)}, u32[]{:S(2)}, u32[]{:S(2)}) collective-permute-start(bf16[1,16,1,48,128]{4,1,3,2,0:T(8,128)(2,1)} %get-tuple-element.7), channel_id=1, source_target_pairs={{0,1},{1,2},{2,3},{3,4},{4,5},{5,6},{6,7},{7,8},{8,9},{9,10},{10,1... | collective-permute-start | bytes 589832 | tf_op jit(solution)/shard_map/ppermute | solution.py:18
  6.2 1.3 %collective-permute-start.1 = (bf16[1,16,1,48,128]{4,1,3,2,0:T(8,128)(2,1)}, bf16[1,16,1,48,128]{4,1,3,2,0:T(8,128)(2,1)}, u32[]{:S(2)}, u32[]{:S(2)}) collective-permute-start(bf16[1,16,1,48,128]{4,1,3,2,0:T(8,128)(2,1)} %get-tuple-element.8), channel_id=1, source_target_pairs={{1,0},{2,1},{3,2},{4,3},{5,4},{6,5},{7,6},{8,7},{9,8},{10,9},{11,1... | collective-permute-start | bytes 589832 | tf_op jit(solution)/shard_map/ppermute | solution.py:20
  7.5 2.3 %copy.51 = bf16[3,3,3,128,128]{3,4,0,2,1:T(8,128)(2,1)} copy(bf16[3,3,3,128,128]{4,3,2,1,0:T(8,128)(2,1)} %param.16) | data formatting | bytes 1769472 | tf_op args[5]
  9.8 0.2 reduce-window.4
  10.0 0.1 convert_reduce_fusion.1
  10.1 0.1 select_reduce_fusion
  10.2 0.2 reshape.205
  10.4 0.2 fusion.12
  10.6 0.1 broadcast_in_dim.6
  10.6 0.1 reshape.222
  10.7 0.2 convolution_reduce_fusion
  11.0 0.1 reshape.225
  11.1 0.3 convert_reduce_fusion
  11.4 0.6 fusion.3
  12.0 0.5 copy-done.2
  12.5 0.7 %fusion.4 = bf16[288,3072]{1,0:T(8,128)(2,1)S(1)} fusion(bf16[1,288,3072]{2,1,0:T(8,128)(2,1)S(1)} %copy-done.2, f32[288]{0:T(512)S(1)} %add_rsqrt_fusion, f32[288]{0:T(512)S(1)} %broadcast_multiply_fusion), kind=kLoop, calls=%fused_computation.6 | loop fusion | flops 3538944 | bytes 3541248 | tf_op jit(solution)/shard_map/convert_element_type | solution.py:171
  13.3 5.6 %fusion.7 = f32[16,4,48,384]{3,0,2,1:T(8,128)S(1)} fusion(bf16[3,3,128,384]{2,3,1,0:T(8,128)(2,1)} %bitcast.83, bf16[1,16,1,48,128]{4,1,3,2,0:T(8,128)(2,1)} %collective-permute-done.1, bf16[1,16,4,48,128]{4,1,3,2,0:T(8,128)(2,1)S(1)} %copy.47, bf16[1,16,1,48,128]{4,1,3,2,0:T(8,128)(2,1)} %collective-permute-done), kind=kOutput, calls=%fused_computation.12 | convolution fusion | flops 2683699200 | bytes 6782976 | tf_op jit(solution)/shard_map/conv_general_dilated | solution.py:32
  18.9 0.1 slice.39
  19.0 0.1 slice.40
  19.1 2.4 %convolution_convert_fusion.1 = bf16[16,1,12,64]{3,0,2,1:T(8,128)(2,1)S(1)} fusion(f32[16,4,48,384]{3,0,2,1:T(8,128)S(1)} %fusion.7, f32[14,4,48,128]{3,0,2,1:T(8,128)S(1)} %slice.40, f32[15,4,48,128]{3,0,2,1:T(8,128)S(1)} %slice.39, f32[16]{0:T(128)S(1)} %get-tuple-element.14, f32[16]{0:T(128)S(1)} %get-tuple-element.13, ...), kind=kOutput, calls=%fused_computation.19 | convolution fusion | flops 54669312 | bytes 5792768 | tf_op jit(solution)/shard_map/conv_general_dilated | solution.py:118
  21.5 0.0 copy-start.5
  21.6 0.2 convolution_convert_fusion
  21.8 0.1 copy.55
  22.0 0.7 %reshape.234 = bf16[16,2,608]{2,1,0:T(2,128)(2,1)} reshape(bf16[16,19,64]{2,1,0:T(8,128)(2,1)S(1)} %fusion.19) | data formatting | bytes 77824
  22.8 8.6 %all-to-all-start = ((bf16[16,2,608]{2,1,0:T(2,128)(2,1)}), bf16[16,2,608]{2,1,0:T(2,128)(2,1)S(1)}, u32[]{:S(2)}, u32[]{:S(2)}) async-start(bf16[16,2,608]{2,1,0:T(2,128)(2,1)} %reshape.234), calls=%async_computation | async-start | bytes 81920 | tf_op jit(solution)/shard_map/all_to_all | solution.py:151
  31.4 6.7 %all-to-all-done = bf16[16,2,608]{2,1,0:T(2,128)(2,1)S(1)} async-done(((bf16[16,2,608]{2,1,0:T(2,128)(2,1)}), bf16[16,2,608]{2,1,0:T(2,128)(2,1)S(1)}, u32[]{:S(2)}, u32[]{:S(2)}) %all-to-all-start) | async-done | bytes 38944 | tf_op jit(solution)/shard_map/all_to_all | solution.py:151
  38.1 0.1 reshape.235
  38.3 0.1 reshape.218
  38.4 0.1 fusion.27
  38.5 0.1 copy.57
  38.7 0.7 %multiply_reduce_fusion = (f32[288]{0:T(512)S(1)}, f32[288,64]{0,1:T(8,128)S(1)}) fusion(f32[288,64]{0,1:T(8,128)S(1)} %copy.57, f32[1,288,64]{1,2,0:T(8,128)S(1)} %copy-done.4, f32[288]{0:T(512)S(1)} %broadcast_subtract_fusion, f32[1,288,64]{1,2,0:T(8,128)S(1)} %copy-done.5, f32[288]{0:T(512)S(1)} %fusion.27, bf16[288,3072]{1,0:T(8,128)(2,1)S(1)} %fusion.4, ...), kind=kOutput, calls=%fused_computation.42 | convolution fusion | flops 113374944 | bytes 2461056 | tf_op jit(solution)/shard_map/dot_general | solution.py:172
  39.4 0.2 fusion.26
  39.6 0.5 fusion.22
  40.1 1.0 %reshape.211 = f32[64,8,2,192]{3,2,1,0:T(2,128)S(1)} reshape(f32[64,3072]{1,0:T(8,128)S(1)} %fusion.22) | data formatting | bytes 1572864 | tf_op jit(solution)/shard_map/reshape | solution.py:57
  41.1 0.5 constant_dynamic-slice_fusion.7
  41.7 0.2 copy.74
  41.9 0.3 reshape.212
  42.2 0.1 multiply_dynamic-update-slice_fusion
  42.3 0.1 collective-permute-start.2
  42.4 0.6 constant_dynamic-slice_fusion.6
  43.0 0.2 copy.73
  43.1 0.3 reshape.213
  43.4 0.7 %collective-permute-done.2 = f32[8,97,128]{2,1,0:T(8,128)S(1)} collective-permute-done((f32[8,97,128]{2,1,0:T(8,128)S(1)}, f32[8,97,128]{2,1,0:T(8,128)S(1)}, u32[]{:S(2)}, u32[]{:S(2)}) %collective-permute-start.2) | collective-permute-done | bytes 397344 | tf_op jit(solution)/shard_map/ppermute | solution.py:67
  44.2 0.1 copy.60
  44.3 0.3 constant_dynamic-slice_fusion.4
  44.6 0.4 collective-permute-start.3
  45.0 0.6 collective-permute-start.4
  45.6 2.6 %collective-permute-start.5 = (f32[2,97,128]{2,0,1:T(2,128)S(1)}, f32[2,97,128]{2,0,1:T(2,128)S(1)}, u32[]{:S(2)}, u32[]{:S(2)}) collective-permute-start(f32[2,97,128]{2,0,1:T(2,128)S(1)} %bitcast.85), channel_id=1, source_target_pairs={{0,6},{1,7},{2,4},{3,5},{4,2},{5,3},{6,0},{7,1},{8,14},{9,15},{10,... | collective-permute-start | bytes 297992 | tf_op jit(solution)/shard_map/ppermute | solution.py:80
  48.2 1.4 %collective-permute-done.3 = f32[2,97,128]{2,0,1:T(2,128)S(1)} collective-permute-done((f32[2,97,128]{2,0,1:T(2,128)S(1)}, f32[2,97,128]{2,0,1:T(2,128)S(1)}, u32[]{:S(2)}, u32[]{:S(2)}) %collective-permute-start.3) | collective-permute-done | bytes 99360 | tf_op jit(solution)/shard_map/ppermute | solution.py:80
  49.6 1.1 %collective-permute-done.4 = f32[2,97,128]{2,0,1:T(2,128)S(1)} collective-permute-done((f32[2,97,128]{2,0,1:T(2,128)S(1)}, f32[2,97,128]{2,0,1:T(2,128)S(1)}, u32[]{:S(2)}, u32[]{:S(2)}) %collective-permute-start.4) | collective-permute-done | bytes 99360 | tf_op jit(solution)/shard_map/ppermute | solution.py:80
  50.6 2.2 %collective-permute-done.5 = f32[2,97,128]{2,0,1:T(2,128)S(1)} collective-permute-done((f32[2,97,128]{2,0,1:T(2,128)S(1)}, f32[2,97,128]{2,0,1:T(2,128)S(1)}, u32[]{:S(2)}, u32[]{:S(2)}) %collective-permute-start.5) | collective-permute-done | bytes 99360 | tf_op jit(solution)/shard_map/ppermute | solution.py:80
  52.9 0.1 add_add_fusion
  53.0 0.4 collective-permute-start.6
  53.4 5.0 %collective-permute-done.6 = f32[1,97,128]{2,0,1:T(1,128)S(1)} collective-permute-done((f32[1,97,128]{2,0,1:T(1,128)S(1)}, f32[1,97,128]{2,0,1:T(1,128)S(1)}, u32[]{:S(2)}, u32[]{:S(2)}) %collective-permute-start.6) | collective-permute-done | bytes 49696 | tf_op jit(solution)/shard_map/ppermute | solution.py:80
  58.4 0.1 dynamic-slice_add_fusion
  58.5 1.6 %collective-permute-start.7 = (f32[97,128]{1,0:T(8,128)S(1)}, f32[97,128]{1,0:T(8,128)S(1)}, u32[]{:S(2)}, u32[]{:S(2)}) collective-permute-start(f32[97,128]{1,0:T(8,128)S(1)} %bitcast.89), channel_id=1, source_target_pairs={{0,16},{16,0},{1,17},{17,1},{2,18},{18,2},{3,19},{19,3},{4,20},{20... | collective-permute-start | bytes 149000 | tf_op jit(solution)/shard_map/ppermute | solution.py:85
  60.0 0.7 %reshape.206 = bf16[1,16,1,768]{3,1,2,0:T(8,128)(2,1)} reshape(bf16[16,1,12,64]{3,2,0,1:T(8,128)(2,1)S(1)} %copy.53) | data formatting | bytes 49152 | tf_op jit(solution)/shard_map/reshape | solution.py:126
  60.7 1.9 %collective-permute-done.7 = f32[97,128]{1,0:T(8,128)S(1)} collective-permute-done((f32[97,128]{1,0:T(8,128)S(1)}, f32[97,128]{1,0:T(8,128)S(1)}, u32[]{:S(2)}, u32[]{:S(2)}) %collective-permute-start.7) | collective-permute-done | bytes 49696 | tf_op jit(solution)/shard_map/ppermute | solution.py:85
  62.7 0.7 %reshape.216 = f32[64,192]{1,0:T(8,128)} reshape(f32[96,128]{1,0:T(8,128)S(1)} %slice.44) | data formatting | bytes 98304 | tf_op jit(solution)/shard_map/reshape | solution.py:191
  63.4 0.6 constant_dynamic-slice_fusion
  (45 shorter events, 0.5 us)
Async XLA Ops:
  0.6 38.0 %copy-start = (bf16[3072,64]{0,1:T(8,128)(2,1)S(1)}, bf16[3072,64]{0,1:T(8,128)(2,1)}, u32[]{:S(2)}) copy-start(bf16[3072,64]{0,1:T(8,128)(2,1)} %param.21) | copy-start | bytes 1179652
  0.6 9.2 %copy-start.7 = (s32[1,4]{1,0:T(1,128)S(1)}, s32[1,4]{1,0:T(1,128)}, u32[]{:S(2)}) copy-start(s32[1,4]{1,0:T(1,128)} %param.12) | copy-start | bytes 52
  0.7 9.5 %copy-start.3 = (bf16[2048,64]{0,1:T(8,128)(2,1)S(1)}, bf16[2048,64]{0,1:T(8,128)(2,1)}, u32[]{:S(2)}) copy-start(bf16[2048,64]{0,1:T(8,128)(2,1)} %param.17) | copy-start | bytes 786436
  2.4 8.0 %copy-start.6 = (s32[1,1,192,1]{2,3,1,0:T(1,128)S(1)}, s32[1,1,192,1]{2,3,1,0:T(1,128)}, u32[]{:S(2)}) copy-start(s32[1,1,192,1]{2,3,1,0:T(1,128)} %param.15) | copy-start | bytes 2308
  2.4 8.7 %copy-start.1 = (bf16[1,288,3072]{2,1,0:T(8,128)(2,1)S(1)}, bf16[1,288,3072]{2,1,0:T(8,128)(2,1)}, u32[]{:S(2)}) copy-start(bf16[1,288,3072]{2,1,0:T(8,128)(2,1)} %param.18) | copy-start | bytes 5308420
  3.2 10.1 %collective-permute-start = (bf16[1,16,1,48,128]{4,1,3,2,0:T(8,128)(2,1)}, bf16[1,16,1,48,128]{4,1,3,2,0:T(8,128)(2,1)}, u32[]{:S(2)}, u32[]{:S(2)}) collective-permute-start(bf16[1,16,1,48,128]{4,1,3,2,0:T(8,128)(2,1)} %get-tuple-element.7), channel_id=1, source_target_pairs={{0,1},{1,2},{2,3},{3,4},{4,5},{5,6},{6,7},{7,8},{8,9},{9,10},{10,1... | collective-permute-start | bytes 589832 | tf_op jit(solution)/shard_map/ppermute | solution.py:18
  6.2 7.1 %collective-permute-start.1 = (bf16[1,16,1,48,128]{4,1,3,2,0:T(8,128)(2,1)}, bf16[1,16,1,48,128]{4,1,3,2,0:T(8,128)(2,1)}, u32[]{:S(2)}, u32[]{:S(2)}) collective-permute-start(bf16[1,16,1,48,128]{4,1,3,2,0:T(8,128)(2,1)} %get-tuple-element.8), channel_id=1, source_target_pairs={{1,0},{2,1},{3,2},{4,3},{5,4},{6,5},{7,6},{8,7},{9,8},{10,9},{11,1... | collective-permute-start | bytes 589832 | tf_op jit(solution)/shard_map/ppermute | solution.py:20
  11.1 1.5 %copy-start.2 = (bf16[1,288,3072]{2,1,0:T(8,128)(2,1)S(1)}, bf16[1,288,3072]{2,1,0:T(8,128)(2,1)}, u32[]{:S(2)}) copy-start(bf16[1,288,3072]{2,1,0:T(8,128)(2,1)} %param.18) | copy-start | bytes 5308420
  12.5 0.7 %copy-start.8 = (s32[1,4]{1,0:T(1,128)S(1)}, s32[1,4]{1,0:T(1,128)}, u32[]{:S(2)}) copy-start(s32[1,4]{1,0:T(1,128)} %param.14) | copy-start | bytes 52
  12.5 0.7 %copy-start.9 = (s32[1,4]{1,0:T(1,128)S(1)}, s32[1,4]{1,0:T(1,128)}, u32[]{:S(2)}) copy-start(s32[1,4]{1,0:T(1,128)} %param.13) | copy-start | bytes 52
  21.5 17.1 %copy-start.4 = (f32[1,288,64]{1,2,0:T(8,128)S(1)}, f32[1,288,64]{1,2,0:T(8,128)}, u32[]{:S(2)}) copy-start(f32[1,288,64]{1,2,0:T(8,128)} %param.19) | copy-start | bytes 221188
  21.5 17.1 %copy-start.5 = (f32[1,288,64]{1,2,0:T(8,128)S(1)}, f32[1,288,64]{1,2,0:T(8,128)}, u32[]{:S(2)}) copy-start(f32[1,288,64]{1,2,0:T(8,128)} %param.20) | copy-start | bytes 221188
  22.8 15.3 %all-to-all-start = ((bf16[16,2,608]{2,1,0:T(2,128)(2,1)}), bf16[16,2,608]{2,1,0:T(2,128)(2,1)S(1)}, u32[]{:S(2)}, u32[]{:S(2)}) async-start(bf16[16,2,608]{2,1,0:T(2,128)(2,1)} %reshape.234), calls=%async_computation | async-start | bytes 81920 | tf_op jit(solution)/shard_map/all_to_all | solution.py:151
  42.3 1.8 %collective-permute-start.2 = (f32[8,97,128]{2,1,0:T(8,128)S(1)}, f32[8,97,128]{2,1,0:T(8,128)S(1)}, u32[]{:S(2)}, u32[]{:S(2)}) collective-permute-start(f32[8,97,128]{2,1,0:T(8,128)S(1)} %pad_maximum_fusion.1), channel_id=1, source_target_pairs={{0,1},{1,0},{2,3},{3,2},{4,5},{5,4},{6,7},{7,6},{8,9},{9,8},{10,11... | collective-permute-start | bytes 1191944 | tf_op jit(solution)/shard_map/ppermute | solution.py:67
  44.6 4.9 %collective-permute-start.3 = (f32[2,97,128]{2,0,1:T(2,128)S(1)}, f32[2,97,128]{2,0,1:T(2,128)S(1)}, u32[]{:S(2)}, u32[]{:S(2)}) collective-permute-start(f32[2,97,128]{2,0,1:T(2,128)S(1)} %bitcast.87), channel_id=1, source_target_pairs={{0,2},{1,3},{2,0},{3,1},{4,6},{5,7},{6,4},{7,5},{8,10},{9,11},{10,... | collective-permute-start | bytes 297992 | tf_op jit(solution)/shard_map/ppermute | solution.py:80
  45.0 5.7 %collective-permute-start.4 = (f32[2,97,128]{2,0,1:T(2,128)S(1)}, f32[2,97,128]{2,0,1:T(2,128)S(1)}, u32[]{:S(2)}, u32[]{:S(2)}) collective-permute-start(f32[2,97,128]{2,0,1:T(2,128)S(1)} %bitcast.86), channel_id=1, source_target_pairs={{0,4},{1,5},{2,6},{3,7},{4,0},{5,1},{6,2},{7,3},{8,12},{9,13},{10,... | collective-permute-start | bytes 297992 | tf_op jit(solution)/shard_map/ppermute | solution.py:80
  45.6 7.3 %collective-permute-start.5 = (f32[2,97,128]{2,0,1:T(2,128)S(1)}, f32[2,97,128]{2,0,1:T(2,128)S(1)}, u32[]{:S(2)}, u32[]{:S(2)}) collective-permute-start(f32[2,97,128]{2,0,1:T(2,128)S(1)} %bitcast.85), channel_id=1, source_target_pairs={{0,6},{1,7},{2,4},{3,5},{4,2},{5,3},{6,0},{7,1},{8,14},{9,15},{10,... | collective-permute-start | bytes 297992 | tf_op jit(solution)/shard_map/ppermute | solution.py:80
  53.0 5.4 %collective-permute-start.6 = (f32[1,97,128]{2,0,1:T(1,128)S(1)}, f32[1,97,128]{2,0,1:T(1,128)S(1)}, u32[]{:S(2)}, u32[]{:S(2)}) collective-permute-start(f32[1,97,128]{2,0,1:T(1,128)S(1)} %constant_dynamic-slice_fusion.1), channel_id=1, source_target_pairs={{0,8},{1,9},{2,10},{3,11},{4,12},{5,13},{6,14},{7,15},{8,0},{9,1},... | collective-permute-start | bytes 149000 | tf_op jit(solution)/shard_map/ppermute | solution.py:80
  58.5 4.2 %collective-permute-start.7 = (f32[97,128]{1,0:T(8,128)S(1)}, f32[97,128]{1,0:T(8,128)S(1)}, u32[]{:S(2)}, u32[]{:S(2)}) collective-permute-start(f32[97,128]{1,0:T(8,128)S(1)} %bitcast.89), channel_id=1, source_target_pairs={{0,16},{16,0},{1,17},{17,1},{2,18},{18,2},{3,19},{19,3},{4,20},{20... | collective-permute-start | bytes 149000 | tf_op jit(solution)/shard_map/ppermute | solution.py:85

commit v16 on v15

--- a/solution.py
+++ b/solution.py
@@ -81,9 +81,10 @@
         x = total
         low += width
     x = x.reshape(tail)
+    group_sum = x
     for k in range(ndp.bit_length() - 1):
         x = x + lax.ppermute(x, "dp", [(i, i ^ (1 << k)) for i in range(ndp)])
-    return x
+    return x, group_sum
 
 
 def per_device(
@@ -184,12 +185,11 @@
     share = grad_t.shape[1] // nseq
     lanes = 128
     dense = LAT * share // lanes
-    assert ndp * CLIPS <= lanes and dense * lanes == LAT * share
-    place = lax.axis_index("dp") * CLIPS
-    loss_row = lax.dynamic_update_slice(jnp.zeros((lanes,), jnp.float32), partial_loss, (place,))
-    summed = tree_reduce(grad_t, loss_row, nseq, ndp)
+    assert dense * lanes == LAT * share
+    loss_row = jnp.pad(partial_loss, (0, lanes - CLIPS))
+    summed, group_sum = tree_reduce(grad_t, loss_row, nseq, ndp)
     grad_mine = summed[:dense].reshape(LAT, share).T
-    clip_loss = lax.dynamic_slice_in_dim(summed[dense], place, CLIPS).reshape(1, CLIPS)
+    clip_loss = group_sum[dense, :CLIPS].reshape(1, CLIPS)
     return (latent_out, clip_loss, grad_mine)
 
 

time: 64.4 us -> 63.7 us (0.989)
  transfers between devices with their start and end apart: 9 -> 9, of which waited for: 7 -> 7; matrix products, arithmetic and copies ran while one was open for 11% -> 12% of each run, Pallas kernels for 0% -> 0%
where the time goes in v16:
time: 63.7 us; the launch traced here: 63.3 us
  starting transfers between devices  18.6 us (29%)
  waiting for transfers between devices  18.4 us (29%)
  local copies, waits for them, and re-layouts  12.7 us (20%)
  matrix products  9.8 us (15%)
  other arithmetic  2.65 us (4%)
  between operations  1.15 us (2%)
    ppermute x4, waiting for transfers between devices, tree_reduce(): total = total + lax.ppermute(send, 'seq', pairs)  9.62 us
    all_to_all x1, starting transfers between devices, per_device(): lax.all_to_all(jnp.concatenate([outgoing, labels], axis=1), 'seq', split_...  8.64 us
    all_to_all x1, waiting for transfers between devices, per_device(): lax.all_to_all(jnp.concatenate([outgoing, labels], axis=1), 'seq', split_...  6.68 us
    conv_general_dilated x1, matrix products, causal_conv(): lax.conv_general_dilated(padded, kernel, (1, 1), 'VALID', dimension_numbe...  5.56 us
    unnamed x25, local copies, waits for them, and re-layouts  5.43 us
    ppermute x4, starting transfers between devices, tree_reduce(): total = total + lax.ppermute(send, 'seq', pairs)  3.97 us
    ppermute x1, starting transfers between devices, with_halo(): lax.ppermute(tail, axis, [(i, (i + 1) % count) for i in range(ends)])  3.06 us
    conv_general_dilated x1, matrix products, per_device(): lax.conv_general_dilated(cells, w_latent.reshape(4, 4, chans, LAT), (4, 4...  2.42 us
  transfers between devices with their start and end apart: 9, of which 7 were waited for; matrix products, arithmetic and copies ran while one was open for 12% of the time, Pallas kernels for 0%

profile of v16, /device:TPU:0, one launch (start us, length us, event | category | flops | bytes accessed | tf_op | source)
XLA Modules:
  0.0 63.3 jit_solution(13357861129442369879)
XLA Ops:
  0.6 0.0 copy-start
  0.7 1.7 %copy.47 = bf16[1,16,4,48,128]{4,1,3,2,0:T(8,128)(2,1)S(1)} copy(bf16[1,16,4,48,128]{4,3,2,1,0:T(8,128)(2,1)} %param.11) | data formatting | bytes 1572864 | tf_op args[0]
  2.4 0.8 %fusion.35 = (bf16[1,16,1,48,128]{4,1,3,2,0:T(8,128)(2,1)}, bf16[1,16,1,48,128]{4,1,3,2,0:T(8,128)(2,1)}) fusion(bf16[1,16,4,48,128]{4,1,3,2,0:T(8,128)(2,1)S(1)} %copy.47), kind=kLoop, calls=%fused_computation.90 | loop fusion | bytes 786432 | tf_op jit(solution)/shard_map/slice | solution.py:15
  3.2 3.1 %collective-permute-start = (bf16[1,16,1,48,128]{4,1,3,2,0:T(8,128)(2,1)}, bf16[1,16,1,48,128]{4,1,3,2,0:T(8,128)(2,1)}, u32[]{:S(2)}, u32[]{:S(2)}) collective-permute-start(bf16[1,16,1,48,128]{4,1,3,2,0:T(8,128)(2,1)} %get-tuple-element.7), channel_id=1, source_target_pairs={{0,1},{1,2},{2,3},{3,4},{4,5},{5,6},{6,7},{7,8},{8,9},{9,10},{10,1... | collective-permute-start | bytes 589832 | tf_op jit(solution)/shard_map/ppermute | solution.py:18
  6.2 1.3 %collective-permute-start.1 = (bf16[1,16,1,48,128]{4,1,3,2,0:T(8,128)(2,1)}, bf16[1,16,1,48,128]{4,1,3,2,0:T(8,128)(2,1)}, u32[]{:S(2)}, u32[]{:S(2)}) collective-permute-start(bf16[1,16,1,48,128]{4,1,3,2,0:T(8,128)(2,1)} %get-tuple-element.8), channel_id=1, source_target_pairs={{1,0},{2,1},{3,2},{4,3},{5,4},{6,5},{7,6},{8,7},{9,8},{10,9},{11,1... | collective-permute-start | bytes 589832 | tf_op jit(solution)/shard_map/ppermute | solution.py:20
  7.5 2.3 %copy.51 = bf16[3,3,3,128,128]{3,4,0,2,1:T(8,128)(2,1)} copy(bf16[3,3,3,128,128]{4,3,2,1,0:T(8,128)(2,1)} %param.16) | data formatting | bytes 1769472 | tf_op args[5]
  9.8 0.2 reduce-window.4
  10.0 0.1 convert_reduce_fusion.1
  10.1 0.1 select_reduce_fusion
  10.2 0.2 reshape.172
  10.4 0.2 fusion.12
  10.6 0.1 broadcast_in_dim.4
  10.6 0.1 reshape.189
  10.7 0.2 convolution_reduce_fusion
  11.0 0.1 reshape.192
  11.1 0.0 copy-start.2
  11.1 0.3 convert_reduce_fusion
  11.4 0.6 fusion.3
  12.0 0.5 copy-done.2
  12.5 0.7 %fusion.4 = bf16[288,3072]{1,0:T(8,128)(2,1)S(1)} fusion(bf16[1,288,3072]{2,1,0:T(8,128)(2,1)S(1)} %copy-done.2, f32[288]{0:T(512)S(1)} %add_rsqrt_fusion, f32[288]{0:T(512)S(1)} %broadcast_multiply_fusion), kind=kLoop, calls=%fused_computation.6 | loop fusion | flops 3538944 | bytes 3541248 | tf_op jit(solution)/shard_map/convert_element_type | solution.py:172
  13.3 5.6 %fusion.7 = f32[16,4,48,384]{3,0,2,1:T(8,128)S(1)} fusion(bf16[3,3,128,384]{2,3,1,0:T(8,128)(2,1)} %bitcast.81, bf16[1,16,1,48,128]{4,1,3,2,0:T(8,128)(2,1)} %collective-permute-done.1, bf16[1,16,4,48,128]{4,1,3,2,0:T(8,128)(2,1)S(1)} %copy.47, bf16[1,16,1,48,128]{4,1,3,2,0:T(8,128)(2,1)} %collective-permute-done), kind=kOutput, calls=%fused_computation.12 | convolution fusion | flops 2683699200 | bytes 6782976 | tf_op jit(solution)/shard_map/conv_general_dilated | solution.py:32
  18.9 0.1 slice.39
  19.0 0.1 slice.40
  19.1 2.4 %convolution_convert_fusion.1 = bf16[16,1,12,64]{3,0,2,1:T(8,128)(2,1)S(1)} fusion(f32[16,4,48,384]{3,0,2,1:T(8,128)S(1)} %fusion.7, f32[14,4,48,128]{3,0,2,1:T(8,128)S(1)} %slice.40, f32[15,4,48,128]{3,0,2,1:T(8,128)S(1)} %slice.39, f32[16]{0:T(128)S(1)} %get-tuple-element.14, f32[16]{0:T(128)S(1)} %get-tuple-element.13, ...), kind=kOutput, calls=%fused_computation.19 | convolution fusion | flops 54669312 | bytes 5792768 | tf_op jit(solution)/shard_map/conv_general_dilated | solution.py:119
  21.5 0.0 copy-start.4
  21.5 0.0 copy-start.5
  21.6 0.2 convolution_convert_fusion
  21.8 0.1 copy.55
  22.0 0.7 %reshape.201 = bf16[16,2,608]{2,1,0:T(2,128)(2,1)} reshape(bf16[16,19,64]{2,1,0:T(8,128)(2,1)S(1)} %fusion.19) | data formatting | bytes 77824
  22.8 8.6 %all-to-all-start = ((bf16[16,2,608]{2,1,0:T(2,128)(2,1)}), bf16[16,2,608]{2,1,0:T(2,128)(2,1)S(1)}, u32[]{:S(2)}, u32[]{:S(2)}) async-start(bf16[16,2,608]{2,1,0:T(2,128)(2,1)} %reshape.201), calls=%async_computation | async-start | bytes 81920 | tf_op jit(solution)/shard_map/all_to_all | solution.py:152
  31.4 6.7 %all-to-all-done = bf16[16,2,608]{2,1,0:T(2,128)(2,1)S(1)} async-done(((bf16[16,2,608]{2,1,0:T(2,128)(2,1)}), bf16[16,2,608]{2,1,0:T(2,128)(2,1)S(1)}, u32[]{:S(2)}, u32[]{:S(2)}) %all-to-all-start) | async-done | bytes 38944 | tf_op jit(solution)/shard_map/all_to_all | solution.py:152
  38.1 0.1 reshape.202
  38.3 0.1 reshape.185
  38.4 0.1 fusion.27
  38.5 0.1 copy.57
  38.7 0.7 %multiply_reduce_fusion = (f32[288]{0:T(512)S(1)}, f32[288,64]{0,1:T(8,128)S(1)}) fusion(f32[288,64]{0,1:T(8,128)S(1)} %copy.57, f32[1,288,64]{1,2,0:T(8,128)S(1)} %copy-done.4, f32[288]{0:T(512)S(1)} %broadcast_subtract_fusion, f32[1,288,64]{1,2,0:T(8,128)S(1)} %copy-done.5, f32[288]{0:T(512)S(1)} %fusion.27, bf16[288,3072]{1,0:T(8,128)(2,1)S(1)} %fusion.4, ...), kind=kOutput, calls=%fused_computation.42 | convolution fusion | flops 113374944 | bytes 2461056 | tf_op jit(solution)/shard_map/dot_general | solution.py:173
  39.4 0.2 fusion.26
  39.6 0.5 fusion.22
  40.1 1.0 %reshape.178 = f32[64,8,2,192]{3,2,1,0:T(2,128)S(1)} reshape(f32[64,3072]{1,0:T(8,128)S(1)} %fusion.22) | data formatting | bytes 1572864 | tf_op jit(solution)/shard_map/reshape | solution.py:57
  41.1 0.5 constant_dynamic-slice_fusion.6
  41.7 0.2 copy.72
  41.9 0.3 reshape.179
  42.2 0.1 collective-permute-start.2
  42.3 0.6 constant_dynamic-slice_fusion.5
  42.9 0.2 copy.71
  43.1 0.3 reshape.180
  43.3 0.7 %collective-permute-done.2 = f32[8,97,128]{2,1,0:T(8,128)S(1)} collective-permute-done((f32[8,97,128]{2,1,0:T(8,128)S(1)}, f32[8,97,128]{2,1,0:T(8,128)S(1)}, u32[]{:S(2)}, u32[]{:S(2)}) %collective-permute-start.2) | collective-permute-done | bytes 397344 | tf_op jit(solution)/shard_map/ppermute | solution.py:67
  44.1 0.1 copy.60
  44.2 0.3 constant_dynamic-slice_fusion.3
  44.5 0.4 collective-permute-start.3
  44.9 0.6 collective-permute-start.4
  45.5 2.6 %collective-permute-start.5 = (f32[2,97,128]{2,0,1:T(2,128)S(1)}, f32[2,97,128]{2,0,1:T(2,128)S(1)}, u32[]{:S(2)}, u32[]{:S(2)}) collective-permute-start(f32[2,97,128]{2,0,1:T(2,128)S(1)} %bitcast.86), channel_id=1, source_target_pairs={{0,6},{1,7},{2,4},{3,5},{4,2},{5,3},{6,0},{7,1},{8,14},{9,15},{10,... | collective-permute-start | bytes 297992 | tf_op jit(solution)/shard_map/ppermute | solution.py:80
  48.1 1.4 %collective-permute-done.3 = f32[2,97,128]{2,0,1:T(2,128)S(1)} collective-permute-done((f32[2,97,128]{2,0,1:T(2,128)S(1)}, f32[2,97,128]{2,0,1:T(2,128)S(1)}, u32[]{:S(2)}, u32[]{:S(2)}) %collective-permute-start.3) | collective-permute-done | bytes 99360 | tf_op jit(solution)/shard_map/ppermute | solution.py:80
  49.5 1.1 %collective-permute-done.4 = f32[2,97,128]{2,0,1:T(2,128)S(1)} collective-permute-done((f32[2,97,128]{2,0,1:T(2,128)S(1)}, f32[2,97,128]{2,0,1:T(2,128)S(1)}, u32[]{:S(2)}, u32[]{:S(2)}) %collective-permute-start.4) | collective-permute-done | bytes 99360 | tf_op jit(solution)/shard_map/ppermute | solution.py:80
  50.6 2.2 %collective-permute-done.5 = f32[2,97,128]{2,0,1:T(2,128)S(1)} collective-permute-done((f32[2,97,128]{2,0,1:T(2,128)S(1)}, f32[2,97,128]{2,0,1:T(2,128)S(1)}, u32[]{:S(2)}, u32[]{:S(2)}) %collective-permute-start.5) | collective-permute-done | bytes 99360 | tf_op jit(solution)/shard_map/ppermute | solution.py:80
  52.8 0.1 add_add_fusion
  52.9 0.4 collective-permute-start.6
  53.3 4.9 %collective-permute-done.6 = f32[1,97,128]{2,0,1:T(1,128)S(1)} collective-permute-done((f32[1,97,128]{2,0,1:T(1,128)S(1)}, f32[1,97,128]{2,0,1:T(1,128)S(1)}, u32[]{:S(2)}, u32[]{:S(2)}) %collective-permute-start.6) | collective-permute-done | bytes 49696 | tf_op jit(solution)/shard_map/ppermute | solution.py:80
  58.3 0.1 dynamic-slice_add_fusion
  58.4 1.6 %collective-permute-start.7 = (f32[97,128]{1,0:T(8,128)S(1)}, f32[97,128]{1,0:T(8,128)S(1)}, u32[]{:S(2)}, u32[]{:S(2)}) collective-permute-start(f32[97,128]{1,0:T(8,128)S(1)} %bitcast.83), channel_id=1, source_target_pairs={{0,16},{16,0},{1,17},{17,1},{2,18},{18,2},{3,19},{19,3},{4,20},{20... | collective-permute-start | bytes 149000 | tf_op jit(solution)/shard_map/ppermute | solution.py:86
  59.9 0.7 %reshape.173 = bf16[1,16,1,768]{3,1,2,0:T(8,128)(2,1)} reshape(bf16[16,1,12,64]{3,2,0,1:T(8,128)(2,1)S(1)} %copy.53) | data formatting | bytes 49152 | tf_op jit(solution)/shard_map/reshape | solution.py:127
  60.6 0.5 slice.43
  61.2 1.4 %collective-permute-done.7 = f32[97,128]{1,0:T(8,128)S(1)} collective-permute-done((f32[97,128]{1,0:T(8,128)S(1)}, f32[97,128]{1,0:T(8,128)S(1)}, u32[]{:S(2)}, u32[]{:S(2)}) %collective-permute-start.7) | collective-permute-done | bytes 49696 | tf_op jit(solution)/shard_map/ppermute | solution.py:86
  62.6 0.7 %reshape.183 = f32[64,192]{1,0:T(8,128)} reshape(f32[96,128]{1,0:T(8,128)S(1)} %slice_add_fusion.1) | data formatting | bytes 98304 | tf_op jit(solution)/shard_map/reshape | solution.py:191
  (43 shorter events, 0.4 us)
Async XLA Ops:
  0.6 38.0 %copy-start = (bf16[3072,64]{0,1:T(8,128)(2,1)S(1)}, bf16[3072,64]{0,1:T(8,128)(2,1)}, u32[]{:S(2)}) copy-start(bf16[3072,64]{0,1:T(8,128)(2,1)} %param.21) | copy-start | bytes 1179652
  0.6 9.2 %copy-start.7 = (s32[1,4]{1,0:T(1,128)S(1)}, s32[1,4]{1,0:T(1,128)}, u32[]{:S(2)}) copy-start(s32[1,4]{1,0:T(1,128)} %param.12) | copy-start | bytes 52
  0.7 9.5 %copy-start.3 = (bf16[2048,64]{0,1:T(8,128)(2,1)S(1)}, bf16[2048,64]{0,1:T(8,128)(2,1)}, u32[]{:S(2)}) copy-start(bf16[2048,64]{0,1:T(8,128)(2,1)} %param.17) | copy-start | bytes 786436
  2.4 8.0 %copy-start.6 = (s32[1,1,192,1]{2,3,1,0:T(1,128)S(1)}, s32[1,1,192,1]{2,3,1,0:T(1,128)}, u32[]{:S(2)}) copy-start(s32[1,1,192,1]{2,3,1,0:T(1,128)} %param.15) | copy-start | bytes 2308
  2.4 8.7 %copy-start.1 = (bf16[1,288,3072]{2,1,0:T(8,128)(2,1)S(1)}, bf16[1,288,3072]{2,1,0:T(8,128)(2,1)}, u32[]{:S(2)}) copy-start(bf16[1,288,3072]{2,1,0:T(8,128)(2,1)} %param.18) | copy-start | bytes 5308420
  3.2 10.1 %collective-permute-start = (bf16[1,16,1,48,128]{4,1,3,2,0:T(8,128)(2,1)}, bf16[1,16,1,48,128]{4,1,3,2,0:T(8,128)(2,1)}, u32[]{:S(2)}, u32[]{:S(2)}) collective-permute-start(bf16[1,16,1,48,128]{4,1,3,2,0:T(8,128)(2,1)} %get-tuple-element.7), channel_id=1, source_target_pairs={{0,1},{1,2},{2,3},{3,4},{4,5},{5,6},{6,7},{7,8},{8,9},{9,10},{10,1... | collective-permute-start | bytes 589832 | tf_op jit(solution)/shard_map/ppermute | solution.py:18
  6.2 7.1 %collective-permute-start.1 = (bf16[1,16,1,48,128]{4,1,3,2,0:T(8,128)(2,1)}, bf16[1,16,1,48,128]{4,1,3,2,0:T(8,128)(2,1)}, u32[]{:S(2)}, u32[]{:S(2)}) collective-permute-start(bf16[1,16,1,48,128]{4,1,3,2,0:T(8,128)(2,1)} %get-tuple-element.8), channel_id=1, source_target_pairs={{1,0},{2,1},{3,2},{4,3},{5,4},{6,5},{7,6},{8,7},{9,8},{10,9},{11,1... | collective-permute-start | bytes 589832 | tf_op jit(solution)/shard_map/ppermute | solution.py:20
  11.1 1.5 %copy-start.2 = (bf16[1,288,3072]{2,1,0:T(8,128)(2,1)S(1)}, bf16[1,288,3072]{2,1,0:T(8,128)(2,1)}, u32[]{:S(2)}) copy-start(bf16[1,288,3072]{2,1,0:T(8,128)(2,1)} %param.18) | copy-start | bytes 5308420
  12.5 0.7 %copy-start.8 = (s32[1,4]{1,0:T(1,128)S(1)}, s32[1,4]{1,0:T(1,128)}, u32[]{:S(2)}) copy-start(s32[1,4]{1,0:T(1,128)} %param.14) | copy-start | bytes 52
  12.5 0.7 %copy-start.9 = (s32[1,4]{1,0:T(1,128)S(1)}, s32[1,4]{1,0:T(1,128)}, u32[]{:S(2)}) copy-start(s32[1,4]{1,0:T(1,128)} %param.13) | copy-start | bytes 52
  21.5 17.1 %copy-start.4 = (f32[1,288,64]{1,2,0:T(8,128)S(1)}, f32[1,288,64]{1,2,0:T(8,128)}, u32[]{:S(2)}) copy-start(f32[1,288,64]{1,2,0:T(8,128)} %param.19) | copy-start | bytes 221188
  21.5 17.1 %copy-start.5 = (f32[1,288,64]{1,2,0:T(8,128)S(1)}, f32[1,288,64]{1,2,0:T(8,128)}, u32[]{:S(2)}) copy-start(f32[1,288,64]{1,2,0:T(8,128)} %param.20) | copy-start | bytes 221188
  22.8 15.3 %all-to-all-start = ((bf16[16,2,608]{2,1,0:T(2,128)(2,1)}), bf16[16,2,608]{2,1,0:T(2,128)(2,1)S(1)}, u32[]{:S(2)}, u32[]{:S(2)}) async-start(bf16[16,2,608]{2,1,0:T(2,128)(2,1)} %reshape.201), calls=%async_computation | async-start | bytes 81920 | tf_op jit(solution)/shard_map/all_to_all | solution.py:152
  42.2 1.8 %collective-permute-start.2 = (f32[8,97,128]{2,1,0:T(8,128)S(1)}, f32[8,97,128]{2,1,0:T(8,128)S(1)}, u32[]{:S(2)}, u32[]{:S(2)}) collective-permute-start(f32[8,97,128]{2,1,0:T(8,128)S(1)} %pad_maximum_fusion.1), channel_id=1, source_target_pairs={{0,1},{1,0},{2,3},{3,2},{4,5},{5,4},{6,7},{7,6},{8,9},{9,8},{10,11... | collective-permute-start | bytes 1191944 | tf_op jit(solution)/shard_map/ppermute | solution.py:67
  44.5 4.9 %collective-permute-start.3 = (f32[2,97,128]{2,0,1:T(2,128)S(1)}, f32[2,97,128]{2,0,1:T(2,128)S(1)}, u32[]{:S(2)}, u32[]{:S(2)}) collective-permute-start(f32[2,97,128]{2,0,1:T(2,128)S(1)} %bitcast.88), channel_id=1, source_target_pairs={{0,2},{1,3},{2,0},{3,1},{4,6},{5,7},{6,4},{7,5},{8,10},{9,11},{10,... | collective-permute-start | bytes 297992 | tf_op jit(solution)/shard_map/ppermute | solution.py:80
  44.9 5.7 %collective-permute-start.4 = (f32[2,97,128]{2,0,1:T(2,128)S(1)}, f32[2,97,128]{2,0,1:T(2,128)S(1)}, u32[]{:S(2)}, u32[]{:S(2)}) collective-permute-start(f32[2,97,128]{2,0,1:T(2,128)S(1)} %bitcast.87), channel_id=1, source_target_pairs={{0,4},{1,5},{2,6},{3,7},{4,0},{5,1},{6,2},{7,3},{8,12},{9,13},{10,... | collective-permute-start | bytes 297992 | tf_op jit(solution)/shard_map/ppermute | solution.py:80
  45.5 7.3 %collective-permute-start.5 = (f32[2,97,128]{2,0,1:T(2,128)S(1)}, f32[2,97,128]{2,0,1:T(2,128)S(1)}, u32[]{:S(2)}, u32[]{:S(2)}) collective-permute-start(f32[2,97,128]{2,0,1:T(2,128)S(1)} %bitcast.86), channel_id=1, source_target_pairs={{0,6},{1,7},{2,4},{3,5},{4,2},{5,3},{6,0},{7,1},{8,14},{9,15},{10,... | collective-permute-start | bytes 297992 | tf_op jit(solution)/shard_map/ppermute | solution.py:80
  52.9 5.4 %collective-permute-start.6 = (f32[1,97,128]{2,0,1:T(1,128)S(1)}, f32[1,97,128]{2,0,1:T(1,128)S(1)}, u32[]{:S(2)}, u32[]{:S(2)}) collective-permute-start(f32[1,97,128]{2,0,1:T(1,128)S(1)} %constant_dynamic-slice_fusion), channel_id=1, source_target_pairs={{0,8},{1,9},{2,10},{3,11},{4,12},{5,13},{6,14},{7,15},{8,0},{9,1},... | collective-permute-start | bytes 149000 | tf_op jit(solution)/shard_map/ppermute | solution.py:80
  58.4 4.2 %collective-permute-start.7 = (f32[97,128]{1,0:T(8,128)S(1)}, f32[97,128]{1,0:T(8,128)S(1)}, u32[]{:S(2)}, u32[]{:S(2)}) collective-permute-start(f32[97,128]{1,0:T(8,128)S(1)} %bitcast.83), channel_id=1, source_target_pairs={{0,16},{16,0},{1,17},{17,1},{2,18},{18,2},{3,19},{19,3},{4,20},{20... | collective-permute-start | bytes 149000 | tf_op jit(solution)/shard_map/ppermute | solution.py:86

commit v17 on v16

--- a/solution.py
+++ b/solution.py
@@ -74,7 +74,7 @@
         x = x.reshape((x.shape[0] // ways, ways) + tail)
         digit = (me >> low) & (ways - 1)
         total = lax.dynamic_index_in_dim(x, digit, 1, keepdims=False)
-        for step in range(1, ways):
+        for step in range(ways - 1, 0, -1):
             send = lax.dynamic_index_in_dim(x, digit ^ step, 1, keepdims=False)
             pairs = [(i, i ^ (step << low)) for i in range(nseq)]
             total = total + lax.ppermute(send, "seq", pairs)

time: 63.7 us -> 63.3 us (level)
  no operation moved by 1% of the time
where the time goes in v17:
time: 63.3 us; the launch traced here: 63 us
  starting transfers between devices  18.6 us (29%)
  waiting for transfers between devices  18.1 us (29%)
  local copies, waits for them, and re-layouts  12.7 us (20%)
  matrix products  9.8 us (15%)
  other arithmetic  2.65 us (4%)
  between operations  1.15 us (2%)
    ppermute x4, waiting for transfers between devices, tree_reduce(): total = total + lax.ppermute(send, 'seq', pairs)  9.29 us
    all_to_all x1, starting transfers between devices, per_device(): lax.all_to_all(jnp.concatenate([outgoing, labels], axis=1), 'seq', split_...  8.64 us
    all_to_all x1, waiting for transfers between devices, per_device(): lax.all_to_all(jnp.concatenate([outgoing, labels], axis=1), 'seq', split_...  6.68 us
    conv_general_dilated x1, matrix products, causal_conv(): lax.conv_general_dilated(padded, kernel, (1, 1), 'VALID', dimension_numbe...  5.56 us
    unnamed x25, local copies, waits for them, and re-layouts  5.43 us
    ppermute x4, starting transfers between devices, tree_reduce(): total = total + lax.ppermute(send, 'seq', pairs)  3.97 us
    ppermute x1, starting transfers between devices, with_halo(): lax.ppermute(tail, axis, [(i, (i + 1) % count) for i in range(ends)])  3.06 us
    conv_general_dilated x1, matrix products, per_device(): lax.conv_general_dilated(cells, w_latent.reshape(4, 4, chans, LAT), (4, 4...  2.42 us
  transfers between devices with their start and end apart: 9, of which 7 were waited for; matrix products, arithmetic and copies ran while one was open for 12% of the time, Pallas kernels for 0%

profile of v17, /device:TPU:0, one launch (start us, length us, event | category | flops | bytes accessed | tf_op | source)
XLA Modules:
  0.0 63.0 jit_solution(4182880397059377094)
XLA Ops:
  0.6 0.0 copy-start
  0.7 1.7 %copy.47 = bf16[1,16,4,48,128]{4,1,3,2,0:T(8,128)(2,1)S(1)} copy(bf16[1,16,4,48,128]{4,3,2,1,0:T(8,128)(2,1)} %param.11) | data formatting | bytes 1572864 | tf_op args[0]
  2.4 0.8 %fusion.35 = (bf16[1,16,1,48,128]{4,1,3,2,0:T(8,128)(2,1)}, bf16[1,16,1,48,128]{4,1,3,2,0:T(8,128)(2,1)}) fusion(bf16[1,16,4,48,128]{4,1,3,2,0:T(8,128)(2,1)S(1)} %copy.47), kind=kLoop, calls=%fused_computation.90 | loop fusion | bytes 786432 | tf_op jit(solution)/shard_map/slice | solution.py:15
  3.2 3.1 %collective-permute-start = (bf16[1,16,1,48,128]{4,1,3,2,0:T(8,128)(2,1)}, bf16[1,16,1,48,128]{4,1,3,2,0:T(8,128)(2,1)}, u32[]{:S(2)}, u32[]{:S(2)}) collective-permute-start(bf16[1,16,1,48,128]{4,1,3,2,0:T(8,128)(2,1)} %get-tuple-element.7), channel_id=1, source_target_pairs={{0,1},{1,2},{2,3},{3,4},{4,5},{5,6},{6,7},{7,8},{8,9},{9,10},{10,1... | collective-permute-start | bytes 589832 | tf_op jit(solution)/shard_map/ppermute | solution.py:18
  6.2 1.3 %collective-permute-start.1 = (bf16[1,16,1,48,128]{4,1,3,2,0:T(8,128)(2,1)}, bf16[1,16,1,48,128]{4,1,3,2,0:T(8,128)(2,1)}, u32[]{:S(2)}, u32[]{:S(2)}) collective-permute-start(bf16[1,16,1,48,128]{4,1,3,2,0:T(8,128)(2,1)} %get-tuple-element.8), channel_id=1, source_target_pairs={{1,0},{2,1},{3,2},{4,3},{5,4},{6,5},{7,6},{8,7},{9,8},{10,9},{11,1... | collective-permute-start | bytes 589832 | tf_op jit(solution)/shard_map/ppermute | solution.py:20
  7.5 2.3 %copy.51 = bf16[3,3,3,128,128]{3,4,0,2,1:T(8,128)(2,1)} copy(bf16[3,3,3,128,128]{4,3,2,1,0:T(8,128)(2,1)} %param.16) | data formatting | bytes 1769472 | tf_op args[5]
  9.8 0.2 reduce-window.4
  10.0 0.1 convert_reduce_fusion.1
  10.1 0.1 select_reduce_fusion
  10.2 0.2 reshape.172
  10.4 0.2 fusion.12
  10.6 0.1 broadcast_in_dim.4
  10.6 0.1 reshape.189
  10.7 0.2 convolution_reduce_fusion
  11.0 0.1 reshape.192
  11.1 0.0 copy-start.2
  11.1 0.3 convert_reduce_fusion
  11.4 0.6 fusion.3
  12.0 0.5 copy-done.2
  12.5 0.7 %fusion.4 = bf16[288,3072]{1,0:T(8,128)(2,1)S(1)} fusion(bf16[1,288,3072]{2,1,0:T(8,128)(2,1)S(1)} %copy-done.2, f32[288]{0:T(512)S(1)} %add_rsqrt_fusion, f32[288]{0:T(512)S(1)} %broadcast_multiply_fusion), kind=kLoop, calls=%fused_computation.6 | loop fusion | flops 3538944 | bytes 3541248 | tf_op jit(solution)/shard_map/convert_element_type | solution.py:172
  13.3 5.6 %fusion.7 = f32[16,4,48,384]{3,0,2,1:T(8,128)S(1)} fusion(bf16[3,3,128,384]{2,3,1,0:T(8,128)(2,1)} %bitcast.81, bf16[1,16,1,48,128]{4,1,3,2,0:T(8,128)(2,1)} %collective-permute-done.1, bf16[1,16,4,48,128]{4,1,3,2,0:T(8,128)(2,1)S(1)} %copy.47, bf16[1,16,1,48,128]{4,1,3,2,0:T(8,128)(2,1)} %collective-permute-done), kind=kOutput, calls=%fused_computation.12 | convolution fusion | flops 2683699200 | bytes 6782976 | tf_op jit(solution)/shard_map/conv_general_dilated | solution.py:32
  18.9 0.1 slice.39
  19.0 0.1 slice.40
  19.1 2.4 %convolution_convert_fusion.1 = bf16[16,1,12,64]{3,0,2,1:T(8,128)(2,1)S(1)} fusion(f32[16,4,48,384]{3,0,2,1:T(8,128)S(1)} %fusion.7, f32[14,4,48,128]{3,0,2,1:T(8,128)S(1)} %slice.40, f32[15,4,48,128]{3,0,2,1:T(8,128)S(1)} %slice.39, f32[16]{0:T(128)S(1)} %get-tuple-element.14, f32[16]{0:T(128)S(1)} %get-tuple-element.13, ...), kind=kOutput, calls=%fused_computation.19 | convolution fusion | flops 54669312 | bytes 5792768 | tf_op jit(solution)/shard_map/conv_general_dilated | solution.py:119
  21.5 0.0 copy-start.4
  21.5 0.0 copy-start.5
  21.6 0.2 convolution_convert_fusion
  21.8 0.1 copy.55
  22.0 0.7 %reshape.201 = bf16[16,2,608]{2,1,0:T(2,128)(2,1)} reshape(bf16[16,19,64]{2,1,0:T(8,128)(2,1)S(1)} %fusion.19) | data formatting | bytes 77824
  22.8 8.6 %all-to-all-start = ((bf16[16,2,608]{2,1,0:T(2,128)(2,1)}), bf16[16,2,608]{2,1,0:T(2,128)(2,1)S(1)}, u32[]{:S(2)}, u32[]{:S(2)}) async-start(bf16[16,2,608]{2,1,0:T(2,128)(2,1)} %reshape.201), calls=%async_computation | async-start | bytes 81920 | tf_op jit(solution)/shard_map/all_to_all | solution.py:152
  31.4 6.7 %all-to-all-done = bf16[16,2,608]{2,1,0:T(2,128)(2,1)S(1)} async-done(((bf16[16,2,608]{2,1,0:T(2,128)(2,1)}), bf16[16,2,608]{2,1,0:T(2,128)(2,1)S(1)}, u32[]{:S(2)}, u32[]{:S(2)}) %all-to-all-start) | async-done | bytes 38944 | tf_op jit(solution)/shard_map/all_to_all | solution.py:152
  38.1 0.1 reshape.202
  38.3 0.1 reshape.185
  38.4 0.1 fusion.27
  38.5 0.1 copy.57
  38.7 0.7 %multiply_reduce_fusion = (f32[288]{0:T(512)S(1)}, f32[288,64]{0,1:T(8,128)S(1)}) fusion(f32[288,64]{0,1:T(8,128)S(1)} %copy.57, f32[1,288,64]{1,2,0:T(8,128)S(1)} %copy-done.4, f32[288]{0:T(512)S(1)} %broadcast_subtract_fusion, f32[1,288,64]{1,2,0:T(8,128)S(1)} %copy-done.5, f32[288]{0:T(512)S(1)} %fusion.27, bf16[288,3072]{1,0:T(8,128)(2,1)S(1)} %fusion.4, ...), kind=kOutput, calls=%fused_computation.42 | convolution fusion | flops 113374944 | bytes 2461056 | tf_op jit(solution)/shard_map/dot_general | solution.py:173
  39.4 0.2 fusion.26
  39.6 0.5 fusion.22
  40.1 1.0 %reshape.178 = f32[64,8,2,192]{3,2,1,0:T(2,128)S(1)} reshape(f32[64,3072]{1,0:T(8,128)S(1)} %fusion.22) | data formatting | bytes 1572864 | tf_op jit(solution)/shard_map/reshape | solution.py:57
  41.1 0.5 constant_dynamic-slice_fusion.6
  41.7 0.2 copy.72
  41.9 0.3 reshape.179
  42.2 0.1 collective-permute-start.2
  42.3 0.6 constant_dynamic-slice_fusion.5
  42.9 0.2 copy.71
  43.1 0.3 reshape.180
  43.3 0.7 %collective-permute-done.2 = f32[8,97,128]{2,1,0:T(8,128)S(1)} collective-permute-done((f32[8,97,128]{2,1,0:T(8,128)S(1)}, f32[8,97,128]{2,1,0:T(8,128)S(1)}, u32[]{:S(2)}, u32[]{:S(2)}) %collective-permute-start.2) | collective-permute-done | bytes 397344 | tf_op jit(solution)/shard_map/ppermute | solution.py:67
  44.1 0.1 copy.60
  44.2 0.3 constant_dynamic-slice_fusion.3
  44.5 0.4 collective-permute-start.3
  44.9 1.4 %collective-permute-start.4 = (f32[2,97,128]{2,0,1:T(2,128)S(1)}, f32[2,97,128]{2,0,1:T(2,128)S(1)}, u32[]{:S(2)}, u32[]{:S(2)}) collective-permute-start(f32[2,97,128]{2,0,1:T(2,128)S(1)} %bitcast.87), channel_id=1, source_target_pairs={{0,4},{1,5},{2,6},{3,7},{4,0},{5,1},{6,2},{7,3},{8,12},{9,13},{10,... | collective-permute-start | bytes 297992 | tf_op jit(solution)/shard_map/ppermute | solution.py:80
  46.4 1.7 %collective-permute-start.5 = (f32[2,97,128]{2,0,1:T(2,128)S(1)}, f32[2,97,128]{2,0,1:T(2,128)S(1)}, u32[]{:S(2)}, u32[]{:S(2)}) collective-permute-start(f32[2,97,128]{2,0,1:T(2,128)S(1)} %bitcast.86), channel_id=1, source_target_pairs={{0,2},{1,3},{2,0},{3,1},{4,6},{5,7},{6,4},{7,5},{8,10},{9,11},{10,... | collective-permute-start | bytes 297992 | tf_op jit(solution)/shard_map/ppermute | solution.py:80
  48.1 3.1 %collective-permute-done.3 = f32[2,97,128]{2,0,1:T(2,128)S(1)} collective-permute-done((f32[2,97,128]{2,0,1:T(2,128)S(1)}, f32[2,97,128]{2,0,1:T(2,128)S(1)}, u32[]{:S(2)}, u32[]{:S(2)}) %collective-permute-start.3) | collective-permute-done | bytes 99360 | tf_op jit(solution)/shard_map/ppermute | solution.py:80
  51.2 0.1 collective-permute-done.4
  51.3 1.2 %collective-permute-done.5 = f32[2,97,128]{2,0,1:T(2,128)S(1)} collective-permute-done((f32[2,97,128]{2,0,1:T(2,128)S(1)}, f32[2,97,128]{2,0,1:T(2,128)S(1)}, u32[]{:S(2)}, u32[]{:S(2)}) %collective-permute-start.5) | collective-permute-done | bytes 99360 | tf_op jit(solution)/shard_map/ppermute | solution.py:80
  52.5 0.1 add_add_fusion
  52.6 0.4 collective-permute-start.6
  53.1 4.9 %collective-permute-done.6 = f32[1,97,128]{2,0,1:T(1,128)S(1)} collective-permute-done((f32[1,97,128]{2,0,1:T(1,128)S(1)}, f32[1,97,128]{2,0,1:T(1,128)S(1)}, u32[]{:S(2)}, u32[]{:S(2)}) %collective-permute-start.6) | collective-permute-done | bytes 49696 | tf_op jit(solution)/shard_map/ppermute | solution.py:80
  58.0 0.1 dynamic-slice_add_fusion
  58.0 1.6 %collective-permute-start.7 = (f32[97,128]{1,0:T(8,128)S(1)}, f32[97,128]{1,0:T(8,128)S(1)}, u32[]{:S(2)}, u32[]{:S(2)}) collective-permute-start(f32[97,128]{1,0:T(8,128)S(1)} %bitcast.83), channel_id=1, source_target_pairs={{0,16},{16,0},{1,17},{17,1},{2,18},{18,2},{3,19},{19,3},{4,20},{20... | collective-permute-start | bytes 149000 | tf_op jit(solution)/shard_map/ppermute | solution.py:86
  59.6 0.7 %reshape.173 = bf16[1,16,1,768]{3,1,2,0:T(8,128)(2,1)} reshape(bf16[16,1,12,64]{3,2,0,1:T(8,128)(2,1)S(1)} %copy.53) | data formatting | bytes 49152 | tf_op jit(solution)/shard_map/reshape | solution.py:127
  60.3 0.5 slice.43
  60.8 1.4 %collective-permute-done.7 = f32[97,128]{1,0:T(8,128)S(1)} collective-permute-done((f32[97,128]{1,0:T(8,128)S(1)}, f32[97,128]{1,0:T(8,128)S(1)}, u32[]{:S(2)}, u32[]{:S(2)}) %collective-permute-start.7) | collective-permute-done | bytes 49696 | tf_op jit(solution)/shard_map/ppermute | solution.py:86
  62.3 0.7 %reshape.183 = f32[64,192]{1,0:T(8,128)} reshape(f32[96,128]{1,0:T(8,128)S(1)} %slice_add_fusion.1) | data formatting | bytes 98304 | tf_op jit(solution)/shard_map/reshape | solution.py:191
  (43 shorter events, 0.4 us)
Async XLA Ops:
  0.6 38.0 %copy-start = (bf16[3072,64]{0,1:T(8,128)(2,1)S(1)}, bf16[3072,64]{0,1:T(8,128)(2,1)}, u32[]{:S(2)}) copy-start(bf16[3072,64]{0,1:T(8,128)(2,1)} %param.21) | copy-start | bytes 1179652
  0.6 9.2 %copy-start.7 = (s32[1,4]{1,0:T(1,128)S(1)}, s32[1,4]{1,0:T(1,128)}, u32[]{:S(2)}) copy-start(s32[1,4]{1,0:T(1,128)} %param.12) | copy-start | bytes 52
  0.7 9.5 %copy-start.3 = (bf16[2048,64]{0,1:T(8,128)(2,1)S(1)}, bf16[2048,64]{0,1:T(8,128)(2,1)}, u32[]{:S(2)}) copy-start(bf16[2048,64]{0,1:T(8,128)(2,1)} %param.17) | copy-start | bytes 786436
  2.4 8.0 %copy-start.6 = (s32[1,1,192,1]{2,3,1,0:T(1,128)S(1)}, s32[1,1,192,1]{2,3,1,0:T(1,128)}, u32[]{:S(2)}) copy-start(s32[1,1,192,1]{2,3,1,0:T(1,128)} %param.15) | copy-start | bytes 2308
  2.4 8.7 %copy-start.1 = (bf16[1,288,3072]{2,1,0:T(8,128)(2,1)S(1)}, bf16[1,288,3072]{2,1,0:T(8,128)(2,1)}, u32[]{:S(2)}) copy-start(bf16[1,288,3072]{2,1,0:T(8,128)(2,1)} %param.18) | copy-start | bytes 5308420
  3.2 10.1 %collective-permute-start = (bf16[1,16,1,48,128]{4,1,3,2,0:T(8,128)(2,1)}, bf16[1,16,1,48,128]{4,1,3,2,0:T(8,128)(2,1)}, u32[]{:S(2)}, u32[]{:S(2)}) collective-permute-start(bf16[1,16,1,48,128]{4,1,3,2,0:T(8,128)(2,1)} %get-tuple-element.7), channel_id=1, source_target_pairs={{0,1},{1,2},{2,3},{3,4},{4,5},{5,6},{6,7},{7,8},{8,9},{9,10},{10,1... | collective-permute-start | bytes 589832 | tf_op jit(solution)/shard_map/ppermute | solution.py:18
  6.2 7.1 %collective-permute-start.1 = (bf16[1,16,1,48,128]{4,1,3,2,0:T(8,128)(2,1)}, bf16[1,16,1,48,128]{4,1,3,2,0:T(8,128)(2,1)}, u32[]{:S(2)}, u32[]{:S(2)}) collective-permute-start(bf16[1,16,1,48,128]{4,1,3,2,0:T(8,128)(2,1)} %get-tuple-element.8), channel_id=1, source_target_pairs={{1,0},{2,1},{3,2},{4,3},{5,4},{6,5},{7,6},{8,7},{9,8},{10,9},{11,1... | collective-permute-start | bytes 589832 | tf_op jit(solution)/shard_map/ppermute | solution.py:20
  11.1 1.5 %copy-start.2 = (bf16[1,288,3072]{2,1,0:T(8,128)(2,1)S(1)}, bf16[1,288,3072]{2,1,0:T(8,128)(2,1)}, u32[]{:S(2)}) copy-start(bf16[1,288,3072]{2,1,0:T(8,128)(2,1)} %param.18) | copy-start | bytes 5308420
  12.5 0.7 %copy-start.8 = (s32[1,4]{1,0:T(1,128)S(1)}, s32[1,4]{1,0:T(1,128)}, u32[]{:S(2)}) copy-start(s32[1,4]{1,0:T(1,128)} %param.14) | copy-start | bytes 52
  12.5 0.7 %copy-start.9 = (s32[1,4]{1,0:T(1,128)S(1)}, s32[1,4]{1,0:T(1,128)}, u32[]{:S(2)}) copy-start(s32[1,4]{1,0:T(1,128)} %param.13) | copy-start | bytes 52
  21.5 17.1 %copy-start.4 = (f32[1,288,64]{1,2,0:T(8,128)S(1)}, f32[1,288,64]{1,2,0:T(8,128)}, u32[]{:S(2)}) copy-start(f32[1,288,64]{1,2,0:T(8,128)} %param.19) | copy-start | bytes 221188
  21.5 17.1 %copy-start.5 = (f32[1,288,64]{1,2,0:T(8,128)S(1)}, f32[1,288,64]{1,2,0:T(8,128)}, u32[]{:S(2)}) copy-start(f32[1,288,64]{1,2,0:T(8,128)} %param.20) | copy-start | bytes 221188
  22.8 15.3 %all-to-all-start = ((bf16[16,2,608]{2,1,0:T(2,128)(2,1)}), bf16[16,2,608]{2,1,0:T(2,128)(2,1)S(1)}, u32[]{:S(2)}, u32[]{:S(2)}) async-start(bf16[16,2,608]{2,1,0:T(2,128)(2,1)} %reshape.201), calls=%async_computation | async-start | bytes 81920 | tf_op jit(solution)/shard_map/all_to_all | solution.py:152
  42.2 1.8 %collective-permute-start.2 = (f32[8,97,128]{2,1,0:T(8,128)S(1)}, f32[8,97,128]{2,1,0:T(8,128)S(1)}, u32[]{:S(2)}, u32[]{:S(2)}) collective-permute-start(f32[8,97,128]{2,1,0:T(8,128)S(1)} %pad_maximum_fusion.1), channel_id=1, source_target_pairs={{0,1},{1,0},{2,3},{3,2},{4,5},{5,4},{6,7},{7,6},{8,9},{9,8},{10,11... | collective-permute-start | bytes 1191944 | tf_op jit(solution)/shard_map/ppermute | solution.py:67
  44.5 6.7 %collective-permute-start.3 = (f32[2,97,128]{2,0,1:T(2,128)S(1)}, f32[2,97,128]{2,0,1:T(2,128)S(1)}, u32[]{:S(2)}, u32[]{:S(2)}) collective-permute-start(f32[2,97,128]{2,0,1:T(2,128)S(1)} %bitcast.88), channel_id=1, source_target_pairs={{0,6},{1,7},{2,4},{3,5},{4,2},{5,3},{6,0},{7,1},{8,14},{9,15},{10,... | collective-permute-start | bytes 297992 | tf_op jit(solution)/shard_map/ppermute | solution.py:80
  44.9 6.4 %collective-permute-start.4 = (f32[2,97,128]{2,0,1:T(2,128)S(1)}, f32[2,97,128]{2,0,1:T(2,128)S(1)}, u32[]{:S(2)}, u32[]{:S(2)}) collective-permute-start(f32[2,97,128]{2,0,1:T(2,128)S(1)} %bitcast.87), channel_id=1, source_target_pairs={{0,4},{1,5},{2,6},{3,7},{4,0},{5,1},{6,2},{7,3},{8,12},{9,13},{10,... | collective-permute-start | bytes 297992 | tf_op jit(solution)/shard_map/ppermute | solution.py:80
  46.4 6.1 %collective-permute-start.5 = (f32[2,97,128]{2,0,1:T(2,128)S(1)}, f32[2,97,128]{2,0,1:T(2,128)S(1)}, u32[]{:S(2)}, u32[]{:S(2)}) collective-permute-start(f32[2,97,128]{2,0,1:T(2,128)S(1)} %bitcast.86), channel_id=1, source_target_pairs={{0,2},{1,3},{2,0},{3,1},{4,6},{5,7},{6,4},{7,5},{8,10},{9,11},{10,... | collective-permute-start | bytes 297992 | tf_op jit(solution)/shard_map/ppermute | solution.py:80
  52.6 5.3 %collective-permute-start.6 = (f32[1,97,128]{2,0,1:T(1,128)S(1)}, f32[1,97,128]{2,0,1:T(1,128)S(1)}, u32[]{:S(2)}, u32[]{:S(2)}) collective-permute-start(f32[1,97,128]{2,0,1:T(1,128)S(1)} %constant_dynamic-slice_fusion), channel_id=1, source_target_pairs={{0,8},{1,9},{2,10},{3,11},{4,12},{5,13},{6,14},{7,15},{8,0},{9,1},... | collective-permute-start | bytes 149000 | tf_op jit(solution)/shard_map/ppermute | solution.py:80
  58.0 4.2 %collective-permute-start.7 = (f32[97,128]{1,0:T(8,128)S(1)}, f32[97,128]{1,0:T(8,128)S(1)}, u32[]{:S(2)}, u32[]{:S(2)}) collective-permute-start(f32[97,128]{1,0:T(8,128)S(1)} %bitcast.83), channel_id=1, source_target_pairs={{0,16},{16,0},{1,17},{17,1},{2,18},{18,2},{3,19},{19,3},{4,20},{20... | collective-permute-start | bytes 149000 | tf_op jit(solution)/shard_map/ppermute | solution.py:86

commit v18 on v17

--- a/solution.py
+++ b/solution.py
@@ -138,16 +138,12 @@
     dest = owners * capacity + rank
     select = (dest[None, :] == jnp.arange(slots, dtype=jnp.int32)[:, None]).astype(jnp.bfloat16)
     tok_clip = jnp.repeat(clip_of, tok_rows * tok_cols).astype(jnp.float32) + 1.0
-    outgoing = (
-        jnp.dot(select, tokens, preferred_element_type=jnp.float32)
-        .astype(jnp.bfloat16)
-        .reshape(nseq, capacity, LAT)
-    )
-    labels = (
-        jnp.dot(select, tok_clip.astype(jnp.bfloat16)[:, None], preferred_element_type=jnp.float32)
-        .astype(jnp.bfloat16)
-        .reshape(nseq, 1, capacity)
-    )
+    outgoing = jnp.dot(select, tokens, preferred_element_type=jnp.float32).reshape(
+        nseq, capacity, LAT
+    )
+    labels = jnp.dot(
+        select, tok_clip.astype(jnp.bfloat16)[:, None], preferred_element_type=jnp.float32
+    ).reshape(nseq, 1, capacity)
     labels = jnp.pad(labels, ((0, 0), (0, 0), (0, LAT - capacity)))
     arrived = lax.all_to_all(
         jnp.concatenate([outgoing, labels], axis=1), "seq", split_axis=0, concat_axis=0, tiled=True

time: 63.3 us -> 64.6 us (1.021)
  other arithmetic: 2.65 us -> 3.44 us
    all_to_all x0 -> x1, other arithmetic: none -> 0.84 us  [per_device(): lax.all_to_all(jnp.concatenate([outgoing, labels], axis=1), 'seq', split_...]
    unnamed x25 -> x27, local copies, waits for them, and re-layouts: 5.43 us -> 5.5 us
  transfers between devices with their start and end apart: 9 -> 9, of which waited for: 7 -> 6; matrix products, arithmetic and copies ran while one was open for 12% -> 12% of each run, Pallas kernels for 0% -> 0%
where the time goes in v18:
time: 64.6 us; the launch traced here: 64.2 us
  waiting for transfers between devices  18.6 us (29%)
  starting transfers between devices  18.4 us (28%)
  local copies, waits for them, and re-layouts  13 us (20%)
  matrix products  9.65 us (15%)
  other arithmetic  3.44 us (5%)
  between operations  1.13 us (2%)
    ppermute x4, waiting for transfers between devices, tree_reduce(): total = total + lax.ppermute(send, 'seq', pairs)  9.34 us
    all_to_all x1, starting transfers between devices, per_device(): lax.all_to_all(jnp.concatenate([outgoing, labels], axis=1), 'seq', split_...  8.63 us
    all_to_all x1, waiting for transfers between devices, per_device(): lax.all_to_all(jnp.concatenate([outgoing, labels], axis=1), 'seq', split_...  7.08 us
    unnamed x27, local copies, waits for them, and re-layouts  5.5 us
    conv_general_dilated x1, matrix products, causal_conv(): lax.conv_general_dilated(padded, kernel, (1, 1), 'VALID', dimension_numbe...  5.21 us
    ppermute x4, starting transfers between devices, tree_reduce(): total = total + lax.ppermute(send, 'seq', pairs)  3.78 us
    ppermute x1, starting transfers between devices, with_halo(): lax.ppermute(tail, axis, [(i, (i + 1) % count) for i in range(ends)])  3.08 us
    conv_general_dilated x1, matrix products, per_device(): lax.conv_general_dilated(cells, w_latent.reshape(4, 4, chans, LAT), (4, 4...  2.42 us
  transfers between devices with their start and end apart: 9, of which 6 were waited for; matrix products, arithmetic and copies ran while one was open for 12% of the time, Pallas kernels for 0%

profile of v18, /device:TPU:0, one launch (start us, length us, event | category | flops | bytes accessed | tf_op | source)
XLA Modules:
  0.0 64.2 jit_solution(13403925448001215483)
XLA Ops:
  0.6 0.0 copy-start
  0.7 1.7 %copy.46 = bf16[1,16,4,48,128]{4,1,3,2,0:T(8,128)(2,1)S(1)} copy(bf16[1,16,4,48,128]{4,3,2,1,0:T(8,128)(2,1)} %param.11) | data formatting | bytes 1572864 | tf_op args[0]
  2.4 0.0 copy-start.7
  2.4 0.0 copy-start.1
  2.4 0.8 %fusion.38 = (bf16[1,16,1,48,128]{4,1,3,2,0:T(8,128)(2,1)}, bf16[1,16,1,48,128]{4,1,3,2,0:T(8,128)(2,1)}) fusion(bf16[1,16,4,48,128]{4,1,3,2,0:T(8,128)(2,1)S(1)} %copy.46), kind=kLoop, calls=%fused_computation.92 | loop fusion | bytes 786432 | tf_op jit(solution)/shard_map/slice | solution.py:15
  3.2 3.1 %collective-permute-start = (bf16[1,16,1,48,128]{4,1,3,2,0:T(8,128)(2,1)}, bf16[1,16,1,48,128]{4,1,3,2,0:T(8,128)(2,1)}, u32[]{:S(2)}, u32[]{:S(2)}) collective-permute-start(bf16[1,16,1,48,128]{4,1,3,2,0:T(8,128)(2,1)} %get-tuple-element.7), channel_id=1, source_target_pairs={{0,1},{1,2},{2,3},{3,4},{4,5},{5,6},{6,7},{7,8},{8,9},{9,10},{10,1... | collective-permute-start | bytes 589832 | tf_op jit(solution)/shard_map/ppermute | solution.py:18
  6.3 1.3 %collective-permute-start.1 = (bf16[1,16,1,48,128]{4,1,3,2,0:T(8,128)(2,1)}, bf16[1,16,1,48,128]{4,1,3,2,0:T(8,128)(2,1)}, u32[]{:S(2)}, u32[]{:S(2)}) collective-permute-start(bf16[1,16,1,48,128]{4,1,3,2,0:T(8,128)(2,1)} %get-tuple-element.8), channel_id=1, source_target_pairs={{1,0},{2,1},{3,2},{4,3},{5,4},{6,5},{7,6},{8,7},{9,8},{10,9},{11,1... | collective-permute-start | bytes 589832 | tf_op jit(solution)/shard_map/ppermute | solution.py:20
  7.6 2.3 %copy.50 = bf16[3,3,3,128,128]{3,4,0,2,1:T(8,128)(2,1)} copy(bf16[3,3,3,128,128]{4,3,2,1,0:T(8,128)(2,1)} %param.16) | data formatting | bytes 1769472 | tf_op args[5]
  9.8 0.2 reduce-window.4
  10.0 0.1 convert_reduce_fusion.1
  10.1 0.1 select_reduce_fusion
  10.2 0.2 reshape.197
  10.4 0.2 fusion.12
  10.6 0.1 broadcast_in_dim.4
  10.7 0.1 reshape.212
  10.8 0.3 convert_reduce_fusion
  11.1 0.6 fusion.3
  11.8 0.5 copy-done.2
  12.3 0.7 %fusion.4 = bf16[288,3072]{1,0:T(8,128)(2,1)S(1)} fusion(bf16[1,288,3072]{2,1,0:T(8,128)(2,1)S(1)} %copy-done.2, f32[288]{0:T(512)S(1)} %add_rsqrt_fusion, f32[288]{0:T(512)S(1)} %broadcast_multiply_fusion), kind=kLoop, calls=%fused_computation.6 | loop fusion | flops 3538944 | bytes 3541248 | tf_op jit(solution)/shard_map/convert_element_type | solution.py:168
  13.0 0.3 convolution_bitcast_fusion
  13.3 0.0 collective-permute-done
  13.4 0.1 copy-done.3
  13.5 5.2 %fusion.7 = f32[16,4,48,384]{3,0,2,1:T(8,128)S(1)} fusion(bf16[3,3,128,384]{2,3,1,0:T(8,128)(2,1)S(1)} %bitcast.88, bf16[1,16,1,48,128]{4,1,3,2,0:T(8,128)(2,1)} %collective-permute-done.1, bf16[1,16,4,48,128]{4,1,3,2,0:T(8,128)(2,1)S(1)} %copy.46, bf16[1,16,1,48,128]{4,1,3,2,0:T(8,128)(2,1)} %collective-permute-done), kind=kOutput, calls=%fused_computation.12 | convolution fusion | flops 2683699200 | bytes 6782976 | tf_op jit(solution)/shard_map/conv_general_dilated | solution.py:32
  18.7 0.1 slice.39
  18.8 0.1 slice.40
  18.9 2.4 %convolution_convert_fusion = bf16[16,1,12,64]{3,0,2,1:T(8,128)(2,1)S(1)} fusion(f32[16,4,48,384]{3,0,2,1:T(8,128)S(1)} %fusion.7, f32[14,4,48,128]{3,0,2,1:T(8,128)S(1)} %slice.40, f32[15,4,48,128]{3,0,2,1:T(8,128)S(1)} %slice.39, f32[16]{0:T(128)S(1)} %get-tuple-element.14, f32[16]{0:T(128)S(1)} %get-tuple-element.13, ...), kind=kOutput, calls=%fused_computation.18 | convolution fusion | flops 54669312 | bytes 5792768 | tf_op jit(solution)/shard_map/conv_general_dilated | solution.py:119
  21.4 0.3 fusion.15
  21.7 0.8 %reshape.222 = f32[16,1,1216]{2,1,0:T(1,128)} reshape(f32[16,19,64]{2,1,0:T(8,128)S(1)} %select_maximum_fusion) | data formatting | bytes 155648
  22.5 8.6 %all-to-all-start = ((f32[16,1,1216]{2,1,0:T(1,128)}), f32[16,1,1216]{2,1,0:T(1,128)S(1)}, u32[]{:S(2)}, u32[]{:S(2)}) async-start(f32[16,1,1216]{2,1,0:T(1,128)} %reshape.222), calls=%async_computation | async-start | bytes 163840 | tf_op jit(solution)/shard_map/all_to_all | solution.py:148
  31.1 7.1 %all-to-all-done = f32[16,1,1216]{2,1,0:T(1,128)S(1)} async-done(((f32[16,1,1216]{2,1,0:T(1,128)}), f32[16,1,1216]{2,1,0:T(1,128)S(1)}, u32[]{:S(2)}, u32[]{:S(2)}) %all-to-all-start) | async-done | bytes 77856 | tf_op jit(solution)/shard_map/all_to_all | solution.py:148
  38.2 0.5 broadcast.217
  38.7 0.8 %reduce.5 = f32[16,1216]{1,0:T(8,128)S(1)} reduce(f32[16,1,1216]{2,1,0:T(1,128)S(1)} %all-to-all-done, f32[]{:T(128)} %broadcast.217), dimensions={1}, to_apply=%all_to_all.3.reduce_sub_computation | reduce | bytes 155652 | tf_op jit(solution)/shard_map/all_to_all | solution.py:148
  39.6 0.1 reshape.223
  39.7 0.1 eq.82
  39.8 0.1 fusion.30
  39.9 0.1 copy.55
  40.1 0.7 %multiply_reduce_fusion = (f32[288]{0:T(512)S(1)}, f32[288,64]{0,1:T(8,128)S(1)}) fusion(f32[288,64]{0,1:T(8,128)S(1)} %copy.55, f32[1,288,64]{1,2,0:T(8,128)S(1)} %copy-done.5, f32[288]{0:T(512)S(1)} %broadcast_subtract_fusion, f32[1,288,64]{1,2,0:T(8,128)S(1)} %copy-done.6, f32[288]{0:T(512)S(1)} %fusion.30, bf16[288,3072]{1,0:T(8,128)(2,1)S(1)} %fusion.4, ...), kind=kOutput, calls=%fused_computation.43 | convolution fusion | flops 113374944 | bytes 2461056 | tf_op jit(solution)/shard_map/dot_general | solution.py:169
  40.8 0.2 fusion.29
  41.0 0.5 fusion.25
  41.5 1.0 %reshape.202 = f32[64,8,2,192]{3,2,1,0:T(2,128)S(1)} reshape(f32[64,3072]{1,0:T(8,128)S(1)} %fusion.25) | data formatting | bytes 1572864 | tf_op jit(solution)/shard_map/reshape | solution.py:57
  42.5 0.5 constant_dynamic-slice_fusion.6
  43.1 0.2 copy.73
  43.2 0.3 reshape.203
  43.6 0.1 collective-permute-start.2
  43.7 0.6 constant_dynamic-slice_fusion.5
  44.3 0.2 copy.72
  44.4 0.3 reshape.204
  44.7 0.7 %collective-permute-done.2 = f32[8,97,128]{2,1,0:T(8,128)S(1)} collective-permute-done((f32[8,97,128]{2,1,0:T(8,128)S(1)}, f32[8,97,128]{2,1,0:T(8,128)S(1)}, u32[]{:S(2)}, u32[]{:S(2)}) %collective-permute-start.2) | collective-permute-done | bytes 397344 | tf_op jit(solution)/shard_map/ppermute | solution.py:67
  45.5 0.1 copy.58
  45.6 0.3 constant_dynamic-slice_fusion.3
  45.9 0.2 collective-permute-start.3
  46.1 1.3 %collective-permute-start.4 = (f32[2,97,128]{2,0,1:T(2,128)S(1)}, f32[2,97,128]{2,0,1:T(2,128)S(1)}, u32[]{:S(2)}, u32[]{:S(2)}) collective-permute-start(f32[2,97,128]{2,0,1:T(2,128)S(1)} %bitcast.95), channel_id=1, source_target_pairs={{0,4},{1,5},{2,6},{3,7},{4,0},{5,1},{6,2},{7,3},{8,12},{9,13},{10,... | collective-permute-start | bytes 297992 | tf_op jit(solution)/shard_map/ppermute | solution.py:80
  47.5 2.0 %collective-permute-start.5 = (f32[2,97,128]{2,0,1:T(2,128)S(1)}, f32[2,97,128]{2,0,1:T(2,128)S(1)}, u32[]{:S(2)}, u32[]{:S(2)}) collective-permute-start(f32[2,97,128]{2,0,1:T(2,128)S(1)} %bitcast.94), channel_id=1, source_target_pairs={{0,2},{1,3},{2,0},{3,1},{4,6},{5,7},{6,4},{7,5},{8,10},{9,11},{10,... | collective-permute-start | bytes 297992 | tf_op jit(solution)/shard_map/ppermute | solution.py:80
  49.5 3.1 %collective-permute-done.3 = f32[2,97,128]{2,0,1:T(2,128)S(1)} collective-permute-done((f32[2,97,128]{2,0,1:T(2,128)S(1)}, f32[2,97,128]{2,0,1:T(2,128)S(1)}, u32[]{:S(2)}, u32[]{:S(2)}) %collective-permute-start.3) | collective-permute-done | bytes 99360 | tf_op jit(solution)/shard_map/ppermute | solution.py:80
  52.6 1.3 %collective-permute-done.5 = f32[2,97,128]{2,0,1:T(2,128)S(1)} collective-permute-done((f32[2,97,128]{2,0,1:T(2,128)S(1)}, f32[2,97,128]{2,0,1:T(2,128)S(1)}, u32[]{:S(2)}, u32[]{:S(2)}) %collective-permute-start.5) | collective-permute-done | bytes 99360 | tf_op jit(solution)/shard_map/ppermute | solution.py:80
  53.9 0.1 add_add_fusion
  54.0 0.2 collective-permute-start.6
  54.3 4.9 %collective-permute-done.6 = f32[1,97,128]{2,0,1:T(1,128)S(1)} collective-permute-done((f32[1,97,128]{2,0,1:T(1,128)S(1)}, f32[1,97,128]{2,0,1:T(1,128)S(1)}, u32[]{:S(2)}, u32[]{:S(2)}) %collective-permute-start.6) | collective-permute-done | bytes 49696 | tf_op jit(solution)/shard_map/ppermute | solution.py:80
  59.2 0.1 dynamic-slice_add_fusion
  59.3 1.6 %collective-permute-start.7 = (f32[97,128]{1,0:T(8,128)S(1)}, f32[97,128]{1,0:T(8,128)S(1)}, u32[]{:S(2)}, u32[]{:S(2)}) collective-permute-start(f32[97,128]{1,0:T(8,128)S(1)} %bitcast.91), channel_id=1, source_target_pairs={{0,16},{16,0},{1,17},{17,1},{2,18},{18,2},{3,19},{19,3},{4,20},{20... | collective-permute-start | bytes 149000 | tf_op jit(solution)/shard_map/ppermute | solution.py:86
  60.8 0.7 %reshape.198 = bf16[1,16,1,768]{3,1,2,0:T(8,128)(2,1)} reshape(bf16[16,1,12,64]{3,2,0,1:T(8,128)(2,1)S(1)} %copy.52) | data formatting | bytes 49152 | tf_op jit(solution)/shard_map/reshape | solution.py:127
  61.6 0.5 slice.43
  62.1 1.4 %collective-permute-done.7 = f32[97,128]{1,0:T(8,128)S(1)} collective-permute-done((f32[97,128]{1,0:T(8,128)S(1)}, f32[97,128]{1,0:T(8,128)S(1)}, u32[]{:S(2)}, u32[]{:S(2)}) %collective-permute-start.7) | collective-permute-done | bytes 49696 | tf_op jit(solution)/shard_map/ppermute | solution.py:86
  63.5 0.7 %reshape.207 = f32[64,192]{1,0:T(8,128)} reshape(f32[96,128]{1,0:T(8,128)S(1)} %slice_add_fusion.1) | data formatting | bytes 98304 | tf_op jit(solution)/shard_map/reshape | solution.py:187
  (44 shorter events, 0.4 us)
Async XLA Ops:
  0.6 39.4 %copy-start = (bf16[3072,64]{0,1:T(8,128)(2,1)S(1)}, bf16[3072,64]{0,1:T(8,128)(2,1)}, u32[]{:S(2)}) copy-start(bf16[3072,64]{0,1:T(8,128)(2,1)} %param.21) | copy-start | bytes 1179652
  0.6 9.2 %copy-start.8 = (s32[1,4]{1,0:T(1,128)S(1)}, s32[1,4]{1,0:T(1,128)}, u32[]{:S(2)}) copy-start(s32[1,4]{1,0:T(1,128)} %param.12) | copy-start | bytes 52
  0.7 9.6 %copy-start.4 = (bf16[2048,64]{0,1:T(8,128)(2,1)S(1)}, bf16[2048,64]{0,1:T(8,128)(2,1)}, u32[]{:S(2)}) copy-start(bf16[2048,64]{0,1:T(8,128)(2,1)} %param.17) | copy-start | bytes 786436
  2.4 8.0 %copy-start.7 = (s32[1,1,192,1]{2,3,1,0:T(1,128)S(1)}, s32[1,1,192,1]{2,3,1,0:T(1,128)}, u32[]{:S(2)}) copy-start(s32[1,1,192,1]{2,3,1,0:T(1,128)} %param.15) | copy-start | bytes 2308
  2.4 8.4 %copy-start.1 = (bf16[1,288,3072]{2,1,0:T(8,128)(2,1)S(1)}, bf16[1,288,3072]{2,1,0:T(8,128)(2,1)}, u32[]{:S(2)}) copy-start(bf16[1,288,3072]{2,1,0:T(8,128)(2,1)} %param.18) | copy-start | bytes 5308420
  3.2 10.2 %collective-permute-start = (bf16[1,16,1,48,128]{4,1,3,2,0:T(8,128)(2,1)}, bf16[1,16,1,48,128]{4,1,3,2,0:T(8,128)(2,1)}, u32[]{:S(2)}, u32[]{:S(2)}) collective-permute-start(bf16[1,16,1,48,128]{4,1,3,2,0:T(8,128)(2,1)} %get-tuple-element.7), channel_id=1, source_target_pairs={{0,1},{1,2},{2,3},{3,4},{4,5},{5,6},{6,7},{7,8},{8,9},{9,10},{10,1... | collective-permute-start | bytes 589832 | tf_op jit(solution)/shard_map/ppermute | solution.py:18
  6.3 7.1 %collective-permute-start.1 = (bf16[1,16,1,48,128]{4,1,3,2,0:T(8,128)(2,1)}, bf16[1,16,1,48,128]{4,1,3,2,0:T(8,128)(2,1)}, u32[]{:S(2)}, u32[]{:S(2)}) collective-permute-start(bf16[1,16,1,48,128]{4,1,3,2,0:T(8,128)(2,1)} %get-tuple-element.8), channel_id=1, source_target_pairs={{1,0},{2,1},{3,2},{4,3},{5,4},{6,5},{7,6},{8,7},{9,8},{10,9},{11,1... | collective-permute-start | bytes 589832 | tf_op jit(solution)/shard_map/ppermute | solution.py:20
  10.8 1.5 %copy-start.2 = (bf16[1,288,3072]{2,1,0:T(8,128)(2,1)S(1)}, bf16[1,288,3072]{2,1,0:T(8,128)(2,1)}, u32[]{:S(2)}) copy-start(bf16[1,288,3072]{2,1,0:T(8,128)(2,1)} %param.18) | copy-start | bytes 5308420
  12.3 0.7 %copy-start.9 = (s32[1,4]{1,0:T(1,128)S(1)}, s32[1,4]{1,0:T(1,128)}, u32[]{:S(2)}) copy-start(s32[1,4]{1,0:T(1,128)} %param.14) | copy-start | bytes 52
  12.3 0.7 %copy-start.10 = (s32[1,4]{1,0:T(1,128)S(1)}, s32[1,4]{1,0:T(1,128)}, u32[]{:S(2)}) copy-start(s32[1,4]{1,0:T(1,128)} %param.13) | copy-start | bytes 52
  12.3 1.2 %copy-start.3 = (bf16[3,3,3,128,128]{3,4,0,2,1:T(8,128)(2,1)S(1)}, bf16[3,3,3,128,128]{3,4,0,2,1:T(8,128)(2,1)}, u32[]{:S(2)}) copy-start(bf16[3,3,3,128,128]{3,4,0,2,1:T(8,128)(2,1)} %copy.50) | copy-start | bytes 2654212
  21.3 18.7 %copy-start.5 = (f32[1,288,64]{1,2,0:T(8,128)S(1)}, f32[1,288,64]{1,2,0:T(8,128)}, u32[]{:S(2)}) copy-start(f32[1,288,64]{1,2,0:T(8,128)} %param.19) | copy-start | bytes 221188
  21.3 18.7 %copy-start.6 = (f32[1,288,64]{1,2,0:T(8,128)S(1)}, f32[1,288,64]{1,2,0:T(8,128)}, u32[]{:S(2)}) copy-start(f32[1,288,64]{1,2,0:T(8,128)} %param.20) | copy-start | bytes 221188
  22.5 15.7 %all-to-all-start = ((f32[16,1,1216]{2,1,0:T(1,128)}), f32[16,1,1216]{2,1,0:T(1,128)S(1)}, u32[]{:S(2)}, u32[]{:S(2)}) async-start(f32[16,1,1216]{2,1,0:T(1,128)} %reshape.222), calls=%async_computation | async-start | bytes 163840 | tf_op jit(solution)/shard_map/all_to_all | solution.py:148
  43.6 1.8 %collective-permute-start.2 = (f32[8,97,128]{2,1,0:T(8,128)S(1)}, f32[8,97,128]{2,1,0:T(8,128)S(1)}, u32[]{:S(2)}, u32[]{:S(2)}) collective-permute-start(f32[8,97,128]{2,1,0:T(8,128)S(1)} %pad_maximum_fusion.1), channel_id=1, source_target_pairs={{0,1},{1,0},{2,3},{3,2},{4,5},{5,4},{6,7},{7,6},{8,9},{9,8},{10,11... | collective-permute-start | bytes 1191944 | tf_op jit(solution)/shard_map/ppermute | solution.py:67
  45.9 6.7 %collective-permute-start.3 = (f32[2,97,128]{2,0,1:T(2,128)S(1)}, f32[2,97,128]{2,0,1:T(2,128)S(1)}, u32[]{:S(2)}, u32[]{:S(2)}) collective-permute-start(f32[2,97,128]{2,0,1:T(2,128)S(1)} %bitcast.96), channel_id=1, source_target_pairs={{0,6},{1,7},{2,4},{3,5},{4,2},{5,3},{6,0},{7,1},{8,14},{9,15},{10,... | collective-permute-start | bytes 297992 | tf_op jit(solution)/shard_map/ppermute | solution.py:80
  46.1 6.5 %collective-permute-start.4 = (f32[2,97,128]{2,0,1:T(2,128)S(1)}, f32[2,97,128]{2,0,1:T(2,128)S(1)}, u32[]{:S(2)}, u32[]{:S(2)}) collective-permute-start(f32[2,97,128]{2,0,1:T(2,128)S(1)} %bitcast.95), channel_id=1, source_target_pairs={{0,4},{1,5},{2,6},{3,7},{4,0},{5,1},{6,2},{7,3},{8,12},{9,13},{10,... | collective-permute-start | bytes 297992 | tf_op jit(solution)/shard_map/ppermute | solution.py:80
  47.5 6.4 %collective-permute-start.5 = (f32[2,97,128]{2,0,1:T(2,128)S(1)}, f32[2,97,128]{2,0,1:T(2,128)S(1)}, u32[]{:S(2)}, u32[]{:S(2)}) collective-permute-start(f32[2,97,128]{2,0,1:T(2,128)S(1)} %bitcast.94), channel_id=1, source_target_pairs={{0,2},{1,3},{2,0},{3,1},{4,6},{5,7},{6,4},{7,5},{8,10},{9,11},{10,... | collective-permute-start | bytes 297992 | tf_op jit(solution)/shard_map/ppermute | solution.py:80
  54.0 5.2 %collective-permute-start.6 = (f32[1,97,128]{2,0,1:T(1,128)S(1)}, f32[1,97,128]{2,0,1:T(1,128)S(1)}, u32[]{:S(2)}, u32[]{:S(2)}) collective-permute-start(f32[1,97,128]{2,0,1:T(1,128)S(1)} %constant_dynamic-slice_fusion), channel_id=1, source_target_pairs={{0,8},{1,9},{2,10},{3,11},{4,12},{5,13},{6,14},{7,15},{8,0},{9,1},... | collective-permute-start | bytes 149000 | tf_op jit(solution)/shard_map/ppermute | solution.py:80
  59.3 4.2 %collective-permute-start.7 = (f32[97,128]{1,0:T(8,128)S(1)}, f32[97,128]{1,0:T(8,128)S(1)}, u32[]{:S(2)}, u32[]{:S(2)}) collective-permute-start(f32[97,128]{1,0:T(8,128)S(1)} %bitcast.91), channel_id=1, source_target_pairs={{0,16},{16,0},{1,17},{17,1},{2,18},{18,2},{3,19},{19,3},{4,20},{20... | collective-permute-start | bytes 149000 | tf_op jit(solution)/shard_map/ppermute | solution.py:86
